TPU v7x, 32 devices: a whole 2x2x4 slice. The times are simulated.
32 devices in a mesh: dp: 8 (over z, y), tensor: 4 (over x, core).
Axes of the slice: x: 2, y: 2, z: 4, core: 2. Of those that a mesh axis runs over, the one named last changes fastest.
Arguments:
- pre_hidden: bfloat16 [8192, 2048], P(('dp', 'tensor')), may hold values from -6 to 6
- dec_hidden: bfloat16 [16, 2048], P('dp'), may hold values from -6 to 6
- norm_gain: bfloat16 [2048], replicated, may hold values from 0.5 to 1.5
- norm_shift: bfloat16 [2048], replicated, may hold values from -3 to 3
- qkv_weight: bfloat16 [2048, 6144], P(None, 'tensor'), may hold values from -0.125 to 0.125
- qkv_bias: bfloat16 [6144], P('tensor'), may hold values from -3 to 3
- out_weight: bfloat16 [2048, 2048], P('tensor'), may hold values from -0.125 to 0.125
- out_bias: bfloat16 [2048], replicated, may hold values from -3 to 3
- pre_keys: bfloat16 [8, 1024, 2048], P('dp', None, 'tensor'), may hold values from -480 to 480
- pre_values: bfloat16 [8, 1024, 2048], P('dp', None, 'tensor'), may hold values from -6 to 6
- dec_keys: bfloat16 [16, 2048, 2048], P('dp', None, 'tensor'), may hold values from -480 to 480
- dec_values: bfloat16 [16, 2048, 2048], P('dp', None, 'tensor'), may hold values from -6 to 6
- prefix_lengths: int32 [8], P('dp'), may hold values from 0 to 1024, as said below
- cache_lengths: int32 [16], P('dp'), may hold values from 1 to 2048, as said below
- slot_of: int32 [16], replicated, may hold values from 0 to 15, each once
Outputs:
- pre_output: bfloat16 [8192, 2048], P(('dp', 'tensor'))
- dec_output: bfloat16 [16, 2048], P('dp')
Inputs may be any that keep to these rules, and one draw needn't show every extreme that they name: `slot_of`: each decode slot is used by exactly one decode request. `prefix_lengths`: the longest prefix equals 1024. `cache_lengths`: the longest decode cache equals 2048.
All inputs are finite; a program needn't handle non-finite values.
Results may differ from a plain program's by a relative error of at most 0.0049.
The roundings to bfloat16 on the way count: a program that leaves them out, or rounds other values in their place, can miss the bound.
Values may be sent and summed in bfloat16 or wider, within the bound.
No kernel may reach another device: no remote copies, remote signals or barrier semaphores. Data moves between devices by JAX's collectives and lax.ppermute only.
A program may use at most 128 MiB of HBM per device.

v0:
```python
import math

import jax
import jax.numpy as jnp
from jax import lax
from jax.sharding import PartitionSpec as P

H = 16
HD = 128


EPSILON = 1e-05


def normalize(values, norm_gain, norm_shift):
    values = values.astype(jnp.float32)
    center = values - jnp.mean(values, axis=-1, keepdims=True)
    spread = jnp.mean(center * center, axis=-1, keepdims=True)
    scaled = center * lax.rsqrt(spread + EPSILON)
    return (scaled * norm_gain.astype(jnp.float32) + norm_shift.astype(jnp.float32)).astype(
        jnp.bfloat16
    )


def alibi_slopes(first_head, head_count, total_heads):
    head_ids = (first_head + jnp.arange(head_count, dtype=jnp.int32)).astype(jnp.float32)
    return jnp.exp2(-8.0 * (head_ids + 1.0) / total_heads)


def prefill_attention(merged_rows, cache_keys, cache_values, prefix, slopes):
    queries = merged_rows[:, :, 0]
    new_keys = merged_rows[:, :, 1]
    new_values = merged_rows[:, :, 2]
    group_size = merged_rows.shape[0]
    cache_size = cache_keys.shape[0]
    factor = 1.0 / math.sqrt(merged_rows.shape[-1])
    query_pos = prefix + jnp.arange(group_size, dtype=jnp.int32)
    cache_pos = jnp.arange(cache_size, dtype=jnp.int32)
    cache_dist = (query_pos[:, None] - cache_pos[None, :]).astype(jnp.float32)
    new_dist = (query_pos[:, None] - query_pos[None, :]).astype(jnp.float32)
    cache_scores = (
        jnp.einsum("qhd,khd->hqk", queries, cache_keys, preferred_element_type=jnp.float32) * factor
    )
    cache_scores = cache_scores - slopes[:, None, None] * cache_dist[None]
    cache_scores = jnp.where((cache_pos < prefix)[None, None, :], cache_scores, -jnp.inf)
    new_scores = (
        jnp.einsum("qhd,khd->hqk", queries, new_keys, preferred_element_type=jnp.float32) * factor
    )
    new_scores = new_scores - slopes[:, None, None] * new_dist[None]
    causal = (
        jnp.arange(group_size, dtype=jnp.int32)[None, :]
        <= jnp.arange(group_size, dtype=jnp.int32)[:, None]
    )
    new_scores = jnp.where(causal[None], new_scores, -jnp.inf)
    highest = jnp.maximum(
        jnp.max(cache_scores, axis=-1, keepdims=True), jnp.max(new_scores, axis=-1, keepdims=True)
    )
    cache_exp = jnp.exp(cache_scores - highest)
    new_exp = jnp.exp(new_scores - highest)
    denominator = jnp.sum(cache_exp, axis=-1, keepdims=True) + jnp.sum(
        new_exp, axis=-1, keepdims=True
    )
    cache_probs = (cache_exp / denominator).astype(jnp.bfloat16)
    new_probs = (new_exp / denominator).astype(jnp.bfloat16)
    context = jnp.einsum(
        "hqk,khd->qhd", cache_probs, cache_values, preferred_element_type=jnp.float32
    )
    context = context + jnp.einsum(
        "hqk,khd->qhd", new_probs, new_values, preferred_element_type=jnp.float32
    )
    return context.astype(jnp.bfloat16).reshape(group_size, -1)


def decode_attention(query_row, new_key, new_value, cache_keys, cache_values, length, slopes):
    factor = 1.0 / math.sqrt(query_row.shape[-1])
    cache_pos = jnp.arange(cache_keys.shape[0], dtype=jnp.int32)
    distance = (length - cache_pos).astype(jnp.float32)
    cache_scores = (
        jnp.einsum("hd,khd->hk", query_row, cache_keys, preferred_element_type=jnp.float32) * factor
    )
    cache_scores = cache_scores - slopes[:, None] * distance[None, :]
    cache_scores = jnp.where((cache_pos < length)[None, :], cache_scores, -jnp.inf)
    own_score = (
        jnp.einsum("hd,hd->h", query_row, new_key, preferred_element_type=jnp.float32)[:, None]
        * factor
    )
    highest = jnp.maximum(jnp.max(cache_scores, axis=-1, keepdims=True), own_score)
    cache_exp = jnp.exp(cache_scores - highest)
    own_exp = jnp.exp(own_score - highest)
    denominator = jnp.sum(cache_exp, axis=-1, keepdims=True) + own_exp
    cache_probs = (cache_exp / denominator).astype(jnp.bfloat16)
    own_prob = (own_exp / denominator).astype(jnp.bfloat16)
    context = jnp.einsum(
        "hk,khd->hd", cache_probs, cache_values, preferred_element_type=jnp.float32
    )
    context = context + own_prob.astype(jnp.float32) * new_value.astype(jnp.float32)
    return context.astype(jnp.bfloat16).reshape(-1)


def per_device(
    pre_hidden,
    dec_hidden,
    norm_gain,
    norm_shift,
    qkv_weight,
    qkv_bias,
    out_weight,
    out_bias,
    pre_keys,
    pre_values,
    dec_keys,
    dec_values,
    prefix_lengths,
    cache_lengths,
    slot_of,
):
    head_size = HD
    local_heads = qkv_weight.shape[1] // (3 * head_size)
    slopes = alibi_slopes(lax.axis_index("tensor") * local_heads, local_heads, H)
    bias_sum = out_bias.astype(jnp.float32)
    normed = normalize(pre_hidden, norm_gain, norm_shift)
    product = jnp.dot(
        lax.all_gather(normed, "tensor", axis=0, tiled=True),
        qkv_weight,
        preferred_element_type=jnp.float32,
    )
    merged_rows = (product + qkv_bias.astype(jnp.float32)).astype(jnp.bfloat16)
    group_size = merged_rows.shape[0]
    merged_rows = merged_rows.reshape(group_size, local_heads, 3, head_size)
    cache_size = pre_keys.shape[1]
    context = prefill_attention(
        merged_rows,
        pre_keys[0].reshape(cache_size, local_heads, head_size),
        pre_values[0].reshape(cache_size, local_heads, head_size),
        prefix_lengths[0],
        slopes,
    )
    summed = lax.psum_scatter(
        jnp.dot(context, out_weight, preferred_element_type=jnp.float32),
        "tensor",
        scatter_dimension=0,
        tiled=True,
    )
    pre_output = (summed + bias_sum + pre_hidden.astype(jnp.float32)).astype(jnp.bfloat16)
    slot_count = dec_hidden.shape[0]
    request_count = slot_of.shape[0]
    first_slot = lax.axis_index("dp") * slot_count
    slot_ids = first_slot + jnp.arange(slot_count, dtype=jnp.int32)
    slot_pick = (slot_of[None, :] == slot_ids[:, None]).astype(jnp.bfloat16)
    own_slots = lax.dynamic_slice_in_dim(slot_of, first_slot, slot_count)
    send_pick = (jnp.arange(request_count, dtype=jnp.int32)[:, None] == own_slots[None, :]).astype(
        jnp.bfloat16
    )
    gathered = lax.all_gather(dec_hidden, "dp", axis=0, tiled=True)
    arrived = jnp.dot(slot_pick, gathered, preferred_element_type=jnp.float32).astype(jnp.bfloat16)
    normed_slots = normalize(arrived, norm_gain, norm_shift)
    merged_slots = (
        jnp.dot(normed_slots, qkv_weight, preferred_element_type=jnp.float32)
        + qkv_bias.astype(jnp.float32)
    ).astype(jnp.bfloat16)
    merged_slots = merged_slots.reshape(slot_count, local_heads, 3, head_size)
    dec_cache = dec_keys.shape[1]
    slot_context = jax.vmap(decode_attention, in_axes=(0, 0, 0, 0, 0, 0, None))(
        merged_slots[:, :, 0],
        merged_slots[:, :, 1],
        merged_slots[:, :, 2],
        dec_keys.reshape(slot_count, dec_cache, local_heads, head_size),
        dec_values.reshape(slot_count, dec_cache, local_heads, head_size),
        cache_lengths,
        slopes,
    )
    slot_partial = jnp.dot(slot_context, out_weight, preferred_element_type=jnp.float32)
    slot_summed = lax.psum(slot_partial, "tensor")
    slot_rows = (slot_summed + bias_sum + arrived.astype(jnp.float32)).astype(jnp.bfloat16)
    everything = lax.all_gather(slot_rows, "dp", axis=0, tiled=True)
    dec_output = jnp.dot(send_pick.T, everything, preferred_element_type=jnp.float32).astype(
        jnp.bfloat16
    )
    return (pre_output, dec_output)


def solution(mesh):
    placed = (
        P(("dp", "tensor"), None),
        P("dp", None),
        P(),
        P(),
        P(None, "tensor"),
        P("tensor"),
        P("tensor", None),
        P(),
        P("dp", None, "tensor"),
        P("dp", None, "tensor"),
        P("dp", None, "tensor"),
        P("dp", None, "tensor"),
        P("dp"),
        P("dp"),
        P(),
    )
    return jax.shard_map(
        per_device,
        mesh=mesh,
        in_specs=placed,
        out_specs=(P(("dp", "tensor"), None), P("dp", None)),
        check_vma=False,
    )
```

profile of v0, /device:TPU:0, one launch (start us, length us, event | category | flops | bytes accessed | tf_op | source)
XLA Modules:
  0.0 207.5 jit_solution(10675507170763093559)
XLA Ops:
  7.2 0.0 copy-start
  7.2 0.0 copy-start.6
  7.2 0.0 all-gather.4.cloned.1.call-start
  7.2 0.8 convert_element_type.111
  8.1 0.7 convert_element_type.112
  8.8 1.4 convert_reduce_fusion
  10.2 1.6 fusion.11
  11.9 2.8 %fusion.14 = bf16[256,2048]{1,0:T(8,128)(2,1)} fusion(bf16[256,2048]{1,0:T(8,128)(2,1)} %param.15, f32[2048]{0:T(1024)S(1)} %convert_element_type.112, f32[2048]{0:T(1024)S(1)} %convert_element_type.111, f32[256]{0:T(256)S(1)} %add_rsqrt_fusion, f32[256]{0:T(256)S(1)} %broadcast_multiply_fusion), kind=kLoop, calls=%fused_computation.30 | loop fusion | flops 3145728 | bytes 2115584 | tf_op jit(solution)/shard_map/convert_element_type | solution.py:20
  14.6 0.0 all-gather.4.cloned.1.call-update
  14.6 0.0 reduce-scatter.2.cloned.1.call-start
  14.7 0.0 copy-done.6
  15.4 1.3 reshape_squeeze.6
  16.7 2.3 %copy.59 = bf16[1,1024,512]{1,2,0:T(8,128)(2,1)} copy(bf16[1,1024,512]{2,1,0:T(8,128)(2,1)} %param.24) | data formatting | bytes 2097152 | tf_op jit(solution)/shard_map/reshape;squeeze | solution.py:134
  19.0 1.3 iota_compare_fusion
  20.3 3.7 %subtract_convert_fusion = (f32[1024,1024]{0,1:T(8,128)}, f32[1024,1024]{0,1:T(8,128)}) fusion(s32[1024]{0:T(1024)S(1)} %iota_add_fusion), kind=kLoop, calls=%fused_computation.14 | loop fusion | flops 4194304 | bytes 8392704 | tf_op jit(solution)/shard_map/convert_element_type | solution.py:40
  24.0 28.0 %all-gather.4.cloned.1.call-done = bf16[1024,2048]{1,0:T(8,128)(2,1)} async-done(((bf16[256,2048]{1,0:T(8,128)(2,1)}), bf16[1024,2048]{1,0:T(8,128)(2,1)}) %all-gather.4.cloned.1.call-update) | async-done | bytes 4194320 | tf_op jit(solution)/shard_map/all_gather | solution.py:123
  52.0 11.2 %add_convert_fusion = bf16[1024,1536]{1,0:T(8,128)(2,1)} fusion(bf16[1024,2048]{1,0:T(8,128)(2,1)} %all-gather.4.cloned.1.call-done, bf16[2048,1536]{1,0:T(8,128)(2,1)} %param.19, f32[1536]{0:T(1024)S(1)} %convert_element_type.114), kind=kOutput, calls=%fused_computation.10 | convolution fusion | flops 6445596672 | bytes 13637632 | tf_op jit(solution)/shard_map/dot_general | solution.py:122
  63.2 4.7 %copy.40 = bf16[1024,1536]{0,1:T(8,128)(2,1)} copy(bf16[1024,1536]{1,0:T(8,128)(2,1)} %add_convert_fusion) | data formatting | bytes 6291456 | tf_op jit(solution)/shard_map/convert_element_type | solution.py:127
  67.9 0.0 copy-start.1
  67.9 0.0 copy-start.3
  67.9 10.8 %fusion.44 = (f32[4,1024]{1,0:T(4,128)S(1)}, f32[4,1024,1024]{1,2,0:T(8,128)}) fusion(f32[1024,1024]{0,1:T(8,128)} %get-tuple-element.9, f32[4]{0:T(128)S(1)} %multiply_exponential_fusion, bf16[1024,4,3,128]{0,3,2,1:T(8,128)(2,1)} %bitcast.79, pred[1024,1024]{0,1:T(8,128)(4,1)} %iota_compare_fusion), kind=kOutput, calls=%fused_computation.86 | convolution fusion | flops 1094709248 | bytes 24133648 | tf_op jit(solution)/shard_map/qhd,khd->hqk/dot_general | solution.py:47
  78.7 0.0 copy-done.1
  78.7 0.0 copy-done.3
  78.7 3.7 %fusion.43 = (f32[4,1024]{1,0:T(4,128)S(1)}, f32[4,1024,1024]{1,2,0:T(8,128)S(1)}) fusion(f32[1024,1024]{0,1:T(8,128)S(1)} %copy-done.1, f32[4]{0:T(128)S(1)} %multiply_exponential_fusion, bf16[1024,4,3,128]{0,3,2,1:T(8,128)(2,1)S(1)} %bitcast.80, bf16[1024,4,128]{2,1,0:T(4,128)(2,1)S(1)} %reshape_squeeze.6, pred[1024]{0:T(1024)(128)(4,1)S(1)} %iota_compare_fusion.4), kind=kOutput, calls=%fused_computation.85 | convolution fusion | flops 1094709248 | bytes 23086592 | tf_op jit(solution)/shard_map/qhd,khd->hqk/dot_general | solution.py:42
  82.4 0.0 copy-start.4
  82.5 8.4 %fusion.1 = (f32[4,1024]{1,0:T(4,128)S(1)}, f32[4,1024]{1,0:T(4,128)S(1)}) fusion(f32[4,1024,1024]{1,2,0:T(8,128)} %get-tuple-element.16, f32[4,1024]{1,0:T(4,128)S(1)} %max.12, f32[4,1024,1024]{1,2,0:T(8,128)S(1)} %get-tuple-element.14), kind=kLoop, calls=%fused_computation.7 | loop fusion | flops 16769024 | bytes 33603584 | tf_op jit(solution)/shard_map/reduce_sum | solution.py:60
  90.9 0.0 copy-done.4
  90.9 3.7 %fusion.2 = f32[4,1024,128]{1,2,0:T(8,128)S(1)} fusion(bf16[1024,4,128]{0,2,1:T(8,128)(2,1)S(1)} %bitcast.82, f32[4,1024,1024]{1,2,0:T(8,128)S(1)} %get-tuple-element.14, f32[4,1024]{1,0:T(4,128)S(1)} %add.155, f32[4,1024]{1,0:T(4,128)S(1)} %max.12), kind=kOutput, calls=%fused_computation.8 | convolution fusion | flops 1086324736 | bytes 19955712 | tf_op jit(solution)/shard_map/hqk,khd->qhd/dot_general | solution.py:65
  94.6 7.7 %fusion.16 = bf16[1024,4,128]{0,2,1:T(8,128)(2,1)S(1)} fusion(f32[4,1024,128]{1,2,0:T(8,128)S(1)} %fusion.2, f32[4,1024,1024]{1,2,0:T(8,128)} %get-tuple-element.16, f32[4,1024]{1,0:T(4,128)S(1)} %add.155, f32[4,1024]{1,0:T(4,128)S(1)} %max.12, bf16[1024,4,3,128]{0,3,2,1:T(8,128)(2,1)S(1)} %bitcast.81), kind=kOutput, calls=%fused_computation.33 | convolution fusion | flops 1087373312 | bytes 21004288 | tf_op jit(solution)/shard_map/hqk,khd->qhd/dot_general | solution.py:68
  102.3 0.0 copy-done
  102.3 5.6 %fusion.46 = f32[1024,2048]{1,0:T(8,128)} fusion(bf16[1024,512]{0,1:T(8,128)(2,1)S(1)} %bitcast.86, bf16[512,2048]{1,0:T(8,128)(2,1)S(1)} %copy-done), kind=kOutput, calls=%fused_computation.88 | convolution fusion | flops 2147483648 | bytes 11534336 | tf_op jit(solution)/shard_map/dot_general | solution.py:139
  107.9 0.0 copy-start.7
  107.9 0.0 copy-start.5
  107.9 0.0 copy-start.10
  107.9 0.0 reduce-scatter.2.cloned.1.call-update
  107.9 0.7 copy-done.7
  108.6 0.0 copy-done.5
  108.6 30.6 %all-gather = bf16[8,2,2048]{2,1,0:T(2,128)(2,1)S(1)} all-gather(bf16[1,2,2048]{2,1,0:T(2,128)(2,1)S(1)} %bitcast.84), channel_id=1, replica_groups=mesh['dp'=8,'tensor'=4] {'dp'}, dimensions={0}, use_global_device_ids=true | all-gather | bytes 73728 | tf_op jit(solution)/shard_map/all_gather | solution.py:154
  139.2 0.0 copy-done.10
  139.2 0.3 fusion.45
  139.5 0.2 multiply_reduce_fusion
  139.7 4.0 %fusion.9 = bf16[2,1536]{1,0:T(2,128)(2,1)S(1)} fusion(bf16[2048,1536]{1,0:T(8,128)(2,1)} %param.19, f32[2,2048]{1,0:T(2,128)S(1)} %get-tuple-element.18, f32[2]{0:T(128)S(1)} %add_rsqrt_fusion.1, f32[2]{0:T(128)S(1)} %broadcast_multiply_fusion.1, f32[2048]{0:T(1024)S(1)} %convert_element_type.112, f32[2048]{0:T(1024)S(1)} %convert_element_type.111, ...), kind=kOutput, calls=%fused_computation.23 | convolution fusion | flops 12609536 | bytes 6336528 | tf_op jit(solution)/shard_map/dot_general | solution.py:158
  143.8 6.3 %copy.60 = bf16[2,2048,512]{1,2,0:T(8,128)(2,1)} copy(bf16[2,2048,512]{2,1,0:T(8,128)(2,1)} %param.25) | data formatting | bytes 8388608 | tf_op jit(solution)/shard_map/reshape | solution.py:167
  150.1 0.0 copy-start.8
  150.1 0.0 copy-start.9
  150.1 0.1 fusion.27
  150.2 3.2 %fusion.28 = f32[2,4,1,2048]{3,2,1,0:T(1,128)S(1)} fusion(bf16[2,2048,4,128]{1,3,2,0:T(8,128)(2,1)} %bitcast.78, bf16[2,4,3,128]{3,2,1,0:T(4,128)(2,1)S(1)} %reshape.204), kind=kOutput, calls=%fused_computation.59 | convolution fusion | flops 4194304 | bytes 4263936 | tf_op jit(solution)/shard_map/vmap(hd,khd->hk)/dot_general | solution.py:79
  153.4 0.0 copy-done.8
  153.4 0.0 copy-start.2
  153.4 0.1 iota_compare_fusion.1
  153.5 0.1 subtract_convert_fusion.2
  153.6 0.2 fusion.41
  153.8 0.2 fusion.21
  154.0 0.1 fusion.22
  154.1 0.0 copy-done.9
  154.1 0.7 fusion.4
  154.7 0.1 fusion.31
  154.8 0.4 fusion.32
  155.2 11.1 %psum.7 = f32[2,2048]{1,0:T(2,128)S(1)} all-reduce(f32[2,2048]{1,0:T(2,128)S(1)} %fusion.32), channel_id=1, replica_groups=mesh['dp'=8,'tensor'=4] {'tensor'}, use_global_device_ids=true, to_apply=%region_11.12 | all-reduce | flops 4096 | bytes 32768 | tf_op jit(solution)/shard_map/psum | solution.py:173
  166.4 30.5 %all-gather.1 = bf16[8,2,2048]{2,1,0:T(2,128)(2,1)S(1)} all-gather(bf16[1,2,2048]{2,1,0:T(2,128)(2,1)S(1)} %fusion.24), channel_id=1, replica_groups=mesh['dp'=8,'tensor'=4] {'dp'}, dimensions={0}, use_global_device_ids=true | all-gather | bytes 73728 | tf_op jit(solution)/shard_map/all_gather | solution.py:175
  196.9 0.1 dynamic_slice.3
  197.0 0.8 convolution_convert_fusion
  197.8 0.0 copy-done.2
  197.8 2.9 %fusion.15 = bf16[256,2048]{1,0:T(8,128)(2,1)} fusion(bf16[256,2048]{1,0:T(8,128)(2,1)S(1)} %copy-done.2, f32[256,2048]{1,0:T(8,128)} %reduce-scatter.2.cloned.1.call-done, f32[2048]{0:T(1024)S(1)} %convert_element_type.122), kind=kLoop, calls=%fused_computation.31 | loop fusion | flops 2097152 | bytes 4202496 | tf_op jit(solution)/shard_map/convert_element_type | solution.py:144
  (20 shorter events, 0.2 us)
Async XLA Ops:
  7.2 95.1 %copy-start = (bf16[512,2048]{1,0:T(8,128)(2,1)S(1)}, bf16[512,2048]{1,0:T(8,128)(2,1)}, u32[]{:S(2)}) copy-start(bf16[512,2048]{1,0:T(8,128)(2,1)} %param.21) | copy-start | bytes 6291460
  7.2 7.5 %copy-start.6 = (bf16[1536]{0:T(1024)(128)(2,1)S(1)}, bf16[1536]{0:T(1024)(128)(2,1)}, u32[]{:S(2)}) copy-start(bf16[1536]{0:T(1024)(128)(2,1)} %param.20) | copy-start | bytes 9220
  7.2 44.8 %all-gather.4.cloned.1.call-start = ((), (), s32[]{:S(2)}) async-start(), calls=%async_computation.1 | async-start | bytes 5242880 | tf_op jit(solution)/shard_map/all_gather | solution.py:123
  14.6 183.1 %reduce-scatter.2.cloned.1.call-start = ((), (), s32[]{:S(2)}) async-start(), calls=%async_computation.2 | async-start | bytes 10485760 | tf_op jit(solution)/shard_map/reduce_scatter | solution.py:138
  67.9 10.9 %copy-start.1 = (f32[1024,1024]{0,1:T(8,128)S(1)}, f32[1024,1024]{0,1:T(8,128)}, u32[]{:S(2)}) copy-start(f32[1024,1024]{0,1:T(8,128)} %get-tuple-element.10) | copy-start | bytes 12582916
  67.9 10.9 %copy-start.3 = (bf16[1024,1536]{0,1:T(8,128)(2,1)S(1)}, bf16[1024,1536]{0,1:T(8,128)(2,1)}, u32[]{:S(2)}) copy-start(bf16[1024,1536]{0,1:T(8,128)(2,1)} %copy.40) | copy-start | bytes 9437188
  82.4 8.4 %copy-start.4 = (bf16[1,1024,512]{1,2,0:T(8,128)(2,1)S(1)}, bf16[1,1024,512]{1,2,0:T(8,128)(2,1)}, u32[]{:S(2)}) copy-start(bf16[1,1024,512]{1,2,0:T(8,128)(2,1)} %copy.59) | copy-start | bytes 3145732
  107.9 0.7 copy-start.7
  107.9 0.7 copy-start.5
  107.9 31.3 %copy-start.10 = (s32[16]{0:T(128)S(1)}, s32[16]{0:T(128)}, u32[]{:S(2)}) copy-start(s32[16]{0:T(128)} %param.29) | copy-start | bytes 196
  150.1 3.3 %copy-start.8 = (s32[2]{0:T(128)S(1)}, s32[2]{0:T(128)}, u32[]{:S(2)}) copy-start(s32[2]{0:T(128)} %param.28) | copy-start | bytes 28
  150.1 4.0 %copy-start.9 = (bf16[2,2048,512]{2,1,0:T(8,128)(2,1)S(1)}, bf16[2,2048,512]{2,1,0:T(8,128)(2,1)}, u32[]{:S(2)}) copy-start(bf16[2,2048,512]{2,1,0:T(8,128)(2,1)} %param.26) | copy-start | bytes 12582916
  153.4 44.4 %copy-start.2 = (bf16[256,2048]{1,0:T(8,128)(2,1)S(1)}, bf16[256,2048]{1,0:T(8,128)(2,1)}, u32[]{:S(2)}) copy-start(bf16[256,2048]{1,0:T(8,128)(2,1)} %param.15) | copy-start | bytes 3145732
Sparse Core Ops, SparseCore 0:
  14.8 37.1 all-gather.3
  108.0 71.9 reduce-scatter.1
where the time goes:
time: 208 us; the launch traced here: 207 us
  blocking collectives  72.2 us (35%)
  matrix products  52.1 us (25%)
  waiting for transfers between devices  28 us (13%)
  other arithmetic  24.7 us (12%)
  local copies, waits for them, and re-layouts  15.5 us (7%)
  between operations  14.9 us (7%)
    all_gather x1, blocking collectives, per_device(): gathered = lax.all_gather(dec_hidden, 'dp', axis=0, tiled=True)  30.6 us
    all_gather x1, blocking collectives, per_device(): everything = lax.all_gather(slot_rows, 'dp', axis=0, tiled=True)  30.5 us
    all_gather x1, waiting for transfers between devices, per_device(): lax.all_gather(normed, 'tensor', axis=0, tiled=True)  28 us
    dot_general x1, matrix products, per_device(): jnp.dot(lax.all_gather(normed, 'tensor', axis=0, tiled=True), qkv_weight,...  11.2 us
    psum x1, blocking collectives, per_device(): slot_summed = lax.psum(slot_partial, 'tensor')  11.1 us
    dot_general x1, matrix products, prefill_attention(): jnp.einsum('qhd,khd->hqk', queries, new_keys, preferred_element_type=jnp....  10.8 us
    reduce_sum x1, other arithmetic, prefill_attention(): jnp.sum(new_exp, axis=-1, keepdims=True)  8.4 us
    dot_general x1, matrix products, prefill_attention(): jnp.einsum('hqk,khd->qhd', new_probs, new_values, preferred_element_type=...  7.69 us
  transfers between devices with their start and end apart: 2, of which 1 were waited for; matrix products, arithmetic and copies ran while one was open for 12% of the time, Pallas kernels for 0%

commit v1 on v0

--- a/solution.py
+++ b/solution.py
@@ -143,16 +143,15 @@
     )
     pre_output = (summed + bias_sum + pre_hidden.astype(jnp.float32)).astype(jnp.bfloat16)
     slot_count = dec_hidden.shape[0]
-    request_count = slot_of.shape[0]
     first_slot = lax.axis_index("dp") * slot_count
     slot_ids = first_slot + jnp.arange(slot_count, dtype=jnp.int32)
-    slot_pick = (slot_of[None, :] == slot_ids[:, None]).astype(jnp.bfloat16)
-    own_slots = lax.dynamic_slice_in_dim(slot_of, first_slot, slot_count)
-    send_pick = (jnp.arange(request_count, dtype=jnp.int32)[:, None] == own_slots[None, :]).astype(
-        jnp.bfloat16
-    )
-    gathered = lax.all_gather(dec_hidden, "dp", axis=0, tiled=True)
-    arrived = jnp.dot(slot_pick, gathered, preferred_element_type=jnp.float32).astype(jnp.bfloat16)
+    request_ids = jnp.arange(slot_of.shape[0], dtype=jnp.int32)
+    own_requests_slots = lax.dynamic_slice_in_dim(slot_of, first_slot, slot_count)
+    to_slot = request_ids[:, None] == own_requests_slots[None, :]
+    outgoing = jnp.zeros((slot_of.shape[0], dec_hidden.shape[1]), jnp.float32)
+    for j in range(slot_count):
+        outgoing = jnp.where(to_slot[:, j, None], dec_hidden[j][None, :].astype(jnp.float32), outgoing)
+    arrived = lax.psum_scatter(outgoing, "dp", scatter_dimension=0, tiled=True).astype(jnp.bfloat16)
     normed_slots = normalize(arrived, norm_gain, norm_shift)
     merged_slots = (
         jnp.dot(normed_slots, qkv_weight, preferred_element_type=jnp.float32)
@@ -170,12 +169,13 @@
         slopes,
     )
     slot_partial = jnp.dot(slot_context, out_weight, preferred_element_type=jnp.float32)
-    slot_summed = lax.psum(slot_partial, "tensor")
-    slot_rows = (slot_summed + bias_sum + arrived.astype(jnp.float32)).astype(jnp.bfloat16)
-    everything = lax.all_gather(slot_rows, "dp", axis=0, tiled=True)
-    dec_output = jnp.dot(send_pick.T, everything, preferred_element_type=jnp.float32).astype(
-        jnp.bfloat16
-    )
+    from_slot = slot_of[:, None] == slot_ids[None, :]
+    returning = jnp.zeros((slot_of.shape[0], slot_partial.shape[1]), jnp.float32)
+    for j in range(slot_count):
+        returning = jnp.where(from_slot[:, j, None], slot_partial[j][None, :], returning)
+    summed_all = lax.psum(returning, ("dp", "tensor"))
+    slot_summed = lax.dynamic_slice_in_dim(summed_all, first_slot, slot_count)
+    dec_output = (slot_summed + bias_sum + dec_hidden.astype(jnp.float32)).astype(jnp.bfloat16)
     return (pre_output, dec_output)
 
 

time: 208 us -> 233 us (1.12)
  waiting for transfers between devices: 28 us -> 80.9 us
  blocking collectives: 72.2 us -> 40.1 us
  other arithmetic: 24.7 us -> 27.2 us
    psum x0 -> x1, waiting for transfers between devices: none -> 80.9 us  [per_device(): summed_all = lax.psum(returning, ('dp', 'tensor'))]
    all_gather x2 -> x0, blocking collectives: 61.1 us -> none  [the longest x1 30.6 us: per_device(): gathered = lax.all_gather(dec_hidden, 'dp', axis=0, tiled=True)]
    unnamed x0 -> x1, blocking collectives: none -> 40.1 us
    all_gather x1, waiting for transfers between devices: 28 us -> 0.01 us  [per_device(): lax.all_gather(normed, 'tensor', axis=0, tiled=True)]
    psum x1 -> x0, blocking collectives: 11.1 us -> none  [per_device(): slot_summed = lax.psum(slot_partial, 'tensor')]
  transfers between devices with their start and end apart: 2 -> 3, of which waited for: 1 -> 1; matrix products, arithmetic and copies ran while one was open for 12% -> 36% of each run, Pallas kernels for 0% -> 0%
where the time goes in v1:
time: 233 us; the launch traced here: 232 us
  waiting for transfers between devices  80.9 us (35%)
  matrix products  50.6 us (22%)
  blocking collectives  40.1 us (17%)
  other arithmetic  27.2 us (12%)
  between operations  17.1 us (7%)
  local copies, waits for them, and re-layouts  16.2 us (7%)
    psum x1, waiting for transfers between devices, per_device(): summed_all = lax.psum(returning, ('dp', 'tensor'))  80.9 us
    unnamed x1, blocking collectives  40.1 us
    dot_general x1, matrix products, per_device(): jnp.dot(lax.all_gather(normed, 'tensor', axis=0, tiled=True), qkv_weight,...  11.2 us
    dot_general x1, matrix products, prefill_attention(): jnp.einsum('qhd,khd->hqk', queries, new_keys, preferred_element_type=jnp....  10.9 us
    reduce_sum x1, other arithmetic, prefill_attention(): jnp.sum(new_exp, axis=-1, keepdims=True)  8.43 us
    dot_general x1, matrix products, prefill_attention(): jnp.einsum('hqk,khd->qhd', new_probs, new_values, preferred_element_type=...  7.95 us
    reshape x1, local copies, waits for them, and re-layouts, per_device(): dec_keys.reshape(slot_count, dec_cache, local_heads, head_size)  6.41 us
    dot_general x1, matrix products, per_device(): jnp.dot(context, out_weight, preferred_element_type=jnp.float32)  5.61 us
  transfers between devices with their start and end apart: 3, of which 1 were waited for; matrix products, arithmetic and copies ran while one was open for 36% of the time, Pallas kernels for 0%

profile of v1, /device:TPU:0, one launch (start us, length us, event | category | flops | bytes accessed | tf_op | source)
XLA Modules:
  0.0 232.2 jit_solution(11411439349456508695)
XLA Ops:
  8.0 0.0 copy-start
  8.0 0.0 copy-start.11
  8.0 0.0 copy-start.10
  8.0 0.0 copy-start.5
  8.0 0.0 copy-start.6
  8.1 0.0 all-gather.2.cloned.1.call-start
  8.1 0.8 convert_element_type.110
  8.9 0.7 convert_element_type.111
  9.6 1.4 convert_reduce_fusion
  11.1 1.6 fusion.10
  12.7 2.8 %fusion.13 = bf16[256,2048]{1,0:T(8,128)(2,1)} fusion(bf16[256,2048]{1,0:T(8,128)(2,1)} %param.15, f32[2048]{0:T(1024)S(1)} %convert_element_type.111, f32[2048]{0:T(1024)S(1)} %convert_element_type.110, f32[256]{0:T(256)S(1)} %add_rsqrt_fusion, f32[256]{0:T(256)S(1)} %broadcast_multiply_fusion), kind=kLoop, calls=%fused_computation.27 | loop fusion | flops 3145728 | bytes 2115584 | tf_op jit(solution)/shard_map/convert_element_type | solution.py:20
  15.5 0.0 all-gather.2.cloned.1.call-update
  15.5 0.0 all-reduce.4.cloned.1.call-start
  15.6 0.0 copy-done.10
  15.6 0.1 dynamic_slice.6
  15.7 0.1 iota_compare_fusion.3
  15.7 0.0 copy-done.5
  15.8 0.1 select_select_fusion.1
  15.8 40.1 %all-reduce.5 = bf16[16,2048]{1,0:T(8,128)(2,1)S(1)} all-reduce(f32[16,2048]{1,0:T(8,128)S(1)} %select_select_fusion.1), channel_id=3, replica_groups=mesh['dp'=8,'tensor'=4] {'dp'}, use_global_device_ids=true, to_apply=%region_7.8.clone | all-reduce | flops 32768 | bytes 196608
  56.0 0.0 copy-done.6
  56.0 0.0 copy-done.11
  56.0 0.6 dynamic-slice
  57.2 0.1 convert_reduce_fusion.1
  57.4 0.2 fusion.24
  57.6 3.8 %fusion.9 = bf16[2,1536]{1,0:T(2,128)(2,1)S(1)} fusion(bf16[2048,1536]{1,0:T(8,128)(2,1)} %param.19, bf16[2,2048]{1,0:T(2,128)(2,1)S(1)} %get-tuple-element.7, f32[2]{0:T(128)S(1)} %add_rsqrt_fusion.1, f32[2]{0:T(128)S(1)} %broadcast_multiply_fusion.1, f32[2048]{0:T(1024)S(1)} %convert_element_type.111, f32[2048]{0:T(1024)S(1)} %convert_element_type.110, ...), kind=kOutput, calls=%fused_computation.23 | convolution fusion | flops 12613632 | bytes 6328336 | tf_op jit(solution)/shard_map/dot_general | solution.py:157
  61.4 6.4 %copy.60 = bf16[2,2048,512]{1,2,0:T(8,128)(2,1)} copy(bf16[2,2048,512]{2,1,0:T(8,128)(2,1)} %param.25) | data formatting | bytes 8388608 | tf_op jit(solution)/shard_map/reshape | solution.py:166
  67.8 0.1 fusion.33
  67.9 3.0 %fusion.34 = f32[2,4,1,2048]{3,2,1,0:T(1,128)S(1)} fusion(bf16[2,2048,4,128]{1,3,2,0:T(8,128)(2,1)} %bitcast.86, bf16[2,4,3,128]{3,2,1,0:T(4,128)(2,1)S(1)} %reshape.204), kind=kOutput, calls=%fused_computation.66 | convolution fusion | flops 4194304 | bytes 4263936 | tf_op jit(solution)/shard_map/vmap(hd,khd->hk)/dot_general | solution.py:79
  70.9 0.0 copy-done.8
  70.9 0.1 iota_compare_fusion.1
  71.0 0.1 subtract_convert_fusion.2
  71.1 0.2 fusion.43
  71.3 0.2 fusion.20
  71.4 0.1 broadcast_compare_fusion
  71.5 0.1 fusion.21
  71.6 0.0 copy-done.9
  71.7 0.7 fusion.4
  72.3 0.1 fusion.36
  72.4 0.0 copy-done
  72.4 0.4 fusion.37
  72.8 0.7 select_select_fusion
  73.5 0.0 all-reduce.4.cloned.1.call-update
  73.6 0.0 reduce-scatter.2.cloned.1.call-start
  73.6 1.3 iota_compare_fusion
  75.6 3.6 %subtract_convert_fusion = (f32[1024,1024]{0,1:T(8,128)}, f32[1024,1024]{0,1:T(8,128)}) fusion(s32[1024]{0:T(1024)S(1)} %iota_add_fusion), kind=kLoop, calls=%fused_computation.14 | loop fusion | flops 4194304 | bytes 8392704 | tf_op jit(solution)/shard_map/convert_element_type | solution.py:40
  79.1 1.3 reshape_squeeze.6
  80.5 2.3 copy.59
  82.8 11.2 %add_convert_fusion = bf16[1024,1536]{1,0:T(8,128)(2,1)} fusion(bf16[1024,2048]{1,0:T(8,128)(2,1)} %all-gather.2.cloned.1.call-done, bf16[2048,1536]{1,0:T(8,128)(2,1)} %param.19, f32[1536]{0:T(1024)S(1)} %convert_element_type.113), kind=kOutput, calls=%fused_computation.10 | convolution fusion | flops 6445596672 | bytes 13637632 | tf_op jit(solution)/shard_map/dot_general | solution.py:122
  94.0 4.7 %copy.40 = bf16[1024,1536]{0,1:T(8,128)(2,1)} copy(bf16[1024,1536]{1,0:T(8,128)(2,1)} %add_convert_fusion) | data formatting | bytes 6291456 | tf_op jit(solution)/shard_map/convert_element_type | solution.py:127
  98.7 10.9 %fusion.47 = (f32[4,1024]{1,0:T(4,128)S(1)}, f32[4,1024,1024]{1,2,0:T(8,128)}) fusion(f32[1024,1024]{0,1:T(8,128)} %get-tuple-element.15, f32[4]{0:T(128)S(1)} %multiply_exponential_fusion, bf16[1024,4,3,128]{0,3,2,1:T(8,128)(2,1)} %bitcast.87, pred[1024,1024]{0,1:T(8,128)(4,1)} %iota_compare_fusion), kind=kOutput, calls=%fused_computation.96 | convolution fusion | flops 1094709248 | bytes 24133648 | tf_op jit(solution)/shard_map/qhd,khd->hqk/dot_general | solution.py:47
  109.6 0.0 copy-done.1
  109.6 0.0 copy-done.3
  109.6 3.7 %fusion.46 = (f32[4,1024]{1,0:T(4,128)S(1)}, f32[4,1024,1024]{1,2,0:T(8,128)S(1)}) fusion(f32[1024,1024]{0,1:T(8,128)S(1)} %copy-done.1, f32[4]{0:T(128)S(1)} %multiply_exponential_fusion, bf16[1024,4,3,128]{0,3,2,1:T(8,128)(2,1)S(1)} %bitcast.88, bf16[1024,4,128]{2,1,0:T(4,128)(2,1)S(1)} %reshape_squeeze.6, pred[1024]{0:T(1024)(128)(4,1)S(1)} %iota_compare_fusion.2), kind=kOutput, calls=%fused_computation.95 | convolution fusion | flops 1094709248 | bytes 23086592 | tf_op jit(solution)/shard_map/qhd,khd->hqk/dot_general | solution.py:42
  113.3 0.0 copy-start.4
  113.3 8.4 %fusion.1 = (f32[4,1024]{1,0:T(4,128)S(1)}, f32[4,1024]{1,0:T(4,128)S(1)}) fusion(f32[4,1024,1024]{1,2,0:T(8,128)} %get-tuple-element.26, f32[4,1024]{1,0:T(4,128)S(1)} %max.12, f32[4,1024,1024]{1,2,0:T(8,128)S(1)} %get-tuple-element.24), kind=kLoop, calls=%fused_computation.7 | loop fusion | flops 16769024 | bytes 33603584 | tf_op jit(solution)/shard_map/reduce_sum | solution.py:60
  121.7 0.0 copy-done.4
  121.8 3.5 %fusion.2 = f32[4,1024,128]{1,2,0:T(8,128)S(1)} fusion(bf16[1024,4,128]{0,2,1:T(8,128)(2,1)S(1)} %bitcast.90, f32[4,1024,1024]{1,2,0:T(8,128)S(1)} %get-tuple-element.24, f32[4,1024]{1,0:T(4,128)S(1)} %add.158, f32[4,1024]{1,0:T(4,128)S(1)} %max.12), kind=kOutput, calls=%fused_computation.8 | convolution fusion | flops 1086324736 | bytes 19955712 | tf_op jit(solution)/shard_map/hqk,khd->qhd/dot_general | solution.py:65
  125.3 8.0 %fusion.15 = bf16[1024,4,128]{0,2,1:T(8,128)(2,1)S(1)} fusion(f32[4,1024,128]{1,2,0:T(8,128)S(1)} %fusion.2, f32[4,1024,1024]{1,2,0:T(8,128)} %get-tuple-element.26, f32[4,1024]{1,0:T(4,128)S(1)} %add.158, f32[4,1024]{1,0:T(4,128)S(1)} %max.12, bf16[1024,4,3,128]{0,3,2,1:T(8,128)(2,1)S(1)} %bitcast.89), kind=kOutput, calls=%fused_computation.30 | convolution fusion | flops 1087373312 | bytes 21004288 | tf_op jit(solution)/shard_map/hqk,khd->qhd/dot_general | solution.py:68
  133.2 5.6 %fusion.48 = f32[1024,2048]{1,0:T(8,128)} fusion(bf16[1024,512]{0,1:T(8,128)(2,1)S(1)} %bitcast.97, bf16[512,2048]{1,0:T(8,128)(2,1)S(1)} %copy-done), kind=kOutput, calls=%fused_computation.97 | convolution fusion | flops 2147483648 | bytes 11534336 | tf_op jit(solution)/shard_map/dot_general | solution.py:139
  138.8 0.0 reduce-scatter.2.cloned.1.call-update
  138.9 0.7 copy-done.7
  139.5 80.9 %all-reduce.4.cloned.1.call-done = f32[16,2048]{1,0:T(8,128)} async-done(((f32[16,2048]{1,0:T(8,128)}), f32[16,2048]{1,0:T(8,128)}) %all-reduce.4.cloned.1.call-update) | async-done | bytes 131088 | tf_op jit(solution)/shard_map/psum | solution.py:176
  220.4 1.5 add_convert_fusion.1
  221.8 2.9 %fusion.14 = bf16[256,2048]{1,0:T(8,128)(2,1)} fusion(bf16[256,2048]{1,0:T(8,128)(2,1)S(1)} %copy-done.2, f32[256,2048]{1,0:T(8,128)} %reduce-scatter.2.cloned.1.call-done, f32[2048]{0:T(1024)S(1)} %convert_element_type.121), kind=kLoop, calls=%fused_computation.28 | loop fusion | flops 2097152 | bytes 4202496 | tf_op jit(solution)/shard_map/convert_element_type | solution.py:144
  (29 shorter events, 0.2 us)
Async XLA Ops:
  8.0 64.4 %copy-start = (bf16[512,2048]{1,0:T(8,128)(2,1)S(1)}, bf16[512,2048]{1,0:T(8,128)(2,1)}, u32[]{:S(2)}) copy-start(bf16[512,2048]{1,0:T(8,128)(2,1)} %param.21) | copy-start | bytes 6291460
  8.0 48.0 %copy-start.11 = (u32[32]{0:T(128)S(1)}, u32[32]{0:T(128)}, u32[]{:S(2)}) copy-start(u32[32]{0:T(128)} %constant.56) | copy-start | bytes 388
  8.0 7.5 %copy-start.10 = (s32[16]{0:T(128)S(1)}, s32[16]{0:T(128)}, u32[]{:S(2)}) copy-start(s32[16]{0:T(128)} %param.29) | copy-start | bytes 196
  8.0 7.7 %copy-start.5 = (bf16[2,2048]{1,0:T(2,128)(2,1)S(1)}, bf16[2,2048]{1,0:T(2,128)(2,1)}, u32[]{:S(2)}) copy-start(bf16[2,2048]{1,0:T(2,128)(2,1)} %param.16) | copy-start | bytes 24580
  8.0 47.9 %copy-start.6 = (bf16[1536]{0:T(1024)(128)(2,1)S(1)}, bf16[1536]{0:T(1024)(128)(2,1)}, u32[]{:S(2)}) copy-start(bf16[1536]{0:T(1024)(128)(2,1)} %param.20) | copy-start | bytes 9220
  8.1 74.7 %all-gather.2.cloned.1.call-start = ((), (), s32[]{:S(2)}) async-start(), calls=%async_computation.1 | async-start | bytes 5242880 | tf_op jit(solution)/shard_map/all_gather | solution.py:123
  15.5 204.9 %all-reduce.4.cloned.1.call-start = ((), (), s32[]{:S(2)}) async-start(), calls=%async_computation.3 | async-start | bytes 262144 | tf_op jit(solution)/shard_map/psum | solution.py:176
  67.8 3.1 %copy-start.8 = (s32[2]{0:T(128)S(1)}, s32[2]{0:T(128)}, u32[]{:S(2)}) copy-start(s32[2]{0:T(128)} %param.28) | copy-start | bytes 28
  67.8 3.9 %copy-start.9 = (bf16[2,2048,512]{2,1,0:T(8,128)(2,1)S(1)}, bf16[2,2048,512]{2,1,0:T(8,128)(2,1)}, u32[]{:S(2)}) copy-start(bf16[2,2048,512]{2,1,0:T(8,128)(2,1)} %param.26) | copy-start | bytes 12582916
  73.6 148.3 %reduce-scatter.2.cloned.1.call-start = ((), (), s32[]{:S(2)}) async-start(), calls=%async_computation.2 | async-start | bytes 10485760 | tf_op jit(solution)/shard_map/reduce_scatter | solution.py:138
  98.7 10.9 %copy-start.1 = (f32[1024,1024]{0,1:T(8,128)S(1)}, f32[1024,1024]{0,1:T(8,128)}, u32[]{:S(2)}) copy-start(f32[1024,1024]{0,1:T(8,128)} %get-tuple-element.16) | copy-start | bytes 12582916
  98.7 10.9 %copy-start.3 = (bf16[1024,1536]{0,1:T(8,128)(2,1)S(1)}, bf16[1024,1536]{0,1:T(8,128)(2,1)}, u32[]{:S(2)}) copy-start(bf16[1024,1536]{0,1:T(8,128)(2,1)} %copy.40) | copy-start | bytes 9437188
  113.3 8.5 %copy-start.4 = (bf16[1,1024,512]{1,2,0:T(8,128)(2,1)S(1)}, bf16[1,1024,512]{1,2,0:T(8,128)(2,1)}, u32[]{:S(2)}) copy-start(bf16[1,1024,512]{1,2,0:T(8,128)(2,1)} %copy.59) | copy-start | bytes 3145732
  138.8 0.7 copy-start.7
  138.8 83.0 %copy-start.2 = (bf16[256,2048]{1,0:T(8,128)(2,1)S(1)}, bf16[256,2048]{1,0:T(8,128)(2,1)}, u32[]{:S(2)}) copy-start(bf16[256,2048]{1,0:T(8,128)(2,1)} %param.15) | copy-start | bytes 3145732
Sparse Core Ops, SparseCore 0:
  15.6 37.1 all-gather.1
  139.0 69.1 reduce-scatter.1
Sparse Core Ops, SparseCore 1:
  73.6 146.7 all-reduce.3

commit v2 on v0

--- a/solution.py
+++ b/solution.py
@@ -143,16 +143,25 @@
     )
     pre_output = (summed + bias_sum + pre_hidden.astype(jnp.float32)).astype(jnp.bfloat16)
     slot_count = dec_hidden.shape[0]
-    request_count = slot_of.shape[0]
-    first_slot = lax.axis_index("dp") * slot_count
+    dp_size = lax.axis_size("dp")
+    tensor_size = lax.axis_size("tensor")
+    group = lax.axis_index("dp")
+    member = lax.axis_index("tensor")
+    first_slot = group * slot_count
+    shifted_rows = [dec_hidden] + [
+        lax.ppermute(dec_hidden, "dp", [(i, (i + k) % dp_size) for i in range(dp_size)])
+        for k in range(1, dp_size)
+    ]
+    shifted_rows = jnp.concatenate(shifted_rows, axis=0)
     slot_ids = first_slot + jnp.arange(slot_count, dtype=jnp.int32)
-    slot_pick = (slot_of[None, :] == slot_ids[:, None]).astype(jnp.bfloat16)
-    own_slots = lax.dynamic_slice_in_dim(slot_of, first_slot, slot_count)
-    send_pick = (jnp.arange(request_count, dtype=jnp.int32)[:, None] == own_slots[None, :]).astype(
+    request_ids = jnp.arange(slot_of.shape[0], dtype=jnp.int32)
+    uses_slot = slot_of[None, :] == slot_ids[:, None]
+    request_of_slot = jnp.sum(jnp.where(uses_slot, request_ids[None, :], 0), axis=1)
+    arrival = ((group - request_of_slot // slot_count) % dp_size) * slot_count + request_of_slot % slot_count
+    pick = (arrival[:, None] == jnp.arange(shifted_rows.shape[0], dtype=jnp.int32)[None, :]).astype(
         jnp.bfloat16
     )
-    gathered = lax.all_gather(dec_hidden, "dp", axis=0, tiled=True)
-    arrived = jnp.dot(slot_pick, gathered, preferred_element_type=jnp.float32).astype(jnp.bfloat16)
+    arrived = jnp.dot(pick, shifted_rows, preferred_element_type=jnp.float32).astype(jnp.bfloat16)
     normed_slots = normalize(arrived, norm_gain, norm_shift)
     merged_slots = (
         jnp.dot(normed_slots, qkv_weight, preferred_element_type=jnp.float32)
@@ -170,12 +179,26 @@
         slopes,
     )
     slot_partial = jnp.dot(slot_context, out_weight, preferred_element_type=jnp.float32)
-    slot_summed = lax.psum(slot_partial, "tensor")
+    partials = jnp.stack(
+        [slot_partial]
+        + [
+            lax.ppermute(slot_partial, "tensor", [(i, (i + k) % tensor_size) for i in range(tensor_size)])
+            for k in range(1, tensor_size)
+        ]
+    )
+    slot_summed = partials[member % tensor_size]
+    for source in range(1, tensor_size):
+        slot_summed = slot_summed + partials[(member - source) % tensor_size]
     slot_rows = (slot_summed + bias_sum + arrived.astype(jnp.float32)).astype(jnp.bfloat16)
-    everything = lax.all_gather(slot_rows, "dp", axis=0, tiled=True)
-    dec_output = jnp.dot(send_pick.T, everything, preferred_element_type=jnp.float32).astype(
-        jnp.bfloat16
-    )
+    returned = [slot_rows] + [
+        lax.ppermute(slot_rows, "dp", [(i, (i + k) % dp_size) for i in range(dp_size)])
+        for k in range(1, dp_size)
+    ]
+    returned = jnp.concatenate(returned, axis=0)
+    slot_wanted = lax.dynamic_slice_in_dim(slot_of, first_slot, slot_count)
+    back = ((group - slot_wanted // slot_count) % dp_size) * slot_count + slot_wanted % slot_count
+    take = (back[:, None] == jnp.arange(returned.shape[0], dtype=jnp.int32)[None, :]).astype(jnp.bfloat16)
+    dec_output = jnp.dot(take, returned, preferred_element_type=jnp.float32).astype(jnp.bfloat16)
     return (pre_output, dec_output)
 
 

time: 208 us -> 191 us (0.918)
  blocking collectives: 72.2 us -> 0 us
  waiting for transfers between devices: 28 us -> 57 us
  starting transfers between devices: 0.08 us -> 25.8 us
    all_gather x2 -> x0, blocking collectives: 61.1 us -> none  [the longest x1 30.6 us: per_device(): gathered = lax.all_gather(dec_hidden, 'dp', axis=0, tiled=True)]
    reduce_scatter x1, waiting for transfers between devices: 0.01 us -> 26 us  [per_device(): lax.psum_scatter(jnp.dot(context, out_weight, preferred_element_type=jnp....]
    ppermute x0 -> x17, starting transfers between devices: none -> 25.7 us  [the longest x7 12.1 us: per_device(): lax.ppermute(dec_hidden, 'dp', [(i, (i + k) % dp_size) for i in range(dp_...]
    psum x1 -> x0, blocking collectives: 11.1 us -> none  [per_device(): slot_summed = lax.psum(slot_partial, 'tensor')]
    ppermute x0 -> x17, waiting for transfers between devices: none -> 3.03 us  [the longest x3 1.76 us: per_device(): lax.ppermute(slot_partial, 'tensor', [(i, (i + k) % tensor_size) for i in...]
  transfers between devices with their start and end apart: 2 -> 19, of which waited for: 1 -> 5; matrix products, arithmetic and copies ran while one was open for 12% -> 13% of each run, Pallas kernels for 0% -> 0%
where the time goes in v2:
time: 191 us; the launch traced here: 190 us
  waiting for transfers between devices  57 us (30%)
  matrix products  51.6 us (27%)
  starting transfers between devices  25.8 us (14%)
  other arithmetic  25.1 us (13%)
  local copies, waits for them, and re-layouts  15.8 us (8%)
  between operations  15 us (8%)
    all_gather x1, waiting for transfers between devices, per_device(): lax.all_gather(normed, 'tensor', axis=0, tiled=True)  28 us
    reduce_scatter x1, waiting for transfers between devices, per_device(): lax.psum_scatter(jnp.dot(context, out_weight, preferred_element_type=jnp....  26 us
    ppermute x7, starting transfers between devices, per_device(): lax.ppermute(dec_hidden, 'dp', [(i, (i + k) % dp_size) for i in range(dp_...  12.1 us
    dot_general x1, matrix products, per_device(): jnp.dot(lax.all_gather(normed, 'tensor', axis=0, tiled=True), qkv_weight,...  11.2 us
    ppermute x7, starting transfers between devices, per_device(): lax.ppermute(slot_rows, 'dp', [(i, (i + k) % dp_size) for i in range(dp_s...  11.1 us
    dot_general x1, matrix products, prefill_attention(): jnp.einsum('qhd,khd->hqk', queries, new_keys, preferred_element_type=jnp....  10.8 us
    reduce_sum x1, other arithmetic, prefill_attention(): jnp.sum(new_exp, axis=-1, keepdims=True)  8.4 us
    dot_general x1, matrix products, prefill_attention(): jnp.einsum('hqk,khd->qhd', new_probs, new_values, preferred_element_type=...  7.69 us
  transfers between devices with their start and end apart: 19, of which 5 were waited for; matrix products, arithmetic and copies ran while one was open for 13% of the time, Pallas kernels for 0%

profile of v2, /device:TPU:0, one launch (start us, length us, event | category | flops | bytes accessed | tf_op | source)
XLA Modules:
  0.0 190.2 jit_solution(8517511923464856133)
XLA Ops:
  7.2 0.0 copy-start
  7.2 0.0 all-gather.2.cloned.1.call-start
  7.2 0.8 convert_element_type.111
  8.1 0.7 convert_element_type.112
  8.8 1.4 convert_reduce_fusion
  10.2 1.6 fusion.11
  11.9 2.7 %fusion.14 = bf16[256,2048]{1,0:T(8,128)(2,1)} fusion(bf16[256,2048]{1,0:T(8,128)(2,1)} %param.15, f32[2048]{0:T(1024)S(1)} %convert_element_type.112, f32[2048]{0:T(1024)S(1)} %convert_element_type.111, f32[256]{0:T(256)S(1)} %add_rsqrt_fusion, f32[256]{0:T(256)S(1)} %broadcast_multiply_fusion), kind=kLoop, calls=%fused_computation.30 | loop fusion | flops 3145728 | bytes 2115584 | tf_op jit(solution)/shard_map/convert_element_type | solution.py:20
  14.6 0.0 all-gather.2.cloned.1.call-update
  14.6 0.0 reduce-scatter.2.cloned.1.call-start
  15.3 1.3 reshape_squeeze.6
  16.7 2.3 %copy.51 = bf16[1,1024,512]{1,2,0:T(8,128)(2,1)} copy(bf16[1,1024,512]{2,1,0:T(8,128)(2,1)} %param.24) | data formatting | bytes 2097152 | tf_op jit(solution)/shard_map/reshape;squeeze | solution.py:134
  19.0 1.3 iota_compare_fusion
  20.3 3.7 %subtract_convert_fusion = (f32[1024,1024]{0,1:T(8,128)}, f32[1024,1024]{0,1:T(8,128)}) fusion(s32[1024]{0:T(1024)S(1)} %iota_add_fusion), kind=kLoop, calls=%fused_computation.14 | loop fusion | flops 4194304 | bytes 8392704 | tf_op jit(solution)/shard_map/convert_element_type | solution.py:40
  24.0 28.0 %all-gather.2.cloned.1.call-done = bf16[1024,2048]{1,0:T(8,128)(2,1)} async-done(((bf16[256,2048]{1,0:T(8,128)(2,1)}), bf16[1024,2048]{1,0:T(8,128)(2,1)}) %all-gather.2.cloned.1.call-update) | async-done | bytes 4194320 | tf_op jit(solution)/shard_map/all_gather | solution.py:123
  52.0 11.2 %add_convert_fusion = bf16[1024,1536]{1,0:T(8,128)(2,1)} fusion(bf16[1024,2048]{1,0:T(8,128)(2,1)} %all-gather.2.cloned.1.call-done, bf16[2048,1536]{1,0:T(8,128)(2,1)} %param.19, f32[1536]{0:T(1024)S(1)} %convert_element_type.114), kind=kOutput, calls=%fused_computation.10 | convolution fusion | flops 6445596672 | bytes 13637632 | tf_op jit(solution)/shard_map/dot_general | solution.py:122
  63.2 4.7 %copy.32 = bf16[1024,1536]{0,1:T(8,128)(2,1)} copy(bf16[1024,1536]{1,0:T(8,128)(2,1)} %add_convert_fusion) | data formatting | bytes 6291456 | tf_op jit(solution)/shard_map/convert_element_type | solution.py:127
  67.9 10.8 %fusion.54 = (f32[4,1024]{1,0:T(4,128)S(1)}, f32[4,1024,1024]{1,2,0:T(8,128)}) fusion(f32[1024,1024]{0,1:T(8,128)} %get-tuple-element.9, f32[4]{0:T(128)S(1)} %multiply_exponential_fusion, bf16[1024,4,3,128]{0,3,2,1:T(8,128)(2,1)} %bitcast.86, pred[1024,1024]{0,1:T(8,128)(4,1)} %iota_compare_fusion), kind=kOutput, calls=%fused_computation.113 | convolution fusion | flops 1094709248 | bytes 24133648 | tf_op jit(solution)/shard_map/qhd,khd->hqk/dot_general | solution.py:47
  78.7 3.7 %fusion.53 = (f32[4,1024]{1,0:T(4,128)S(1)}, f32[4,1024,1024]{1,2,0:T(8,128)S(1)}) fusion(f32[1024,1024]{0,1:T(8,128)S(1)} %copy-done.1, f32[4]{0:T(128)S(1)} %multiply_exponential_fusion, bf16[1024,4,3,128]{0,3,2,1:T(8,128)(2,1)S(1)} %bitcast.87, bf16[1024,4,128]{2,1,0:T(4,128)(2,1)S(1)} %reshape_squeeze.6, pred[1024]{0:T(1024)(128)(4,1)S(1)} %iota_compare_fusion.2), kind=kOutput, calls=%fused_computation.112 | convolution fusion | flops 1094709248 | bytes 23086592 | tf_op jit(solution)/shard_map/qhd,khd->hqk/dot_general | solution.py:42
  82.5 0.0 copy-start.4
  82.5 8.4 %fusion.1 = (f32[4,1024]{1,0:T(4,128)S(1)}, f32[4,1024]{1,0:T(4,128)S(1)}) fusion(f32[4,1024,1024]{1,2,0:T(8,128)} %get-tuple-element.16, f32[4,1024]{1,0:T(4,128)S(1)} %max.12, f32[4,1024,1024]{1,2,0:T(8,128)S(1)} %get-tuple-element.14), kind=kLoop, calls=%fused_computation.7 | loop fusion | flops 16769024 | bytes 33603584 | tf_op jit(solution)/shard_map/reduce_sum | solution.py:60
  90.9 3.7 %fusion.2 = f32[4,1024,128]{1,2,0:T(8,128)S(1)} fusion(bf16[1024,4,128]{0,2,1:T(8,128)(2,1)S(1)} %bitcast.89, f32[4,1024,1024]{1,2,0:T(8,128)S(1)} %get-tuple-element.14, f32[4,1024]{1,0:T(4,128)S(1)} %add.237, f32[4,1024]{1,0:T(4,128)S(1)} %max.12), kind=kOutput, calls=%fused_computation.8 | convolution fusion | flops 1086324736 | bytes 19955712 | tf_op jit(solution)/shard_map/hqk,khd->qhd/dot_general | solution.py:65
  94.6 7.7 %fusion.16 = bf16[1024,4,128]{0,2,1:T(8,128)(2,1)S(1)} fusion(f32[4,1024,128]{1,2,0:T(8,128)S(1)} %fusion.2, f32[4,1024,1024]{1,2,0:T(8,128)} %get-tuple-element.16, f32[4,1024]{1,0:T(4,128)S(1)} %add.237, f32[4,1024]{1,0:T(4,128)S(1)} %max.12, bf16[1024,4,3,128]{0,3,2,1:T(8,128)(2,1)S(1)} %bitcast.88), kind=kOutput, calls=%fused_computation.33 | convolution fusion | flops 1087373312 | bytes 21004288 | tf_op jit(solution)/shard_map/hqk,khd->qhd/dot_general | solution.py:68
  102.3 5.6 %fusion.56 = f32[1024,2048]{1,0:T(8,128)} fusion(bf16[1024,512]{0,1:T(8,128)(2,1)S(1)} %bitcast.96, bf16[512,2048]{1,0:T(8,128)(2,1)S(1)} %copy-done), kind=kOutput, calls=%fused_computation.115 | convolution fusion | flops 2147483648 | bytes 11534336 | tf_op jit(solution)/shard_map/dot_general | solution.py:139
  107.9 0.0 reduce-scatter.2.cloned.1.call-update
  107.9 0.7 copy-done.5
  108.6 1.5 collective-permute-start
  110.1 1.5 collective-permute-start.1
  111.5 2.4 %collective-permute-start.2 = (bf16[2,2048]{1,0:T(2,128)(2,1)S(1)}, bf16[2,2048]{1,0:T(2,128)(2,1)S(1)}, u32[]{:S(2)}, u32[]{:S(2)}) collective-permute-start(bf16[2,2048]{1,0:T(2,128)(2,1)S(1)} %copy-done.5), channel_id=1, source_target_pairs={{0,12},{4,16},{8,20},{12,24},{16,28},{20,0},{24,4},{28,8},{1,13},{... | collective-permute-start | bytes 24584 | tf_op jit(solution)/shard_map/ppermute | solution.py:152
  113.9 1.4 collective-permute-start.3
  115.4 2.4 %collective-permute-start.4 = (bf16[2,2048]{1,0:T(2,128)(2,1)S(1)}, bf16[2,2048]{1,0:T(2,128)(2,1)S(1)}, u32[]{:S(2)}, u32[]{:S(2)}) collective-permute-start(bf16[2,2048]{1,0:T(2,128)(2,1)S(1)} %copy-done.5), channel_id=1, source_target_pairs={{0,20},{4,24},{8,28},{12,0},{16,4},{20,8},{24,12},{28,16},{1,21},{... | collective-permute-start | bytes 24584 | tf_op jit(solution)/shard_map/ppermute | solution.py:152
  117.8 0.1 iota_compare_fusion.1
  117.9 0.1 subtract_convert_fusion.2
  117.9 0.2 fusion.37
  118.1 1.5 collective-permute-start.5
  119.6 1.5 collective-permute-start.6
  121.1 6.5 %copy.52 = bf16[2,2048,512]{1,2,0:T(8,128)(2,1)} copy(bf16[2,2048,512]{2,1,0:T(8,128)(2,1)} %param.25) | data formatting | bytes 8388608 | tf_op jit(solution)/shard_map/reshape | solution.py:176
  127.6 0.1 concatenate.6
  127.8 0.3 fusion.55
  128.1 0.2 multiply_reduce_fusion
  128.3 3.8 %fusion.9 = bf16[2,1536]{1,0:T(2,128)(2,1)S(1)} fusion(bf16[2048,1536]{1,0:T(8,128)(2,1)} %param.19, f32[2,2048]{1,0:T(2,128)S(1)} %get-tuple-element.18, f32[2]{0:T(128)S(1)} %add_rsqrt_fusion.1, f32[2]{0:T(128)S(1)} %broadcast_multiply_fusion.1, f32[2048]{0:T(1024)S(1)} %convert_element_type.112, f32[2048]{0:T(1024)S(1)} %convert_element_type.111, ...), kind=kOutput, calls=%fused_computation.23 | convolution fusion | flops 12609536 | bytes 6336528 | tf_op jit(solution)/shard_map/dot_general | solution.py:167
  132.1 0.1 fusion.28
  132.2 3.0 %fusion.29 = f32[2,4,1,2048]{3,2,1,0:T(1,128)S(1)} fusion(bf16[2,2048,4,128]{1,3,2,0:T(8,128)(2,1)} %bitcast.85, bf16[2,4,3,128]{3,2,1,0:T(4,128)(2,1)S(1)} %reshape.249), kind=kOutput, calls=%fused_computation.60 | convolution fusion | flops 4194304 | bytes 4263936 | tf_op jit(solution)/shard_map/vmap(hd,khd->hk)/dot_general | solution.py:79
  135.2 0.2 fusion.51
  135.4 0.2 fusion.21
  135.6 0.1 fusion.22
  135.7 0.6 fusion.4
  136.3 0.1 fusion.31
  136.4 0.4 fusion.32
  136.8 1.1 collective-permute-start.8
  137.9 1.4 collective-permute-start.9
  139.3 1.0 collective-permute-done.7
  140.3 0.8 collective-permute-done.8
  141.1 1.1 collective-permute-start.10
  142.3 0.9 collective-permute-start.11
  143.2 1.3 collective-permute-start.12
  144.5 3.1 %collective-permute-start.13 = (bf16[2,2048]{1,0:T(2,128)(2,1)S(1)}, bf16[2,2048]{1,0:T(2,128)(2,1)S(1)}, u32[]{:S(2)}, u32[]{:S(2)}) collective-permute-start(bf16[2,2048]{1,0:T(2,128)(2,1)S(1)} %fusion.24), channel_id=1, source_target_pairs={{0,16},{4,20},{8,24},{12,28},{16,0},{20,4},{24,8},{28,12},{1,17},{... | collective-permute-start | bytes 24584 | tf_op jit(solution)/shard_map/ppermute | solution.py:194
  147.6 2.4 %collective-permute-start.15 = (bf16[2,2048]{1,0:T(2,128)(2,1)S(1)}, bf16[2,2048]{1,0:T(2,128)(2,1)S(1)}, u32[]{:S(2)}, u32[]{:S(2)}) collective-permute-start(bf16[2,2048]{1,0:T(2,128)(2,1)S(1)} %fusion.24), channel_id=1, source_target_pairs={{0,24},{4,28},{8,0},{12,4},{16,8},{20,12},{24,16},{28,20},{1,25},{... | collective-permute-start | bytes 24584 | tf_op jit(solution)/shard_map/ppermute | solution.py:194
  149.9 2.3 %collective-permute-start.16 = (bf16[2,2048]{1,0:T(2,128)(2,1)S(1)}, bf16[2,2048]{1,0:T(2,128)(2,1)S(1)}, u32[]{:S(2)}, u32[]{:S(2)}) collective-permute-start(bf16[2,2048]{1,0:T(2,128)(2,1)S(1)} %fusion.24), channel_id=1, source_target_pairs={{0,28},{4,0},{8,4},{12,8},{16,12},{20,16},{24,20},{28,24},{1,29},{... | collective-permute-start | bytes 24584 | tf_op jit(solution)/shard_map/ppermute | solution.py:194
  152.2 0.1 fusion.40
  152.4 1.2 collective-permute-done.16
  153.6 0.1 concatenate.7
  153.7 0.8 convolution_convert_fusion
  154.5 26.0 %reduce-scatter.2.cloned.1.call-done = f32[256,2048]{1,0:T(8,128)} async-done(((f32[1024,2048]{1,0:T(8,128)}), f32[256,2048]{1,0:T(8,128)}) %reduce-scatter.2.cloned.1.call-update) | async-done | bytes 2097168 | tf_op jit(solution)/shard_map/reduce_scatter | solution.py:138
  180.5 2.9 %fusion.15 = bf16[256,2048]{1,0:T(8,128)(2,1)} fusion(bf16[256,2048]{1,0:T(8,128)(2,1)S(1)} %copy-done.2, f32[256,2048]{1,0:T(8,128)} %reduce-scatter.2.cloned.1.call-done, f32[2048]{0:T(1024)S(1)} %convert_element_type.122), kind=kLoop, calls=%fused_computation.31 | loop fusion | flops 2097152 | bytes 4202496 | tf_op jit(solution)/shard_map/convert_element_type | solution.py:144
  (54 shorter events, 0.3 us)
Async XLA Ops:
  7.2 95.1 %copy-start = (bf16[512,2048]{1,0:T(8,128)(2,1)S(1)}, bf16[512,2048]{1,0:T(8,128)(2,1)}, u32[]{:S(2)}) copy-start(bf16[512,2048]{1,0:T(8,128)(2,1)} %param.21) | copy-start | bytes 6291460
  7.2 7.5 %copy-start.6 = (bf16[1536]{0:T(1024)(128)(2,1)S(1)}, bf16[1536]{0:T(1024)(128)(2,1)}, u32[]{:S(2)}) copy-start(bf16[1536]{0:T(1024)(128)(2,1)} %param.20) | copy-start | bytes 9220
  7.2 44.8 %all-gather.2.cloned.1.call-start = ((), (), s32[]{:S(2)}) async-start(), calls=%async_computation.1 | async-start | bytes 5242880 | tf_op jit(solution)/shard_map/all_gather | solution.py:123
  14.6 165.8 %reduce-scatter.2.cloned.1.call-start = ((), (), s32[]{:S(2)}) async-start(), calls=%async_computation.2 | async-start | bytes 10485760 | tf_op jit(solution)/shard_map/reduce_scatter | solution.py:138
  67.9 10.8 %copy-start.1 = (f32[1024,1024]{0,1:T(8,128)S(1)}, f32[1024,1024]{0,1:T(8,128)}, u32[]{:S(2)}) copy-start(f32[1024,1024]{0,1:T(8,128)} %get-tuple-element.10) | copy-start | bytes 12582916
  67.9 10.9 %copy-start.3 = (bf16[1024,1536]{0,1:T(8,128)(2,1)S(1)}, bf16[1024,1536]{0,1:T(8,128)(2,1)}, u32[]{:S(2)}) copy-start(bf16[1024,1536]{0,1:T(8,128)(2,1)} %copy.32) | copy-start | bytes 9437188
  82.5 8.4 %copy-start.4 = (bf16[1,1024,512]{1,2,0:T(8,128)(2,1)S(1)}, bf16[1,1024,512]{1,2,0:T(8,128)(2,1)}, u32[]{:S(2)}) copy-start(bf16[1,1024,512]{1,2,0:T(8,128)(2,1)} %copy.51) | copy-start | bytes 3145732
  107.9 0.7 copy-start.5
  107.9 9.9 %copy-start.8 = (s32[2]{0:T(128)S(1)}, s32[2]{0:T(128)}, u32[]{:S(2)}) copy-start(s32[2]{0:T(128)} %param.28) | copy-start | bytes 28
  107.9 10.1 %copy-start.9 = (s32[16]{0:T(128)S(1)}, s32[16]{0:T(128)}, u32[]{:S(2)}) copy-start(s32[16]{0:T(128)} %param.29) | copy-start | bytes 196
  108.6 9.5 %collective-permute-start = (bf16[2,2048]{1,0:T(2,128)(2,1)S(1)}, bf16[2,2048]{1,0:T(2,128)(2,1)S(1)}, u32[]{:S(2)}, u32[]{:S(2)}) collective-permute-start(bf16[2,2048]{1,0:T(2,128)(2,1)S(1)} %copy-done.5), channel_id=1, source_target_pairs={{0,4},{4,8},{8,12},{12,16},{16,20},{20,24},{24,28},{28,0},{1,5},{5... | collective-permute-start | bytes 24584 | tf_op jit(solution)/shard_map/ppermute | solution.py:152
  110.1 9.6 %collective-permute-start.1 = (bf16[2,2048]{1,0:T(2,128)(2,1)S(1)}, bf16[2,2048]{1,0:T(2,128)(2,1)S(1)}, u32[]{:S(2)}, u32[]{:S(2)}) collective-permute-start(bf16[2,2048]{1,0:T(2,128)(2,1)S(1)} %copy-done.5), channel_id=1, source_target_pairs={{0,8},{4,12},{8,16},{12,20},{16,24},{20,28},{24,0},{28,4},{1,9},{5... | collective-permute-start | bytes 24584 | tf_op jit(solution)/shard_map/ppermute | solution.py:152
  111.5 16.1 %collective-permute-start.2 = (bf16[2,2048]{1,0:T(2,128)(2,1)S(1)}, bf16[2,2048]{1,0:T(2,128)(2,1)S(1)}, u32[]{:S(2)}, u32[]{:S(2)}) collective-permute-start(bf16[2,2048]{1,0:T(2,128)(2,1)S(1)} %copy-done.5), channel_id=1, source_target_pairs={{0,12},{4,16},{8,20},{12,24},{16,28},{20,0},{24,4},{28,8},{1,13},{... | collective-permute-start | bytes 24584 | tf_op jit(solution)/shard_map/ppermute | solution.py:152
  113.9 13.7 %collective-permute-start.3 = (bf16[2,2048]{1,0:T(2,128)(2,1)S(1)}, bf16[2,2048]{1,0:T(2,128)(2,1)S(1)}, u32[]{:S(2)}, u32[]{:S(2)}) collective-permute-start(bf16[2,2048]{1,0:T(2,128)(2,1)S(1)} %copy-done.5), channel_id=1, source_target_pairs={{0,16},{4,20},{8,24},{12,28},{16,0},{20,4},{24,8},{28,12},{1,17},{... | collective-permute-start | bytes 24584 | tf_op jit(solution)/shard_map/ppermute | solution.py:152
  115.4 12.3 %collective-permute-start.4 = (bf16[2,2048]{1,0:T(2,128)(2,1)S(1)}, bf16[2,2048]{1,0:T(2,128)(2,1)S(1)}, u32[]{:S(2)}, u32[]{:S(2)}) collective-permute-start(bf16[2,2048]{1,0:T(2,128)(2,1)S(1)} %copy-done.5), channel_id=1, source_target_pairs={{0,20},{4,24},{8,28},{12,0},{16,4},{20,8},{24,12},{28,16},{1,21},{... | collective-permute-start | bytes 24584 | tf_op jit(solution)/shard_map/ppermute | solution.py:152
  118.1 9.5 %collective-permute-start.5 = (bf16[2,2048]{1,0:T(2,128)(2,1)S(1)}, bf16[2,2048]{1,0:T(2,128)(2,1)S(1)}, u32[]{:S(2)}, u32[]{:S(2)}) collective-permute-start(bf16[2,2048]{1,0:T(2,128)(2,1)S(1)} %copy-done.5), channel_id=1, source_target_pairs={{0,24},{4,28},{8,0},{12,4},{16,8},{20,12},{24,16},{28,20},{1,25},{... | collective-permute-start | bytes 24584 | tf_op jit(solution)/shard_map/ppermute | solution.py:152
  119.6 8.0 %collective-permute-start.6 = (bf16[2,2048]{1,0:T(2,128)(2,1)S(1)}, bf16[2,2048]{1,0:T(2,128)(2,1)S(1)}, u32[]{:S(2)}, u32[]{:S(2)}) collective-permute-start(bf16[2,2048]{1,0:T(2,128)(2,1)S(1)} %copy-done.5), channel_id=1, source_target_pairs={{0,28},{4,0},{8,4},{12,8},{16,12},{20,16},{24,20},{28,24},{1,29},{... | collective-permute-start | bytes 24584 | tf_op jit(solution)/shard_map/ppermute | solution.py:152
  132.1 3.6 %copy-start.10 = (bf16[2,2048,512]{2,1,0:T(8,128)(2,1)S(1)}, bf16[2,2048,512]{2,1,0:T(8,128)(2,1)}, u32[]{:S(2)}) copy-start(bf16[2,2048,512]{2,1,0:T(8,128)(2,1)} %param.26) | copy-start | bytes 12582916
  135.2 4.1 %copy-start.7 = (bf16[2048]{0:T(1024)(128)(2,1)S(1)}, bf16[2048]{0:T(1024)(128)(2,1)}, u32[]{:S(2)}) copy-start(bf16[2048]{0:T(1024)(128)(2,1)} %param.22) | copy-start | bytes 12292
  135.2 45.3 %copy-start.2 = (bf16[256,2048]{1,0:T(8,128)(2,1)S(1)}, bf16[256,2048]{1,0:T(8,128)(2,1)}, u32[]{:S(2)}) copy-start(bf16[256,2048]{1,0:T(8,128)(2,1)} %param.15) | copy-start | bytes 3145732
  136.8 3.5 %collective-permute-start.7 = (f32[2,2048]{1,0:T(2,128)S(1)}, f32[2,2048]{1,0:T(2,128)S(1)}, u32[]{:S(2)}, u32[]{:S(2)}) collective-permute-start(f32[2,2048]{1,0:T(2,128)S(1)} %fusion.32), channel_id=1, source_target_pairs={{0,1},{1,2},{2,3},{3,0},{4,5},{5,6},{6,7},{7,4},{8,9},{9,10},{10,1... | collective-permute-start | bytes 49160 | tf_op jit(solution)/shard_map/ppermute | solution.py:185
  136.8 4.2 %collective-permute-start.8 = (f32[2,2048]{1,0:T(2,128)S(1)}, f32[2,2048]{1,0:T(2,128)S(1)}, u32[]{:S(2)}, u32[]{:S(2)}) collective-permute-start(f32[2,2048]{1,0:T(2,128)S(1)} %fusion.32), channel_id=1, source_target_pairs={{0,2},{1,3},{2,0},{3,1},{4,6},{5,7},{6,4},{7,5},{8,10},{9,11},{10,... | collective-permute-start | bytes 49160 | tf_op jit(solution)/shard_map/ppermute | solution.py:185
  137.9 3.2 %collective-permute-start.9 = (f32[2,2048]{1,0:T(2,128)S(1)}, f32[2,2048]{1,0:T(2,128)S(1)}, u32[]{:S(2)}, u32[]{:S(2)}) collective-permute-start(f32[2,2048]{1,0:T(2,128)S(1)} %fusion.32), channel_id=1, source_target_pairs={{0,3},{1,0},{2,1},{3,2},{4,7},{5,4},{6,5},{7,6},{8,11},{9,8},{10,9... | collective-permute-start | bytes 49160 | tf_op jit(solution)/shard_map/ppermute | solution.py:185
  141.1 6.4 %collective-permute-start.10 = (bf16[2,2048]{1,0:T(2,128)(2,1)S(1)}, bf16[2,2048]{1,0:T(2,128)(2,1)S(1)}, u32[]{:S(2)}, u32[]{:S(2)}) collective-permute-start(bf16[2,2048]{1,0:T(2,128)(2,1)S(1)} %fusion.24), channel_id=1, source_target_pairs={{0,4},{4,8},{8,12},{12,16},{16,20},{20,24},{24,28},{28,0},{1,5},{5... | collective-permute-start | bytes 24584 | tf_op jit(solution)/shard_map/ppermute | solution.py:194
  142.3 7.7 %collective-permute-start.11 = (bf16[2,2048]{1,0:T(2,128)(2,1)S(1)}, bf16[2,2048]{1,0:T(2,128)(2,1)S(1)}, u32[]{:S(2)}, u32[]{:S(2)}) collective-permute-start(bf16[2,2048]{1,0:T(2,128)(2,1)S(1)} %fusion.24), channel_id=1, source_target_pairs={{0,8},{4,12},{8,16},{12,20},{16,24},{20,28},{24,0},{28,4},{1,9},{5... | collective-permute-start | bytes 24584 | tf_op jit(solution)/shard_map/ppermute | solution.py:194
  143.2 9.1 %collective-permute-start.12 = (bf16[2,2048]{1,0:T(2,128)(2,1)S(1)}, bf16[2,2048]{1,0:T(2,128)(2,1)S(1)}, u32[]{:S(2)}, u32[]{:S(2)}) collective-permute-start(bf16[2,2048]{1,0:T(2,128)(2,1)S(1)} %fusion.24), channel_id=1, source_target_pairs={{0,12},{4,16},{8,20},{12,24},{16,28},{20,0},{24,4},{28,8},{1,13},{... | collective-permute-start | bytes 24584 | tf_op jit(solution)/shard_map/ppermute | solution.py:194
  144.5 7.9 %collective-permute-start.13 = (bf16[2,2048]{1,0:T(2,128)(2,1)S(1)}, bf16[2,2048]{1,0:T(2,128)(2,1)S(1)}, u32[]{:S(2)}, u32[]{:S(2)}) collective-permute-start(bf16[2,2048]{1,0:T(2,128)(2,1)S(1)} %fusion.24), channel_id=1, source_target_pairs={{0,16},{4,20},{8,24},{12,28},{16,0},{20,4},{24,8},{28,12},{1,17},{... | collective-permute-start | bytes 24584 | tf_op jit(solution)/shard_map/ppermute | solution.py:194
  147.5 4.8 %collective-permute-start.14 = (bf16[2,2048]{1,0:T(2,128)(2,1)S(1)}, bf16[2,2048]{1,0:T(2,128)(2,1)S(1)}, u32[]{:S(2)}, u32[]{:S(2)}) collective-permute-start(bf16[2,2048]{1,0:T(2,128)(2,1)S(1)} %fusion.24), channel_id=1, source_target_pairs={{0,20},{4,24},{8,28},{12,0},{16,4},{20,8},{24,12},{28,16},{1,21},{... | collective-permute-start | bytes 24584 | tf_op jit(solution)/shard_map/ppermute | solution.py:194
  147.6 4.8 %collective-permute-start.15 = (bf16[2,2048]{1,0:T(2,128)(2,1)S(1)}, bf16[2,2048]{1,0:T(2,128)(2,1)S(1)}, u32[]{:S(2)}, u32[]{:S(2)}) collective-permute-start(bf16[2,2048]{1,0:T(2,128)(2,1)S(1)} %fusion.24), channel_id=1, source_target_pairs={{0,24},{4,28},{8,0},{12,4},{16,8},{20,12},{24,16},{28,20},{1,25},{... | collective-permute-start | bytes 24584 | tf_op jit(solution)/shard_map/ppermute | solution.py:194
  149.9 3.7 %collective-permute-start.16 = (bf16[2,2048]{1,0:T(2,128)(2,1)S(1)}, bf16[2,2048]{1,0:T(2,128)(2,1)S(1)}, u32[]{:S(2)}, u32[]{:S(2)}) collective-permute-start(bf16[2,2048]{1,0:T(2,128)(2,1)S(1)} %fusion.24), channel_id=1, source_target_pairs={{0,28},{4,0},{8,4},{12,8},{16,12},{20,16},{24,20},{28,24},{1,29},{... | collective-permute-start | bytes 24584 | tf_op jit(solution)/shard_map/ppermute | solution.py:194
Sparse Core Ops, SparseCore 0:
  14.7 37.1 all-gather.1
  108.0 72.3 reduce-scatter.1

commit v3 on v2

--- a/solution.py
+++ b/solution.py
@@ -27,17 +27,13 @@
     return jnp.exp2(-8.0 * (head_ids + 1.0) / total_heads)
 
 
-def prefill_attention(merged_rows, cache_keys, cache_values, prefix, slopes):
-    queries = merged_rows[:, :, 0]
-    new_keys = merged_rows[:, :, 1]
-    new_values = merged_rows[:, :, 2]
-    group_size = merged_rows.shape[0]
+def prefill_attention(queries, query_tok, new_keys, new_values, key_tok, cache_keys, cache_values, prefix, slopes):
     cache_size = cache_keys.shape[0]
-    factor = 1.0 / math.sqrt(merged_rows.shape[-1])
-    query_pos = prefix + jnp.arange(group_size, dtype=jnp.int32)
+    factor = 1.0 / math.sqrt(queries.shape[-1])
+    query_pos = prefix + query_tok
     cache_pos = jnp.arange(cache_size, dtype=jnp.int32)
     cache_dist = (query_pos[:, None] - cache_pos[None, :]).astype(jnp.float32)
-    new_dist = (query_pos[:, None] - query_pos[None, :]).astype(jnp.float32)
+    new_dist = (query_tok[:, None] - key_tok[None, :]).astype(jnp.float32)
     cache_scores = (
         jnp.einsum("qhd,khd->hqk", queries, cache_keys, preferred_element_type=jnp.float32) * factor
     )
@@ -47,10 +43,7 @@
         jnp.einsum("qhd,khd->hqk", queries, new_keys, preferred_element_type=jnp.float32) * factor
     )
     new_scores = new_scores - slopes[:, None, None] * new_dist[None]
-    causal = (
-        jnp.arange(group_size, dtype=jnp.int32)[None, :]
-        <= jnp.arange(group_size, dtype=jnp.int32)[:, None]
-    )
+    causal = key_tok[None, :] <= query_tok[:, None]
     new_scores = jnp.where(causal[None], new_scores, -jnp.inf)
     highest = jnp.maximum(
         jnp.max(cache_scores, axis=-1, keepdims=True), jnp.max(new_scores, axis=-1, keepdims=True)
@@ -68,7 +61,7 @@
     context = context + jnp.einsum(
         "hqk,khd->qhd", new_probs, new_values, preferred_element_type=jnp.float32
     )
-    return context.astype(jnp.bfloat16).reshape(group_size, -1)
+    return context.astype(jnp.bfloat16).reshape(queries.shape[0], -1)
 
 
 def decode_attention(query_row, new_key, new_value, cache_keys, cache_values, length, slopes):
@@ -118,35 +111,58 @@
     local_heads = qkv_weight.shape[1] // (3 * head_size)
     slopes = alibi_slopes(lax.axis_index("tensor") * local_heads, local_heads, H)
     bias_sum = out_bias.astype(jnp.float32)
+    tensor_size = lax.axis_size("tensor")
+    chips = tensor_size // 2
+    member = lax.axis_index("tensor")
+    chip = member // 2
+    core = member % 2
+    sibling = [(i, i ^ 1) for i in range(tensor_size)]
+
+    def across(k):
+        return [(i, ((i // 2 + k) % chips) * 2 + i % 2) for i in range(tensor_size)]
+
+    block = pre_hidden.shape[0]
     normed = normalize(pre_hidden, norm_gain, norm_shift)
-    product = jnp.dot(
-        lax.all_gather(normed, "tensor", axis=0, tiled=True),
-        qkv_weight,
-        preferred_element_type=jnp.float32,
-    )
+    same_core = jnp.concatenate(
+        [normed] + [lax.ppermute(normed, "tensor", across(k)) for k in range(1, chips)], axis=0
+    )
+    other_core = lax.ppermute(same_core, "tensor", sibling)
+    tokens = jnp.concatenate([same_core, other_core], axis=0)
+    block_chip = (chip - jnp.arange(chips, dtype=jnp.int32)) % chips
+    block_member = jnp.concatenate([block_chip * 2 + core, block_chip * 2 + (1 - core)])
+    token_index = block_member[:, None] * block + jnp.arange(block, dtype=jnp.int32)[None, :]
+    product = jnp.dot(tokens, qkv_weight, preferred_element_type=jnp.float32)
     merged_rows = (product + qkv_bias.astype(jnp.float32)).astype(jnp.bfloat16)
-    group_size = merged_rows.shape[0]
-    merged_rows = merged_rows.reshape(group_size, local_heads, 3, head_size)
+    merged_rows = merged_rows.reshape(tensor_size, block, local_heads, 3, head_size)
+    all_tok = token_index.reshape(-1)
+    new_keys = merged_rows[:, :, :, 1].reshape(tensor_size * block, local_heads, head_size)
+    new_values = merged_rows[:, :, :, 2].reshape(tensor_size * block, local_heads, head_size)
     cache_size = pre_keys.shape[1]
-    context = prefill_attention(
-        merged_rows,
-        pre_keys[0].reshape(cache_size, local_heads, head_size),
-        pre_values[0].reshape(cache_size, local_heads, head_size),
-        prefix_lengths[0],
-        slopes,
-    )
-    summed = lax.psum_scatter(
-        jnp.dot(context, out_weight, preferred_element_type=jnp.float32),
-        "tensor",
-        scatter_dimension=0,
-        tiled=True,
-    )
+    cache_keys = pre_keys[0].reshape(cache_size, local_heads, head_size)
+    cache_values = pre_values[0].reshape(cache_size, local_heads, head_size)
+    chunks = 2
+    part = block // chunks
+    pieces = []
+    for h in range(chunks):
+        rows = slice(h * part, (h + 1) * part)
+        queries = merged_rows[:, rows, :, 0].reshape(tensor_size * part, local_heads, head_size)
+        query_tok = token_index[:, rows].reshape(-1)
+        context = prefill_attention(
+            queries, query_tok, new_keys, new_values, all_tok, cache_keys, cache_values,
+            prefix_lengths[0], slopes,
+        )
+        partial = jnp.dot(context, out_weight, preferred_element_type=jnp.float32)
+        partial = partial.reshape(2, chips, part, partial.shape[-1])
+        chip_sum = partial[0] + lax.ppermute(partial[1], "tensor", sibling)
+        total = chip_sum[0]
+        for k in range(1, chips):
+            total = total + lax.ppermute(chip_sum[k], "tensor", across(-k))
+        pieces.append(total)
+    summed = jnp.concatenate(pieces, axis=0)
     pre_output = (summed + bias_sum + pre_hidden.astype(jnp.float32)).astype(jnp.bfloat16)
     slot_count = dec_hidden.shape[0]
     dp_size = lax.axis_size("dp")
-    tensor_size = lax.axis_size("tensor")
     group = lax.axis_index("dp")
-    member = lax.axis_index("tensor")
     first_slot = group * slot_count
     shifted_rows = [dec_hidden] + [
         lax.ppermute(dec_hidden, "dp", [(i, (i + k) % dp_size) for i in range(dp_size)])

time: 191 us -> 229 us (1.20); the launches traced: 190 us -> 225 us
  local copies, waits for them, and re-layouts: 15.8 us -> 44.8 us
  waiting for transfers between devices: 57 us -> 34.3 us
  other arithmetic: 25.1 us -> 45.4 us
  matrix products: 51.6 us -> 70.4 us
  between operations: 15 us -> 2.28 us
    all_gather x1 -> x0, waiting for transfers between devices: 28 us -> none  [per_device(): lax.all_gather(normed, 'tensor', axis=0, tiled=True)]
    reduce_scatter x1 -> x0, waiting for transfers between devices: 26 us -> none  [per_device(): lax.psum_scatter(jnp.dot(context, out_weight, preferred_element_type=jnp....]
    ppermute x0 -> x6, waiting for transfers between devices: none -> 25 us  [the longest x2 25 us: per_device(): total = total + lax.ppermute(chip_sum[k], 'tensor', across(-k))]
    slice x0 -> x7, local copies, waits for them, and re-layouts: none -> 17.4 us  [the longest x3 6.68 us: per_device(): merged_rows[:, rows, :, 0]]
    dot_general x1 -> x2, matrix products: 10.8 us -> 24.6 us  [prefill_attention(): jnp.einsum('qhd,khd->hqk', queries, new_keys, preferred_element_type=jnp....]
    reduce_sum x1, other arithmetic: 8.4 us -> 17.3 us  [prefill_attention(): jnp.sum(new_exp, axis=-1, keepdims=True)]
    add x1 -> x7, other arithmetic: 0.01 us -> 7.86 us  [the longest x2 4.46 us: per_device(): chip_sum = partial[0] + lax.ppermute(partial[1], 'tensor', sibling)]
    dot_general x1 -> x2, matrix products: 3.69 us -> 10 us  [prefill_attention(): jnp.einsum('qhd,khd->hqk', queries, cache_keys, preferred_element_type=jn...]
  transfers between devices with their start and end apart: 19 -> 23, of which waited for: 5 -> 8; matrix products, arithmetic and copies ran while one was open for 13% -> 24% of each run, Pallas kernels for 0% -> 0%
where the time goes in v3:
time: 229 us; the launch traced here: 225 us
  matrix products  70.4 us (31%)
  other arithmetic  45.4 us (20%)
  local copies, waits for them, and re-layouts  44.8 us (20%)
  waiting for transfers between devices  34.3 us (15%)
  starting transfers between devices  27.6 us (12%)
    ppermute x2, waiting for transfers between devices, per_device(): total = total + lax.ppermute(chip_sum[k], 'tensor', across(-k))  25 us
    dot_general x2, matrix products, prefill_attention(): jnp.einsum('qhd,khd->hqk', queries, new_keys, preferred_element_type=jnp....  24.6 us
    reduce_sum x1, other arithmetic, prefill_attention(): jnp.sum(new_exp, axis=-1, keepdims=True)  17.3 us
    ppermute x7, starting transfers between devices, per_device(): lax.ppermute(dec_hidden, 'dp', [(i, (i + k) % dp_size) for i in range(dp_...  14 us
    dot_general x1, matrix products, per_device(): product = jnp.dot(tokens, qkv_weight, preferred_element_type=jnp.float32)  11.2 us
    dot_general x2, matrix products, prefill_attention(): jnp.einsum('qhd,khd->hqk', queries, cache_keys, preferred_element_type=jn...  10 us
    dot_general x2, matrix products, prefill_attention(): jnp.einsum('hqk,khd->qhd', new_probs, new_values, preferred_element_type=...  7.42 us
    ppermute x7, starting transfers between devices, per_device(): lax.ppermute(slot_rows, 'dp', [(i, (i + k) % dp_size) for i in range(dp_s...  7.32 us
  transfers between devices with their start and end apart: 23, of which 8 were waited for; matrix products, arithmetic and copies ran while one was open for 24% of the time, Pallas kernels for 0%

profile of v3, /device:TPU:0, one launch (start us, length us, event | category | flops | bytes accessed | tf_op | source)
XLA Modules:
  0.0 224.8 jit_solution(8159556290987529364)
XLA Ops:
  0.7 5.0 %collective-permute-start.10 = (bf16[2,2048]{1,0:T(2,128)(2,1)}, bf16[2,2048]{1,0:T(2,128)(2,1)S(1)}, u32[]{:S(2)}, u32[]{:S(2)}) collective-permute-start(bf16[2,2048]{1,0:T(2,128)(2,1)} %param.16), channel_id=1, source_target_pairs={{0,20},{4,24},{8,28},{12,0},{16,4},{20,8},{24,12},{28,16},{1,21},{... | collective-permute-start | bytes 24584 | tf_op jit(solution)/shard_map/ppermute | solution.py:168
  5.7 1.3 collective-permute-start.11
  7.6 1.5 collective-permute-start.6
  10.5 1.4 convert_reduce_fusion
  11.9 1.7 fusion.24
  13.6 2.7 %fusion.27 = bf16[256,2048]{1,0:T(8,128)(2,1)} fusion(bf16[256,2048]{1,0:T(8,128)(2,1)} %param.15, f32[2048]{0:T(1024)S(1)} %convert_element_type.135, f32[2048]{0:T(1024)S(1)} %convert_element_type.134, f32[256]{0:T(256)S(1)} %add_rsqrt_fusion, f32[256]{0:T(256)S(1)} %broadcast_multiply_fusion), kind=kLoop, calls=%fused_computation.46 | loop fusion | flops 3145728 | bytes 2115584 | tf_op jit(solution)/shard_map/convert_element_type | solution.py:20
  16.3 1.5 collective-permute-start
  18.0 2.3 %subtract_convert_fusion = (f32[512,1024]{1,0:T(8,128)}, f32[512,1024]{1,0:T(8,128)}) fusion(s32[1024]{0:T(1024)S(1)} %bitcast.138, s32[512]{0:T(512)S(1)} %get-tuple-element.33, s32[512]{0:T(512)S(1)} %get-tuple-element.34), kind=kLoop, calls=%fused_computation.50 | loop fusion | flops 2097152 | bytes 4202496 | tf_op jit(solution)/shard_map/convert_element_type | solution.py:36
  20.3 1.6 broadcast_compare_fusion
  22.6 1.6 subtract_convert_fusion.1
  24.2 1.6 subtract_convert_fusion.3
  26.8 2.1 collective-permute-start.8
  28.9 2.7 %collective-permute-start.9 = (bf16[2,2048]{1,0:T(2,128)(2,1)S(1)}, bf16[2,2048]{1,0:T(2,128)(2,1)S(1)}, u32[]{:S(2)}, u32[]{:S(2)}) collective-permute-start(bf16[2,2048]{1,0:T(2,128)(2,1)S(1)} %copy-done.15), channel_id=1, source_target_pairs={{0,16},{4,20},{8,24},{12,28},{16,0},{20,4},{24,8},{28,12},{1,17},{... | collective-permute-start | bytes 24584 | tf_op jit(solution)/shard_map/ppermute | solution.py:168
  31.7 6.3 %copy.50 = bf16[2,2048,512]{1,2,0:T(8,128)(2,1)} copy(bf16[2,2048,512]{2,1,0:T(8,128)(2,1)} %param.25) | data formatting | bytes 8388608 | tf_op jit(solution)/shard_map/reshape | solution.py:192
  38.0 1.3 reshape_squeeze.19
  39.3 2.3 %copy.52 = bf16[1,1024,512]{1,2,0:T(8,128)(2,1)} copy(bf16[1,1024,512]{2,1,0:T(8,128)(2,1)} %param.24) | data formatting | bytes 2097152 | tf_op jit(solution)/shard_map/reshape;squeeze | solution.py:142
  42.1 3.2 %pad_maximum_fusion = bf16[512,2048]{1,0:T(8,128)(2,1)} fusion(bf16[256,2048]{1,0:T(8,128)(2,1)} %collective-permute-done, bf16[256,2048]{1,0:T(8,128)(2,1)} %fusion.27), kind=kLoop, calls=%fused_computation.48 | loop fusion | flops 4194304 | bytes 4194304 | tf_op jit(solution)/shard_map/concatenate | solution.py:126
  45.5 3.8 %fusion.22 = bf16[2,1536]{1,0:T(2,128)(2,1)S(1)} fusion(bf16[2048,1536]{1,0:T(8,128)(2,1)} %param.19, f32[2,2048]{1,0:T(2,128)S(1)} %get-tuple-element.41, f32[2]{0:T(128)S(1)} %add_rsqrt_fusion.1, f32[2]{0:T(128)S(1)} %broadcast_multiply_fusion.1, f32[2048]{0:T(1024)S(1)} %convert_element_type.135, f32[2048]{0:T(1024)S(1)} %convert_element_type.134, ...), kind=kOutput, calls=%fused_computation.39 | convolution fusion | flops 12609536 | bytes 6336528 | tf_op jit(solution)/shard_map/dot_general | solution.py:183
  49.3 2.8 %fusion.54 = f32[2,4,1,2048]{3,2,1,0:T(1,128)S(1)} fusion(bf16[2,2048,4,128]{1,3,2,0:T(8,128)(2,1)} %bitcast.122, bf16[2,4,3,128]{3,2,1,0:T(4,128)(2,1)S(1)} %reshape.409), kind=kOutput, calls=%fused_computation.96 | convolution fusion | flops 4194304 | bytes 4263936 | tf_op jit(solution)/shard_map/vmap(hd,khd->hk)/dot_general | solution.py:72
  52.6 11.2 %add_convert_fusion = bf16[1024,1536]{1,0:T(8,128)(2,1)} fusion(bf16[2048,1536]{1,0:T(8,128)(2,1)} %param.19, bf16[512,2048]{1,0:T(8,128)(2,1)} %collective-permute-done.1, bf16[256,2048]{1,0:T(8,128)(2,1)} %collective-permute-done, bf16[256,2048]{1,0:T(8,128)(2,1)} %fusion.27, f32[1536]{0:T(1024)S(1)} %convert_element_type.137), kind=kOutput, calls=%fused_computation.16 | convolution fusion | flops 6458179584 | bytes 13637632 | tf_op jit(solution)/shard_map/dot_general | solution.py:134
  63.8 4.6 %copy.33 = bf16[1024,1536]{0,1:T(8,128)(2,1)} copy(bf16[1024,1536]{1,0:T(8,128)(2,1)} %add_convert_fusion) | data formatting | bytes 6291456 | tf_op jit(solution)/shard_map/convert_element_type | solution.py:135
  68.4 6.2 %reshape.404 = bf16[4,256,4,3,128]{1,0,4,3,2:T(4,128)(2,1)} reshape(bf16[1024,1536]{0,1:T(8,128)(2,1)} %copy.33) | data formatting | bytes 6291456 | tf_op jit(solution)/shard_map/reshape | solution.py:136
  74.6 3.7 %fusion.92 = (bf16[4,256,4,1,128]{1,0,4,3,2:T(4,128)(2,1)}, bf16[4,256,4,1,128]{1,0,4,3,2:T(4,128)(2,1)}) fusion(bf16[4,256,4,3,128]{1,0,4,3,2:T(4,128)(2,1)} %reshape.404), kind=kLoop, calls=%fused_computation.172 | loop fusion | bytes 4194304 | tf_op jit(solution)/shard_map/slice | solution.py:139
  78.2 2.6 %fusion.93 = (bf16[4,128,4,1,128]{1,0,4,3,2:T(4,128)(2,1)}, bf16[4,128,4,1,128]{1,0,4,3,2:T(4,128)(2,1)}) fusion(bf16[4,256,4,3,128]{1,0,4,3,2:T(4,128)(2,1)} %reshape.404), kind=kLoop, calls=%fused_computation.173 | loop fusion | bytes 2097152 | tf_op jit(solution)/shard_map/slice | solution.py:148
  80.8 2.4 %copy.36 = bf16[4,256,4,1,128]{4,1,0,2,3:T(8,128)(2,1)} copy(bf16[4,256,4,1,128]{1,0,4,3,2:T(4,128)(2,1)} %get-tuple-element.21) | data formatting | bytes 2097152 | tf_op jit(solution)/shard_map/slice | solution.py:138
  83.2 2.0 copy.38
  85.3 5.9 %fusion.96 = f32[4,512,1024]{2,1,0:T(8,128)} fusion(bf16[512,4,128]{2,0,1:T(8,128)(2,1)} %bitcast.127, bf16[1024,4,128]{2,0,1:T(8,128)(2,1)} %bitcast.129), kind=kOutput, calls=%fused_computation.176 | convolution fusion | flops 536870912 | bytes 9961472 | tf_op jit(solution)/shard_map/qhd,khd->hqk/dot_general | solution.py:43
  91.2 4.5 %fusion.39 = f32[4,512,1024]{2,1,0:T(8,128)} fusion(bf16[512,4,128]{2,0,1:T(8,128)(2,1)S(1)} %bitcast.128, bf16[1024,4,128]{2,1,0:T(4,128)(2,1)S(1)} %reshape_squeeze.19), kind=kOutput, calls=%fused_computation.70 | convolution fusion | flops 536870912 | bytes 9961472 | tf_op jit(solution)/shard_map/qhd,khd->hqk/dot_general | solution.py:38
  95.7 2.1 copy.34
  97.8 5.5 %fusion.41 = f32[4,512,1024]{2,1,0:T(8,128)} fusion(bf16[512,4,128]{2,0,1:T(8,128)(2,1)} %bitcast.131, bf16[1024,4,128]{2,1,0:T(4,128)(2,1)S(1)} %reshape_squeeze.19), kind=kOutput, calls=%fused_computation.72 | convolution fusion | flops 536870912 | bytes 9961472 | tf_op jit(solution)/shard_map/qhd,khd->hqk/dot_general | solution.py:38
  103.3 2.6 %reshape_squeeze.22 = bf16[1024,4,128]{0,2,1:T(8,128)(2,1)} reshape(bf16[4,256,4,1,128]{1,0,4,3,2:T(4,128)(2,1)} %get-tuple-element.20) | data formatting | bytes 2097152 | tf_op jit(solution)/shard_map/reshape;squeeze | solution.py:139
  105.9 18.7 %fusion.5 = (f32[4,512]{1,0:T(4,128)S(1)}, f32[4,512]{1,0:T(4,128)S(1)}, f32[4,512]{1,0:T(4,128)S(1)}, f32[4,512]{1,0:T(4,128)S(1)}, f32[4,512,1024]{2,1,0:T(8,128)}) fusion(f32[512,1024]{1,0:T(8,128)} %get-tuple-element.32, f32[4]{0:T(128)S(1)} %multiply_exponential_fusion, pred[512,1024]{1,0:T(8,128)(4,1)} %get-tuple-element.30, ...), kind=kOutput, calls=%fused_computation.18 | convolution fusion | flops 578805760 | bytes 44598288 | tf_op jit(solution)/shard_map/qhd,khd->hqk/dot_general | solution.py:43
  124.7 17.3 %fusion.3 = (f32[4,512]{1,0:T(4,128)S(1)}, f32[4,512]{1,0:T(4,128)S(1)}, f32[4,512]{1,0:T(4,128)S(1)}, f32[4,512]{1,0:T(4,128)S(1)}) fusion(f32[4,512,1024]{2,1,0:T(8,128)} %fusion.96, f32[4,512]{1,0:T(4,128)S(1)} %max.21, f32[512,1024]{1,0:T(8,128)} %get-tuple-element.31, f32[4]{0:T(128)S(1)} %multiply_exponential_fusion, ...), kind=kLoop, calls=%fused_computation.15 | loop fusion | flops 50323456 | bytes 43041808 | tf_op jit(solution)/shard_map/reduce_sum | solution.py:53
  142.0 2.9 %fusion.30 = f32[512,4,128]{0,2,1:T(8,128)S(1)} fusion(bf16[1024,4,128]{0,2,1:T(8,128)(2,1)S(1)} %bitcast.133, f32[4,512,1024]{2,1,0:T(8,128)S(1)} %copy-done.1, f32[4,512]{1,0:T(4,128)S(1)} %add.323, f32[4,512]{1,0:T(4,128)S(1)} %max.20, f32[512,1024]{1,0:T(8,128)S(1)} %copy-done.9, f32[4]{0:T(128)S(1)} %multiply_exponential_fusion, ...), kind=kOutput, calls=%fused_computation.55 | convolution fusion | flops 551550976 | bytes 12600336 | tf_op jit(solution)/shard_map/hqk,khd->qhd/dot_general | solution.py:58
  145.2 3.8 %fusion.36 = bf16[512,4,128]{0,2,1:T(8,128)(2,1)S(1)} fusion(f32[512,4,128]{0,2,1:T(8,128)S(1)} %fusion.30, bf16[1024,4,128]{0,2,1:T(8,128)(2,1)S(1)} %copy-done.14, f32[4,512,1024]{2,1,0:T(8,128)S(1)} %bitcast.126, f32[4,512]{1,0:T(4,128)S(1)} %add.323, f32[4,512]{1,0:T(4,128)S(1)} %max.20, f32[512,1024]{1,0:T(8,128)S(1)} %copy-done.7, ...), kind=kOutput, calls=%fused_computation.61 | convolution fusion | flops 552075264 | bytes 13647888 | tf_op jit(solution)/shard_map/hqk,khd->qhd/dot_general | solution.py:61
  149.1 1.3 fusion.95
  150.4 2.4 %fusion.90 = (f32[256,2048]{1,0:T(8,128)}, f32[256,2048]{1,0:T(8,128)}) fusion(f32[512,2048]{1,0:T(8,128)S(1)} %fusion.95), kind=kLoop, calls=%fused_computation.170 | loop fusion | bytes 8388608 | tf_op jit(solution)/shard_map/slice | solution.py:156
  153.3 2.9 %fusion.29 = f32[512,4,128]{0,2,1:T(8,128)S(1)} fusion(bf16[1024,4,128]{0,2,1:T(8,128)(2,1)S(1)} %bitcast.134, f32[4,512,1024]{2,1,0:T(8,128)S(1)} %bitcast.121, f32[4,512]{1,0:T(4,128)S(1)} %add.328, f32[4,512]{1,0:T(4,128)S(1)} %max.21, f32[512,1024]{1,0:T(8,128)S(1)} %copy-done.8, f32[4]{0:T(128)S(1)} %multiply_exponential_fusion, ...), kind=kOutput, calls=%fused_computation.54 | convolution fusion | flops 551550976 | bytes 12600336 | tf_op jit(solution)/shard_map/hqk,khd->qhd/dot_general | solution.py:58
  156.3 3.6 %fusion.35 = bf16[512,4,128]{0,2,1:T(8,128)(2,1)S(1)} fusion(f32[512,4,128]{0,2,1:T(8,128)S(1)} %fusion.29, bf16[1024,4,128]{0,2,1:T(8,128)(2,1)S(1)} %copy-done.14, f32[4,512,1024]{2,1,0:T(8,128)S(1)} %bitcast.119, f32[4,512]{1,0:T(4,128)S(1)} %add.328, f32[4,512]{1,0:T(4,128)S(1)} %max.21, f32[512,1024]{1,0:T(8,128)S(1)} %copy-done.6, ...), kind=kOutput, calls=%fused_computation.60 | convolution fusion | flops 552075264 | bytes 13647888 | tf_op jit(solution)/shard_map/hqk,khd->qhd/dot_general | solution.py:61
  159.9 1.3 fusion.97
  161.2 2.2 fusion.91
  165.7 1.2 collective-permute-start.15
  167.0 1.1 collective-permute-done.13
  168.1 0.8 collective-permute-done.14
  169.0 2.5 %add.325 = f32[2,128,2048]{2,1,0:T(8,128)S(1)} add(f32[2,128,2048]{2,1,0:T(8,128)} %bitcast.123, f32[2,128,2048]{2,1,0:T(8,128)} %collective-permute-done.2) | non-fusion elementwise | flops 524288 | bytes 6291456 | tf_op jit(solution)/shard_map/add | solution.py:156
  171.5 1.1 slice_bitcast_fusion.2
  172.6 1.0 collective-permute-start.3
  173.6 2.0 add.330
  175.6 1.3 copy-done.4
  176.9 1.0 slice_bitcast_fusion
  178.0 1.1 collective-permute-start.5
  179.4 1.6 collective-permute-start.17
  181.0 1.5 collective-permute-start.18
  182.5 3.0 %collective-permute-done.16 = bf16[2,2048]{1,0:T(2,128)(2,1)S(1)} collective-permute-done((bf16[2,2048]{1,0:T(2,128)(2,1)S(1)}, bf16[2,2048]{1,0:T(2,128)(2,1)S(1)}, u32[]{:S(2)}, u32[]{:S(2)}) %collective-permute-start.16) | collective-permute-done | bytes 8224 | tf_op jit(solution)/shard_map/ppermute | solution.py:210
  186.5 2.2 collective-permute-start.21
  188.7 1.4 collective-permute-done.19
  190.1 0.8 collective-permute-start.22
  191.0 2.7 %collective-permute-done.22 = bf16[2,2048]{1,0:T(2,128)(2,1)S(1)} collective-permute-done((bf16[2,2048]{1,0:T(2,128)(2,1)S(1)}, bf16[2,2048]{1,0:T(2,128)(2,1)S(1)}, u32[]{:S(2)}, u32[]{:S(2)}) %collective-permute-start.22) | collective-permute-done | bytes 8224 | tf_op jit(solution)/shard_map/ppermute | solution.py:210
  193.9 0.8 convolution_convert_fusion
  194.6 4.2 %collective-permute-done.3 = f32[128,2048]{1,0:T(8,128)} collective-permute-done((f32[128,2048]{1,0:T(8,128)}, f32[128,2048]{1,0:T(8,128)}, u32[]{:S(2)}, u32[]{:S(2)}) %collective-permute-start.3) | collective-permute-done | bytes 1048608 | tf_op jit(solution)/shard_map/ppermute | solution.py:159
  198.9 1.7 fusion.38
  200.5 20.8 %collective-permute-done.5 = f32[128,2048]{1,0:T(8,128)} collective-permute-done((f32[128,2048]{1,0:T(8,128)}, f32[128,2048]{1,0:T(8,128)}, u32[]{:S(2)}, u32[]{:S(2)}) %collective-permute-start.5) | collective-permute-done | bytes 1048608 | tf_op jit(solution)/shard_map/ppermute | solution.py:159
  221.3 1.7 fusion.37
  223.0 1.3 fusion.28
  (125 shorter events, 9.1 us)
Async XLA Ops:
  0.6 148.4 %copy-start = (bf16[512,2048]{1,0:T(8,128)(2,1)S(1)}, bf16[512,2048]{1,0:T(8,128)(2,1)}, u32[]{:S(2)}) copy-start(bf16[512,2048]{1,0:T(8,128)(2,1)} %param.21) | copy-start | bytes 6291460
  0.6 21.2 %copy-start.18 = (s32[2]{0:T(128)S(1)}, s32[2]{0:T(128)}, u32[]{:S(2)}) copy-start(s32[2]{0:T(128)} %param.28) | copy-start | bytes 28
  0.7 25.4 %collective-permute-start.10 = (bf16[2,2048]{1,0:T(2,128)(2,1)}, bf16[2,2048]{1,0:T(2,128)(2,1)S(1)}, u32[]{:S(2)}, u32[]{:S(2)}) collective-permute-start(bf16[2,2048]{1,0:T(2,128)(2,1)} %param.16), channel_id=1, source_target_pairs={{0,20},{4,24},{8,28},{12,0},{16,4},{20,8},{24,12},{28,16},{1,21},{... | collective-permute-start | bytes 24584 | tf_op jit(solution)/shard_map/ppermute | solution.py:168
  5.7 21.1 %collective-permute-start.11 = (bf16[2,2048]{1,0:T(2,128)(2,1)}, bf16[2,2048]{1,0:T(2,128)(2,1)S(1)}, u32[]{:S(2)}, u32[]{:S(2)}) collective-permute-start(bf16[2,2048]{1,0:T(2,128)(2,1)} %param.16), channel_id=1, source_target_pairs={{0,24},{4,28},{8,0},{12,4},{16,8},{20,12},{24,16},{28,20},{1,25},{... | collective-permute-start | bytes 24584 | tf_op jit(solution)/shard_map/ppermute | solution.py:168
  7.0 21.9 %collective-permute-start.12 = (bf16[2,2048]{1,0:T(2,128)(2,1)}, bf16[2,2048]{1,0:T(2,128)(2,1)S(1)}, u32[]{:S(2)}, u32[]{:S(2)}) collective-permute-start(bf16[2,2048]{1,0:T(2,128)(2,1)} %param.16), channel_id=1, source_target_pairs={{0,28},{4,0},{8,4},{12,8},{16,12},{20,16},{24,20},{28,24},{1,29},{... | collective-permute-start | bytes 24584 | tf_op jit(solution)/shard_map/ppermute | solution.py:168
  7.6 34.1 %collective-permute-start.6 = (bf16[2,2048]{1,0:T(2,128)(2,1)}, bf16[2,2048]{1,0:T(2,128)(2,1)S(1)}, u32[]{:S(2)}, u32[]{:S(2)}) collective-permute-start(bf16[2,2048]{1,0:T(2,128)(2,1)} %param.16), channel_id=1, source_target_pairs={{0,4},{4,8},{8,12},{12,16},{16,20},{20,24},{24,28},{28,0},{1,5},{5... | collective-permute-start | bytes 24584 | tf_op jit(solution)/shard_map/ppermute | solution.py:168
  11.9 13.9 %copy-start.19 = (s32[16]{0:T(128)S(1)}, s32[16]{0:T(128)}, u32[]{:S(2)}) copy-start(s32[16]{0:T(128)} %param.29) | copy-start | bytes 196
  11.9 14.2 %copy-start.15 = (bf16[2,2048]{1,0:T(2,128)(2,1)S(1)}, bf16[2,2048]{1,0:T(2,128)(2,1)}, u32[]{:S(2)}) copy-start(bf16[2,2048]{1,0:T(2,128)(2,1)} %param.16) | copy-start | bytes 24580
  11.9 19.7 %copy-start.16 = (bf16[1536]{0:T(1024)(128)(2,1)S(1)}, bf16[1536]{0:T(1024)(128)(2,1)}, u32[]{:S(2)}) copy-start(bf16[1536]{0:T(1024)(128)(2,1)} %param.20) | copy-start | bytes 9220
  16.3 25.7 %collective-permute-start = (bf16[256,2048]{1,0:T(8,128)(2,1)}, bf16[256,2048]{1,0:T(8,128)(2,1)}, u32[]{:S(2)}, u32[]{:S(2)}) collective-permute-start(bf16[256,2048]{1,0:T(8,128)(2,1)} %fusion.27), channel_id=1, source_target_pairs={{0,2},{1,3},{2,0},{3,1},{4,6},{5,7},{6,4},{7,5},{8,10},{9,11},{10,... | collective-permute-start | bytes 3145736 | tf_op jit(solution)/shard_map/ppermute | solution.py:127
  26.1 15.5 %collective-permute-start.7 = (bf16[2,2048]{1,0:T(2,128)(2,1)S(1)}, bf16[2,2048]{1,0:T(2,128)(2,1)S(1)}, u32[]{:S(2)}, u32[]{:S(2)}) collective-permute-start(bf16[2,2048]{1,0:T(2,128)(2,1)S(1)} %copy-done.15), channel_id=1, source_target_pairs={{0,8},{4,12},{8,16},{12,20},{16,24},{20,28},{24,0},{28,4},{1,9},{5... | collective-permute-start | bytes 24584 | tf_op jit(solution)/shard_map/ppermute | solution.py:168
  26.8 14.8 %collective-permute-start.8 = (bf16[2,2048]{1,0:T(2,128)(2,1)S(1)}, bf16[2,2048]{1,0:T(2,128)(2,1)S(1)}, u32[]{:S(2)}, u32[]{:S(2)}) collective-permute-start(bf16[2,2048]{1,0:T(2,128)(2,1)S(1)} %copy-done.15), channel_id=1, source_target_pairs={{0,12},{4,16},{8,20},{12,24},{16,28},{20,0},{24,4},{28,8},{1,13},{... | collective-permute-start | bytes 24584 | tf_op jit(solution)/shard_map/ppermute | solution.py:168
  28.9 12.7 %collective-permute-start.9 = (bf16[2,2048]{1,0:T(2,128)(2,1)S(1)}, bf16[2,2048]{1,0:T(2,128)(2,1)S(1)}, u32[]{:S(2)}, u32[]{:S(2)}) collective-permute-start(bf16[2,2048]{1,0:T(2,128)(2,1)S(1)} %copy-done.15), channel_id=1, source_target_pairs={{0,16},{4,20},{8,24},{12,28},{16,0},{20,4},{24,8},{28,12},{1,17},{... | collective-permute-start | bytes 24584 | tf_op jit(solution)/shard_map/ppermute | solution.py:168
  45.2 7.3 %collective-permute-start.1 = (bf16[512,2048]{1,0:T(8,128)(2,1)}, bf16[512,2048]{1,0:T(8,128)(2,1)}, u32[]{:S(2)}, u32[]{:S(2)}) collective-permute-start(bf16[512,2048]{1,0:T(8,128)(2,1)} %pad_maximum_fusion), channel_id=1, source_target_pairs={{0,1},{1,0},{2,3},{3,2},{4,5},{5,4},{6,7},{7,6},{8,9},{9,8},{10,11... | collective-permute-start | bytes 6291464 | tf_op jit(solution)/shard_map/ppermute | solution.py:129
  85.3 5.9 %copy-start.10 = (bf16[4,128,4,1,128]{4,1,0,2,3:T(8,128)(2,1)S(1)}, bf16[4,128,4,1,128]{4,1,0,2,3:T(8,128)(2,1)}, u32[]{:S(2)}) copy-start(bf16[4,128,4,1,128]{4,1,0,2,3:T(8,128)(2,1)} %copy.38) | copy-start | bytes 1572868
  105.9 18.7 %copy-start.11 = (pred[512,1024]{1,0:T(8,128)(4,1)S(1)}, pred[512,1024]{1,0:T(8,128)(4,1)}, u32[]{:S(2)}) copy-start(pred[512,1024]{1,0:T(8,128)(4,1)} %get-tuple-element.29) | copy-start | bytes 1572868
  105.9 18.7 %copy-start.12 = (pred[512,1024]{1,0:T(8,128)(4,1)S(1)}, pred[512,1024]{1,0:T(8,128)(4,1)}, u32[]{:S(2)}) copy-start(pred[512,1024]{1,0:T(8,128)(4,1)} %get-tuple-element.30) | copy-start | bytes 1572868
  124.6 17.4 %copy-start.1 = (f32[4,512,1024]{2,1,0:T(8,128)S(1)}, f32[4,512,1024]{2,1,0:T(8,128)}, u32[]{:S(2)}) copy-start(f32[4,512,1024]{2,1,0:T(8,128)} %fusion.41) | copy-start | bytes 25165828
  124.6 17.4 %copy-start.9 = (f32[512,1024]{1,0:T(8,128)S(1)}, f32[512,1024]{1,0:T(8,128)}, u32[]{:S(2)}) copy-start(f32[512,1024]{1,0:T(8,128)} %subtract_convert_fusion.3) | copy-start | bytes 6291460
  124.6 17.4 %copy-start.13 = (bf16[1,1024,512]{1,2,0:T(8,128)(2,1)S(1)}, bf16[1,1024,512]{1,2,0:T(8,128)(2,1)}, u32[]{:S(2)}) copy-start(bf16[1,1024,512]{1,2,0:T(8,128)(2,1)} %copy.52) | copy-start | bytes 3145732
  124.6 20.3 %slice-start.4 = ((s8[8388608]{0:T(1024)(128)(4,1)}), s8[4194304]{0:T(1024)(128)(4,1)S(1)}, s32[]{:S(2)}) async-start(s8[8388608]{0:T(1024)(128)(4,1)} %bitcast.125), calls=%async_computation.4 | async-start | bytes 8388608
  142.0 3.2 %slice-start.5 = ((s8[8388608]{0:T(1024)(128)(4,1)}), s8[4194304]{0:T(1024)(128)(4,1)S(1)}, s32[]{:S(2)}) async-start(s8[8388608]{0:T(1024)(128)(4,1)} %bitcast.125), calls=%async_computation.5 | async-start | bytes 8388608
  142.0 3.2 %copy-start.7 = (f32[512,1024]{1,0:T(8,128)S(1)}, f32[512,1024]{1,0:T(8,128)}, u32[]{:S(2)}) copy-start(f32[512,1024]{1,0:T(8,128)} %get-tuple-element.32) | copy-start | bytes 6291460
  142.0 3.2 %copy-start.14 = (bf16[1024,4,128]{0,2,1:T(8,128)(2,1)S(1)}, bf16[1024,4,128]{0,2,1:T(8,128)(2,1)}, u32[]{:S(2)}) copy-start(bf16[1024,4,128]{0,2,1:T(8,128)(2,1)} %reshape_squeeze.22) | copy-start | bytes 3145732
  142.0 11.2 %slice-start.2 = ((s8[8388608]{0:T(1024)(128)(4,1)}), s8[4194304]{0:T(1024)(128)(4,1)S(1)}, s32[]{:S(2)}) async-start(s8[8388608]{0:T(1024)(128)(4,1)} %bitcast.120), calls=%async_computation.2 | async-start | bytes 8388608
  145.2 8.1 %slice-start.3 = ((s8[8388608]{0:T(1024)(128)(4,1)}), s8[4194304]{0:T(1024)(128)(4,1)S(1)}, s32[]{:S(2)}) async-start(s8[8388608]{0:T(1024)(128)(4,1)} %bitcast.120), calls=%async_computation.3 | async-start | bytes 8388608
  149.0 4.2 %copy-start.8 = (f32[512,1024]{1,0:T(8,128)S(1)}, f32[512,1024]{1,0:T(8,128)}, u32[]{:S(2)}) copy-start(f32[512,1024]{1,0:T(8,128)} %subtract_convert_fusion.1) | copy-start | bytes 6291460
  150.3 5.9 %slice-start = ((s8[8388608]{0:T(1024)(128)(4,1)}), s8[4194304]{0:T(1024)(128)(4,1)S(1)}, s32[]{:S(2)}) async-start(s8[8388608]{0:T(1024)(128)(4,1)} %bitcast.118), calls=%async_computation | async-start | bytes 8388608
  152.8 16.2 %collective-permute-start.2 = (f32[2,128,2048]{2,1,0:T(8,128)}, f32[2,128,2048]{2,1,0:T(8,128)}, u32[]{:S(2)}, u32[]{:S(2)}) collective-permute-start(f32[2,128,2048]{2,1,0:T(8,128)} %bitcast.8), channel_id=1, source_target_pairs={{0,1},{1,0},{2,3},{3,2},{4,5},{5,4},{6,7},{7,6},{8,9},{9,8},{10,11... | collective-permute-start | bytes 6291464 | tf_op jit(solution)/shard_map/ppermute | solution.py:156
  153.3 3.0 %slice-start.1 = ((s8[8388608]{0:T(1024)(128)(4,1)}), s8[4194304]{0:T(1024)(128)(4,1)S(1)}, s32[]{:S(2)}) async-start(s8[8388608]{0:T(1024)(128)(4,1)} %bitcast.118), calls=%async_computation.1 | async-start | bytes 8388608
  153.3 3.0 %copy-start.6 = (f32[512,1024]{1,0:T(8,128)S(1)}, f32[512,1024]{1,0:T(8,128)}, u32[]{:S(2)}) copy-start(f32[512,1024]{1,0:T(8,128)} %get-tuple-element.31) | copy-start | bytes 6291460
  159.9 3.9 %copy-start.20 = (bf16[2,2048,512]{2,1,0:T(8,128)(2,1)S(1)}, bf16[2,2048,512]{2,1,0:T(8,128)(2,1)}, u32[]{:S(2)}) copy-start(bf16[2,2048,512]{2,1,0:T(8,128)(2,1)} %param.26) | copy-start | bytes 12582916
  161.2 5.8 %copy-start.17 = (bf16[2048]{0:T(1024)(128)(2,1)S(1)}, bf16[2048]{0:T(1024)(128)(2,1)}, u32[]{:S(2)}) copy-start(bf16[2048]{0:T(1024)(128)(2,1)} %param.22) | copy-start | bytes 12292
  163.4 10.2 %collective-permute-start.4 = (f32[2,128,2048]{2,1,0:T(8,128)}, f32[2,128,2048]{2,1,0:T(8,128)}, u32[]{:S(2)}, u32[]{:S(2)}) collective-permute-start(f32[2,128,2048]{2,1,0:T(8,128)} %bitcast.17), channel_id=1, source_target_pairs={{0,1},{1,0},{2,3},{3,2},{4,5},{5,4},{6,7},{7,6},{8,9},{9,8},{10,11... | collective-permute-start | bytes 6291464 | tf_op jit(solution)/shard_map/ppermute | solution.py:156
  165.0 3.2 %collective-permute-start.13 = (f32[2,2048]{1,0:T(2,128)S(1)}, f32[2,2048]{1,0:T(2,128)S(1)}, u32[]{:S(2)}, u32[]{:S(2)}) collective-permute-start(f32[2,2048]{1,0:T(2,128)S(1)} %fusion.57), channel_id=1, source_target_pairs={{0,1},{1,2},{2,3},{3,0},{4,5},{5,6},{6,7},{7,4},{8,9},{9,10},{10,1... | collective-permute-start | bytes 49160 | tf_op jit(solution)/shard_map/ppermute | solution.py:201
  165.2 3.7 %collective-permute-start.14 = (f32[2,2048]{1,0:T(2,128)S(1)}, f32[2,2048]{1,0:T(2,128)S(1)}, u32[]{:S(2)}, u32[]{:S(2)}) collective-permute-start(f32[2,2048]{1,0:T(2,128)S(1)} %fusion.57), channel_id=1, source_target_pairs={{0,2},{1,3},{2,0},{3,1},{4,6},{5,7},{6,4},{7,5},{8,10},{9,11},{10,... | collective-permute-start | bytes 49160 | tf_op jit(solution)/shard_map/ppermute | solution.py:201
  165.7 3.2 %collective-permute-start.15 = (f32[2,2048]{1,0:T(2,128)S(1)}, f32[2,2048]{1,0:T(2,128)S(1)}, u32[]{:S(2)}, u32[]{:S(2)}) collective-permute-start(f32[2,2048]{1,0:T(2,128)S(1)} %fusion.57), channel_id=1, source_target_pairs={{0,3},{1,0},{2,1},{3,2},{4,7},{5,4},{6,5},{7,6},{8,11},{9,8},{10,9... | collective-permute-start | bytes 49160 | tf_op jit(solution)/shard_map/ppermute | solution.py:201
  167.0 6.6 %copy-start.5 = (f32[256,2048]{1,0:T(8,128)S(1)}, f32[256,2048]{1,0:T(8,128)}, u32[]{:S(2)}) copy-start(f32[256,2048]{1,0:T(8,128)} %get-tuple-element.19) | copy-start | bytes 6291460
  171.5 2.1 copy-start.3
  172.6 26.3 %collective-permute-start.3 = (f32[128,2048]{1,0:T(8,128)}, f32[128,2048]{1,0:T(8,128)}, u32[]{:S(2)}, u32[]{:S(2)}) collective-permute-start(f32[128,2048]{1,0:T(8,128)} %slice_bitcast_fusion.2), channel_id=1, source_target_pairs={{0,2},{1,3},{2,0},{3,1},{4,6},{5,7},{6,4},{7,5},{8,10},{9,11},{10,... | collective-permute-start | bytes 3145736 | tf_op jit(solution)/shard_map/ppermute | solution.py:159
  173.6 49.4 %copy-start.2 = (bf16[256,2048]{1,0:T(8,128)(2,1)S(1)}, bf16[256,2048]{1,0:T(8,128)(2,1)}, u32[]{:S(2)}) copy-start(bf16[256,2048]{1,0:T(8,128)(2,1)} %param.15) | copy-start | bytes 3145732
  175.6 1.3 copy-start.4
  178.0 43.4 %collective-permute-start.5 = (f32[128,2048]{1,0:T(8,128)}, f32[128,2048]{1,0:T(8,128)}, u32[]{:S(2)}, u32[]{:S(2)}) collective-permute-start(f32[128,2048]{1,0:T(8,128)} %slice_bitcast_fusion), channel_id=1, source_target_pairs={{0,2},{1,3},{2,0},{3,1},{4,6},{5,7},{6,4},{7,5},{8,10},{9,11},{10,... | collective-permute-start | bytes 3145736 | tf_op jit(solution)/shard_map/ppermute | solution.py:159
  179.0 6.5 %collective-permute-start.16 = (bf16[2,2048]{1,0:T(2,128)(2,1)S(1)}, bf16[2,2048]{1,0:T(2,128)(2,1)S(1)}, u32[]{:S(2)}, u32[]{:S(2)}) collective-permute-start(bf16[2,2048]{1,0:T(2,128)(2,1)S(1)} %fusion.49), channel_id=1, source_target_pairs={{0,4},{4,8},{8,12},{12,16},{16,20},{20,24},{24,28},{28,0},{1,5},{5... | collective-permute-start | bytes 24584 | tf_op jit(solution)/shard_map/ppermute | solution.py:210
  179.4 6.5 %collective-permute-start.17 = (bf16[2,2048]{1,0:T(2,128)(2,1)S(1)}, bf16[2,2048]{1,0:T(2,128)(2,1)S(1)}, u32[]{:S(2)}, u32[]{:S(2)}) collective-permute-start(bf16[2,2048]{1,0:T(2,128)(2,1)S(1)} %fusion.49), channel_id=1, source_target_pairs={{0,8},{4,12},{8,16},{12,20},{16,24},{20,28},{24,0},{28,4},{1,9},{5... | collective-permute-start | bytes 24584 | tf_op jit(solution)/shard_map/ppermute | solution.py:210
  181.0 5.4 %collective-permute-start.18 = (bf16[2,2048]{1,0:T(2,128)(2,1)S(1)}, bf16[2,2048]{1,0:T(2,128)(2,1)S(1)}, u32[]{:S(2)}, u32[]{:S(2)}) collective-permute-start(bf16[2,2048]{1,0:T(2,128)(2,1)S(1)} %fusion.49), channel_id=1, source_target_pairs={{0,12},{4,16},{8,20},{12,24},{16,28},{20,0},{24,4},{28,8},{1,13},{... | collective-permute-start | bytes 24584 | tf_op jit(solution)/shard_map/ppermute | solution.py:210
  185.5 4.6 %collective-permute-start.19 = (bf16[2,2048]{1,0:T(2,128)(2,1)S(1)}, bf16[2,2048]{1,0:T(2,128)(2,1)S(1)}, u32[]{:S(2)}, u32[]{:S(2)}) collective-permute-start(bf16[2,2048]{1,0:T(2,128)(2,1)S(1)} %fusion.49), channel_id=1, source_target_pairs={{0,16},{4,20},{8,24},{12,28},{16,0},{20,4},{24,8},{28,12},{1,17},{... | collective-permute-start | bytes 24584 | tf_op jit(solution)/shard_map/ppermute | solution.py:210
  186.0 5.0 %collective-permute-start.20 = (bf16[2,2048]{1,0:T(2,128)(2,1)S(1)}, bf16[2,2048]{1,0:T(2,128)(2,1)S(1)}, u32[]{:S(2)}, u32[]{:S(2)}) collective-permute-start(bf16[2,2048]{1,0:T(2,128)(2,1)S(1)} %fusion.49), channel_id=1, source_target_pairs={{0,20},{4,24},{8,28},{12,0},{16,4},{20,8},{24,12},{28,16},{1,21},{... | collective-permute-start | bytes 24584 | tf_op jit(solution)/shard_map/ppermute | solution.py:210
  186.5 4.5 %collective-permute-start.21 = (bf16[2,2048]{1,0:T(2,128)(2,1)S(1)}, bf16[2,2048]{1,0:T(2,128)(2,1)S(1)}, u32[]{:S(2)}, u32[]{:S(2)}) collective-permute-start(bf16[2,2048]{1,0:T(2,128)(2,1)S(1)} %fusion.49), channel_id=1, source_target_pairs={{0,24},{4,28},{8,0},{12,4},{16,8},{20,12},{24,16},{28,20},{1,25},{... | collective-permute-start | bytes 24584 | tf_op jit(solution)/shard_map/ppermute | solution.py:210
  190.1 3.7 %collective-permute-start.22 = (bf16[2,2048]{1,0:T(2,128)(2,1)S(1)}, bf16[2,2048]{1,0:T(2,128)(2,1)S(1)}, u32[]{:S(2)}, u32[]{:S(2)}) collective-permute-start(bf16[2,2048]{1,0:T(2,128)(2,1)S(1)} %fusion.49), channel_id=1, source_target_pairs={{0,28},{4,0},{8,4},{12,8},{16,12},{20,16},{24,20},{28,24},{1,29},{... | collective-permute-start | bytes 24584 | tf_op jit(solution)/shard_map/ppermute | solution.py:210

commit v4 on v2

--- a/solution.py
+++ b/solution.py
@@ -4,6 +4,9 @@
 import jax.numpy as jnp
 from jax import lax
 from jax.sharding import PartitionSpec as P
+from jax.experimental import pallas as pl
+from jax.experimental.pallas import tpu as pltpu
+import functools
 
 H = 16
 HD = 128
@@ -69,6 +72,64 @@
         "hqk,khd->qhd", new_probs, new_values, preferred_element_type=jnp.float32
     )
     return context.astype(jnp.bfloat16).reshape(group_size, -1)
+
+
+def _prefill_kernel(prefix_ref, slopes_ref, q_ref, kn_ref, vn_ref, kc_ref, vc_ref, o_ref, *, tq):
+    h = pl.program_id(0)
+    i = pl.program_id(1)
+    prefix = prefix_ref[0]
+    slope = slopes_ref[h]
+    factor = 1.0 / math.sqrt(q_ref.shape[-1])
+    q = q_ref[...]
+    dims = (((1,), (1,)), ((), ()))
+    cache_size = kc_ref.shape[0]
+    group = kn_ref.shape[0]
+    q_tok = i * tq + lax.broadcasted_iota(jnp.int32, (tq, 1), 0)
+    q_pos = prefix + q_tok
+    c_pos = lax.broadcasted_iota(jnp.int32, (1, cache_size), 1)
+    k_tok = lax.broadcasted_iota(jnp.int32, (1, group), 1)
+    s_c = lax.dot_general(q, kc_ref[...], dims, preferred_element_type=jnp.float32) * factor
+    s_c = s_c - slope * (q_pos - c_pos).astype(jnp.float32)
+    s_c = jnp.where(c_pos < prefix, s_c, -jnp.inf)
+    s_n = lax.dot_general(q, kn_ref[...], dims, preferred_element_type=jnp.float32) * factor
+    s_n = s_n - slope * (q_tok - k_tok).astype(jnp.float32)
+    s_n = jnp.where(k_tok <= q_tok, s_n, -jnp.inf)
+    m = jnp.maximum(jnp.max(s_c, axis=-1, keepdims=True), jnp.max(s_n, axis=-1, keepdims=True))
+    e_c = jnp.exp(s_c - m)
+    e_n = jnp.exp(s_n - m)
+    l = jnp.sum(e_c, axis=-1, keepdims=True) + jnp.sum(e_n, axis=-1, keepdims=True)
+    p_c = (e_c / l).astype(jnp.bfloat16)
+    p_n = (e_n / l).astype(jnp.bfloat16)
+    ctx = jnp.dot(p_c, vc_ref[...], preferred_element_type=jnp.float32)
+    ctx = ctx + jnp.dot(p_n, vn_ref[...], preferred_element_type=jnp.float32)
+    o_ref[...] = ctx.astype(o_ref.dtype)
+
+def prefill_attention_kernel(merged, cache_keys, cache_values, prefix, slopes, head_size, tq=256):
+    group = merged.shape[0]
+    heads = merged.shape[1] // (3 * head_size)
+    cache_size = cache_keys.shape[0]
+    col = lambda c: (lambda h, i, *_: (0, h * 3 + c))
+    return pl.pallas_call(
+        functools.partial(_prefill_kernel, tq=tq),
+        out_shape=jax.ShapeDtypeStruct((group, heads * head_size), jnp.bfloat16),
+        grid_spec=pltpu.PrefetchScalarGridSpec(
+            num_scalar_prefetch=2,
+            grid=(heads, group // tq),
+            in_specs=[
+                pl.BlockSpec((tq, head_size), lambda h, i, *_: (i, h * 3)),
+                pl.BlockSpec((group, head_size), col(1)),
+                pl.BlockSpec((group, head_size), col(2)),
+                pl.BlockSpec((cache_size, head_size), lambda h, i, *_: (0, h)),
+                pl.BlockSpec((cache_size, head_size), lambda h, i, *_: (0, h)),
+            ],
+            out_specs=pl.BlockSpec((tq, head_size), lambda h, i, *_: (i, h)),
+        ),
+        cost_estimate=pl.CostEstimate(
+            flops=4 * heads * group * (group + cache_size) * head_size,
+            transcendentals=heads * group * (group + cache_size),
+            bytes_accessed=2 * (group * heads * 3 * head_size + 2 * cache_size * heads * head_size + group * heads * head_size),
+        ),
+    )(prefix, slopes, merged, merged, merged, cache_keys, cache_values)
 
 
 def decode_attention(query_row, new_key, new_value, cache_keys, cache_values, length, slopes):
@@ -125,15 +186,8 @@
         preferred_element_type=jnp.float32,
     )
     merged_rows = (product + qkv_bias.astype(jnp.float32)).astype(jnp.bfloat16)
-    group_size = merged_rows.shape[0]
-    merged_rows = merged_rows.reshape(group_size, local_heads, 3, head_size)
-    cache_size = pre_keys.shape[1]
-    context = prefill_attention(
-        merged_rows,
-        pre_keys[0].reshape(cache_size, local_heads, head_size),
-        pre_values[0].reshape(cache_size, local_heads, head_size),
-        prefix_lengths[0],
-        slopes,
+    context = prefill_attention_kernel(
+        merged_rows, pre_keys[0], pre_values[0], prefix_lengths, slopes, head_size
     )
     summed = lax.psum_scatter(
         jnp.dot(context, out_weight, preferred_element_type=jnp.float32),

time: 191 us -> 180 us (0.942)
  Pallas kernels: 0 us -> 27.1 us
  matrix products: 51.6 us -> 27.3 us
  other arithmetic: 25.1 us -> 12.1 us
  waiting for transfers between devices: 57 us -> 68.4 us
  local copies, waits for them, and re-layouts: 15.8 us -> 7.3 us
  starting transfers between devices: 25.8 us -> 22.2 us
    pallas_call x0 -> x1, Pallas kernels: none -> 27.1 us  [prefill_attention_kernel(): pl.pallas_call(functools.partial(_prefill_kernel, tq=tq), out_shape=jax.S...]
    dot_general x4 -> x0, matrix products: 25.9 us -> none  [the longest x1 10.8 us: prefill_attention(): jnp.einsum('qhd,khd->hqk', queries, new_keys, preferred_element_type=jnp....]
    reduce_sum x1 -> x0, other arithmetic: 8.4 us -> none  [prefill_attention(): jnp.sum(new_exp, axis=-1, keepdims=True)]
    all_gather x1, waiting for transfers between devices: 28 us -> 36.1 us  [per_device(): lax.all_gather(normed, 'tensor', axis=0, tiled=True)]
    ppermute x7, waiting for transfers between devices: 1.25 us -> 6.1 us  [per_device(): lax.ppermute(slot_rows, 'dp', [(i, (i + k) % dp_size) for i in range(dp_s...]
    convert_element_type x1 -> x0, local copies, waits for them, and re-layouts: 4.69 us -> none  [per_device(): merged_rows = (product + qkv_bias.astype(jnp.float32)).astype(jnp.bfloat16)]
    convert_element_type x1 -> x0, other arithmetic: 3.69 us -> none  [prefill_attention(): new_dist = (query_pos[:, None] - query_pos[None, :]).astype(jnp.float32)]
    another operation x2 -> x0, local copies, waits for them, and re-layouts: 3.62 us -> none  [the longest x1 2.27 us: per_device(): pre_values[0].reshape(cache_size, local_heads, head_size)]
  transfers between devices with their start and end apart: 19 -> 19, of which waited for: 5 -> 6; matrix products, arithmetic and copies ran while one was open for 13% -> 10% of each run, Pallas kernels for 0% -> 0%
where the time goes in v4:
time: 180 us; the launch traced here: 179 us
  waiting for transfers between devices  68.4 us (38%)
  matrix products  27.3 us (15%)
  Pallas kernels  27.1 us (15%)
  starting transfers between devices  22.2 us (12%)
  between operations  14.9 us (8%)
  other arithmetic  12.1 us (7%)
  local copies, waits for them, and re-layouts  7.3 us (4%)
    all_gather x1, waiting for transfers between devices, per_device(): lax.all_gather(normed, 'tensor', axis=0, tiled=True)  36.1 us
    pallas_call x1, Pallas kernels, prefill_attention_kernel(): pl.pallas_call(functools.partial(_prefill_kernel, tq=tq), out_shape=jax.S...  27.1 us
    reduce_scatter x1, waiting for transfers between devices, per_device(): lax.psum_scatter(jnp.dot(context, out_weight, preferred_element_type=jnp....  22.5 us
    ppermute x7, starting transfers between devices, per_device(): lax.ppermute(dec_hidden, 'dp', [(i, (i + k) % dp_size) for i in range(dp_...  13 us
    dot_general x1, matrix products, per_device(): jnp.dot(lax.all_gather(normed, 'tensor', axis=0, tiled=True), qkv_weight,...  11.2 us
    ppermute x7, starting transfers between devices, per_device(): lax.ppermute(slot_rows, 'dp', [(i, (i + k) % dp_size) for i in range(dp_s...  8.54 us
    dot_general x1, matrix products, per_device(): jnp.dot(context, out_weight, preferred_element_type=jnp.float32)  6.79 us
    reshape x1, local copies, waits for them, and re-layouts, per_device(): dec_keys.reshape(slot_count, dec_cache, local_heads, head_size)  6.34 us
  transfers between devices with their start and end apart: 19, of which 6 were waited for; matrix products, arithmetic and copies ran while one was open for 10% of the time, Pallas kernels for 0%

profile of v4, /device:TPU:0, one launch (start us, length us, event | category | flops | bytes accessed | tf_op | source)
XLA Modules:
  0.0 179.3 jit_solution(10193886818331232027)
XLA Ops:
  7.2 0.0 copy-start
  7.2 0.0 all-gather.2.cloned.1.call-start
  7.2 1.6 convert_reduce_fusion
  8.8 1.6 fusion.7
  10.5 0.7 convert_element_type.85
  11.2 0.7 convert_element_type.86
  11.9 2.7 %fusion.10 = bf16[256,2048]{1,0:T(8,128)(2,1)} fusion(bf16[256,2048]{1,0:T(8,128)(2,1)} %param.15, f32[2048]{0:T(1024)S(1)} %convert_element_type.86, f32[2048]{0:T(1024)S(1)} %convert_element_type.85, f32[256]{0:T(256)S(1)} %add_rsqrt_fusion, f32[256]{0:T(256)S(1)} %broadcast_multiply_fusion), kind=kLoop, calls=%fused_computation.17 | loop fusion | flops 3145728 | bytes 2115584 | tf_op jit(solution)/shard_map/convert_element_type | solution.py:23
  14.5 0.0 all-gather.2.cloned.1.call-update
  14.5 0.0 reduce-scatter.2.cloned.1.call-start
  15.3 0.5 multiply_exponential_fusion.slopes_ref
  15.8 36.1 %all-gather.2.cloned.1.call-done = bf16[1024,2048]{1,0:T(8,128)(2,1)} async-done(((bf16[256,2048]{1,0:T(8,128)(2,1)}), bf16[1024,2048]{1,0:T(8,128)(2,1)}) %all-gather.2.cloned.1.call-update) | async-done | bytes 4194320 | tf_op jit(solution)/shard_map/all_gather | solution.py:184
  51.9 11.2 %add_convert_fusion.q_ref.kn_ref.vn_ref = bf16[1024,1536]{1,0:T(8,128)(2,1)} fusion(bf16[1024,2048]{1,0:T(8,128)(2,1)} %all-gather.2.cloned.1.call-done, bf16[2048,1536]{1,0:T(8,128)(2,1)} %param.19, f32[1536]{0:T(1024)S(1)} %convert_element_type.88), kind=kOutput, calls=%fused_computation | convolution fusion | flops 6445596672 | bytes 13637632 | tf_op jit(solution)/shard_map/dot_general | solution.py:183
  63.1 27.1 %shard_map.158 = bf16[1024,512]{1,0:T(8,128)(2,1)} custom-call(s32[1]{0:T(128)S(6)} %copy.46.prefix_ref, f32[4]{0:T(128)} %multiply_exponential_fusion.slopes_ref, bf16[1024,1536]{1,0:T(8,128)(2,1)} %add_convert_fusion.q_ref.kn_ref.vn_ref, bf16[1024,1536]{1,0:T(8,128)(2,1)} %add_convert_fusion.q_ref.kn_ref.vn_ref, ...), custom_call_target="tpu_custom_call" | custom-call | flops 4294967296 | bytes 6291456 | tf_op jit(solution)/shard_map/pallas_call | solution.py:112
  90.2 6.8 %fusion.48 = f32[1024,2048]{1,0:T(8,128)} fusion(bf16[1024,512]{1,0:T(8,128)(2,1)} %shard_map.158, bf16[512,2048]{1,0:T(8,128)(2,1)S(1)} %copy-done), kind=kOutput, calls=%fused_computation.92 | convolution fusion | flops 2147483648 | bytes 11534336 | tf_op jit(solution)/shard_map/dot_general | solution.py:193
  97.0 0.0 reduce-scatter.2.cloned.1.call-update
  97.0 0.7 copy-done.2
  97.7 3.3 %collective-permute-start.5 = (bf16[2,2048]{1,0:T(2,128)(2,1)S(1)}, bf16[2,2048]{1,0:T(2,128)(2,1)S(1)}, u32[]{:S(2)}, u32[]{:S(2)}) collective-permute-start(bf16[2,2048]{1,0:T(2,128)(2,1)S(1)} %copy-done.2), channel_id=1, source_target_pairs={{0,24},{4,28},{8,0},{12,4},{16,8},{20,12},{24,16},{28,20},{1,25},{... | collective-permute-start | bytes 24584 | tf_op jit(solution)/shard_map/ppermute | solution.py:206
  101.0 0.5 collective-permute-start.4
  101.5 3.3 %collective-permute-start.3 = (bf16[2,2048]{1,0:T(2,128)(2,1)S(1)}, bf16[2,2048]{1,0:T(2,128)(2,1)S(1)}, u32[]{:S(2)}, u32[]{:S(2)}) collective-permute-start(bf16[2,2048]{1,0:T(2,128)(2,1)S(1)} %copy-done.2), channel_id=1, source_target_pairs={{0,16},{4,20},{8,24},{12,28},{16,0},{20,4},{24,8},{28,12},{1,17},{... | collective-permute-start | bytes 24584 | tf_op jit(solution)/shard_map/ppermute | solution.py:206
  104.8 0.0 collective-permute-start.2
  104.9 1.1 collective-permute-start.1
  106.0 0.1 iota_compare_fusion
  106.0 0.1 subtract_convert_fusion
  106.1 0.2 fusion.31
  106.3 0.0 collective-permute-done.5
  106.3 1.5 collective-permute-start
  107.8 0.0 collective-permute-done.4
  107.8 3.3 %collective-permute-start.6 = (bf16[2,2048]{1,0:T(2,128)(2,1)S(1)}, bf16[2,2048]{1,0:T(2,128)(2,1)S(1)}, u32[]{:S(2)}, u32[]{:S(2)}) collective-permute-start(bf16[2,2048]{1,0:T(2,128)(2,1)S(1)} %copy-done.2), channel_id=1, source_target_pairs={{0,28},{4,0},{8,4},{12,8},{16,12},{20,16},{24,20},{28,24},{1,29},{... | collective-permute-start | bytes 24584 | tf_op jit(solution)/shard_map/ppermute | solution.py:206
  111.1 6.3 %copy.26 = bf16[2,2048,512]{1,2,0:T(8,128)(2,1)} copy(bf16[2,2048,512]{2,1,0:T(8,128)(2,1)} %param.25) | data formatting | bytes 8388608 | tf_op jit(solution)/shard_map/reshape | solution.py:230
  117.5 0.0 collective-permute-done.1
  117.5 0.0 collective-permute-done
  117.5 0.1 concatenate.6
  117.6 0.3 fusion.47
  117.9 0.2 multiply_reduce_fusion
  118.1 4.1 %fusion.5 = bf16[2,1536]{1,0:T(2,128)(2,1)S(1)} fusion(bf16[2048,1536]{1,0:T(8,128)(2,1)} %param.19, f32[2,2048]{1,0:T(2,128)S(1)} %get-tuple-element.10, f32[2]{0:T(128)S(1)} %add_rsqrt_fusion.1, f32[2]{0:T(128)S(1)} %broadcast_multiply_fusion.1, f32[2048]{0:T(1024)S(1)} %convert_element_type.86, f32[2048]{0:T(1024)S(1)} %convert_element_type.85, ...), kind=kOutput, calls=%fused_computation.10 | convolution fusion | flops 12609536 | bytes 6336528 | tf_op jit(solution)/shard_map/dot_general | solution.py:221
  122.3 0.0 copy-start.8
  122.3 0.1 fusion.22
  122.4 3.0 %fusion.23 = f32[2,4,1,2048]{3,2,1,0:T(1,128)S(1)} fusion(bf16[2,2048,4,128]{1,3,2,0:T(8,128)(2,1)} %bitcast.53, bf16[2,4,3,128]{3,2,1,0:T(4,128)(2,1)S(1)} %reshape.149), kind=kOutput, calls=%fused_computation.41 | convolution fusion | flops 4194304 | bytes 4263936 | tf_op jit(solution)/shard_map/vmap(hd,khd->hk)/dot_general | solution.py:140
  125.4 0.2 fusion.45
  125.6 0.2 fusion.15
  125.8 0.1 fusion.16
  125.9 0.0 copy-start.4
  125.9 0.0 copy-start.1
  126.0 0.7 fusion
  126.6 0.1 fusion.25
  126.7 0.4 fusion.26
  127.1 0.4 collective-permute-start.8
  127.5 0.2 collective-permute-start.7
  127.7 1.1 collective-permute-done.9
  128.8 2.5 %collective-permute-done.8 = f32[2,2048]{1,0:T(2,128)S(1)} collective-permute-done((f32[2,2048]{1,0:T(2,128)S(1)}, f32[2,2048]{1,0:T(2,128)S(1)}, u32[]{:S(2)}, u32[]{:S(2)}) %collective-permute-start.8) | collective-permute-done | bytes 16416 | tf_op jit(solution)/shard_map/ppermute | solution.py:239
  131.3 0.0 collective-permute-done.7
  131.5 1.4 collective-permute-start.16
  132.9 0.6 collective-permute-start.15
  133.4 1.2 collective-permute-start.14
  134.6 2.8 %collective-permute-start.13 = (bf16[2,2048]{1,0:T(2,128)(2,1)S(1)}, bf16[2,2048]{1,0:T(2,128)(2,1)S(1)}, u32[]{:S(2)}, u32[]{:S(2)}) collective-permute-start(bf16[2,2048]{1,0:T(2,128)(2,1)S(1)} %fusion.18), channel_id=1, source_target_pairs={{0,16},{4,20},{8,24},{12,28},{16,0},{20,4},{24,8},{28,12},{1,17},{... | collective-permute-start | bytes 24584 | tf_op jit(solution)/shard_map/ppermute | solution.py:248
  137.4 2.4 %collective-permute-start.11 = (bf16[2,2048]{1,0:T(2,128)(2,1)S(1)}, bf16[2,2048]{1,0:T(2,128)(2,1)S(1)}, u32[]{:S(2)}, u32[]{:S(2)}) collective-permute-start(bf16[2,2048]{1,0:T(2,128)(2,1)S(1)} %fusion.18), channel_id=1, source_target_pairs={{0,8},{4,12},{8,16},{12,20},{16,24},{20,28},{24,0},{28,4},{1,9},{5... | collective-permute-start | bytes 24584 | tf_op jit(solution)/shard_map/ppermute | solution.py:248
  139.9 0.1 collective-permute-start.10
  140.0 0.1 fusion.34
  140.1 2.9 %collective-permute-done.12 = bf16[2,2048]{1,0:T(2,128)(2,1)S(1)} collective-permute-done((bf16[2,2048]{1,0:T(2,128)(2,1)S(1)}, bf16[2,2048]{1,0:T(2,128)(2,1)S(1)}, u32[]{:S(2)}, u32[]{:S(2)}) %collective-permute-start.12) | collective-permute-done | bytes 8224 | tf_op jit(solution)/shard_map/ppermute | solution.py:248
  143.0 3.2 %collective-permute-done.10 = bf16[2,2048]{1,0:T(2,128)(2,1)S(1)} collective-permute-done((bf16[2,2048]{1,0:T(2,128)(2,1)S(1)}, bf16[2,2048]{1,0:T(2,128)(2,1)S(1)}, u32[]{:S(2)}, u32[]{:S(2)}) %collective-permute-start.10) | collective-permute-done | bytes 8224 | tf_op jit(solution)/shard_map/ppermute | solution.py:248
  146.2 0.1 concatenate.7
  146.3 0.8 convolution_convert_fusion
  147.1 22.5 %reduce-scatter.2.cloned.1.call-done = f32[256,2048]{1,0:T(8,128)} async-done(((f32[1024,2048]{1,0:T(8,128)}), f32[256,2048]{1,0:T(8,128)}) %reduce-scatter.2.cloned.1.call-update) | async-done | bytes 2097168 | tf_op jit(solution)/shard_map/reduce_scatter | solution.py:192
  169.6 2.9 %fusion.11 = bf16[256,2048]{1,0:T(8,128)(2,1)} fusion(bf16[256,2048]{1,0:T(8,128)(2,1)S(1)} %copy-done.1, f32[256,2048]{1,0:T(8,128)} %reduce-scatter.2.cloned.1.call-done, f32[2048]{0:T(1024)S(1)} %convert_element_type.90), kind=kLoop, calls=%fused_computation.18 | loop fusion | flops 2097152 | bytes 4202496 | tf_op jit(solution)/shard_map/convert_element_type | solution.py:198
  (37 shorter events, 0.2 us)
Async XLA Ops:
  7.2 83.0 %copy-start = (bf16[512,2048]{1,0:T(8,128)(2,1)S(1)}, bf16[512,2048]{1,0:T(8,128)(2,1)}, u32[]{:S(2)}) copy-start(bf16[512,2048]{1,0:T(8,128)(2,1)} %param.21) | copy-start | bytes 6291460
  7.2 8.1 %copy-start.3 = (bf16[1536]{0:T(1024)(128)(2,1)S(1)}, bf16[1536]{0:T(1024)(128)(2,1)}, u32[]{:S(2)}) copy-start(bf16[1536]{0:T(1024)(128)(2,1)} %param.20) | copy-start | bytes 9220
  7.2 44.7 %all-gather.2.cloned.1.call-start = ((), (), s32[]{:S(2)}) async-start(), calls=%async_computation.1 | async-start | bytes 5242880 | tf_op jit(solution)/shard_map/all_gather | solution.py:184
  14.5 155.1 %reduce-scatter.2.cloned.1.call-start = ((), (), s32[]{:S(2)}) async-start(), calls=%async_computation.2 | async-start | bytes 10485760 | tf_op jit(solution)/shard_map/reduce_scatter | solution.py:192
  97.0 0.7 copy-start.2
  97.0 9.0 %copy-start.5 = (s32[2]{0:T(128)S(1)}, s32[2]{0:T(128)}, u32[]{:S(2)}) copy-start(s32[2]{0:T(128)} %param.28) | copy-start | bytes 28
  97.0 9.1 %copy-start.7 = (s32[16]{0:T(128)S(1)}, s32[16]{0:T(128)}, u32[]{:S(2)}) copy-start(s32[16]{0:T(128)} %param.29) | copy-start | bytes 196
  97.7 8.6 %collective-permute-start.5 = (bf16[2,2048]{1,0:T(2,128)(2,1)S(1)}, bf16[2,2048]{1,0:T(2,128)(2,1)S(1)}, u32[]{:S(2)}, u32[]{:S(2)}) collective-permute-start(bf16[2,2048]{1,0:T(2,128)(2,1)S(1)} %copy-done.2), channel_id=1, source_target_pairs={{0,24},{4,28},{8,0},{12,4},{16,8},{20,12},{24,16},{28,20},{1,25},{... | collective-permute-start | bytes 24584 | tf_op jit(solution)/shard_map/ppermute | solution.py:206
  101.0 6.8 %collective-permute-start.4 = (bf16[2,2048]{1,0:T(2,128)(2,1)S(1)}, bf16[2,2048]{1,0:T(2,128)(2,1)S(1)}, u32[]{:S(2)}, u32[]{:S(2)}) collective-permute-start(bf16[2,2048]{1,0:T(2,128)(2,1)S(1)} %copy-done.2), channel_id=1, source_target_pairs={{0,20},{4,24},{8,28},{12,0},{16,4},{20,8},{24,12},{28,16},{1,21},{... | collective-permute-start | bytes 24584 | tf_op jit(solution)/shard_map/ppermute | solution.py:206
  101.5 15.9 %collective-permute-start.3 = (bf16[2,2048]{1,0:T(2,128)(2,1)S(1)}, bf16[2,2048]{1,0:T(2,128)(2,1)S(1)}, u32[]{:S(2)}, u32[]{:S(2)}) collective-permute-start(bf16[2,2048]{1,0:T(2,128)(2,1)S(1)} %copy-done.2), channel_id=1, source_target_pairs={{0,16},{4,20},{8,24},{12,28},{16,0},{20,4},{24,8},{28,12},{1,17},{... | collective-permute-start | bytes 24584 | tf_op jit(solution)/shard_map/ppermute | solution.py:206
  104.8 12.6 %collective-permute-start.2 = (bf16[2,2048]{1,0:T(2,128)(2,1)S(1)}, bf16[2,2048]{1,0:T(2,128)(2,1)S(1)}, u32[]{:S(2)}, u32[]{:S(2)}) collective-permute-start(bf16[2,2048]{1,0:T(2,128)(2,1)S(1)} %copy-done.2), channel_id=1, source_target_pairs={{0,12},{4,16},{8,20},{12,24},{16,28},{20,0},{24,4},{28,8},{1,13},{... | collective-permute-start | bytes 24584 | tf_op jit(solution)/shard_map/ppermute | solution.py:206
  104.9 12.6 %collective-permute-start.1 = (bf16[2,2048]{1,0:T(2,128)(2,1)S(1)}, bf16[2,2048]{1,0:T(2,128)(2,1)S(1)}, u32[]{:S(2)}, u32[]{:S(2)}) collective-permute-start(bf16[2,2048]{1,0:T(2,128)(2,1)S(1)} %copy-done.2), channel_id=1, source_target_pairs={{0,8},{4,12},{8,16},{12,20},{16,24},{20,28},{24,0},{28,4},{1,9},{5... | collective-permute-start | bytes 24584 | tf_op jit(solution)/shard_map/ppermute | solution.py:206
  106.3 11.2 %collective-permute-start = (bf16[2,2048]{1,0:T(2,128)(2,1)S(1)}, bf16[2,2048]{1,0:T(2,128)(2,1)S(1)}, u32[]{:S(2)}, u32[]{:S(2)}) collective-permute-start(bf16[2,2048]{1,0:T(2,128)(2,1)S(1)} %copy-done.2), channel_id=1, source_target_pairs={{0,4},{4,8},{8,12},{12,16},{16,20},{20,24},{24,28},{28,0},{1,5},{5... | collective-permute-start | bytes 24584 | tf_op jit(solution)/shard_map/ppermute | solution.py:206
  107.8 9.6 %collective-permute-start.6 = (bf16[2,2048]{1,0:T(2,128)(2,1)S(1)}, bf16[2,2048]{1,0:T(2,128)(2,1)S(1)}, u32[]{:S(2)}, u32[]{:S(2)}) collective-permute-start(bf16[2,2048]{1,0:T(2,128)(2,1)S(1)} %copy-done.2), channel_id=1, source_target_pairs={{0,28},{4,0},{8,4},{12,8},{16,12},{20,16},{24,20},{28,24},{1,29},{... | collective-permute-start | bytes 24584 | tf_op jit(solution)/shard_map/ppermute | solution.py:206
  122.3 3.1 %copy-start.6 = (f32[4]{0:T(128)S(1)}, f32[4]{0:T(128)}, u32[]{:S(2)}) copy-start(f32[4]{0:T(128)} %multiply_exponential_fusion.slopes_ref) | copy-start | bytes 52
  122.3 3.6 %copy-start.8 = (bf16[2,2048,512]{2,1,0:T(8,128)(2,1)S(1)}, bf16[2,2048,512]{2,1,0:T(8,128)(2,1)}, u32[]{:S(2)}) copy-start(bf16[2,2048,512]{2,1,0:T(8,128)(2,1)} %param.26) | copy-start | bytes 12582916
  125.9 1.7 copy-start.4
  125.9 43.7 %copy-start.1 = (bf16[256,2048]{1,0:T(8,128)(2,1)S(1)}, bf16[256,2048]{1,0:T(8,128)(2,1)}, u32[]{:S(2)}) copy-start(bf16[256,2048]{1,0:T(8,128)(2,1)} %param.15) | copy-start | bytes 3145732
  127.1 1.7 collective-permute-start.9
  127.1 4.3 %collective-permute-start.8 = (f32[2,2048]{1,0:T(2,128)S(1)}, f32[2,2048]{1,0:T(2,128)S(1)}, u32[]{:S(2)}, u32[]{:S(2)}) collective-permute-start(f32[2,2048]{1,0:T(2,128)S(1)} %fusion.26), channel_id=1, source_target_pairs={{0,2},{1,3},{2,0},{3,1},{4,6},{5,7},{6,4},{7,5},{8,10},{9,11},{10,... | collective-permute-start | bytes 49160 | tf_op jit(solution)/shard_map/ppermute | solution.py:239
  127.5 3.9 %collective-permute-start.7 = (f32[2,2048]{1,0:T(2,128)S(1)}, f32[2,2048]{1,0:T(2,128)S(1)}, u32[]{:S(2)}, u32[]{:S(2)}) collective-permute-start(f32[2,2048]{1,0:T(2,128)S(1)} %fusion.26), channel_id=1, source_target_pairs={{0,1},{1,2},{2,3},{3,0},{4,5},{5,6},{6,7},{7,4},{8,9},{9,10},{10,1... | collective-permute-start | bytes 49160 | tf_op jit(solution)/shard_map/ppermute | solution.py:239
  131.5 6.0 %collective-permute-start.16 = (bf16[2,2048]{1,0:T(2,128)(2,1)S(1)}, bf16[2,2048]{1,0:T(2,128)(2,1)S(1)}, u32[]{:S(2)}, u32[]{:S(2)}) collective-permute-start(bf16[2,2048]{1,0:T(2,128)(2,1)S(1)} %fusion.18), channel_id=1, source_target_pairs={{0,28},{4,0},{8,4},{12,8},{16,12},{20,16},{24,20},{28,24},{1,29},{... | collective-permute-start | bytes 24584 | tf_op jit(solution)/shard_map/ppermute | solution.py:248
  132.9 7.0 %collective-permute-start.15 = (bf16[2,2048]{1,0:T(2,128)(2,1)S(1)}, bf16[2,2048]{1,0:T(2,128)(2,1)S(1)}, u32[]{:S(2)}, u32[]{:S(2)}) collective-permute-start(bf16[2,2048]{1,0:T(2,128)(2,1)S(1)} %fusion.18), channel_id=1, source_target_pairs={{0,24},{4,28},{8,0},{12,4},{16,8},{20,12},{24,16},{28,20},{1,25},{... | collective-permute-start | bytes 24584 | tf_op jit(solution)/shard_map/ppermute | solution.py:248
  133.4 6.7 %collective-permute-start.14 = (bf16[2,2048]{1,0:T(2,128)(2,1)S(1)}, bf16[2,2048]{1,0:T(2,128)(2,1)S(1)}, u32[]{:S(2)}, u32[]{:S(2)}) collective-permute-start(bf16[2,2048]{1,0:T(2,128)(2,1)S(1)} %fusion.18), channel_id=1, source_target_pairs={{0,20},{4,24},{8,28},{12,0},{16,4},{20,8},{24,12},{28,16},{1,21},{... | collective-permute-start | bytes 24584 | tf_op jit(solution)/shard_map/ppermute | solution.py:248
  134.6 5.5 %collective-permute-start.13 = (bf16[2,2048]{1,0:T(2,128)(2,1)S(1)}, bf16[2,2048]{1,0:T(2,128)(2,1)S(1)}, u32[]{:S(2)}, u32[]{:S(2)}) collective-permute-start(bf16[2,2048]{1,0:T(2,128)(2,1)S(1)} %fusion.18), channel_id=1, source_target_pairs={{0,16},{4,20},{8,24},{12,28},{16,0},{20,4},{24,8},{28,12},{1,17},{... | collective-permute-start | bytes 24584 | tf_op jit(solution)/shard_map/ppermute | solution.py:248
  137.4 5.6 %collective-permute-start.12 = (bf16[2,2048]{1,0:T(2,128)(2,1)S(1)}, bf16[2,2048]{1,0:T(2,128)(2,1)S(1)}, u32[]{:S(2)}, u32[]{:S(2)}) collective-permute-start(bf16[2,2048]{1,0:T(2,128)(2,1)S(1)} %fusion.18), channel_id=1, source_target_pairs={{0,12},{4,16},{8,20},{12,24},{16,28},{20,0},{24,4},{28,8},{1,13},{... | collective-permute-start | bytes 24584 | tf_op jit(solution)/shard_map/ppermute | solution.py:248
  137.4 5.6 %collective-permute-start.11 = (bf16[2,2048]{1,0:T(2,128)(2,1)S(1)}, bf16[2,2048]{1,0:T(2,128)(2,1)S(1)}, u32[]{:S(2)}, u32[]{:S(2)}) collective-permute-start(bf16[2,2048]{1,0:T(2,128)(2,1)S(1)} %fusion.18), channel_id=1, source_target_pairs={{0,8},{4,12},{8,16},{12,20},{16,24},{20,28},{24,0},{28,4},{1,9},{5... | collective-permute-start | bytes 24584 | tf_op jit(solution)/shard_map/ppermute | solution.py:248
  139.9 6.3 %collective-permute-start.10 = (bf16[2,2048]{1,0:T(2,128)(2,1)S(1)}, bf16[2,2048]{1,0:T(2,128)(2,1)S(1)}, u32[]{:S(2)}, u32[]{:S(2)}) collective-permute-start(bf16[2,2048]{1,0:T(2,128)(2,1)S(1)} %fusion.18), channel_id=1, source_target_pairs={{0,4},{4,8},{8,12},{12,16},{16,20},{20,24},{24,28},{28,0},{1,5},{5... | collective-permute-start | bytes 24584 | tf_op jit(solution)/shard_map/ppermute | solution.py:248
Sparse Core Ops, SparseCore 0:
  14.7 37.1 all-gather.1
  97.1 72.4 reduce-scatter.1

commit v5 on v4

--- a/solution.py
+++ b/solution.py
@@ -74,9 +74,9 @@
     return context.astype(jnp.bfloat16).reshape(group_size, -1)
 
 
-def _prefill_kernel(prefix_ref, slopes_ref, q_ref, kn_ref, vn_ref, kc_ref, vc_ref, o_ref, *, tq):
+def _prefill_kernel(prefix_ref, slopes_ref, q_ref, kn_ref, vn_ref, kc_ref, vc_ref, o_ref, *, tq, chunks, chunk):
     h = pl.program_id(0)
-    i = pl.program_id(1)
+    i = pl.program_id(1) * chunks + chunk
     prefix = prefix_ref[0]
     slope = slopes_ref[h]
     factor = 1.0 / math.sqrt(q_ref.shape[-1])
@@ -104,19 +104,19 @@
     ctx = ctx + jnp.dot(p_n, vn_ref[...], preferred_element_type=jnp.float32)
     o_ref[...] = ctx.astype(o_ref.dtype)
 
-def prefill_attention_kernel(merged, cache_keys, cache_values, prefix, slopes, head_size, tq=256):
+def prefill_attention_kernel(merged, cache_keys, cache_values, prefix, slopes, head_size, tq, chunks, chunk):
     group = merged.shape[0]
     heads = merged.shape[1] // (3 * head_size)
     cache_size = cache_keys.shape[0]
     col = lambda c: (lambda h, i, *_: (0, h * 3 + c))
     return pl.pallas_call(
-        functools.partial(_prefill_kernel, tq=tq),
-        out_shape=jax.ShapeDtypeStruct((group, heads * head_size), jnp.bfloat16),
+        functools.partial(_prefill_kernel, tq=tq, chunks=chunks, chunk=chunk),
+        out_shape=jax.ShapeDtypeStruct((group // chunks, heads * head_size), jnp.bfloat16),
         grid_spec=pltpu.PrefetchScalarGridSpec(
             num_scalar_prefetch=2,
-            grid=(heads, group // tq),
+            grid=(heads, group // (tq * chunks)),
             in_specs=[
-                pl.BlockSpec((tq, head_size), lambda h, i, *_: (i, h * 3)),
+                pl.BlockSpec((tq, head_size), lambda h, i, *_: (i * chunks + chunk, h * 3)),
                 pl.BlockSpec((group, head_size), col(1)),
                 pl.BlockSpec((group, head_size), col(2)),
                 pl.BlockSpec((cache_size, head_size), lambda h, i, *_: (0, h)),
@@ -125,9 +125,9 @@
             out_specs=pl.BlockSpec((tq, head_size), lambda h, i, *_: (i, h)),
         ),
         cost_estimate=pl.CostEstimate(
-            flops=4 * heads * group * (group + cache_size) * head_size,
-            transcendentals=heads * group * (group + cache_size),
-            bytes_accessed=2 * (group * heads * 3 * head_size + 2 * cache_size * heads * head_size + group * heads * head_size),
+            flops=4 * heads * group * (group + cache_size) * head_size // chunks,
+            transcendentals=heads * group * (group + cache_size) // chunks,
+            bytes_accessed=2 * (group * heads * 3 * head_size + 2 * cache_size * heads * head_size) // chunks,
         ),
     )(prefix, slopes, merged, merged, merged, cache_keys, cache_values)
 
@@ -186,15 +186,22 @@
         preferred_element_type=jnp.float32,
     )
     merged_rows = (product + qkv_bias.astype(jnp.float32)).astype(jnp.bfloat16)
-    context = prefill_attention_kernel(
-        merged_rows, pre_keys[0], pre_values[0], prefix_lengths, slopes, head_size
-    )
-    summed = lax.psum_scatter(
-        jnp.dot(context, out_weight, preferred_element_type=jnp.float32),
-        "tensor",
-        scatter_dimension=0,
-        tiled=True,
-    )
+    chunks = 2
+    part = pre_hidden.shape[0] // chunks
+    pieces = []
+    for chunk in range(chunks):
+        context = prefill_attention_kernel(
+            merged_rows, pre_keys[0], pre_values[0], prefix_lengths, slopes, head_size, part, chunks, chunk
+        )
+        pieces.append(
+            lax.psum_scatter(
+                jnp.dot(context, out_weight, preferred_element_type=jnp.float32),
+                "tensor",
+                scatter_dimension=0,
+                tiled=True,
+            )
+        )
+    summed = jnp.concatenate(pieces, axis=0)
     pre_output = (summed + bias_sum + pre_hidden.astype(jnp.float32)).astype(jnp.bfloat16)
     slot_count = dec_hidden.shape[0]
     dp_size = lax.axis_size("dp")

time: 180 us -> 188 us (1.044)
  Pallas kernels: 27.1 us -> 37.8 us
  waiting for transfers between devices: 68.4 us -> 65 us
    pallas_call x1 -> x2, Pallas kernels: 27.1 us -> 37.8 us  [prefill_attention_kernel(): pl.pallas_call(functools.partial(_prefill_kernel, tq=tq, chunks=chunks, c...]
    reduce_scatter x1 -> x2, waiting for transfers between devices: 22.5 us -> 19.5 us  [per_device(): lax.psum_scatter(jnp.dot(context, out_weight, preferred_element_type=jnp....]
    dot_general x1 -> x2, matrix products: 6.79 us -> 8.59 us  [per_device(): jnp.dot(context, out_weight, preferred_element_type=jnp.float32)]
  transfers between devices with their start and end apart: 19 -> 20, of which waited for: 6 -> 7; matrix products, arithmetic and copies ran while one was open for 10% -> 12% of each run, Pallas kernels for 0% -> 10%
where the time goes in v5:
time: 188 us; the launch traced here: 187 us
  waiting for transfers between devices  65 us (35%)
  Pallas kernels  37.8 us (20%)
  matrix products  28.7 us (15%)
  starting transfers between devices  22 us (12%)
  between operations  14.6 us (8%)
  other arithmetic  12 us (6%)
  local copies, waits for them, and re-layouts  7.26 us (4%)
    pallas_call x2, Pallas kernels, prefill_attention_kernel(): pl.pallas_call(functools.partial(_prefill_kernel, tq=tq, chunks=chunks, c...  37.8 us
    all_gather x1, waiting for transfers between devices, per_device(): lax.all_gather(normed, 'tensor', axis=0, tiled=True)  36.1 us
    reduce_scatter x2, waiting for transfers between devices, per_device(): lax.psum_scatter(jnp.dot(context, out_weight, preferred_element_type=jnp....  19.5 us
    ppermute x7, starting transfers between devices, per_device(): lax.ppermute(dec_hidden, 'dp', [(i, (i + k) % dp_size) for i in range(dp_...  13.1 us
    dot_general x1, matrix products, per_device(): jnp.dot(lax.all_gather(normed, 'tensor', axis=0, tiled=True), qkv_weight,...  11.2 us
    dot_general x2, matrix products, per_device(): jnp.dot(context, out_weight, preferred_element_type=jnp.float32)  8.59 us
    ppermute x7, starting transfers between devices, per_device(): lax.ppermute(slot_rows, 'dp', [(i, (i + k) % dp_size) for i in range(dp_s...  8.09 us
    reshape x1, local copies, waits for them, and re-layouts, per_device(): dec_keys.reshape(slot_count, dec_cache, local_heads, head_size)  6.3 us
  transfers between devices with their start and end apart: 20, of which 7 were waited for; matrix products, arithmetic and copies ran while one was open for 12% of the time, Pallas kernels for 10%

profile of v5, /device:TPU:0, one launch (start us, length us, event | category | flops | bytes accessed | tf_op | source)
XLA Modules:
  0.0 187.4 jit_solution(17438604312900615573)
XLA Ops:
  7.2 0.0 copy-start
  7.2 0.0 all-gather.2.cloned.1.call-start
  7.2 1.6 convert_reduce_fusion
  8.8 1.6 fusion.7
  10.5 0.7 convert_element_type.85
  11.2 0.7 convert_element_type.86
  11.9 2.7 %fusion.10 = bf16[256,2048]{1,0:T(8,128)(2,1)} fusion(bf16[256,2048]{1,0:T(8,128)(2,1)} %param.15, f32[2048]{0:T(1024)S(1)} %convert_element_type.86, f32[2048]{0:T(1024)S(1)} %convert_element_type.85, f32[256]{0:T(256)S(1)} %add_rsqrt_fusion, f32[256]{0:T(256)S(1)} %broadcast_multiply_fusion), kind=kLoop, calls=%fused_computation.17 | loop fusion | flops 3145728 | bytes 2115584 | tf_op jit(solution)/shard_map/convert_element_type | solution.py:23
  14.5 0.0 all-gather.2.cloned.1.call-update
  14.5 0.0 reduce-scatter.3.cloned.1.call-start
  15.3 0.5 multiply_exponential_fusion.slopes_ref
  15.8 36.1 %all-gather.2.cloned.1.call-done = bf16[1024,2048]{1,0:T(8,128)(2,1)} async-done(((bf16[256,2048]{1,0:T(8,128)(2,1)}), bf16[1024,2048]{1,0:T(8,128)(2,1)}) %all-gather.2.cloned.1.call-update) | async-done | bytes 4194320 | tf_op jit(solution)/shard_map/all_gather | solution.py:184
  51.9 11.2 %add_convert_fusion.q_ref.kn_ref.vn_ref = bf16[1024,1536]{1,0:T(8,128)(2,1)} fusion(bf16[1024,2048]{1,0:T(8,128)(2,1)} %all-gather.2.cloned.1.call-done, bf16[2048,1536]{1,0:T(8,128)(2,1)} %param.19, f32[1536]{0:T(1024)S(1)} %convert_element_type.88), kind=kOutput, calls=%fused_computation | convolution fusion | flops 6445596672 | bytes 13637632 | tf_op jit(solution)/shard_map/dot_general | solution.py:183
  63.1 18.7 %shard_map.158 = bf16[512,512]{1,0:T(8,128)(2,1)} custom-call(s32[1]{0:T(128)S(6)} %copy.46.prefix_ref, f32[4]{0:T(128)} %multiply_exponential_fusion.slopes_ref, bf16[1024,1536]{1,0:T(8,128)(2,1)} %add_convert_fusion.q_ref.kn_ref.vn_ref, bf16[1024,1536]{1,0:T(8,128)(2,1)} %add_convert_fusion.q_ref.kn_ref.vn_ref, ...), custom_call_target="tpu_custom_call" | custom-call | flops 2147483648 | bytes 2621440 | tf_op jit(solution)/shard_map/pallas_call | solution.py:112
  81.8 4.2 %fusion.48 = f32[512,2048]{1,0:T(8,128)} fusion(bf16[512,512]{1,0:T(8,128)(2,1)} %shard_map.158, bf16[512,2048]{1,0:T(8,128)(2,1)S(1)} %copy-done), kind=kOutput, calls=%fused_computation.93 | convolution fusion | flops 1073741824 | bytes 6815744 | tf_op jit(solution)/shard_map/dot_general | solution.py:198
  86.1 0.0 reduce-scatter.3.cloned.1.call-update
  86.1 0.0 reduce-scatter.5.cloned.1.call-start
  86.1 19.1 %shard_map.159 = bf16[512,512]{1,0:T(8,128)(2,1)} custom-call(s32[1]{0:T(128)S(6)} %copy.46.prefix_ref, f32[4]{0:T(128)} %multiply_exponential_fusion.slopes_ref, bf16[1024,1536]{1,0:T(8,128)(2,1)} %add_convert_fusion.q_ref.kn_ref.vn_ref, bf16[1024,1536]{1,0:T(8,128)(2,1)} %add_convert_fusion.q_ref.kn_ref.vn_ref, ...), custom_call_target="tpu_custom_call" | custom-call | flops 2147483648 | bytes 2621440 | tf_op jit(solution)/shard_map/pallas_call | solution.py:112
  105.2 4.3 %fusion.49 = f32[512,2048]{1,0:T(8,128)} fusion(bf16[512,512]{1,0:T(8,128)(2,1)} %shard_map.159, bf16[512,2048]{1,0:T(8,128)(2,1)S(1)} %copy-done), kind=kOutput, calls=%fused_computation.94 | convolution fusion | flops 1073741824 | bytes 6815744 | tf_op jit(solution)/shard_map/dot_general | solution.py:198
  109.6 0.0 reduce-scatter.5.cloned.1.call-update
  109.6 0.7 copy-done.2
  110.3 3.4 %collective-permute-start.5 = (bf16[2,2048]{1,0:T(2,128)(2,1)S(1)}, bf16[2,2048]{1,0:T(2,128)(2,1)S(1)}, u32[]{:S(2)}, u32[]{:S(2)}) collective-permute-start(bf16[2,2048]{1,0:T(2,128)(2,1)S(1)} %copy-done.2), channel_id=1, source_target_pairs={{0,24},{4,28},{8,0},{12,4},{16,8},{20,12},{24,16},{28,20},{1,25},{... | collective-permute-start | bytes 24584 | tf_op jit(solution)/shard_map/ppermute | solution.py:213
  113.6 0.5 collective-permute-start.4
  114.2 3.3 %collective-permute-start.3 = (bf16[2,2048]{1,0:T(2,128)(2,1)S(1)}, bf16[2,2048]{1,0:T(2,128)(2,1)S(1)}, u32[]{:S(2)}, u32[]{:S(2)}) collective-permute-start(bf16[2,2048]{1,0:T(2,128)(2,1)S(1)} %copy-done.2), channel_id=1, source_target_pairs={{0,16},{4,20},{8,24},{12,28},{16,0},{20,4},{24,8},{28,12},{1,17},{... | collective-permute-start | bytes 24584 | tf_op jit(solution)/shard_map/ppermute | solution.py:213
  117.5 0.0 collective-permute-start.2
  117.5 1.1 collective-permute-start.1
  118.6 0.1 iota_compare_fusion
  118.7 0.1 subtract_convert_fusion
  118.7 0.2 fusion.31
  118.9 1.5 collective-permute-start
  120.4 3.3 %collective-permute-start.6 = (bf16[2,2048]{1,0:T(2,128)(2,1)S(1)}, bf16[2,2048]{1,0:T(2,128)(2,1)S(1)}, u32[]{:S(2)}, u32[]{:S(2)}) collective-permute-start(bf16[2,2048]{1,0:T(2,128)(2,1)S(1)} %copy-done.2), channel_id=1, source_target_pairs={{0,28},{4,0},{8,4},{12,8},{16,12},{20,16},{24,20},{28,24},{1,29},{... | collective-permute-start | bytes 24584 | tf_op jit(solution)/shard_map/ppermute | solution.py:213
  123.7 6.3 %copy.26 = bf16[2,2048,512]{1,2,0:T(8,128)(2,1)} copy(bf16[2,2048,512]{2,1,0:T(8,128)(2,1)} %param.25) | data formatting | bytes 8388608 | tf_op jit(solution)/shard_map/reshape | solution.py:237
  130.1 0.1 concatenate.10
  130.2 0.3 fusion.47
  130.5 0.2 multiply_reduce_fusion
  130.7 3.8 %fusion.5 = bf16[2,1536]{1,0:T(2,128)(2,1)S(1)} fusion(bf16[2048,1536]{1,0:T(8,128)(2,1)} %param.19, f32[2,2048]{1,0:T(2,128)S(1)} %get-tuple-element.10, f32[2]{0:T(128)S(1)} %add_rsqrt_fusion.1, f32[2]{0:T(128)S(1)} %broadcast_multiply_fusion.1, f32[2048]{0:T(1024)S(1)} %convert_element_type.86, f32[2048]{0:T(1024)S(1)} %convert_element_type.85, ...), kind=kOutput, calls=%fused_computation.10 | convolution fusion | flops 12609536 | bytes 6336528 | tf_op jit(solution)/shard_map/dot_general | solution.py:228
  134.5 0.0 copy-start.8
  134.5 0.1 fusion.22
  134.6 3.0 %fusion.23 = f32[2,4,1,2048]{3,2,1,0:T(1,128)S(1)} fusion(bf16[2,2048,4,128]{1,3,2,0:T(8,128)(2,1)} %bitcast.55, bf16[2,4,3,128]{3,2,1,0:T(4,128)(2,1)S(1)} %reshape.149), kind=kOutput, calls=%fused_computation.42 | convolution fusion | flops 4194304 | bytes 4263936 | tf_op jit(solution)/shard_map/vmap(hd,khd->hk)/dot_general | solution.py:140
  137.6 0.2 fusion.45
  137.8 0.2 fusion.15
  138.0 0.1 fusion.16
  138.1 0.0 copy-start.5
  138.1 0.0 copy-start.1
  138.1 0.7 fusion
  138.8 0.1 fusion.25
  138.9 0.4 fusion.26
  139.3 0.5 collective-permute-start.8
  139.8 0.2 collective-permute-start.7
  140.0 0.7 collective-permute-done.9
  140.7 2.4 %collective-permute-done.8 = f32[2,2048]{1,0:T(2,128)S(1)} collective-permute-done((f32[2,2048]{1,0:T(2,128)S(1)}, f32[2,2048]{1,0:T(2,128)S(1)}, u32[]{:S(2)}, u32[]{:S(2)}) %collective-permute-start.8) | collective-permute-done | bytes 16416 | tf_op jit(solution)/shard_map/ppermute | solution.py:246
  143.2 1.0 collective-permute-start.16
  144.2 0.6 collective-permute-start.15
  144.8 1.1 collective-permute-start.14
  145.9 2.7 %collective-permute-start.13 = (bf16[2,2048]{1,0:T(2,128)(2,1)S(1)}, bf16[2,2048]{1,0:T(2,128)(2,1)S(1)}, u32[]{:S(2)}, u32[]{:S(2)}) collective-permute-start(bf16[2,2048]{1,0:T(2,128)(2,1)S(1)} %fusion.18), channel_id=1, source_target_pairs={{0,16},{4,20},{8,24},{12,28},{16,0},{20,4},{24,8},{28,12},{1,17},{... | collective-permute-start | bytes 24584 | tf_op jit(solution)/shard_map/ppermute | solution.py:255
  148.6 2.6 %collective-permute-start.11 = (bf16[2,2048]{1,0:T(2,128)(2,1)S(1)}, bf16[2,2048]{1,0:T(2,128)(2,1)S(1)}, u32[]{:S(2)}, u32[]{:S(2)}) collective-permute-start(bf16[2,2048]{1,0:T(2,128)(2,1)S(1)} %fusion.18), channel_id=1, source_target_pairs={{0,8},{4,12},{8,16},{12,20},{16,24},{20,28},{24,0},{28,4},{1,9},{5... | collective-permute-start | bytes 24584 | tf_op jit(solution)/shard_map/ppermute | solution.py:255
  151.3 0.0 collective-permute-start.10
  151.3 0.1 fusion.34
  151.4 2.7 %collective-permute-done.12 = bf16[2,2048]{1,0:T(2,128)(2,1)S(1)} collective-permute-done((bf16[2,2048]{1,0:T(2,128)(2,1)S(1)}, bf16[2,2048]{1,0:T(2,128)(2,1)S(1)}, u32[]{:S(2)}, u32[]{:S(2)}) %collective-permute-start.12) | collective-permute-done | bytes 8224 | tf_op jit(solution)/shard_map/ppermute | solution.py:255
  154.1 0.1 collective-permute-done.11
  154.1 3.5 %collective-permute-done.10 = bf16[2,2048]{1,0:T(2,128)(2,1)S(1)} collective-permute-done((bf16[2,2048]{1,0:T(2,128)(2,1)S(1)}, bf16[2,2048]{1,0:T(2,128)(2,1)S(1)}, u32[]{:S(2)}, u32[]{:S(2)}) %collective-permute-start.10) | collective-permute-done | bytes 8224 | tf_op jit(solution)/shard_map/ppermute | solution.py:255
  157.6 0.1 concatenate.11
  157.7 0.8 convolution_convert_fusion
  158.5 19.5 %reduce-scatter.5.cloned.1.call-done = f32[128,2048]{1,0:T(8,128)} async-done(((f32[512,2048]{1,0:T(8,128)}), f32[128,2048]{1,0:T(8,128)}) %reduce-scatter.5.cloned.1.call-update) | async-done | bytes 1048592 | tf_op jit(solution)/shard_map/reduce_scatter | solution.py:197
  178.0 2.8 %fusion.11 = bf16[256,2048]{1,0:T(8,128)(2,1)} fusion(bf16[256,2048]{1,0:T(8,128)(2,1)S(1)} %copy-done.1, f32[128,2048]{1,0:T(8,128)} %reduce-scatter.5.cloned.1.call-done, f32[128,2048]{1,0:T(8,128)} %reduce-scatter.3.cloned.1.call-done, f32[2048]{0:T(1024)S(1)} %convert_element_type.90), kind=kLoop, calls=%fused_computation.18 | loop fusion | flops 2621440 | bytes 4202496 | tf_op jit(solution)/shard_map/convert_element_type | solution.py:205
  (42 shorter events, 0.2 us)
Async XLA Ops:
  7.2 74.6 %copy-start = (bf16[512,2048]{1,0:T(8,128)(2,1)S(1)}, bf16[512,2048]{1,0:T(8,128)(2,1)}, u32[]{:S(2)}) copy-start(bf16[512,2048]{1,0:T(8,128)(2,1)} %param.21) | copy-start | bytes 6291460
  7.2 8.1 %copy-start.4 = (bf16[1536]{0:T(1024)(128)(2,1)S(1)}, bf16[1536]{0:T(1024)(128)(2,1)}, u32[]{:S(2)}) copy-start(bf16[1536]{0:T(1024)(128)(2,1)} %param.20) | copy-start | bytes 9220
  7.2 44.7 %all-gather.2.cloned.1.call-start = ((), (), s32[]{:S(2)}) async-start(), calls=%async_computation.2 | async-start | bytes 5242880 | tf_op jit(solution)/shard_map/all_gather | solution.py:184
  14.5 144.0 %reduce-scatter.3.cloned.1.call-start = ((), (), s32[]{:S(2)}) async-start(), calls=%async_computation.3 | async-start | bytes 5242880 | tf_op jit(solution)/shard_map/reduce_scatter | solution.py:197
  86.1 91.9 %reduce-scatter.5.cloned.1.call-start = ((), (), s32[]{:S(2)}) async-start(), calls=%async_computation.4 | async-start | bytes 5242880 | tf_op jit(solution)/shard_map/reduce_scatter | solution.py:197
  109.6 0.7 copy-start.2
  109.6 9.0 %copy-start.6 = (s32[2]{0:T(128)S(1)}, s32[2]{0:T(128)}, u32[]{:S(2)}) copy-start(s32[2]{0:T(128)} %param.28) | copy-start | bytes 28
  109.6 9.2 %copy-start.7 = (s32[16]{0:T(128)S(1)}, s32[16]{0:T(128)}, u32[]{:S(2)}) copy-start(s32[16]{0:T(128)} %param.29) | copy-start | bytes 196
  110.3 8.6 %collective-permute-start.5 = (bf16[2,2048]{1,0:T(2,128)(2,1)S(1)}, bf16[2,2048]{1,0:T(2,128)(2,1)S(1)}, u32[]{:S(2)}, u32[]{:S(2)}) collective-permute-start(bf16[2,2048]{1,0:T(2,128)(2,1)S(1)} %copy-done.2), channel_id=1, source_target_pairs={{0,24},{4,28},{8,0},{12,4},{16,8},{20,12},{24,16},{28,20},{1,25},{... | collective-permute-start | bytes 24584 | tf_op jit(solution)/shard_map/ppermute | solution.py:213
  113.6 6.8 %collective-permute-start.4 = (bf16[2,2048]{1,0:T(2,128)(2,1)S(1)}, bf16[2,2048]{1,0:T(2,128)(2,1)S(1)}, u32[]{:S(2)}, u32[]{:S(2)}) collective-permute-start(bf16[2,2048]{1,0:T(2,128)(2,1)S(1)} %copy-done.2), channel_id=1, source_target_pairs={{0,20},{4,24},{8,28},{12,0},{16,4},{20,8},{24,12},{28,16},{1,21},{... | collective-permute-start | bytes 24584 | tf_op jit(solution)/shard_map/ppermute | solution.py:213
  114.2 15.9 %collective-permute-start.3 = (bf16[2,2048]{1,0:T(2,128)(2,1)S(1)}, bf16[2,2048]{1,0:T(2,128)(2,1)S(1)}, u32[]{:S(2)}, u32[]{:S(2)}) collective-permute-start(bf16[2,2048]{1,0:T(2,128)(2,1)S(1)} %copy-done.2), channel_id=1, source_target_pairs={{0,16},{4,20},{8,24},{12,28},{16,0},{20,4},{24,8},{28,12},{1,17},{... | collective-permute-start | bytes 24584 | tf_op jit(solution)/shard_map/ppermute | solution.py:213
  117.5 12.6 %collective-permute-start.2 = (bf16[2,2048]{1,0:T(2,128)(2,1)S(1)}, bf16[2,2048]{1,0:T(2,128)(2,1)S(1)}, u32[]{:S(2)}, u32[]{:S(2)}) collective-permute-start(bf16[2,2048]{1,0:T(2,128)(2,1)S(1)} %copy-done.2), channel_id=1, source_target_pairs={{0,12},{4,16},{8,20},{12,24},{16,28},{20,0},{24,4},{28,8},{1,13},{... | collective-permute-start | bytes 24584 | tf_op jit(solution)/shard_map/ppermute | solution.py:213
  117.5 12.6 %collective-permute-start.1 = (bf16[2,2048]{1,0:T(2,128)(2,1)S(1)}, bf16[2,2048]{1,0:T(2,128)(2,1)S(1)}, u32[]{:S(2)}, u32[]{:S(2)}) collective-permute-start(bf16[2,2048]{1,0:T(2,128)(2,1)S(1)} %copy-done.2), channel_id=1, source_target_pairs={{0,8},{4,12},{8,16},{12,20},{16,24},{20,28},{24,0},{28,4},{1,9},{5... | collective-permute-start | bytes 24584 | tf_op jit(solution)/shard_map/ppermute | solution.py:213
  118.9 11.1 %collective-permute-start = (bf16[2,2048]{1,0:T(2,128)(2,1)S(1)}, bf16[2,2048]{1,0:T(2,128)(2,1)S(1)}, u32[]{:S(2)}, u32[]{:S(2)}) collective-permute-start(bf16[2,2048]{1,0:T(2,128)(2,1)S(1)} %copy-done.2), channel_id=1, source_target_pairs={{0,4},{4,8},{8,12},{12,16},{16,20},{20,24},{24,28},{28,0},{1,5},{5... | collective-permute-start | bytes 24584 | tf_op jit(solution)/shard_map/ppermute | solution.py:213
  120.4 9.6 %collective-permute-start.6 = (bf16[2,2048]{1,0:T(2,128)(2,1)S(1)}, bf16[2,2048]{1,0:T(2,128)(2,1)S(1)}, u32[]{:S(2)}, u32[]{:S(2)}) collective-permute-start(bf16[2,2048]{1,0:T(2,128)(2,1)S(1)} %copy-done.2), channel_id=1, source_target_pairs={{0,28},{4,0},{8,4},{12,8},{16,12},{20,16},{24,20},{28,24},{1,29},{... | collective-permute-start | bytes 24584 | tf_op jit(solution)/shard_map/ppermute | solution.py:213
  134.5 3.1 %copy-start.3 = (f32[4]{0:T(128)S(1)}, f32[4]{0:T(128)}, u32[]{:S(2)}) copy-start(f32[4]{0:T(128)} %multiply_exponential_fusion.slopes_ref) | copy-start | bytes 52
  134.5 3.6 %copy-start.8 = (bf16[2,2048,512]{2,1,0:T(8,128)(2,1)S(1)}, bf16[2,2048,512]{2,1,0:T(8,128)(2,1)}, u32[]{:S(2)}) copy-start(bf16[2,2048,512]{2,1,0:T(8,128)(2,1)} %param.26) | copy-start | bytes 12582916
  138.1 1.9 copy-start.5
  138.1 39.9 %copy-start.1 = (bf16[256,2048]{1,0:T(8,128)(2,1)S(1)}, bf16[256,2048]{1,0:T(8,128)(2,1)}, u32[]{:S(2)}) copy-start(bf16[256,2048]{1,0:T(8,128)(2,1)} %param.15) | copy-start | bytes 3145732
  139.3 1.4 collective-permute-start.9
  139.3 3.8 %collective-permute-start.8 = (f32[2,2048]{1,0:T(2,128)S(1)}, f32[2,2048]{1,0:T(2,128)S(1)}, u32[]{:S(2)}, u32[]{:S(2)}) collective-permute-start(f32[2,2048]{1,0:T(2,128)S(1)} %fusion.26), channel_id=1, source_target_pairs={{0,2},{1,3},{2,0},{3,1},{4,6},{5,7},{6,4},{7,5},{8,10},{9,11},{10,... | collective-permute-start | bytes 49160 | tf_op jit(solution)/shard_map/ppermute | solution.py:246
  139.8 3.3 %collective-permute-start.7 = (f32[2,2048]{1,0:T(2,128)S(1)}, f32[2,2048]{1,0:T(2,128)S(1)}, u32[]{:S(2)}, u32[]{:S(2)}) collective-permute-start(f32[2,2048]{1,0:T(2,128)S(1)} %fusion.26), channel_id=1, source_target_pairs={{0,1},{1,2},{2,3},{3,0},{4,5},{5,6},{6,7},{7,4},{8,9},{9,10},{10,1... | collective-permute-start | bytes 49160 | tf_op jit(solution)/shard_map/ppermute | solution.py:246
  143.2 5.4 %collective-permute-start.16 = (bf16[2,2048]{1,0:T(2,128)(2,1)S(1)}, bf16[2,2048]{1,0:T(2,128)(2,1)S(1)}, u32[]{:S(2)}, u32[]{:S(2)}) collective-permute-start(bf16[2,2048]{1,0:T(2,128)(2,1)S(1)} %fusion.18), channel_id=1, source_target_pairs={{0,28},{4,0},{8,4},{12,8},{16,12},{20,16},{24,20},{28,24},{1,29},{... | collective-permute-start | bytes 24584 | tf_op jit(solution)/shard_map/ppermute | solution.py:255
  144.2 7.1 %collective-permute-start.15 = (bf16[2,2048]{1,0:T(2,128)(2,1)S(1)}, bf16[2,2048]{1,0:T(2,128)(2,1)S(1)}, u32[]{:S(2)}, u32[]{:S(2)}) collective-permute-start(bf16[2,2048]{1,0:T(2,128)(2,1)S(1)} %fusion.18), channel_id=1, source_target_pairs={{0,24},{4,28},{8,0},{12,4},{16,8},{20,12},{24,16},{28,20},{1,25},{... | collective-permute-start | bytes 24584 | tf_op jit(solution)/shard_map/ppermute | solution.py:255
  144.8 6.6 %collective-permute-start.14 = (bf16[2,2048]{1,0:T(2,128)(2,1)S(1)}, bf16[2,2048]{1,0:T(2,128)(2,1)S(1)}, u32[]{:S(2)}, u32[]{:S(2)}) collective-permute-start(bf16[2,2048]{1,0:T(2,128)(2,1)S(1)} %fusion.18), channel_id=1, source_target_pairs={{0,20},{4,24},{8,28},{12,0},{16,4},{20,8},{24,12},{28,16},{1,21},{... | collective-permute-start | bytes 24584 | tf_op jit(solution)/shard_map/ppermute | solution.py:255
  145.9 5.5 %collective-permute-start.13 = (bf16[2,2048]{1,0:T(2,128)(2,1)S(1)}, bf16[2,2048]{1,0:T(2,128)(2,1)S(1)}, u32[]{:S(2)}, u32[]{:S(2)}) collective-permute-start(bf16[2,2048]{1,0:T(2,128)(2,1)S(1)} %fusion.18), channel_id=1, source_target_pairs={{0,16},{4,20},{8,24},{12,28},{16,0},{20,4},{24,8},{28,12},{1,17},{... | collective-permute-start | bytes 24584 | tf_op jit(solution)/shard_map/ppermute | solution.py:255
  148.6 5.4 %collective-permute-start.12 = (bf16[2,2048]{1,0:T(2,128)(2,1)S(1)}, bf16[2,2048]{1,0:T(2,128)(2,1)S(1)}, u32[]{:S(2)}, u32[]{:S(2)}) collective-permute-start(bf16[2,2048]{1,0:T(2,128)(2,1)S(1)} %fusion.18), channel_id=1, source_target_pairs={{0,12},{4,16},{8,20},{12,24},{16,28},{20,0},{24,4},{28,8},{1,13},{... | collective-permute-start | bytes 24584 | tf_op jit(solution)/shard_map/ppermute | solution.py:255
  148.6 5.5 %collective-permute-start.11 = (bf16[2,2048]{1,0:T(2,128)(2,1)S(1)}, bf16[2,2048]{1,0:T(2,128)(2,1)S(1)}, u32[]{:S(2)}, u32[]{:S(2)}) collective-permute-start(bf16[2,2048]{1,0:T(2,128)(2,1)S(1)} %fusion.18), channel_id=1, source_target_pairs={{0,8},{4,12},{8,16},{12,20},{16,24},{20,28},{24,0},{28,4},{1,9},{5... | collective-permute-start | bytes 24584 | tf_op jit(solution)/shard_map/ppermute | solution.py:255
  151.3 6.3 %collective-permute-start.10 = (bf16[2,2048]{1,0:T(2,128)(2,1)S(1)}, bf16[2,2048]{1,0:T(2,128)(2,1)S(1)}, u32[]{:S(2)}, u32[]{:S(2)}) collective-permute-start(bf16[2,2048]{1,0:T(2,128)(2,1)S(1)} %fusion.18), channel_id=1, source_target_pairs={{0,4},{4,8},{8,12},{12,16},{16,20},{20,24},{24,28},{28,0},{1,5},{5... | collective-permute-start | bytes 24584 | tf_op jit(solution)/shard_map/ppermute | solution.py:255
Sparse Core Ops, SparseCore 0:
  14.7 37.1 all-gather.1
  86.2 44.5 reduce-scatter.2
  133.5 44.5 reduce-scatter.4

commit v6 on v4

--- a/solution.py
+++ b/solution.py
@@ -180,22 +180,7 @@
     slopes = alibi_slopes(lax.axis_index("tensor") * local_heads, local_heads, H)
     bias_sum = out_bias.astype(jnp.float32)
     normed = normalize(pre_hidden, norm_gain, norm_shift)
-    product = jnp.dot(
-        lax.all_gather(normed, "tensor", axis=0, tiled=True),
-        qkv_weight,
-        preferred_element_type=jnp.float32,
-    )
-    merged_rows = (product + qkv_bias.astype(jnp.float32)).astype(jnp.bfloat16)
-    context = prefill_attention_kernel(
-        merged_rows, pre_keys[0], pre_values[0], prefix_lengths, slopes, head_size
-    )
-    summed = lax.psum_scatter(
-        jnp.dot(context, out_weight, preferred_element_type=jnp.float32),
-        "tensor",
-        scatter_dimension=0,
-        tiled=True,
-    )
-    pre_output = (summed + bias_sum + pre_hidden.astype(jnp.float32)).astype(jnp.bfloat16)
+    gathered = lax.all_gather(normed, "tensor", axis=0, tiled=True)
     slot_count = dec_hidden.shape[0]
     dp_size = lax.axis_size("dp")
     tensor_size = lax.axis_size("tensor")
@@ -244,6 +229,39 @@
     for source in range(1, tensor_size):
         slot_summed = slot_summed + partials[(member - source) % tensor_size]
     slot_rows = (slot_summed + bias_sum + arrived.astype(jnp.float32)).astype(jnp.bfloat16)
+    tensor_size = lax.axis_size("tensor")
+    chips = tensor_size // 2
+    member = lax.axis_index("tensor")
+    chip = member // 2
+    core = member % 2
+    block = pre_hidden.shape[0]
+
+    def route(k, flip):
+        return [(i, ((i // 2 + k) % chips) * 2 + ((i % 2) ^ flip)) for i in range(tensor_size)]
+
+    gathered, slot_rows = lax.optimization_barrier((gathered, slot_rows))
+    across_chips = [lax.ppermute(out_weight, "tensor", route(k, 0)) for k in range(1, chips)]
+    product = jnp.dot(gathered, qkv_weight, preferred_element_type=jnp.float32)
+    merged_rows = (product + qkv_bias.astype(jnp.float32)).astype(jnp.bfloat16)
+    merged_rows, across_chips = lax.optimization_barrier((merged_rows, across_chips))
+    same_core = [out_weight] + list(across_chips)
+    other_core = lax.ppermute(jnp.concatenate(same_core, axis=0), "tensor", route(0, 1))
+    weight_all = jnp.concatenate(same_core + [other_core], axis=0)
+    context = prefill_attention_kernel(
+        merged_rows, pre_keys[0], pre_values[0], prefix_lengths, slopes, head_size
+    )
+    pieces = []
+    for flip in (0, 1):
+        for k in range(chips):
+            if k == 0 and flip == 0:
+                pieces.append(lax.dynamic_slice_in_dim(context, member * block, block))
+                continue
+            target = ((chip + k) % chips) * 2 + (core ^ flip)
+            outgoing = lax.dynamic_slice_in_dim(context, target * block, block)
+            pieces.append(lax.ppermute(outgoing, "tensor", route(k, flip)))
+    context_all = jnp.concatenate(pieces, axis=1)
+    summed = jnp.dot(context_all, weight_all, preferred_element_type=jnp.float32)
+    pre_output = (summed + bias_sum + pre_hidden.astype(jnp.float32)).astype(jnp.bfloat16)
     returned = [slot_rows] + [
         lax.ppermute(slot_rows, "dp", [(i, (i + k) % dp_size) for i in range(dp_size)])
         for k in range(1, dp_size)

time: 180 us -> 167 us (0.928)
  waiting for transfers between devices: 68.4 us -> 47.9 us
  starting transfers between devices: 22.2 us -> 28.7 us
    ppermute x0 -> x5, waiting for transfers between devices: none -> 37.9 us  [the longest x1 31.5 us: per_device(): lax.ppermute(out_weight, 'tensor', route(k, 0))]
    all_gather x1, waiting for transfers between devices: 36.1 us -> 2.87 us  [per_device(): gathered = lax.all_gather(normed, 'tensor', axis=0, tiled=True)]
    reduce_scatter x1 -> x0, waiting for transfers between devices: 22.5 us -> none  [per_device(): lax.psum_scatter(jnp.dot(context, out_weight, preferred_element_type=jnp....]
    concatenate x0 -> x1, other arithmetic: none -> 4.14 us  [per_device(): jnp.concatenate(same_core, axis=0)]
    convert_element_type x2 -> x1, other arithmetic: 2.88 us -> 0.01 us  [per_device(): qkv_bias.astype(jnp.float32)]
    ppermute x7, starting transfers between devices: 8.54 us -> 10.7 us  [per_device(): lax.ppermute(slot_rows, 'dp', [(i, (i + k) % dp_size) for i in range(dp_s...]
    dynamic_slice x0 -> x1, local copies, waits for them, and re-layouts: none -> 2.11 us  [per_device(): pieces.append(lax.dynamic_slice_in_dim(context, member * block, block))]
    ppermute x7, waiting for transfers between devices: 6.1 us -> 4.3 us  [per_device(): lax.ppermute(slot_rows, 'dp', [(i, (i + k) % dp_size) for i in range(dp_s...]
  transfers between devices with their start and end apart: 19 -> 23, of which waited for: 6 -> 9; matrix products, arithmetic and copies ran while one was open for 10% -> 18% of each run, Pallas kernels for 0% -> 16%
where the time goes in v6:
time: 167 us; the launch traced here: 166 us
  waiting for transfers between devices  47.9 us (29%)
  starting transfers between devices  28.7 us (17%)
  Pallas kernels  27.2 us (16%)
  matrix products  25.6 us (15%)
  between operations  14.9 us (9%)
  other arithmetic  12.7 us (8%)
  local copies, waits for them, and re-layouts  8.71 us (5%)
    ppermute x1, waiting for transfers between devices, per_device(): lax.ppermute(out_weight, 'tensor', route(k, 0))  31.5 us
    pallas_call x1, Pallas kernels, prefill_attention_kernel(): pl.pallas_call(functools.partial(_prefill_kernel, tq=tq), out_shape=jax.S...  27.2 us
    ppermute x7, starting transfers between devices, per_device(): lax.ppermute(dec_hidden, 'dp', [(i, (i + k) % dp_size) for i in range(dp_...  14.7 us
    dot_general x1, matrix products, per_device(): product = jnp.dot(gathered, qkv_weight, preferred_element_type=jnp.float32)  11.2 us
    ppermute x7, starting transfers between devices, per_device(): lax.ppermute(slot_rows, 'dp', [(i, (i + k) % dp_size) for i in range(dp_s...  10.7 us
    ppermute x3, waiting for transfers between devices, per_device(): pieces.append(lax.ppermute(outgoing, 'tensor', route(k, flip)))  6.41 us
    reshape x1, local copies, waits for them, and re-layouts, per_device(): dec_keys.reshape(slot_count, dec_cache, local_heads, head_size)  6.32 us
    dot_general x1, matrix products, per_device(): jnp.dot(context_all, weight_all, preferred_element_type=jnp.float32)  5.43 us
  transfers between devices with their start and end apart: 23, of which 9 were waited for; matrix products, arithmetic and copies ran while one was open for 18% of the time, Pallas kernels for 16%

profile of v6, /device:TPU:0, one launch (start us, length us, event | category | flops | bytes accessed | tf_op | source)
XLA Modules:
  0.0 165.8 jit_solution(14339654645349092419)
XLA Ops:
  7.2 0.0 all-gather.2.cloned.1.call-start
  7.2 1.4 convert_reduce_fusion
  8.7 1.6 fusion.21
  10.4 0.7 convert_element_type.85
  11.1 0.7 convert_element_type.86
  11.7 2.7 %fusion.24 = bf16[256,2048]{1,0:T(8,128)(2,1)} fusion(bf16[256,2048]{1,0:T(8,128)(2,1)} %param.15, f32[2048]{0:T(1024)S(1)} %convert_element_type.86, f32[2048]{0:T(1024)S(1)} %convert_element_type.85, f32[256]{0:T(256)S(1)} %add_rsqrt_fusion, f32[256]{0:T(256)S(1)} %broadcast_multiply_fusion), kind=kLoop, calls=%fused_computation.26 | loop fusion | flops 3145728 | bytes 2115584 | tf_op jit(solution)/shard_map/convert_element_type | solution.py:23
  14.4 0.0 all-gather.2.cloned.1.call-update
  14.4 5.1 %collective-permute-start.5 = (bf16[2,2048]{1,0:T(2,128)(2,1)S(1)}, bf16[2,2048]{1,0:T(2,128)(2,1)S(1)}, u32[]{:S(2)}, u32[]{:S(2)}) collective-permute-start(bf16[2,2048]{1,0:T(2,128)(2,1)S(1)} %copy-done.2), channel_id=1, source_target_pairs={{0,24},{4,28},{8,0},{12,4},{16,8},{20,12},{24,16},{28,20},{1,25},{... | collective-permute-start | bytes 24584 | tf_op jit(solution)/shard_map/ppermute | solution.py:191
  19.5 0.4 collective-permute-start.4
  19.9 3.5 %collective-permute-start.3 = (bf16[2,2048]{1,0:T(2,128)(2,1)S(1)}, bf16[2,2048]{1,0:T(2,128)(2,1)S(1)}, u32[]{:S(2)}, u32[]{:S(2)}) collective-permute-start(bf16[2,2048]{1,0:T(2,128)(2,1)S(1)} %copy-done.2), channel_id=1, source_target_pairs={{0,16},{4,20},{8,24},{12,28},{16,0},{20,4},{24,8},{28,12},{1,17},{... | collective-permute-start | bytes 24584 | tf_op jit(solution)/shard_map/ppermute | solution.py:191
  23.4 0.0 collective-permute-start.2
  23.4 1.0 collective-permute-start.1
  24.4 0.2 fusion.51
  24.6 0.1 iota_compare_fusion
  24.6 0.1 subtract_convert_fusion
  24.7 0.0 collective-permute-done.5
  24.8 1.6 collective-permute-start
  26.3 0.0 collective-permute-done.4
  26.3 3.2 %collective-permute-start.6 = (bf16[2,2048]{1,0:T(2,128)(2,1)S(1)}, bf16[2,2048]{1,0:T(2,128)(2,1)S(1)}, u32[]{:S(2)}, u32[]{:S(2)}) collective-permute-start(bf16[2,2048]{1,0:T(2,128)(2,1)S(1)} %copy-done.2), channel_id=1, source_target_pairs={{0,28},{4,0},{8,4},{12,8},{16,12},{20,16},{24,20},{28,24},{1,29},{... | collective-permute-start | bytes 24584 | tf_op jit(solution)/shard_map/ppermute | solution.py:191
  29.6 0.0 copy-start.6
  29.6 6.3 %copy.26 = bf16[2,2048,512]{1,2,0:T(8,128)(2,1)} copy(bf16[2,2048,512]{2,1,0:T(8,128)(2,1)} %param.25) | data formatting | bytes 8388608 | tf_op jit(solution)/shard_map/reshape | solution.py:215
  35.9 0.0 collective-permute-done.3
  35.9 0.0 collective-permute-done.2
  35.9 0.1 concatenate.15
  36.0 0.3 fusion.68
  36.4 0.2 multiply_reduce_fusion
  36.6 3.8 %fusion.19 = bf16[2,1536]{1,0:T(2,128)(2,1)S(1)} fusion(bf16[2048,1536]{1,0:T(8,128)(2,1)} %param.19, f32[2,2048]{1,0:T(2,128)S(1)} %get-tuple-element.22, f32[2]{0:T(128)S(1)} %add_rsqrt_fusion.1, f32[2]{0:T(128)S(1)} %broadcast_multiply_fusion.1, f32[2048]{0:T(1024)S(1)} %convert_element_type.86, f32[2048]{0:T(1024)S(1)} %convert_element_type.85, ...), kind=kOutput, calls=%fused_computation.19 | convolution fusion | flops 12609536 | bytes 6336528 | tf_op jit(solution)/shard_map/dot_general | solution.py:206
  40.4 0.0 copy-start.8
  40.4 0.1 fusion.42
  40.5 3.0 %fusion.43 = f32[2,4,1,2048]{3,2,1,0:T(1,128)S(1)} fusion(bf16[2,2048,4,128]{1,3,2,0:T(8,128)(2,1)} %bitcast.51, bf16[2,4,3,128]{3,2,1,0:T(4,128)(2,1)S(1)} %reshape.149), kind=kOutput, calls=%fused_computation.56 | convolution fusion | flops 4194304 | bytes 4263936 | tf_op jit(solution)/shard_map/vmap(hd,khd->hk)/dot_general | solution.py:140
  43.5 0.2 fusion.66
  43.7 0.2 fusion.35
  43.9 0.1 fusion.36
  44.0 0.7 fusion.6
  44.7 0.1 fusion.45
  44.8 0.4 fusion.46
  45.2 1.6 collective-permute-start.8
  46.8 0.2 collective-permute-start.7
  47.0 0.5 collective-permute-start.10
  47.4 2.0 %collective-permute-done.8 = f32[2,2048]{1,0:T(2,128)S(1)} collective-permute-done((f32[2,2048]{1,0:T(2,128)S(1)}, f32[2,2048]{1,0:T(2,128)S(1)}, u32[]{:S(2)}, u32[]{:S(2)}) %collective-permute-start.8) | collective-permute-done | bytes 16416 | tf_op jit(solution)/shard_map/ppermute | solution.py:224
  49.5 0.8 collective-permute-done.7
  50.3 2.9 %all-gather.2.cloned.1.call-done = bf16[1024,2048]{1,0:T(8,128)(2,1)} async-done(((bf16[256,2048]{1,0:T(8,128)(2,1)}), bf16[1024,2048]{1,0:T(8,128)(2,1)}) %all-gather.2.cloned.1.call-update) | async-done | bytes 4194320 | tf_op jit(solution)/shard_map/all_gather | solution.py:183
  53.2 11.2 %add_convert_fusion.q_ref.kn_ref.vn_ref = bf16[1024,1536]{1,0:T(8,128)(2,1)} fusion(bf16[1024,2048]{1,0:T(8,128)(2,1)} %all-gather.2.cloned.1.call-done, bf16[2048,1536]{1,0:T(8,128)(2,1)} %param.19, f32[1536]{0:T(1024)S(1)} %convert_element_type.91), kind=kOutput, calls=%fused_computation.6 | convolution fusion | flops 6445596672 | bytes 13637632 | tf_op jit(solution)/shard_map/dot_general | solution.py:244
  64.4 31.5 %collective-permute-done.10 = bf16[512,2048]{1,0:T(8,128)(2,1)} collective-permute-done((bf16[512,2048]{1,0:T(8,128)(2,1)S(1)}, bf16[512,2048]{1,0:T(8,128)(2,1)}, u32[]{:S(2)}, u32[]{:S(2)}) %collective-permute-start.10) | collective-permute-done | bytes 2097184 | tf_op jit(solution)/shard_map/ppermute | solution.py:243
  95.9 4.1 %pad_maximum_fusion = bf16[1024,2048]{1,0:T(8,128)(2,1)} fusion(bf16[512,2048]{1,0:T(8,128)(2,1)} %collective-permute-done.10, bf16[512,2048]{1,0:T(8,128)(2,1)S(1)} %copy-done.1), kind=kLoop, calls=%fused_computation.10 | loop fusion | flops 8388608 | bytes 8388608 | tf_op jit(solution)/shard_map/concatenate | solution.py:248
  100.0 0.0 collective-permute-start.14
  100.7 4.3 %collective-permute-start.21 = (bf16[2,2048]{1,0:T(2,128)(2,1)S(1)}, bf16[2,2048]{1,0:T(2,128)(2,1)S(1)}, u32[]{:S(2)}, u32[]{:S(2)}) collective-permute-start(bf16[2,2048]{1,0:T(2,128)(2,1)S(1)} %fusion.38), channel_id=1, source_target_pairs={{0,28},{4,0},{8,4},{12,8},{16,12},{20,16},{24,20},{28,24},{1,29},{... | collective-permute-start | bytes 24584 | tf_op jit(solution)/shard_map/ppermute | solution.py:266
  105.0 0.5 collective-permute-start.20
  105.6 2.9 %collective-permute-start.18 = (bf16[2,2048]{1,0:T(2,128)(2,1)S(1)}, bf16[2,2048]{1,0:T(2,128)(2,1)S(1)}, u32[]{:S(2)}, u32[]{:S(2)}) collective-permute-start(bf16[2,2048]{1,0:T(2,128)(2,1)S(1)} %fusion.38), channel_id=1, source_target_pairs={{0,16},{4,20},{8,24},{12,28},{16,0},{20,4},{24,8},{28,12},{1,17},{... | collective-permute-start | bytes 24584 | tf_op jit(solution)/shard_map/ppermute | solution.py:266
  108.5 27.2 %shard_map.158 = bf16[1024,512]{1,0:T(8,128)(2,1)} custom-call(s32[1]{0:T(128)S(6)} %copy.46.prefix_ref, f32[4]{0:T(128)} %copy-done.6, bf16[1024,1536]{1,0:T(8,128)(2,1)} %add_convert_fusion.q_ref.kn_ref.vn_ref, bf16[1024,1536]{1,0:T(8,128)(2,1)} %add_convert_fusion.q_ref.kn_ref.vn_ref, bf16[1024,1536]{1,0:T(8,128)(2,1)} %add_convert_fusion.q_ref.kn_ref.vn_ref, ...), custom_call_target="tpu_custom_call" | custom-call | flops 4294967296 | bytes 6291456 | tf_op jit(solution)/shard_map/pallas_call | solution.py:112
  135.7 2.0 %collective-permute-start.16 = (bf16[2,2048]{1,0:T(2,128)(2,1)S(1)}, bf16[2,2048]{1,0:T(2,128)(2,1)S(1)}, u32[]{:S(2)}, u32[]{:S(2)}) collective-permute-start(bf16[2,2048]{1,0:T(2,128)(2,1)S(1)} %fusion.38), channel_id=1, source_target_pairs={{0,8},{4,12},{8,16},{12,20},{16,24},{20,28},{24,0},{28,4},{1,9},{5... | collective-permute-start | bytes 24584 | tf_op jit(solution)/shard_map/ppermute | solution.py:266
  137.7 2.1 %constant_dynamic-slice_fusion.2 = (bf16[256,512]{1,0:T(8,128)(2,1)S(1)}, bf16[256,512]{1,0:T(8,128)(2,1)}, bf16[256,512]{1,0:T(8,128)(2,1)}, bf16[256,512]{1,0:T(8,128)(2,1)}) fusion(bf16[1024,512]{1,0:T(8,128)(2,1)} %shard_map.158, s32[]{:T(128)S(6)} %select_n.123, s32[]{:T(128)S(6)} %select_n.130, s32[]{:T(128)S(6)} %select_n.129, s32[]{:T(128)S(6)} %select_n.127), kind=kLoop, calls=%fused_computation.69 | loop fusion | bytes 2097168 | tf_op jit(solution)/shard_map/dynamic_slice | solution.py:257
  139.8 0.9 collective-permute-start.15
  140.8 0.4 collective-permute-done.17
  141.2 0.3 collective-permute-start.12
  141.4 0.7 collective-permute-done.16
  142.2 0.8 collective-permute-start.11
  142.9 0.1 fusion.55
  143.0 3.2 %collective-permute-done.15 = bf16[2,2048]{1,0:T(2,128)(2,1)S(1)} collective-permute-done((bf16[2,2048]{1,0:T(2,128)(2,1)S(1)}, bf16[2,2048]{1,0:T(2,128)(2,1)S(1)}, u32[]{:S(2)}, u32[]{:S(2)}) %collective-permute-start.15) | collective-permute-done | bytes 8224 | tf_op jit(solution)/shard_map/ppermute | solution.py:266
  146.2 0.1 concatenate.19
  146.3 0.8 convolution_convert_fusion
  147.1 2.6 %collective-permute-done.13 = bf16[256,512]{1,0:T(8,128)(2,1)} collective-permute-done((bf16[256,512]{1,0:T(8,128)(2,1)}, bf16[256,512]{1,0:T(8,128)(2,1)}, u32[]{:S(2)}, u32[]{:S(2)}) %collective-permute-start.13) | collective-permute-done | bytes 262176 | tf_op jit(solution)/shard_map/ppermute | solution.py:261
  149.7 3.8 %collective-permute-done.11 = bf16[256,512]{1,0:T(8,128)(2,1)} collective-permute-done((bf16[256,512]{1,0:T(8,128)(2,1)}, bf16[256,512]{1,0:T(8,128)(2,1)}, u32[]{:S(2)}, u32[]{:S(2)}) %collective-permute-start.11) | collective-permute-done | bytes 262176 | tf_op jit(solution)/shard_map/ppermute | solution.py:261
  153.5 5.4 %fusion.14 = bf16[256,2048]{1,0:T(8,128)(2,1)} fusion(bf16[256,2048]{1,0:T(8,128)(2,1)S(1)} %copy-done, bf16[1024,2048]{1,0:T(8,128)(2,1)} %collective-permute-done.14, bf16[512,2048]{1,0:T(8,128)(2,1)} %collective-permute-done.10, bf16[512,2048]{1,0:T(8,128)(2,1)S(1)} %copy-done.1, bf16[256,512]{1,0:T(8,128)(2,1)} %collective-permute-done.13, ...), kind=kOutput, calls=%fused_computation.15 | convolution fusion | flops 2178940928 | bytes 11542528 | tf_op jit(solution)/shard_map/dot_general | solution.py:263
  (45 shorter events, 0.2 us)
Async XLA Ops:
  7.2 7.3 %copy-start.2 = (bf16[2,2048]{1,0:T(2,128)(2,1)S(1)}, bf16[2,2048]{1,0:T(2,128)(2,1)}, u32[]{:S(2)}) copy-start(bf16[2,2048]{1,0:T(2,128)(2,1)} %param.16) | copy-start | bytes 24580
  7.2 17.2 %copy-start.7 = (s32[16]{0:T(128)S(1)}, s32[16]{0:T(128)}, u32[]{:S(2)}) copy-start(s32[16]{0:T(128)} %param.29) | copy-start | bytes 196
  7.2 17.4 %copy-start.5 = (s32[2]{0:T(128)S(1)}, s32[2]{0:T(128)}, u32[]{:S(2)}) copy-start(s32[2]{0:T(128)} %param.28) | copy-start | bytes 28
  7.2 22.4 %copy-start.3 = (bf16[1536]{0:T(1024)(128)(2,1)S(1)}, bf16[1536]{0:T(1024)(128)(2,1)}, u32[]{:S(2)}) copy-start(bf16[1536]{0:T(1024)(128)(2,1)} %param.20) | copy-start | bytes 9220
  7.2 46.0 %all-gather.2.cloned.1.call-start = ((), (), s32[]{:S(2)}) async-start(), calls=%async_computation | async-start | bytes 5242880 | tf_op jit(solution)/shard_map/all_gather | solution.py:183
  14.4 10.3 %collective-permute-start.5 = (bf16[2,2048]{1,0:T(2,128)(2,1)S(1)}, bf16[2,2048]{1,0:T(2,128)(2,1)S(1)}, u32[]{:S(2)}, u32[]{:S(2)}) collective-permute-start(bf16[2,2048]{1,0:T(2,128)(2,1)S(1)} %copy-done.2), channel_id=1, source_target_pairs={{0,24},{4,28},{8,0},{12,4},{16,8},{20,12},{24,16},{28,20},{1,25},{... | collective-permute-start | bytes 24584 | tf_op jit(solution)/shard_map/ppermute | solution.py:191
  19.5 6.8 %collective-permute-start.4 = (bf16[2,2048]{1,0:T(2,128)(2,1)S(1)}, bf16[2,2048]{1,0:T(2,128)(2,1)S(1)}, u32[]{:S(2)}, u32[]{:S(2)}) collective-permute-start(bf16[2,2048]{1,0:T(2,128)(2,1)S(1)} %copy-done.2), channel_id=1, source_target_pairs={{0,20},{4,24},{8,28},{12,0},{16,4},{20,8},{24,12},{28,16},{1,21},{... | collective-permute-start | bytes 24584 | tf_op jit(solution)/shard_map/ppermute | solution.py:191
  19.9 16.0 %collective-permute-start.3 = (bf16[2,2048]{1,0:T(2,128)(2,1)S(1)}, bf16[2,2048]{1,0:T(2,128)(2,1)S(1)}, u32[]{:S(2)}, u32[]{:S(2)}) collective-permute-start(bf16[2,2048]{1,0:T(2,128)(2,1)S(1)} %copy-done.2), channel_id=1, source_target_pairs={{0,16},{4,20},{8,24},{12,28},{16,0},{20,4},{24,8},{28,12},{1,17},{... | collective-permute-start | bytes 24584 | tf_op jit(solution)/shard_map/ppermute | solution.py:191
  23.4 12.5 %collective-permute-start.2 = (bf16[2,2048]{1,0:T(2,128)(2,1)S(1)}, bf16[2,2048]{1,0:T(2,128)(2,1)S(1)}, u32[]{:S(2)}, u32[]{:S(2)}) collective-permute-start(bf16[2,2048]{1,0:T(2,128)(2,1)S(1)} %copy-done.2), channel_id=1, source_target_pairs={{0,12},{4,16},{8,20},{12,24},{16,28},{20,0},{24,4},{28,8},{1,13},{... | collective-permute-start | bytes 24584 | tf_op jit(solution)/shard_map/ppermute | solution.py:191
  23.4 12.5 %collective-permute-start.1 = (bf16[2,2048]{1,0:T(2,128)(2,1)S(1)}, bf16[2,2048]{1,0:T(2,128)(2,1)S(1)}, u32[]{:S(2)}, u32[]{:S(2)}) collective-permute-start(bf16[2,2048]{1,0:T(2,128)(2,1)S(1)} %copy-done.2), channel_id=1, source_target_pairs={{0,8},{4,12},{8,16},{12,20},{16,24},{20,28},{24,0},{28,4},{1,9},{5... | collective-permute-start | bytes 24584 | tf_op jit(solution)/shard_map/ppermute | solution.py:191
  24.8 11.2 %collective-permute-start = (bf16[2,2048]{1,0:T(2,128)(2,1)S(1)}, bf16[2,2048]{1,0:T(2,128)(2,1)S(1)}, u32[]{:S(2)}, u32[]{:S(2)}) collective-permute-start(bf16[2,2048]{1,0:T(2,128)(2,1)S(1)} %copy-done.2), channel_id=1, source_target_pairs={{0,4},{4,8},{8,12},{12,16},{16,20},{20,24},{24,28},{28,0},{1,5},{5... | collective-permute-start | bytes 24584 | tf_op jit(solution)/shard_map/ppermute | solution.py:191
  26.3 9.6 %collective-permute-start.6 = (bf16[2,2048]{1,0:T(2,128)(2,1)S(1)}, bf16[2,2048]{1,0:T(2,128)(2,1)S(1)}, u32[]{:S(2)}, u32[]{:S(2)}) collective-permute-start(bf16[2,2048]{1,0:T(2,128)(2,1)S(1)} %copy-done.2), channel_id=1, source_target_pairs={{0,28},{4,0},{8,4},{12,8},{16,12},{20,16},{24,20},{28,24},{1,29},{... | collective-permute-start | bytes 24584 | tf_op jit(solution)/shard_map/ppermute | solution.py:191
  29.6 14.0 %copy-start.6 = (f32[4]{0:T(128)}, f32[4]{0:T(128)S(1)}, u32[]{:S(2)}) copy-start(f32[4]{0:T(128)S(1)} %multiply_exponential_fusion.slopes_ref) | copy-start | bytes 52
  40.4 3.6 %copy-start.8 = (bf16[2,2048,512]{2,1,0:T(8,128)(2,1)S(1)}, bf16[2,2048,512]{2,1,0:T(8,128)(2,1)}, u32[]{:S(2)}) copy-start(bf16[2,2048,512]{2,1,0:T(8,128)(2,1)} %param.26) | copy-start | bytes 12582916
  40.5 4.3 %copy-start.1 = (bf16[512,2048]{1,0:T(8,128)(2,1)S(1)}, bf16[512,2048]{1,0:T(8,128)(2,1)}, u32[]{:S(2)}) copy-start(bf16[512,2048]{1,0:T(8,128)(2,1)} %param.21) | copy-start | bytes 6291460
  43.5 3.9 %copy-start.4 = (bf16[2048]{0:T(1024)(128)(2,1)S(1)}, bf16[2048]{0:T(1024)(128)(2,1)}, u32[]{:S(2)}) copy-start(bf16[2048]{0:T(1024)(128)(2,1)} %param.22) | copy-start | bytes 12292
  45.2 2.3 %collective-permute-start.9 = (f32[2,2048]{1,0:T(2,128)S(1)}, f32[2,2048]{1,0:T(2,128)S(1)}, u32[]{:S(2)}, u32[]{:S(2)}) collective-permute-start(f32[2,2048]{1,0:T(2,128)S(1)} %fusion.46), channel_id=1, source_target_pairs={{0,3},{1,0},{2,1},{3,2},{4,7},{5,4},{6,5},{7,6},{8,11},{9,8},{10,9... | collective-permute-start | bytes 49160 | tf_op jit(solution)/shard_map/ppermute | solution.py:224
  45.2 4.3 %collective-permute-start.8 = (f32[2,2048]{1,0:T(2,128)S(1)}, f32[2,2048]{1,0:T(2,128)S(1)}, u32[]{:S(2)}, u32[]{:S(2)}) collective-permute-start(f32[2,2048]{1,0:T(2,128)S(1)} %fusion.46), channel_id=1, source_target_pairs={{0,2},{1,3},{2,0},{3,1},{4,6},{5,7},{6,4},{7,5},{8,10},{9,11},{10,... | collective-permute-start | bytes 49160 | tf_op jit(solution)/shard_map/ppermute | solution.py:224
  46.8 3.5 %collective-permute-start.7 = (f32[2,2048]{1,0:T(2,128)S(1)}, f32[2,2048]{1,0:T(2,128)S(1)}, u32[]{:S(2)}, u32[]{:S(2)}) collective-permute-start(f32[2,2048]{1,0:T(2,128)S(1)} %fusion.46), channel_id=1, source_target_pairs={{0,1},{1,2},{2,3},{3,0},{4,5},{5,6},{6,7},{7,4},{8,9},{9,10},{10,1... | collective-permute-start | bytes 49160 | tf_op jit(solution)/shard_map/ppermute | solution.py:224
  47.0 48.9 %collective-permute-start.10 = (bf16[512,2048]{1,0:T(8,128)(2,1)S(1)}, bf16[512,2048]{1,0:T(8,128)(2,1)}, u32[]{:S(2)}, u32[]{:S(2)}) collective-permute-start(bf16[512,2048]{1,0:T(8,128)(2,1)S(1)} %copy-done.1), channel_id=1, source_target_pairs={{0,2},{1,3},{2,0},{3,1},{4,6},{5,7},{6,4},{7,5},{8,10},{9,11},{10,... | collective-permute-start | bytes 6291464 | tf_op jit(solution)/shard_map/ppermute | solution.py:243
  100.0 53.4 %collective-permute-start.14 = (bf16[1024,2048]{1,0:T(8,128)(2,1)}, bf16[1024,2048]{1,0:T(8,128)(2,1)}, u32[]{:S(2)}, u32[]{:S(2)}) collective-permute-start(bf16[1024,2048]{1,0:T(8,128)(2,1)} %pad_maximum_fusion), channel_id=1, source_target_pairs={{0,1},{1,0},{2,3},{3,2},{4,5},{5,4},{6,7},{7,6},{8,9},{9,8},{10,11... | collective-permute-start | bytes 12582920 | tf_op jit(solution)/shard_map/ppermute | solution.py:248
  100.7 35.0 %collective-permute-start.21 = (bf16[2,2048]{1,0:T(2,128)(2,1)S(1)}, bf16[2,2048]{1,0:T(2,128)(2,1)S(1)}, u32[]{:S(2)}, u32[]{:S(2)}) collective-permute-start(bf16[2,2048]{1,0:T(2,128)(2,1)S(1)} %fusion.38), channel_id=1, source_target_pairs={{0,28},{4,0},{8,4},{12,8},{16,12},{20,16},{24,20},{28,24},{1,29},{... | collective-permute-start | bytes 24584 | tf_op jit(solution)/shard_map/ppermute | solution.py:266
  105.0 30.7 %collective-permute-start.20 = (bf16[2,2048]{1,0:T(2,128)(2,1)S(1)}, bf16[2,2048]{1,0:T(2,128)(2,1)S(1)}, u32[]{:S(2)}, u32[]{:S(2)}) collective-permute-start(bf16[2,2048]{1,0:T(2,128)(2,1)S(1)} %fusion.38), channel_id=1, source_target_pairs={{0,24},{4,28},{8,0},{12,4},{16,8},{20,12},{24,16},{28,20},{1,25},{... | collective-permute-start | bytes 24584 | tf_op jit(solution)/shard_map/ppermute | solution.py:266
  105.6 34.2 %collective-permute-start.19 = (bf16[2,2048]{1,0:T(2,128)(2,1)S(1)}, bf16[2,2048]{1,0:T(2,128)(2,1)S(1)}, u32[]{:S(2)}, u32[]{:S(2)}) collective-permute-start(bf16[2,2048]{1,0:T(2,128)(2,1)S(1)} %fusion.38), channel_id=1, source_target_pairs={{0,20},{4,24},{8,28},{12,0},{16,4},{20,8},{24,12},{28,16},{1,21},{... | collective-permute-start | bytes 24584 | tf_op jit(solution)/shard_map/ppermute | solution.py:266
  105.6 35.2 %collective-permute-start.18 = (bf16[2,2048]{1,0:T(2,128)(2,1)S(1)}, bf16[2,2048]{1,0:T(2,128)(2,1)S(1)}, u32[]{:S(2)}, u32[]{:S(2)}) collective-permute-start(bf16[2,2048]{1,0:T(2,128)(2,1)S(1)} %fusion.38), channel_id=1, source_target_pairs={{0,16},{4,20},{8,24},{12,28},{16,0},{20,4},{24,8},{28,12},{1,17},{... | collective-permute-start | bytes 24584 | tf_op jit(solution)/shard_map/ppermute | solution.py:266
  108.5 45.0 %copy-start = (bf16[256,2048]{1,0:T(8,128)(2,1)S(1)}, bf16[256,2048]{1,0:T(8,128)(2,1)}, u32[]{:S(2)}) copy-start(bf16[256,2048]{1,0:T(8,128)(2,1)} %param.15) | copy-start | bytes 3145732
  135.7 5.4 %collective-permute-start.17 = (bf16[2,2048]{1,0:T(2,128)(2,1)S(1)}, bf16[2,2048]{1,0:T(2,128)(2,1)S(1)}, u32[]{:S(2)}, u32[]{:S(2)}) collective-permute-start(bf16[2,2048]{1,0:T(2,128)(2,1)S(1)} %fusion.38), channel_id=1, source_target_pairs={{0,12},{4,16},{8,20},{12,24},{16,28},{20,0},{24,4},{28,8},{1,13},{... | collective-permute-start | bytes 24584 | tf_op jit(solution)/shard_map/ppermute | solution.py:266
  135.7 6.4 %collective-permute-start.16 = (bf16[2,2048]{1,0:T(2,128)(2,1)S(1)}, bf16[2,2048]{1,0:T(2,128)(2,1)S(1)}, u32[]{:S(2)}, u32[]{:S(2)}) collective-permute-start(bf16[2,2048]{1,0:T(2,128)(2,1)S(1)} %fusion.38), channel_id=1, source_target_pairs={{0,8},{4,12},{8,16},{12,20},{16,24},{20,28},{24,0},{28,4},{1,9},{5... | collective-permute-start | bytes 24584 | tf_op jit(solution)/shard_map/ppermute | solution.py:266
  139.8 6.3 %collective-permute-start.15 = (bf16[2,2048]{1,0:T(2,128)(2,1)S(1)}, bf16[2,2048]{1,0:T(2,128)(2,1)S(1)}, u32[]{:S(2)}, u32[]{:S(2)}) collective-permute-start(bf16[2,2048]{1,0:T(2,128)(2,1)S(1)} %fusion.38), channel_id=1, source_target_pairs={{0,4},{4,8},{8,12},{12,16},{16,20},{20,24},{24,28},{28,0},{1,5},{5... | collective-permute-start | bytes 24584 | tf_op jit(solution)/shard_map/ppermute | solution.py:266
  140.8 8.9 %collective-permute-start.13 = (bf16[256,512]{1,0:T(8,128)(2,1)}, bf16[256,512]{1,0:T(8,128)(2,1)}, u32[]{:S(2)}, u32[]{:S(2)}) collective-permute-start(bf16[256,512]{1,0:T(8,128)(2,1)} %get-tuple-element.13), channel_id=1, source_target_pairs={{0,3},{1,2},{2,1},{3,0},{4,7},{5,6},{6,5},{7,4},{8,11},{9,10},{10,... | collective-permute-start | bytes 786440 | tf_op jit(solution)/shard_map/ppermute | solution.py:261
  141.2 8.5 %collective-permute-start.12 = (bf16[256,512]{1,0:T(8,128)(2,1)}, bf16[256,512]{1,0:T(8,128)(2,1)}, u32[]{:S(2)}, u32[]{:S(2)}) collective-permute-start(bf16[256,512]{1,0:T(8,128)(2,1)} %get-tuple-element.14), channel_id=1, source_target_pairs={{0,1},{1,0},{2,3},{3,2},{4,5},{5,4},{6,7},{7,6},{8,9},{9,8},{10,11... | collective-permute-start | bytes 786440 | tf_op jit(solution)/shard_map/ppermute | solution.py:261
  142.2 11.3 %collective-permute-start.11 = (bf16[256,512]{1,0:T(8,128)(2,1)}, bf16[256,512]{1,0:T(8,128)(2,1)}, u32[]{:S(2)}, u32[]{:S(2)}) collective-permute-start(bf16[256,512]{1,0:T(8,128)(2,1)} %get-tuple-element.15), channel_id=1, source_target_pairs={{0,2},{1,3},{2,0},{3,1},{4,6},{5,7},{6,4},{7,5},{8,10},{9,11},{10,... | collective-permute-start | bytes 786440 | tf_op jit(solution)/shard_map/ppermute | solution.py:261
Sparse Core Ops, SparseCore 0:
  14.5 38.5 all-gather.1

commit v7 on v6

--- a/solution.py
+++ b/solution.py
@@ -243,13 +243,13 @@
     across_chips = [lax.ppermute(out_weight, "tensor", route(k, 0)) for k in range(1, chips)]
     product = jnp.dot(gathered, qkv_weight, preferred_element_type=jnp.float32)
     merged_rows = (product + qkv_bias.astype(jnp.float32)).astype(jnp.bfloat16)
-    merged_rows, across_chips = lax.optimization_barrier((merged_rows, across_chips))
+    context = prefill_attention_kernel(
+        merged_rows, pre_keys[0], pre_values[0], prefix_lengths, slopes, head_size
+    )
+    context, across_chips = lax.optimization_barrier((context, across_chips))
     same_core = [out_weight] + list(across_chips)
     other_core = lax.ppermute(jnp.concatenate(same_core, axis=0), "tensor", route(0, 1))
     weight_all = jnp.concatenate(same_core + [other_core], axis=0)
-    context = prefill_attention_kernel(
-        merged_rows, pre_keys[0], pre_values[0], prefix_lengths, slopes, head_size
-    )
     pieces = []
     for flip in (0, 1):
         for k in range(chips):

time: 167 us -> 139 us (0.83)
  waiting for transfers between devices: 47.9 us -> 20.3 us
    ppermute x1, waiting for transfers between devices: 31.5 us -> 4.4 us  [per_device(): lax.ppermute(out_weight, 'tensor', route(k, 0))]
  transfers between devices with their start and end apart: 23 -> 23, of which waited for: 9 -> 10; matrix products, arithmetic and copies ran while one was open for 18% -> 22% of each run, Pallas kernels for 16% -> 20%
where the time goes in v7:
time: 139 us; the launch traced here: 138 us
  starting transfers between devices  28.5 us (21%)
  Pallas kernels  27.1 us (19%)
  matrix products  25.6 us (18%)
  waiting for transfers between devices  20.3 us (15%)
  between operations  14.9 us (11%)
  other arithmetic  12.7 us (9%)
  local copies, waits for them, and re-layouts  8.7 us (6%)
    pallas_call x1, Pallas kernels, prefill_attention_kernel(): pl.pallas_call(functools.partial(_prefill_kernel, tq=tq), out_shape=jax.S...  27.1 us
    ppermute x7, starting transfers between devices, per_device(): lax.ppermute(dec_hidden, 'dp', [(i, (i + k) % dp_size) for i in range(dp_...  14.7 us
    dot_general x1, matrix products, per_device(): product = jnp.dot(gathered, qkv_weight, preferred_element_type=jnp.float32)  11.2 us
    ppermute x7, starting transfers between devices, per_device(): lax.ppermute(slot_rows, 'dp', [(i, (i + k) % dp_size) for i in range(dp_s...  10.5 us
    ppermute x3, waiting for transfers between devices, per_device(): pieces.append(lax.ppermute(outgoing, 'tensor', route(k, flip)))  6.4 us
    reshape x1, local copies, waits for them, and re-layouts, per_device(): dec_keys.reshape(slot_count, dec_cache, local_heads, head_size)  6.32 us
    dot_general x1, matrix products, per_device(): jnp.dot(context_all, weight_all, preferred_element_type=jnp.float32)  5.43 us
    ppermute x7, waiting for transfers between devices, per_device(): lax.ppermute(slot_rows, 'dp', [(i, (i + k) % dp_size) for i in range(dp_s...  4.49 us
  transfers between devices with their start and end apart: 23, of which 10 were waited for; matrix products, arithmetic and copies ran while one was open for 22% of the time, Pallas kernels for 20%

profile of v7, /device:TPU:0, one launch (start us, length us, event | category | flops | bytes accessed | tf_op | source)
XLA Modules:
  0.0 137.8 jit_solution(12797674507455378833)
XLA Ops:
  7.2 0.0 all-gather.2.cloned.1.call-start
  7.2 1.4 %convert_reduce_fusion = f32[256]{0:T(256)S(1)} fusion(bf16[256,2048]{1,0:T(8,128)(2,1)} %param.15), kind=kLoop, calls=%fused_computation.13 | loop fusion | flops 1048320 | bytes 1049600 | tf_op jit(solution)/shard_map/reduce_sum | solution.py:20
  8.7 1.6 %fusion.21 = f32[256]{0:T(256)S(1)} fusion(bf16[256,2048]{1,0:T(8,128)(2,1)} %param.15, f32[256]{0:T(256)S(1)} %broadcast_multiply_fusion), kind=kLoop, calls=%fused_computation.23 | loop fusion | flops 2096896 | bytes 1050624 | tf_op jit(solution)/shard_map/reduce_sum | solution.py:21
  10.4 0.7 convert_element_type.85
  11.1 0.7 convert_element_type.86
  11.7 2.7 %fusion.24 = bf16[256,2048]{1,0:T(8,128)(2,1)} fusion(bf16[256,2048]{1,0:T(8,128)(2,1)} %param.15, f32[2048]{0:T(1024)S(1)} %convert_element_type.86, f32[2048]{0:T(1024)S(1)} %convert_element_type.85, f32[256]{0:T(256)S(1)} %add_rsqrt_fusion, f32[256]{0:T(256)S(1)} %broadcast_multiply_fusion), kind=kLoop, calls=%fused_computation.26 | loop fusion | flops 3145728 | bytes 2115584 | tf_op jit(solution)/shard_map/convert_element_type | solution.py:23
  14.4 0.0 all-gather.2.cloned.1.call-update
  14.4 5.1 %collective-permute-start.5 = (bf16[2,2048]{1,0:T(2,128)(2,1)S(1)}, bf16[2,2048]{1,0:T(2,128)(2,1)S(1)}, u32[]{:S(2)}, u32[]{:S(2)}) collective-permute-start(bf16[2,2048]{1,0:T(2,128)(2,1)S(1)} %copy-done.2), channel_id=1, source_target_pairs={{0,24},{4,28},{8,0},{12,4},{16,8},{20,12},{24,16},{28,20},{1,25},{... | collective-permute-start | bytes 24584 | tf_op jit(solution)/shard_map/ppermute | solution.py:191
  19.5 0.4 collective-permute-start.4
  19.9 3.5 %collective-permute-start.3 = (bf16[2,2048]{1,0:T(2,128)(2,1)S(1)}, bf16[2,2048]{1,0:T(2,128)(2,1)S(1)}, u32[]{:S(2)}, u32[]{:S(2)}) collective-permute-start(bf16[2,2048]{1,0:T(2,128)(2,1)S(1)} %copy-done.2), channel_id=1, source_target_pairs={{0,16},{4,20},{8,24},{12,28},{16,0},{20,4},{24,8},{28,12},{1,17},{... | collective-permute-start | bytes 24584 | tf_op jit(solution)/shard_map/ppermute | solution.py:191
  23.4 0.0 collective-permute-start.2
  23.4 1.0 collective-permute-start.1
  24.4 0.2 fusion.51
  24.6 0.1 iota_compare_fusion
  24.6 0.1 subtract_convert_fusion
  24.7 0.0 collective-permute-done.5
  24.8 1.6 %collective-permute-start = (bf16[2,2048]{1,0:T(2,128)(2,1)S(1)}, bf16[2,2048]{1,0:T(2,128)(2,1)S(1)}, u32[]{:S(2)}, u32[]{:S(2)}) collective-permute-start(bf16[2,2048]{1,0:T(2,128)(2,1)S(1)} %copy-done.2), channel_id=1, source_target_pairs={{0,4},{4,8},{8,12},{12,16},{16,20},{20,24},{24,28},{28,0},{1,5},{5... | collective-permute-start | bytes 24584 | tf_op jit(solution)/shard_map/ppermute | solution.py:191
  26.3 0.0 collective-permute-done.4
  26.3 3.2 %collective-permute-start.6 = (bf16[2,2048]{1,0:T(2,128)(2,1)S(1)}, bf16[2,2048]{1,0:T(2,128)(2,1)S(1)}, u32[]{:S(2)}, u32[]{:S(2)}) collective-permute-start(bf16[2,2048]{1,0:T(2,128)(2,1)S(1)} %copy-done.2), channel_id=1, source_target_pairs={{0,28},{4,0},{8,4},{12,8},{16,12},{20,16},{24,20},{28,24},{1,29},{... | collective-permute-start | bytes 24584 | tf_op jit(solution)/shard_map/ppermute | solution.py:191
  29.6 0.0 copy-start.6
  29.6 6.3 %copy.26 = bf16[2,2048,512]{1,2,0:T(8,128)(2,1)} copy(bf16[2,2048,512]{2,1,0:T(8,128)(2,1)} %param.25) | data formatting | bytes 8388608 | tf_op jit(solution)/shard_map/reshape | solution.py:215
  35.9 0.0 collective-permute-done.3
  35.9 0.1 concatenate.15
  36.0 0.3 fusion.68
  36.4 0.2 multiply_reduce_fusion
  36.6 3.8 %fusion.19 = bf16[2,1536]{1,0:T(2,128)(2,1)S(1)} fusion(bf16[2048,1536]{1,0:T(8,128)(2,1)} %param.19, f32[2,2048]{1,0:T(2,128)S(1)} %get-tuple-element.22, f32[2]{0:T(128)S(1)} %add_rsqrt_fusion.1, f32[2]{0:T(128)S(1)} %broadcast_multiply_fusion.1, f32[2048]{0:T(1024)S(1)} %convert_element_type.86, f32[2048]{0:T(1024)S(1)} %convert_element_type.85, ...), kind=kOutput, calls=%fused_computation.19 | convolution fusion | flops 12609536 | bytes 6336528 | tf_op jit(solution)/shard_map/dot_general | solution.py:206
  40.4 0.0 copy-start.8
  40.4 0.1 fusion.42
  40.5 3.0 %fusion.43 = f32[2,4,1,2048]{3,2,1,0:T(1,128)S(1)} fusion(bf16[2,2048,4,128]{1,3,2,0:T(8,128)(2,1)} %bitcast.51, bf16[2,4,3,128]{3,2,1,0:T(4,128)(2,1)S(1)} %reshape.149), kind=kOutput, calls=%fused_computation.56 | convolution fusion | flops 4194304 | bytes 4263936 | tf_op jit(solution)/shard_map/vmap(hd,khd->hk)/dot_general | solution.py:140
  43.5 0.2 fusion.66
  43.7 0.2 fusion.35
  43.9 0.1 fusion.36
  44.0 0.7 fusion.6
  44.7 0.1 fusion.45
  44.8 0.4 fusion.46
  45.2 1.6 %collective-permute-start.8 = (f32[2,2048]{1,0:T(2,128)S(1)}, f32[2,2048]{1,0:T(2,128)S(1)}, u32[]{:S(2)}, u32[]{:S(2)}) collective-permute-start(f32[2,2048]{1,0:T(2,128)S(1)} %fusion.46), channel_id=1, source_target_pairs={{0,2},{1,3},{2,0},{3,1},{4,6},{5,7},{6,4},{7,5},{8,10},{9,11},{10,... | collective-permute-start | bytes 49160 | tf_op jit(solution)/shard_map/ppermute | solution.py:224
  46.8 0.2 collective-permute-start.7
  47.0 0.5 collective-permute-start.10
  48.1 1.3 collective-permute-done.8
  49.5 0.8 collective-permute-done.7
  50.3 2.9 %all-gather.2.cloned.1.call-done = bf16[1024,2048]{1,0:T(8,128)(2,1)} async-done(((bf16[256,2048]{1,0:T(8,128)(2,1)}), bf16[1024,2048]{1,0:T(8,128)(2,1)}) %all-gather.2.cloned.1.call-update) | async-done | bytes 4194320 | tf_op jit(solution)/shard_map/all_gather | solution.py:183
  53.2 11.2 %add_convert_fusion.q_ref.kn_ref.vn_ref = bf16[1024,1536]{1,0:T(8,128)(2,1)} fusion(bf16[1024,2048]{1,0:T(8,128)(2,1)} %all-gather.2.cloned.1.call-done, bf16[2048,1536]{1,0:T(8,128)(2,1)} %param.19, f32[1536]{0:T(1024)S(1)} %convert_element_type.91), kind=kOutput, calls=%fused_computation.6 | convolution fusion | flops 6445596672 | bytes 13637632 | tf_op jit(solution)/shard_map/dot_general | solution.py:244
  64.4 27.1 %shard_map.158 = bf16[1024,512]{1,0:T(8,128)(2,1)} custom-call(s32[1]{0:T(128)S(6)} %copy.46.prefix_ref, f32[4]{0:T(128)} %copy-done.6, bf16[1024,1536]{1,0:T(8,128)(2,1)} %add_convert_fusion.q_ref.kn_ref.vn_ref, bf16[1024,1536]{1,0:T(8,128)(2,1)} %add_convert_fusion.q_ref.kn_ref.vn_ref, bf16[1024,1536]{1,0:T(8,128)(2,1)} %add_convert_fusion.q_ref.kn_ref.vn_ref, ...), custom_call_target="tpu_custom_call" | custom-call | flops 4294967296 | bytes 6291456 | tf_op jit(solution)/shard_map/pallas_call | solution.py:112
  91.5 4.4 %collective-permute-done.10 = bf16[512,2048]{1,0:T(8,128)(2,1)} collective-permute-done((bf16[512,2048]{1,0:T(8,128)(2,1)S(1)}, bf16[512,2048]{1,0:T(8,128)(2,1)}, u32[]{:S(2)}, u32[]{:S(2)}) %collective-permute-start.10) | collective-permute-done | bytes 2097184 | tf_op jit(solution)/shard_map/ppermute | solution.py:243
  95.9 4.1 %pad_maximum_fusion = bf16[1024,2048]{1,0:T(8,128)(2,1)} fusion(bf16[512,2048]{1,0:T(8,128)(2,1)} %collective-permute-done.10, bf16[512,2048]{1,0:T(8,128)(2,1)S(1)} %copy-done.1), kind=kLoop, calls=%fused_computation.10 | loop fusion | flops 8388608 | bytes 8388608 | tf_op jit(solution)/shard_map/concatenate | solution.py:251
  100.0 0.0 collective-permute-start.14
  100.1 4.2 %collective-permute-start.21 = (bf16[2,2048]{1,0:T(2,128)(2,1)S(1)}, bf16[2,2048]{1,0:T(2,128)(2,1)S(1)}, u32[]{:S(2)}, u32[]{:S(2)}) collective-permute-start(bf16[2,2048]{1,0:T(2,128)(2,1)S(1)} %fusion.38), channel_id=1, source_target_pairs={{0,28},{4,0},{8,4},{12,8},{16,12},{20,16},{24,20},{28,24},{1,29},{... | collective-permute-start | bytes 24584 | tf_op jit(solution)/shard_map/ppermute | solution.py:266
  104.3 0.5 collective-permute-start.20
  104.9 2.9 %collective-permute-start.18 = (bf16[2,2048]{1,0:T(2,128)(2,1)S(1)}, bf16[2,2048]{1,0:T(2,128)(2,1)S(1)}, u32[]{:S(2)}, u32[]{:S(2)}) collective-permute-start(bf16[2,2048]{1,0:T(2,128)(2,1)S(1)} %fusion.38), channel_id=1, source_target_pairs={{0,16},{4,20},{8,24},{12,28},{16,0},{20,4},{24,8},{28,12},{1,17},{... | collective-permute-start | bytes 24584 | tf_op jit(solution)/shard_map/ppermute | solution.py:266
  107.8 0.2 collective-permute-done.20
  108.0 1.8 %collective-permute-start.16 = (bf16[2,2048]{1,0:T(2,128)(2,1)S(1)}, bf16[2,2048]{1,0:T(2,128)(2,1)S(1)}, u32[]{:S(2)}, u32[]{:S(2)}) collective-permute-start(bf16[2,2048]{1,0:T(2,128)(2,1)S(1)} %fusion.38), channel_id=1, source_target_pairs={{0,8},{4,12},{8,16},{12,20},{16,24},{20,28},{24,0},{28,4},{1,9},{5... | collective-permute-start | bytes 24584 | tf_op jit(solution)/shard_map/ppermute | solution.py:266
  109.8 2.1 %constant_dynamic-slice_fusion.2 = (bf16[256,512]{1,0:T(8,128)(2,1)S(1)}, bf16[256,512]{1,0:T(8,128)(2,1)}, bf16[256,512]{1,0:T(8,128)(2,1)}, bf16[256,512]{1,0:T(8,128)(2,1)}) fusion(bf16[1024,512]{1,0:T(8,128)(2,1)} %shard_map.158, s32[]{:T(128)S(6)} %select_n.123, s32[]{:T(128)S(6)} %select_n.130, s32[]{:T(128)S(6)} %select_n.129, s32[]{:T(128)S(6)} %select_n.127), kind=kLoop, calls=%fused_computation.69 | loop fusion | bytes 2097168 | tf_op jit(solution)/shard_map/dynamic_slice | solution.py:257
  111.9 0.9 collective-permute-start.15
  112.8 0.4 collective-permute-done.17
  113.2 0.2 collective-permute-start.12
  113.5 0.8 collective-permute-done.16
  114.2 0.7 collective-permute-start.11
  115.0 0.1 fusion.55
  115.1 3.2 %collective-permute-done.15 = bf16[2,2048]{1,0:T(2,128)(2,1)S(1)} collective-permute-done((bf16[2,2048]{1,0:T(2,128)(2,1)S(1)}, bf16[2,2048]{1,0:T(2,128)(2,1)S(1)}, u32[]{:S(2)}, u32[]{:S(2)}) %collective-permute-start.15) | collective-permute-done | bytes 8224 | tf_op jit(solution)/shard_map/ppermute | solution.py:266
  118.2 0.1 concatenate.19
  118.3 0.8 convolution_convert_fusion
  119.1 2.6 %collective-permute-done.13 = bf16[256,512]{1,0:T(8,128)(2,1)} collective-permute-done((bf16[256,512]{1,0:T(8,128)(2,1)}, bf16[256,512]{1,0:T(8,128)(2,1)}, u32[]{:S(2)}, u32[]{:S(2)}) %collective-permute-start.13) | collective-permute-done | bytes 262176 | tf_op jit(solution)/shard_map/ppermute | solution.py:261
  121.7 3.8 %collective-permute-done.11 = bf16[256,512]{1,0:T(8,128)(2,1)} collective-permute-done((bf16[256,512]{1,0:T(8,128)(2,1)}, bf16[256,512]{1,0:T(8,128)(2,1)}, u32[]{:S(2)}, u32[]{:S(2)}) %collective-permute-start.11) | collective-permute-done | bytes 262176 | tf_op jit(solution)/shard_map/ppermute | solution.py:261
  125.5 5.4 %fusion.14 = bf16[256,2048]{1,0:T(8,128)(2,1)} fusion(bf16[256,2048]{1,0:T(8,128)(2,1)S(1)} %copy-done, bf16[1024,2048]{1,0:T(8,128)(2,1)} %collective-permute-done.14, bf16[512,2048]{1,0:T(8,128)(2,1)} %collective-permute-done.10, bf16[512,2048]{1,0:T(8,128)(2,1)S(1)} %copy-done.1, bf16[256,512]{1,0:T(8,128)(2,1)} %collective-permute-done.13, ...), kind=kOutput, calls=%fused_computation.15 | convolution fusion | flops 2178940928 | bytes 11542528 | tf_op jit(solution)/shard_map/dot_general | solution.py:263
  (45 shorter events, 0.2 us)
Async XLA Ops:
  7.2 7.3 %copy-start.2 = (bf16[2,2048]{1,0:T(2,128)(2,1)S(1)}, bf16[2,2048]{1,0:T(2,128)(2,1)}, u32[]{:S(2)}) copy-start(bf16[2,2048]{1,0:T(2,128)(2,1)} %param.16) | copy-start | bytes 24580
  7.2 17.2 %copy-start.7 = (s32[16]{0:T(128)S(1)}, s32[16]{0:T(128)}, u32[]{:S(2)}) copy-start(s32[16]{0:T(128)} %param.29) | copy-start | bytes 196
  7.2 17.4 %copy-start.5 = (s32[2]{0:T(128)S(1)}, s32[2]{0:T(128)}, u32[]{:S(2)}) copy-start(s32[2]{0:T(128)} %param.28) | copy-start | bytes 28
  7.2 22.4 %copy-start.3 = (bf16[1536]{0:T(1024)(128)(2,1)S(1)}, bf16[1536]{0:T(1024)(128)(2,1)}, u32[]{:S(2)}) copy-start(bf16[1536]{0:T(1024)(128)(2,1)} %param.20) | copy-start | bytes 9220
  7.2 46.0 %all-gather.2.cloned.1.call-start = ((), (), s32[]{:S(2)}) async-start(), calls=%async_computation | async-start | bytes 5242880 | tf_op jit(solution)/shard_map/all_gather | solution.py:183
  14.4 10.3 %collective-permute-start.5 = (bf16[2,2048]{1,0:T(2,128)(2,1)S(1)}, bf16[2,2048]{1,0:T(2,128)(2,1)S(1)}, u32[]{:S(2)}, u32[]{:S(2)}) collective-permute-start(bf16[2,2048]{1,0:T(2,128)(2,1)S(1)} %copy-done.2), channel_id=1, source_target_pairs={{0,24},{4,28},{8,0},{12,4},{16,8},{20,12},{24,16},{28,20},{1,25},{... | collective-permute-start | bytes 24584 | tf_op jit(solution)/shard_map/ppermute | solution.py:191
  19.5 6.8 %collective-permute-start.4 = (bf16[2,2048]{1,0:T(2,128)(2,1)S(1)}, bf16[2,2048]{1,0:T(2,128)(2,1)S(1)}, u32[]{:S(2)}, u32[]{:S(2)}) collective-permute-start(bf16[2,2048]{1,0:T(2,128)(2,1)S(1)} %copy-done.2), channel_id=1, source_target_pairs={{0,20},{4,24},{8,28},{12,0},{16,4},{20,8},{24,12},{28,16},{1,21},{... | collective-permute-start | bytes 24584 | tf_op jit(solution)/shard_map/ppermute | solution.py:191
  19.9 16.0 %collective-permute-start.3 = (bf16[2,2048]{1,0:T(2,128)(2,1)S(1)}, bf16[2,2048]{1,0:T(2,128)(2,1)S(1)}, u32[]{:S(2)}, u32[]{:S(2)}) collective-permute-start(bf16[2,2048]{1,0:T(2,128)(2,1)S(1)} %copy-done.2), channel_id=1, source_target_pairs={{0,16},{4,20},{8,24},{12,28},{16,0},{20,4},{24,8},{28,12},{1,17},{... | collective-permute-start | bytes 24584 | tf_op jit(solution)/shard_map/ppermute | solution.py:191
  23.4 12.5 %collective-permute-start.2 = (bf16[2,2048]{1,0:T(2,128)(2,1)S(1)}, bf16[2,2048]{1,0:T(2,128)(2,1)S(1)}, u32[]{:S(2)}, u32[]{:S(2)}) collective-permute-start(bf16[2,2048]{1,0:T(2,128)(2,1)S(1)} %copy-done.2), channel_id=1, source_target_pairs={{0,12},{4,16},{8,20},{12,24},{16,28},{20,0},{24,4},{28,8},{1,13},{... | collective-permute-start | bytes 24584 | tf_op jit(solution)/shard_map/ppermute | solution.py:191
  23.4 12.5 %collective-permute-start.1 = (bf16[2,2048]{1,0:T(2,128)(2,1)S(1)}, bf16[2,2048]{1,0:T(2,128)(2,1)S(1)}, u32[]{:S(2)}, u32[]{:S(2)}) collective-permute-start(bf16[2,2048]{1,0:T(2,128)(2,1)S(1)} %copy-done.2), channel_id=1, source_target_pairs={{0,8},{4,12},{8,16},{12,20},{16,24},{20,28},{24,0},{28,4},{1,9},{5... | collective-permute-start | bytes 24584 | tf_op jit(solution)/shard_map/ppermute | solution.py:191
  24.8 11.2 %collective-permute-start = (bf16[2,2048]{1,0:T(2,128)(2,1)S(1)}, bf16[2,2048]{1,0:T(2,128)(2,1)S(1)}, u32[]{:S(2)}, u32[]{:S(2)}) collective-permute-start(bf16[2,2048]{1,0:T(2,128)(2,1)S(1)} %copy-done.2), channel_id=1, source_target_pairs={{0,4},{4,8},{8,12},{12,16},{16,20},{20,24},{24,28},{28,0},{1,5},{5... | collective-permute-start | bytes 24584 | tf_op jit(solution)/shard_map/ppermute | solution.py:191
  26.3 9.6 %collective-permute-start.6 = (bf16[2,2048]{1,0:T(2,128)(2,1)S(1)}, bf16[2,2048]{1,0:T(2,128)(2,1)S(1)}, u32[]{:S(2)}, u32[]{:S(2)}) collective-permute-start(bf16[2,2048]{1,0:T(2,128)(2,1)S(1)} %copy-done.2), channel_id=1, source_target_pairs={{0,28},{4,0},{8,4},{12,8},{16,12},{20,16},{24,20},{28,24},{1,29},{... | collective-permute-start | bytes 24584 | tf_op jit(solution)/shard_map/ppermute | solution.py:191
  29.6 14.0 %copy-start.6 = (f32[4]{0:T(128)}, f32[4]{0:T(128)S(1)}, u32[]{:S(2)}) copy-start(f32[4]{0:T(128)S(1)} %multiply_exponential_fusion.slopes_ref) | copy-start | bytes 52
  40.4 3.6 %copy-start.8 = (bf16[2,2048,512]{2,1,0:T(8,128)(2,1)S(1)}, bf16[2,2048,512]{2,1,0:T(8,128)(2,1)}, u32[]{:S(2)}) copy-start(bf16[2,2048,512]{2,1,0:T(8,128)(2,1)} %param.26) | copy-start | bytes 12582916
  40.5 4.3 %copy-start.1 = (bf16[512,2048]{1,0:T(8,128)(2,1)S(1)}, bf16[512,2048]{1,0:T(8,128)(2,1)}, u32[]{:S(2)}) copy-start(bf16[512,2048]{1,0:T(8,128)(2,1)} %param.21) | copy-start | bytes 6291460
  43.5 4.6 %copy-start.4 = (bf16[2048]{0:T(1024)(128)(2,1)S(1)}, bf16[2048]{0:T(1024)(128)(2,1)}, u32[]{:S(2)}) copy-start(bf16[2048]{0:T(1024)(128)(2,1)} %param.22) | copy-start | bytes 12292
  45.2 3.0 %collective-permute-start.9 = (f32[2,2048]{1,0:T(2,128)S(1)}, f32[2,2048]{1,0:T(2,128)S(1)}, u32[]{:S(2)}, u32[]{:S(2)}) collective-permute-start(f32[2,2048]{1,0:T(2,128)S(1)} %fusion.46), channel_id=1, source_target_pairs={{0,3},{1,0},{2,1},{3,2},{4,7},{5,4},{6,5},{7,6},{8,11},{9,8},{10,9... | collective-permute-start | bytes 49160 | tf_op jit(solution)/shard_map/ppermute | solution.py:224
  45.2 4.3 %collective-permute-start.8 = (f32[2,2048]{1,0:T(2,128)S(1)}, f32[2,2048]{1,0:T(2,128)S(1)}, u32[]{:S(2)}, u32[]{:S(2)}) collective-permute-start(f32[2,2048]{1,0:T(2,128)S(1)} %fusion.46), channel_id=1, source_target_pairs={{0,2},{1,3},{2,0},{3,1},{4,6},{5,7},{6,4},{7,5},{8,10},{9,11},{10,... | collective-permute-start | bytes 49160 | tf_op jit(solution)/shard_map/ppermute | solution.py:224
  46.8 3.5 %collective-permute-start.7 = (f32[2,2048]{1,0:T(2,128)S(1)}, f32[2,2048]{1,0:T(2,128)S(1)}, u32[]{:S(2)}, u32[]{:S(2)}) collective-permute-start(f32[2,2048]{1,0:T(2,128)S(1)} %fusion.46), channel_id=1, source_target_pairs={{0,1},{1,2},{2,3},{3,0},{4,5},{5,6},{6,7},{7,4},{8,9},{9,10},{10,1... | collective-permute-start | bytes 49160 | tf_op jit(solution)/shard_map/ppermute | solution.py:224
  47.0 48.9 %collective-permute-start.10 = (bf16[512,2048]{1,0:T(8,128)(2,1)S(1)}, bf16[512,2048]{1,0:T(8,128)(2,1)}, u32[]{:S(2)}, u32[]{:S(2)}) collective-permute-start(bf16[512,2048]{1,0:T(8,128)(2,1)S(1)} %copy-done.1), channel_id=1, source_target_pairs={{0,2},{1,3},{2,0},{3,1},{4,6},{5,7},{6,4},{7,5},{8,10},{9,11},{10,... | collective-permute-start | bytes 6291464 | tf_op jit(solution)/shard_map/ppermute | solution.py:243
  91.5 34.1 %copy-start = (bf16[256,2048]{1,0:T(8,128)(2,1)S(1)}, bf16[256,2048]{1,0:T(8,128)(2,1)}, u32[]{:S(2)}) copy-start(bf16[256,2048]{1,0:T(8,128)(2,1)} %param.15) | copy-start | bytes 3145732
  100.0 25.5 %collective-permute-start.14 = (bf16[1024,2048]{1,0:T(8,128)(2,1)}, bf16[1024,2048]{1,0:T(8,128)(2,1)}, u32[]{:S(2)}, u32[]{:S(2)}) collective-permute-start(bf16[1024,2048]{1,0:T(8,128)(2,1)} %pad_maximum_fusion), channel_id=1, source_target_pairs={{0,1},{1,0},{2,3},{3,2},{4,5},{5,4},{6,7},{7,6},{8,9},{9,8},{10,11... | collective-permute-start | bytes 12582920 | tf_op jit(solution)/shard_map/ppermute | solution.py:251
  100.1 7.7 %collective-permute-start.21 = (bf16[2,2048]{1,0:T(2,128)(2,1)S(1)}, bf16[2,2048]{1,0:T(2,128)(2,1)S(1)}, u32[]{:S(2)}, u32[]{:S(2)}) collective-permute-start(bf16[2,2048]{1,0:T(2,128)(2,1)S(1)} %fusion.38), channel_id=1, source_target_pairs={{0,28},{4,0},{8,4},{12,8},{16,12},{20,16},{24,20},{28,24},{1,29},{... | collective-permute-start | bytes 24584 | tf_op jit(solution)/shard_map/ppermute | solution.py:266
  104.3 3.7 %collective-permute-start.20 = (bf16[2,2048]{1,0:T(2,128)(2,1)S(1)}, bf16[2,2048]{1,0:T(2,128)(2,1)S(1)}, u32[]{:S(2)}, u32[]{:S(2)}) collective-permute-start(bf16[2,2048]{1,0:T(2,128)(2,1)S(1)} %fusion.38), channel_id=1, source_target_pairs={{0,24},{4,28},{8,0},{12,4},{16,8},{20,12},{24,16},{28,20},{1,25},{... | collective-permute-start | bytes 24584 | tf_op jit(solution)/shard_map/ppermute | solution.py:266
  104.8 7.0 %collective-permute-start.19 = (bf16[2,2048]{1,0:T(2,128)(2,1)S(1)}, bf16[2,2048]{1,0:T(2,128)(2,1)S(1)}, u32[]{:S(2)}, u32[]{:S(2)}) collective-permute-start(bf16[2,2048]{1,0:T(2,128)(2,1)S(1)} %fusion.38), channel_id=1, source_target_pairs={{0,20},{4,24},{8,28},{12,0},{16,4},{20,8},{24,12},{28,16},{1,21},{... | collective-permute-start | bytes 24584 | tf_op jit(solution)/shard_map/ppermute | solution.py:266
  104.9 8.0 %collective-permute-start.18 = (bf16[2,2048]{1,0:T(2,128)(2,1)S(1)}, bf16[2,2048]{1,0:T(2,128)(2,1)S(1)}, u32[]{:S(2)}, u32[]{:S(2)}) collective-permute-start(bf16[2,2048]{1,0:T(2,128)(2,1)S(1)} %fusion.38), channel_id=1, source_target_pairs={{0,16},{4,20},{8,24},{12,28},{16,0},{20,4},{24,8},{28,12},{1,17},{... | collective-permute-start | bytes 24584 | tf_op jit(solution)/shard_map/ppermute | solution.py:266
  107.8 5.4 %collective-permute-start.17 = (bf16[2,2048]{1,0:T(2,128)(2,1)S(1)}, bf16[2,2048]{1,0:T(2,128)(2,1)S(1)}, u32[]{:S(2)}, u32[]{:S(2)}) collective-permute-start(bf16[2,2048]{1,0:T(2,128)(2,1)S(1)} %fusion.38), channel_id=1, source_target_pairs={{0,12},{4,16},{8,20},{12,24},{16,28},{20,0},{24,4},{28,8},{1,13},{... | collective-permute-start | bytes 24584 | tf_op jit(solution)/shard_map/ppermute | solution.py:266
  108.0 6.3 %collective-permute-start.16 = (bf16[2,2048]{1,0:T(2,128)(2,1)S(1)}, bf16[2,2048]{1,0:T(2,128)(2,1)S(1)}, u32[]{:S(2)}, u32[]{:S(2)}) collective-permute-start(bf16[2,2048]{1,0:T(2,128)(2,1)S(1)} %fusion.38), channel_id=1, source_target_pairs={{0,8},{4,12},{8,16},{12,20},{16,24},{20,28},{24,0},{28,4},{1,9},{5... | collective-permute-start | bytes 24584 | tf_op jit(solution)/shard_map/ppermute | solution.py:266
  111.9 6.3 %collective-permute-start.15 = (bf16[2,2048]{1,0:T(2,128)(2,1)S(1)}, bf16[2,2048]{1,0:T(2,128)(2,1)S(1)}, u32[]{:S(2)}, u32[]{:S(2)}) collective-permute-start(bf16[2,2048]{1,0:T(2,128)(2,1)S(1)} %fusion.38), channel_id=1, source_target_pairs={{0,4},{4,8},{8,12},{12,16},{16,20},{20,24},{24,28},{28,0},{1,5},{5... | collective-permute-start | bytes 24584 | tf_op jit(solution)/shard_map/ppermute | solution.py:266
  112.8 8.9 %collective-permute-start.13 = (bf16[256,512]{1,0:T(8,128)(2,1)}, bf16[256,512]{1,0:T(8,128)(2,1)}, u32[]{:S(2)}, u32[]{:S(2)}) collective-permute-start(bf16[256,512]{1,0:T(8,128)(2,1)} %get-tuple-element.13), channel_id=1, source_target_pairs={{0,3},{1,2},{2,1},{3,0},{4,7},{5,6},{6,5},{7,4},{8,11},{9,10},{10,... | collective-permute-start | bytes 786440 | tf_op jit(solution)/shard_map/ppermute | solution.py:261
  113.2 8.5 %collective-permute-start.12 = (bf16[256,512]{1,0:T(8,128)(2,1)}, bf16[256,512]{1,0:T(8,128)(2,1)}, u32[]{:S(2)}, u32[]{:S(2)}) collective-permute-start(bf16[256,512]{1,0:T(8,128)(2,1)} %get-tuple-element.14), channel_id=1, source_target_pairs={{0,1},{1,0},{2,3},{3,2},{4,5},{5,4},{6,7},{7,6},{8,9},{9,8},{10,11... | collective-permute-start | bytes 786440 | tf_op jit(solution)/shard_map/ppermute | solution.py:261
  114.2 11.3 %collective-permute-start.11 = (bf16[256,512]{1,0:T(8,128)(2,1)}, bf16[256,512]{1,0:T(8,128)(2,1)}, u32[]{:S(2)}, u32[]{:S(2)}) collective-permute-start(bf16[256,512]{1,0:T(8,128)(2,1)} %get-tuple-element.15), channel_id=1, source_target_pairs={{0,2},{1,3},{2,0},{3,1},{4,6},{5,7},{6,4},{7,5},{8,10},{9,11},{10,... | collective-permute-start | bytes 786440 | tf_op jit(solution)/shard_map/ppermute | solution.py:261
Sparse Core Ops, SparseCore 0:
  14.5 38.5 all-gather.1

commit v8 on v7

--- a/solution.py
+++ b/solution.py
@@ -133,12 +133,14 @@
 
 
 def decode_attention(query_row, new_key, new_value, cache_keys, cache_values, length, slopes):
-    factor = 1.0 / math.sqrt(query_row.shape[-1])
+    heads, head_size = query_row.shape
+    factor = 1.0 / math.sqrt(head_size)
     cache_pos = jnp.arange(cache_keys.shape[0], dtype=jnp.int32)
     distance = (length - cache_pos).astype(jnp.float32)
-    cache_scores = (
-        jnp.einsum("hd,khd->hk", query_row, cache_keys, preferred_element_type=jnp.float32) * factor
-    )
+    head_of_col = jnp.arange(heads * head_size, dtype=jnp.int32) // head_size
+    own_head = head_of_col[:, None] == jnp.arange(heads, dtype=jnp.int32)[None, :]
+    block_query = jnp.where(own_head, query_row.reshape(-1)[:, None], jnp.zeros((), query_row.dtype))
+    cache_scores = jnp.dot(cache_keys, block_query, preferred_element_type=jnp.float32).T * factor
     cache_scores = cache_scores - slopes[:, None] * distance[None, :]
     cache_scores = jnp.where((cache_pos < length)[None, :], cache_scores, -jnp.inf)
     own_score = (
@@ -151,9 +153,8 @@
     denominator = jnp.sum(cache_exp, axis=-1, keepdims=True) + own_exp
     cache_probs = (cache_exp / denominator).astype(jnp.bfloat16)
     own_prob = (own_exp / denominator).astype(jnp.bfloat16)
-    context = jnp.einsum(
-        "hk,khd->hd", cache_probs, cache_values, preferred_element_type=jnp.float32
-    )
+    every_head = jnp.dot(cache_probs, cache_values, preferred_element_type=jnp.float32)
+    context = jnp.sum(jnp.where(own_head.T, every_head, 0.0), axis=0).reshape(heads, head_size)
     context = context + own_prob.astype(jnp.float32) * new_value.astype(jnp.float32)
     return context.astype(jnp.bfloat16).reshape(-1)
 
@@ -187,16 +188,18 @@
     group = lax.axis_index("dp")
     member = lax.axis_index("tensor")
     first_slot = group * slot_count
-    shifted_rows = [dec_hidden] + [
-        lax.ppermute(dec_hidden, "dp", [(i, (i + k) % dp_size) for i in range(dp_size)])
-        for k in range(1, dp_size)
-    ]
-    shifted_rows = jnp.concatenate(shifted_rows, axis=0)
+    shifted_rows = dec_hidden
+    step = 1
+    while step < dp_size:
+        shifted_rows = jnp.concatenate(
+            [shifted_rows, lax.ppermute(shifted_rows, "dp", [(i, i ^ step) for i in range(dp_size)])], axis=0
+        )
+        step *= 2
     slot_ids = first_slot + jnp.arange(slot_count, dtype=jnp.int32)
     request_ids = jnp.arange(slot_of.shape[0], dtype=jnp.int32)
     uses_slot = slot_of[None, :] == slot_ids[:, None]
     request_of_slot = jnp.sum(jnp.where(uses_slot, request_ids[None, :], 0), axis=1)
-    arrival = ((group - request_of_slot // slot_count) % dp_size) * slot_count + request_of_slot % slot_count
+    arrival = ((request_of_slot // slot_count) ^ group) * slot_count + request_of_slot % slot_count
     pick = (arrival[:, None] == jnp.arange(shifted_rows.shape[0], dtype=jnp.int32)[None, :]).astype(
         jnp.bfloat16
     )
@@ -212,22 +215,23 @@
         merged_slots[:, :, 0],
         merged_slots[:, :, 1],
         merged_slots[:, :, 2],
-        dec_keys.reshape(slot_count, dec_cache, local_heads, head_size),
-        dec_values.reshape(slot_count, dec_cache, local_heads, head_size),
+        dec_keys,
+        dec_values,
         cache_lengths,
         slopes,
     )
     slot_partial = jnp.dot(slot_context, out_weight, preferred_element_type=jnp.float32)
-    partials = jnp.stack(
-        [slot_partial]
-        + [
-            lax.ppermute(slot_partial, "tensor", [(i, (i + k) % tensor_size) for i in range(tensor_size)])
-            for k in range(1, tensor_size)
-        ]
-    )
-    slot_summed = partials[member % tensor_size]
+    partials = slot_partial
+    step = 1
+    while step < tensor_size:
+        partials = jnp.concatenate(
+            [partials, lax.ppermute(partials, "tensor", [(i, i ^ step) for i in range(tensor_size)])], axis=0
+        )
+        step *= 2
+    partials = partials.reshape(tensor_size, slot_count, -1)
+    slot_summed = partials[member ^ 0]
     for source in range(1, tensor_size):
-        slot_summed = slot_summed + partials[(member - source) % tensor_size]
+        slot_summed = slot_summed + partials[member ^ source]
     slot_rows = (slot_summed + bias_sum + arrived.astype(jnp.float32)).astype(jnp.bfloat16)
     tensor_size = lax.axis_size("tensor")
     chips = tensor_size // 2
@@ -248,8 +252,7 @@
     )
     context, across_chips = lax.optimization_barrier((context, across_chips))
     same_core = [out_weight] + list(across_chips)
-    other_core = lax.ppermute(jnp.concatenate(same_core, axis=0), "tensor", route(0, 1))
-    weight_all = jnp.concatenate(same_core + [other_core], axis=0)
+    weight_blocks = same_core + [lax.ppermute(w, "tensor", route(0, 1)) for w in same_core]
     pieces = []
     for flip in (0, 1):
         for k in range(chips):
@@ -259,16 +262,19 @@
             target = ((chip + k) % chips) * 2 + (core ^ flip)
             outgoing = lax.dynamic_slice_in_dim(context, target * block, block)
             pieces.append(lax.ppermute(outgoing, "tensor", route(k, flip)))
-    context_all = jnp.concatenate(pieces, axis=1)
-    summed = jnp.dot(context_all, weight_all, preferred_element_type=jnp.float32)
+    summed = jnp.dot(pieces[0], weight_blocks[0], preferred_element_type=jnp.float32)
+    for piece, weight in zip(pieces[1:], weight_blocks[1:]):
+        summed = summed + jnp.dot(piece, weight, preferred_element_type=jnp.float32)
     pre_output = (summed + bias_sum + pre_hidden.astype(jnp.float32)).astype(jnp.bfloat16)
-    returned = [slot_rows] + [
-        lax.ppermute(slot_rows, "dp", [(i, (i + k) % dp_size) for i in range(dp_size)])
-        for k in range(1, dp_size)
-    ]
-    returned = jnp.concatenate(returned, axis=0)
+    returned = slot_rows
+    step = 1
+    while step < dp_size:
+        returned = jnp.concatenate(
+            [returned, lax.ppermute(returned, "dp", [(i, i ^ step) for i in range(dp_size)])], axis=0
+        )
+        step *= 2
     slot_wanted = lax.dynamic_slice_in_dim(slot_of, first_slot, slot_count)
-    back = ((group - slot_wanted // slot_count) % dp_size) * slot_count + slot_wanted % slot_count
+    back = ((slot_wanted // slot_count) ^ group) * slot_count + slot_wanted % slot_count
     take = (back[:, None] == jnp.arange(returned.shape[0], dtype=jnp.int32)[None, :]).astype(jnp.bfloat16)
     dec_output = jnp.dot(take, returned, preferred_element_type=jnp.float32).astype(jnp.bfloat16)
     return (pre_output, dec_output)

time: 139 us -> 132 us (0.950)
  waiting for transfers between devices: 20.3 us -> 34.2 us
  starting transfers between devices: 28.5 us -> 15.8 us
  other arithmetic: 12.7 us -> 5.76 us
  local copies, waits for them, and re-layouts: 8.7 us -> 3.04 us
  matrix products: 25.6 us -> 30.7 us
    all_gather x1, waiting for transfers between devices: 2.87 us -> 18.5 us  [per_device(): gathered = lax.all_gather(normed, 'tensor', axis=0, tiled=True)]
    ppermute x18 -> x10, starting transfers between devices: 27 us -> 15.2 us  [the longest x3 7.33 us: per_device(): lax.ppermute(shifted_rows, 'dp', [(i, i ^ step) for i in range(dp_size)])]
    reshape x1, local copies, waits for them, and re-layouts: 6.32 us -> 0.04 us  [per_device(): partials = partials.reshape(tensor_size, slot_count, -1)]
    ppermute x18 -> x10, waiting for transfers between devices: 6.62 us -> 12.2 us  [the longest x3 4.52 us: per_device(): lax.ppermute(returned, 'dp', [(i, i ^ step) for i in range(dp_size)])]
    dot_general x3 -> x6, matrix products: 9.08 us -> 14.2 us  [the longest x3 8.12 us: per_device(): summed = summed + jnp.dot(piece, weight, preferred_element_type=jnp.float32)]
    ppermute x1, waiting for transfers between devices: 4.4 us -> 0.01 us  [per_device(): lax.ppermute(out_weight, 'tensor', route(k, 0))]
    concatenate x1 -> x6, other arithmetic: 4.14 us -> 0.16 us  [the longest x2 0.06 us: per_device(): jnp.concatenate([shifted_rows, lax.ppermute(shifted_rows, 'dp', [(i, i ^...]
    ppermute x3, waiting for transfers between devices: 6.4 us -> 3.44 us  [per_device(): pieces.append(lax.ppermute(outgoing, 'tensor', route(k, flip)))]
  transfers between devices with their start and end apart: 23 -> 15, of which waited for: 10 -> 10; matrix products, arithmetic and copies ran while one was open for 22% -> 27% of each run, Pallas kernels for 20% -> 21%
where the time goes in v8:
time: 132 us
  waiting for transfers between devices  34.2 us (26%)
  matrix products  30.7 us (23%)
  Pallas kernels  27.1 us (21%)
  starting transfers between devices  15.8 us (12%)
  between operations  15 us (11%)
  other arithmetic  5.76 us (4%)
  local copies, waits for them, and re-layouts  3.04 us (2%)
    pallas_call x1, Pallas kernels, prefill_attention_kernel(): pl.pallas_call(functools.partial(_prefill_kernel, tq=tq), out_shape=jax.S...  27.1 us
    all_gather x1, waiting for transfers between devices, per_device(): gathered = lax.all_gather(normed, 'tensor', axis=0, tiled=True)  18.5 us
    dot_general x1, matrix products, per_device(): product = jnp.dot(gathered, qkv_weight, preferred_element_type=jnp.float32)  11.2 us
    dot_general x3, matrix products, per_device(): summed = summed + jnp.dot(piece, weight, preferred_element_type=jnp.float32)  8.12 us
    ppermute x3, starting transfers between devices, per_device(): lax.ppermute(shifted_rows, 'dp', [(i, i ^ step) for i in range(dp_size)])  7.33 us
    ppermute x3, starting transfers between devices, per_device(): lax.ppermute(returned, 'dp', [(i, i ^ step) for i in range(dp_size)])  5.77 us
    ppermute x3, waiting for transfers between devices, per_device(): lax.ppermute(returned, 'dp', [(i, i ^ step) for i in range(dp_size)])  4.52 us
    ppermute x3, waiting for transfers between devices, per_device(): lax.ppermute(shifted_rows, 'dp', [(i, i ^ step) for i in range(dp_size)])  4.34 us
  transfers between devices with their start and end apart: 15, of which 10 were waited for; matrix products, arithmetic and copies ran while one was open for 27% of the time, Pallas kernels for 21%

profile of v8, /device:TPU:0, one launch (start us, length us, event | category | flops | bytes accessed | tf_op | source)
XLA Modules:
  0.0 131.6 jit_solution(3554147554683120162)
XLA Ops:
  7.2 0.0 copy-start
  7.2 0.0 all-gather.2.cloned.1.call-start
  7.2 3.0 %collective-permute-start = (bf16[2,2048]{1,0:T(2,128)(2,1)}, bf16[2,2048]{1,0:T(2,128)(2,1)S(1)}, u32[]{:S(2)}, u32[]{:S(2)}) collective-permute-start(bf16[2,2048]{1,0:T(2,128)(2,1)} %param.16), channel_id=1, source_target_pairs={{0,4},{4,0},{8,12},{12,8},{16,20},{20,16},{24,28},{28,24},{1,5},{5... | collective-permute-start | bytes 24584 | tf_op jit(solution)/shard_map/ppermute | solution.py:195
  10.3 1.4 %convert_reduce_fusion = f32[256]{0:T(256)S(1)} fusion(bf16[256,2048]{1,0:T(8,128)(2,1)} %param.15), kind=kLoop, calls=%fused_computation.3 | loop fusion | flops 1048320 | bytes 1049600 | tf_op jit(solution)/shard_map/reduce_sum | solution.py:20
  11.7 0.0 copy-start.8
  11.7 0.0 copy-start.10
  11.8 0.0 copy-start.3
  11.8 0.0 copy-start.6
  11.8 1.7 %fusion.9 = f32[256]{0:T(256)S(1)} fusion(bf16[256,2048]{1,0:T(8,128)(2,1)} %param.15, f32[256]{0:T(256)S(1)} %broadcast_multiply_fusion), kind=kLoop, calls=%fused_computation.19 | loop fusion | flops 2096896 | bytes 1050624 | tf_op jit(solution)/shard_map/reduce_sum | solution.py:21
  13.5 1.4 %fusion.12 = bf16[256,2048]{1,0:T(8,128)(2,1)} fusion(bf16[256,2048]{1,0:T(8,128)(2,1)S(1)} %copy-done, f32[2048]{0:T(1024)S(1)} %convert_element_type.88, f32[2048]{0:T(1024)S(1)} %convert_element_type.87, f32[256]{0:T(256)S(1)} %add_rsqrt_fusion, f32[256]{0:T(256)S(1)} %broadcast_multiply_fusion), kind=kLoop, calls=%fused_computation.22 | loop fusion | flops 3145728 | bytes 2115584 | tf_op jit(solution)/shard_map/convert_element_type | solution.py:23
  14.9 0.0 all-gather.2.cloned.1.call-update
  15.0 0.1 iota_compare_fusion
  15.1 0.1 subtract_convert_fusion
  15.2 0.2 fusion.53
  15.4 0.0 collective-permute-done
  15.4 1.6 %collective-permute-start.1 = (bf16[4,2048]{1,0:T(4,128)(2,1)S(1)}, bf16[4,2048]{1,0:T(4,128)(2,1)S(1)}, u32[]{:S(2)}, u32[]{:S(2)}) collective-permute-start(bf16[4,2048]{1,0:T(4,128)(2,1)S(1)} %pad_maximum_fusion.4), channel_id=1, source_target_pairs={{0,8},{4,12},{8,0},{12,4},{16,24},{20,28},{24,16},{28,20},{1,9},{5... | collective-permute-start | bytes 49160 | tf_op jit(solution)/shard_map/ppermute | solution.py:195
  17.1 2.1 %collective-permute-done.1 = bf16[4,2048]{1,0:T(4,128)(2,1)S(1)} collective-permute-done((bf16[4,2048]{1,0:T(4,128)(2,1)S(1)}, bf16[4,2048]{1,0:T(4,128)(2,1)S(1)}, u32[]{:S(2)}, u32[]{:S(2)}) %collective-permute-start.1) | collective-permute-done | bytes 16416 | tf_op jit(solution)/shard_map/ppermute | solution.py:195
  19.2 2.7 %collective-permute-start.2 = (bf16[8,2048]{1,0:T(8,128)(2,1)S(1)}, bf16[8,2048]{1,0:T(8,128)(2,1)S(1)}, u32[]{:S(2)}, u32[]{:S(2)}) collective-permute-start(bf16[8,2048]{1,0:T(8,128)(2,1)S(1)} %pad_maximum_fusion.1), channel_id=1, source_target_pairs={{0,16},{4,20},{8,24},{12,28},{16,0},{20,4},{24,8},{28,12},{1,17},{... | collective-permute-start | bytes 98312 | tf_op jit(solution)/shard_map/ppermute | solution.py:195
  21.9 0.0 copy-start.9
  21.9 2.2 %collective-permute-done.2 = bf16[8,2048]{1,0:T(8,128)(2,1)S(1)} collective-permute-done((bf16[8,2048]{1,0:T(8,128)(2,1)S(1)}, bf16[8,2048]{1,0:T(8,128)(2,1)S(1)}, u32[]{:S(2)}, u32[]{:S(2)}) %collective-permute-start.2) | collective-permute-done | bytes 32800 | tf_op jit(solution)/shard_map/ppermute | solution.py:195
  24.1 0.3 fusion.66
  24.4 0.2 multiply_reduce_fusion
  24.7 3.8 %fusion.7 = bf16[2,1536]{1,0:T(2,128)(2,1)S(1)} fusion(bf16[2048,1536]{1,0:T(8,128)(2,1)} %param.19, f32[2,2048]{1,0:T(2,128)S(1)} %get-tuple-element.19, f32[2]{0:T(128)S(1)} %add_rsqrt_fusion.1, f32[2]{0:T(128)S(1)} %broadcast_multiply_fusion.1, f32[2048]{0:T(1024)S(1)} %convert_element_type.88, f32[2048]{0:T(1024)S(1)} %convert_element_type.87, ...), kind=kOutput, calls=%fused_computation.15 | convolution fusion | flops 12609536 | bytes 6336528 | tf_op jit(solution)/shard_map/dot_general | solution.py:209
  28.5 0.1 fusion.42
  28.7 0.0 copy-start.2
  28.7 3.7 %fusion.67 = (f32[2,4]{1,0:T(2,128)S(1)}, f32[2,4,2048]{2,1,0:T(4,128)S(1)}) fusion(f32[2,2048]{1,0:T(2,128)S(1)} %subtract_convert_fusion, f32[4]{0:T(128)S(1)} %multiply_exponential_fusion.slopes_ref, bf16[2,2048,512]{2,1,0:T(8,128)(2,1)} %param.25, pred[512,4]{0,1:T(4,128)(4,1)S(1)} %iota_compare_fusion.1, bf16[2,512]{1,0:T(2,128)(2,1)S(1)} %bitcast.43, ...), kind=kOutput, calls=%fused_computation.125 | convolution fusion | flops 16863224 | bytes 4284464 | tf_op jit(solution)/shard_map/vmap()/dot_general | solution.py:143
  32.3 0.2 fusion.29
  32.6 0.1 broadcast_bitcast_fusion
  32.6 0.7 fusion.13
  33.4 0.0 copy-start.7
  33.4 0.9 copy-done.1
  34.2 0.4 fusion.47
  34.6 0.0 collective-permute-start.3
  34.6 1.2 collective-permute-done.3
  35.8 1.6 %collective-permute-start.4 = (f32[4,2048]{1,0:T(4,128)S(1)}, f32[4,2048]{1,0:T(4,128)S(1)}, u32[]{:S(2)}, u32[]{:S(2)}) collective-permute-start(f32[4,2048]{1,0:T(4,128)S(1)} %pad_maximum_fusion.2), channel_id=1, source_target_pairs={{0,2},{1,3},{2,0},{3,1},{4,6},{5,7},{6,4},{7,5},{8,10},{9,11},{10,... | collective-permute-start | bytes 98312 | tf_op jit(solution)/shard_map/ppermute | solution.py:228
  37.4 0.5 collective-permute-start.5
  38.6 2.2 %collective-permute-done.4 = f32[4,2048]{1,0:T(4,128)S(1)} collective-permute-done((f32[4,2048]{1,0:T(4,128)S(1)}, f32[4,2048]{1,0:T(4,128)S(1)}, u32[]{:S(2)}, u32[]{:S(2)}) %collective-permute-start.4) | collective-permute-done | bytes 32800 | tf_op jit(solution)/shard_map/ppermute | solution.py:228
  40.9 18.5 %all-gather.2.cloned.1.call-done = bf16[1024,2048]{1,0:T(8,128)(2,1)} async-done(((bf16[256,2048]{1,0:T(8,128)(2,1)}), bf16[1024,2048]{1,0:T(8,128)(2,1)}) %all-gather.2.cloned.1.call-update) | async-done | bytes 4194320 | tf_op jit(solution)/shard_map/all_gather | solution.py:184
  59.4 11.2 %add_convert_fusion.q_ref.kn_ref.vn_ref = bf16[1024,1536]{1,0:T(8,128)(2,1)} fusion(bf16[1024,2048]{1,0:T(8,128)(2,1)} %all-gather.2.cloned.1.call-done, bf16[2048,1536]{1,0:T(8,128)(2,1)} %param.19, f32[1536]{0:T(1024)S(1)} %convert_element_type.93), kind=kOutput, calls=%fused_computation | convolution fusion | flops 6445596672 | bytes 13637632 | tf_op jit(solution)/shard_map/dot_general | solution.py:248
  70.6 27.1 %shard_map.158 = bf16[1024,512]{1,0:T(8,128)(2,1)} custom-call(s32[1]{0:T(128)S(6)} %copy.35.prefix_ref, f32[4]{0:T(128)} %copy-done.9, bf16[1024,1536]{1,0:T(8,128)(2,1)} %add_convert_fusion.q_ref.kn_ref.vn_ref, bf16[1024,1536]{1,0:T(8,128)(2,1)} %add_convert_fusion.q_ref.kn_ref.vn_ref, bf16[1024,1536]{1,0:T(8,128)(2,1)} %add_convert_fusion.q_ref.kn_ref.vn_ref, ...), custom_call_target="tpu_custom_call" | custom-call | flops 4294967296 | bytes 6291456 | tf_op jit(solution)/shard_map/pallas_call | solution.py:112
  97.7 0.0 collective-permute-done.5
  97.7 0.2 collective-permute-start.10
  97.9 0.3 collective-permute-start.8
  98.2 2.1 %collective-permute-start.11 = (bf16[2,2048]{1,0:T(2,128)(2,1)S(1)}, bf16[2,2048]{1,0:T(2,128)(2,1)S(1)}, u32[]{:S(2)}, u32[]{:S(2)}) collective-permute-start(bf16[2,2048]{1,0:T(2,128)(2,1)S(1)} %fusion.33), channel_id=1, source_target_pairs={{0,4},{4,0},{8,12},{12,8},{16,20},{20,16},{24,28},{28,24},{1,5},{5... | collective-permute-start | bytes 24584 | tf_op jit(solution)/shard_map/ppermute | solution.py:273
  100.2 1.6 %collective-permute-done.11 = bf16[2,2048]{1,0:T(2,128)(2,1)S(1)} collective-permute-done((bf16[2,2048]{1,0:T(2,128)(2,1)S(1)}, bf16[2,2048]{1,0:T(2,128)(2,1)S(1)}, u32[]{:S(2)}, u32[]{:S(2)}) %collective-permute-start.11) | collective-permute-done | bytes 8224 | tf_op jit(solution)/shard_map/ppermute | solution.py:273
  101.9 1.4 %collective-permute-start.12 = (bf16[4,2048]{1,0:T(4,128)(2,1)S(1)}, bf16[4,2048]{1,0:T(4,128)(2,1)S(1)}, u32[]{:S(2)}, u32[]{:S(2)}) collective-permute-start(bf16[4,2048]{1,0:T(4,128)(2,1)S(1)} %pad_maximum_fusion.5), channel_id=1, source_target_pairs={{0,8},{4,12},{8,0},{12,4},{16,24},{20,28},{24,16},{28,20},{1,9},{5... | collective-permute-start | bytes 49160 | tf_op jit(solution)/shard_map/ppermute | solution.py:273
  103.3 1.9 %constant_dynamic-slice_fusion = (bf16[256,512]{1,0:T(8,128)(2,1)S(1)}, bf16[256,512]{1,0:T(8,128)(2,1)}, bf16[256,512]{1,0:T(8,128)(2,1)}) fusion(bf16[1024,512]{1,0:T(8,128)(2,1)} %shard_map.158, s32[]{:T(128)S(6)} %select_n.118, s32[]{:T(128)S(6)} %select_n.119, s32[]{:T(128)S(6)} %select_n.116), kind=kLoop, calls=%fused_computation.83 | loop fusion | bytes 1572876 | tf_op jit(solution)/shard_map/dynamic_slice | solution.py:263
  105.3 0.0 collective-permute-start.6
  105.3 0.4 collective-permute-done.12
  105.7 2.3 %collective-permute-start.13 = (bf16[8,2048]{1,0:T(8,128)(2,1)S(1)}, bf16[8,2048]{1,0:T(8,128)(2,1)S(1)}, u32[]{:S(2)}, u32[]{:S(2)}) collective-permute-start(bf16[8,2048]{1,0:T(8,128)(2,1)S(1)} %pad_maximum_fusion.3), channel_id=1, source_target_pairs={{0,16},{4,20},{8,24},{12,28},{16,0},{20,4},{24,8},{28,12},{1,17},{... | collective-permute-start | bytes 98312 | tf_op jit(solution)/shard_map/ppermute | solution.py:273
  108.0 0.1 fusion.57
  108.1 0.0 collective-permute-start.7
  108.1 2.5 %collective-permute-done.13 = bf16[8,2048]{1,0:T(8,128)(2,1)S(1)} collective-permute-done((bf16[8,2048]{1,0:T(8,128)(2,1)S(1)}, bf16[8,2048]{1,0:T(8,128)(2,1)S(1)}, u32[]{:S(2)}, u32[]{:S(2)}) %collective-permute-start.13) | collective-permute-done | bytes 32800 | tf_op jit(solution)/shard_map/ppermute | solution.py:273
  110.6 0.0 collective-permute-start.9
  110.6 0.8 convolution_convert_fusion
  111.4 1.5 %collective-permute-done.6 = bf16[256,512]{1,0:T(8,128)(2,1)} collective-permute-done((bf16[256,512]{1,0:T(8,128)(2,1)}, bf16[256,512]{1,0:T(8,128)(2,1)}, u32[]{:S(2)}, u32[]{:S(2)}) %collective-permute-start.6) | collective-permute-done | bytes 262176 | tf_op jit(solution)/shard_map/ppermute | solution.py:264
  112.9 2.4 %fusion.68 = f32[256,2048]{1,0:T(8,128)S(1)} fusion(bf16[256,512]{1,0:T(8,128)(2,1)} %collective-permute-done.6, bf16[512,2048]{1,0:T(8,128)(2,1)} %collective-permute-done.5), kind=kOutput, calls=%fused_computation.126 | convolution fusion | flops 536870912 | bytes 4456448 | tf_op jit(solution)/shard_map/dot_general | solution.py:267
  115.3 1.7 %convolution_add_fusion.1 = f32[256,2048]{1,0:T(8,128)S(1)} fusion(f32[256,2048]{1,0:T(8,128)S(1)} %fusion.68, bf16[512,2048]{1,0:T(8,128)(2,1)S(1)} %copy-done.1, bf16[1024,512]{1,0:T(8,128)(2,1)} %shard_map.158, s32[]{:T(128)S(6)} %select_n.112), kind=kOutput, calls=%fused_computation.6 | convolution fusion | flops 537395200 | bytes 6553604 | tf_op jit(solution)/shard_map/dot_general | solution.py:265
  117.0 1.9 %collective-permute-done.9 = bf16[256,512]{1,0:T(8,128)(2,1)S(1)} collective-permute-done((bf16[256,512]{1,0:T(8,128)(2,1)}, bf16[256,512]{1,0:T(8,128)(2,1)S(1)}, u32[]{:S(2)}, u32[]{:S(2)}) %collective-permute-start.9) | collective-permute-done | bytes 262176 | tf_op jit(solution)/shard_map/ppermute | solution.py:264
  119.0 0.0 collective-permute-done.10
  119.0 2.3 %fusion.69 = f32[256,2048]{1,0:T(8,128)S(1)} fusion(bf16[256,512]{1,0:T(8,128)(2,1)S(1)} %collective-permute-done.9, bf16[512,2048]{1,0:T(8,128)(2,1)} %collective-permute-done.10), kind=kOutput, calls=%fused_computation.127 | convolution fusion | flops 536870912 | bytes 4456448 | tf_op jit(solution)/shard_map/dot_general | solution.py:267
  121.3 0.0 collective-permute-done.8
  121.3 0.0 collective-permute-done.7
  121.3 3.4 %fusion.2 = bf16[256,2048]{1,0:T(8,128)(2,1)} fusion(bf16[256,2048]{1,0:T(8,128)(2,1)S(1)} %copy-done, f32[256,2048]{1,0:T(8,128)S(1)} %fusion.69, f32[256,2048]{1,0:T(8,128)S(1)} %convolution_add_fusion.1, bf16[256,512]{1,0:T(8,128)(2,1)S(1)} %collective-permute-done.7, bf16[512,2048]{1,0:T(8,128)(2,1)} %collective-permute-done.8, ...), kind=kOutput, calls=%fused_computation.8 | convolution fusion | flops 540016640 | bytes 8658944 | tf_op jit(solution)/shard_map/dot_general | solution.py:267
  (41 shorter events, 0.4 us)
Async XLA Ops:
  7.2 6.3 %copy-start = (bf16[256,2048]{1,0:T(8,128)(2,1)S(1)}, bf16[256,2048]{1,0:T(8,128)(2,1)}, u32[]{:S(2)}) copy-start(bf16[256,2048]{1,0:T(8,128)(2,1)} %param.15) | copy-start | bytes 3145732
  7.2 6.3 %copy-start.4 = (bf16[2048]{0:T(1024)(128)(2,1)S(1)}, bf16[2048]{0:T(1024)(128)(2,1)}, u32[]{:S(2)}) copy-start(bf16[2048]{0:T(1024)(128)(2,1)} %param.17) | copy-start | bytes 12292
  7.2 6.3 %copy-start.5 = (bf16[2048]{0:T(1024)(128)(2,1)S(1)}, bf16[2048]{0:T(1024)(128)(2,1)}, u32[]{:S(2)}) copy-start(bf16[2048]{0:T(1024)(128)(2,1)} %param.18) | copy-start | bytes 12292
  7.2 52.2 %all-gather.2.cloned.1.call-start = ((), (), s32[]{:S(2)}) async-start(), calls=%async_computation | async-start | bytes 5242880 | tf_op jit(solution)/shard_map/all_gather | solution.py:184
  7.2 8.1 %collective-permute-start = (bf16[2,2048]{1,0:T(2,128)(2,1)}, bf16[2,2048]{1,0:T(2,128)(2,1)S(1)}, u32[]{:S(2)}, u32[]{:S(2)}) collective-permute-start(bf16[2,2048]{1,0:T(2,128)(2,1)} %param.16), channel_id=1, source_target_pairs={{0,4},{4,0},{8,12},{12,8},{16,20},{20,16},{24,28},{28,24},{1,5},{5... | collective-permute-start | bytes 24584 | tf_op jit(solution)/shard_map/ppermute | solution.py:195
  11.7 3.3 %copy-start.8 = (s32[2]{0:T(128)S(1)}, s32[2]{0:T(128)}, u32[]{:S(2)}) copy-start(s32[2]{0:T(128)} %param.28) | copy-start | bytes 28
  11.7 3.4 %copy-start.10 = (s32[16]{0:T(128)S(1)}, s32[16]{0:T(128)}, u32[]{:S(2)}) copy-start(s32[16]{0:T(128)} %param.29) | copy-start | bytes 196
  11.8 3.6 %copy-start.3 = (bf16[2,2048]{1,0:T(2,128)(2,1)S(1)}, bf16[2,2048]{1,0:T(2,128)(2,1)}, u32[]{:S(2)}) copy-start(bf16[2,2048]{1,0:T(2,128)(2,1)} %param.16) | copy-start | bytes 24580
  11.8 10.1 %copy-start.6 = (bf16[1536]{0:T(1024)(128)(2,1)S(1)}, bf16[1536]{0:T(1024)(128)(2,1)}, u32[]{:S(2)}) copy-start(bf16[1536]{0:T(1024)(128)(2,1)} %param.20) | copy-start | bytes 9220
  15.4 3.8 %collective-permute-start.1 = (bf16[4,2048]{1,0:T(4,128)(2,1)S(1)}, bf16[4,2048]{1,0:T(4,128)(2,1)S(1)}, u32[]{:S(2)}, u32[]{:S(2)}) collective-permute-start(bf16[4,2048]{1,0:T(4,128)(2,1)S(1)} %pad_maximum_fusion.4), channel_id=1, source_target_pairs={{0,8},{4,12},{8,0},{12,4},{16,24},{20,28},{24,16},{28,20},{1,9},{5... | collective-permute-start | bytes 49160 | tf_op jit(solution)/shard_map/ppermute | solution.py:195
  19.2 4.9 %collective-permute-start.2 = (bf16[8,2048]{1,0:T(8,128)(2,1)S(1)}, bf16[8,2048]{1,0:T(8,128)(2,1)S(1)}, u32[]{:S(2)}, u32[]{:S(2)}) collective-permute-start(bf16[8,2048]{1,0:T(8,128)(2,1)S(1)} %pad_maximum_fusion.1), channel_id=1, source_target_pairs={{0,16},{4,20},{8,24},{12,28},{16,0},{20,4},{24,8},{28,12},{1,17},{... | collective-permute-start | bytes 98312 | tf_op jit(solution)/shard_map/ppermute | solution.py:195
  21.9 6.7 %copy-start.9 = (f32[4]{0:T(128)}, f32[4]{0:T(128)S(1)}, u32[]{:S(2)}) copy-start(f32[4]{0:T(128)S(1)} %multiply_exponential_fusion.slopes_ref) | copy-start | bytes 52
  28.7 4.0 %copy-start.2 = (bf16[2,2048,512]{2,1,0:T(8,128)(2,1)S(1)}, bf16[2,2048,512]{2,1,0:T(8,128)(2,1)}, u32[]{:S(2)}) copy-start(bf16[2,2048,512]{2,1,0:T(8,128)(2,1)} %param.26) | copy-start | bytes 12582916
  32.6 1.6 %copy-start.1 = (bf16[512,2048]{1,0:T(8,128)(2,1)S(1)}, bf16[512,2048]{1,0:T(8,128)(2,1)}, u32[]{:S(2)}) copy-start(bf16[512,2048]{1,0:T(8,128)(2,1)} %param.21) | copy-start | bytes 6291460
  33.4 5.2 %copy-start.7 = (bf16[2048]{0:T(1024)(128)(2,1)S(1)}, bf16[2048]{0:T(1024)(128)(2,1)}, u32[]{:S(2)}) copy-start(bf16[2048]{0:T(1024)(128)(2,1)} %param.22) | copy-start | bytes 12292
  34.6 1.2 collective-permute-start.3
  35.8 5.0 %collective-permute-start.4 = (f32[4,2048]{1,0:T(4,128)S(1)}, f32[4,2048]{1,0:T(4,128)S(1)}, u32[]{:S(2)}, u32[]{:S(2)}) collective-permute-start(f32[4,2048]{1,0:T(4,128)S(1)} %pad_maximum_fusion.2), channel_id=1, source_target_pairs={{0,2},{1,3},{2,0},{3,1},{4,6},{5,7},{6,4},{7,5},{8,10},{9,11},{10,... | collective-permute-start | bytes 98312 | tf_op jit(solution)/shard_map/ppermute | solution.py:228
  37.4 60.2 %collective-permute-start.5 = (bf16[512,2048]{1,0:T(8,128)(2,1)S(1)}, bf16[512,2048]{1,0:T(8,128)(2,1)}, u32[]{:S(2)}, u32[]{:S(2)}) collective-permute-start(bf16[512,2048]{1,0:T(8,128)(2,1)S(1)} %copy-done.1), channel_id=1, source_target_pairs={{0,2},{1,3},{2,0},{3,1},{4,6},{5,7},{6,4},{7,5},{8,10},{9,11},{10,... | collective-permute-start | bytes 6291464 | tf_op jit(solution)/shard_map/ppermute | solution.py:247
  97.7 21.3 %collective-permute-start.10 = (bf16[512,2048]{1,0:T(8,128)(2,1)}, bf16[512,2048]{1,0:T(8,128)(2,1)}, u32[]{:S(2)}, u32[]{:S(2)}) collective-permute-start(bf16[512,2048]{1,0:T(8,128)(2,1)} %collective-permute-done.5), channel_id=1, source_target_pairs={{0,1},{1,0},{2,3},{3,2},{4,5},{5,4},{6,7},{7,6},{8,9},{9,8},{10,11... | collective-permute-start | bytes 6291464 | tf_op jit(solution)/shard_map/ppermute | solution.py:255
  97.9 23.4 %collective-permute-start.8 = (bf16[512,2048]{1,0:T(8,128)(2,1)S(1)}, bf16[512,2048]{1,0:T(8,128)(2,1)}, u32[]{:S(2)}, u32[]{:S(2)}) collective-permute-start(bf16[512,2048]{1,0:T(8,128)(2,1)S(1)} %copy-done.1), channel_id=1, source_target_pairs={{0,1},{1,0},{2,3},{3,2},{4,5},{5,4},{6,7},{7,6},{8,9},{9,8},{10,11... | collective-permute-start | bytes 6291464 | tf_op jit(solution)/shard_map/ppermute | solution.py:255
  98.2 3.7 %collective-permute-start.11 = (bf16[2,2048]{1,0:T(2,128)(2,1)S(1)}, bf16[2,2048]{1,0:T(2,128)(2,1)S(1)}, u32[]{:S(2)}, u32[]{:S(2)}) collective-permute-start(bf16[2,2048]{1,0:T(2,128)(2,1)S(1)} %fusion.33), channel_id=1, source_target_pairs={{0,4},{4,0},{8,12},{12,8},{16,20},{20,16},{24,28},{28,24},{1,5},{5... | collective-permute-start | bytes 24584 | tf_op jit(solution)/shard_map/ppermute | solution.py:273
  101.9 3.8 %collective-permute-start.12 = (bf16[4,2048]{1,0:T(4,128)(2,1)S(1)}, bf16[4,2048]{1,0:T(4,128)(2,1)S(1)}, u32[]{:S(2)}, u32[]{:S(2)}) collective-permute-start(bf16[4,2048]{1,0:T(4,128)(2,1)S(1)} %pad_maximum_fusion.5), channel_id=1, source_target_pairs={{0,8},{4,12},{8,0},{12,4},{16,24},{20,28},{24,16},{28,20},{1,9},{5... | collective-permute-start | bytes 49160 | tf_op jit(solution)/shard_map/ppermute | solution.py:273
  105.3 7.6 %collective-permute-start.6 = (bf16[256,512]{1,0:T(8,128)(2,1)}, bf16[256,512]{1,0:T(8,128)(2,1)}, u32[]{:S(2)}, u32[]{:S(2)}) collective-permute-start(bf16[256,512]{1,0:T(8,128)(2,1)} %get-tuple-element.12), channel_id=1, source_target_pairs={{0,2},{1,3},{2,0},{3,1},{4,6},{5,7},{6,4},{7,5},{8,10},{9,11},{10,... | collective-permute-start | bytes 786440 | tf_op jit(solution)/shard_map/ppermute | solution.py:264
  105.7 4.9 %collective-permute-start.13 = (bf16[8,2048]{1,0:T(8,128)(2,1)S(1)}, bf16[8,2048]{1,0:T(8,128)(2,1)S(1)}, u32[]{:S(2)}, u32[]{:S(2)}) collective-permute-start(bf16[8,2048]{1,0:T(8,128)(2,1)S(1)} %pad_maximum_fusion.3), channel_id=1, source_target_pairs={{0,16},{4,20},{8,24},{12,28},{16,0},{20,4},{24,8},{28,12},{1,17},{... | collective-permute-start | bytes 98312 | tf_op jit(solution)/shard_map/ppermute | solution.py:273
  108.1 13.3 %collective-permute-start.7 = (bf16[256,512]{1,0:T(8,128)(2,1)S(1)}, bf16[256,512]{1,0:T(8,128)(2,1)S(1)}, u32[]{:S(2)}, u32[]{:S(2)}) collective-permute-start(bf16[256,512]{1,0:T(8,128)(2,1)S(1)} %get-tuple-element.10), channel_id=1, source_target_pairs={{0,1},{1,0},{2,3},{3,2},{4,5},{5,4},{6,7},{7,6},{8,9},{9,8},{10,11... | collective-permute-start | bytes 786440 | tf_op jit(solution)/shard_map/ppermute | solution.py:264
  110.6 8.4 %collective-permute-start.9 = (bf16[256,512]{1,0:T(8,128)(2,1)}, bf16[256,512]{1,0:T(8,128)(2,1)S(1)}, u32[]{:S(2)}, u32[]{:S(2)}) collective-permute-start(bf16[256,512]{1,0:T(8,128)(2,1)} %get-tuple-element.11), channel_id=1, source_target_pairs={{0,3},{1,2},{2,1},{3,0},{4,7},{5,6},{6,5},{7,4},{8,11},{9,10},{10,... | collective-permute-start | bytes 786440 | tf_op jit(solution)/shard_map/ppermute | solution.py:264
Sparse Core Ops, SparseCore 0:
  15.1 44.2 all-gather.1

commit v9 on v8

--- a/solution.py
+++ b/solution.py
@@ -181,7 +181,6 @@
     slopes = alibi_slopes(lax.axis_index("tensor") * local_heads, local_heads, H)
     bias_sum = out_bias.astype(jnp.float32)
     normed = normalize(pre_hidden, norm_gain, norm_shift)
-    gathered = lax.all_gather(normed, "tensor", axis=0, tiled=True)
     slot_count = dec_hidden.shape[0]
     dp_size = lax.axis_size("dp")
     tensor_size = lax.axis_size("tensor")
@@ -243,10 +242,21 @@
     def route(k, flip):
         return [(i, ((i // 2 + k) % chips) * 2 + ((i % 2) ^ flip)) for i in range(tensor_size)]
 
-    gathered, slot_rows = lax.optimization_barrier((gathered, slot_rows))
-    across_chips = [lax.ppermute(out_weight, "tensor", route(k, 0)) for k in range(1, chips)]
-    product = jnp.dot(gathered, qkv_weight, preferred_element_type=jnp.float32)
-    merged_rows = (product + qkv_bias.astype(jnp.float32)).astype(jnp.bfloat16)
+    across_tokens = [lax.ppermute(normed, "tensor", route(k, 0)) for k in range(1, chips)]
+    across_tokens, held_weight = lax.optimization_barrier((across_tokens, out_weight))
+    same_core_tokens = [normed] + list(across_tokens)
+    sibling_tokens = [lax.ppermute(t, "tensor", route(0, 1)) for t in same_core_tokens]
+    sibling_tokens, slot_rows = lax.optimization_barrier((sibling_tokens, slot_rows))
+    across_chips = [lax.ppermute(held_weight, "tensor", route(k, 0)) for k in range(1, chips)]
+    bias_row = qkv_bias.astype(jnp.float32)
+    merged_rows = jnp.zeros((tensor_size * block, qkv_weight.shape[1]), jnp.bfloat16)
+    for flip, token_blocks in ((0, same_core_tokens), (1, sibling_tokens)):
+        for k, token_block in enumerate(token_blocks):
+            source = ((chip - k) % chips) * 2 + (core ^ flip)
+            projected = (
+                jnp.dot(token_block, qkv_weight, preferred_element_type=jnp.float32) + bias_row
+            ).astype(jnp.bfloat16)
+            merged_rows = lax.dynamic_update_slice_in_dim(merged_rows, projected, source * block, 0)
     context = prefill_attention_kernel(
         merged_rows, pre_keys[0], pre_values[0], prefix_lengths, slopes, head_size
     )

time: 132 us -> 135 us (1.023)
  between operations: 15 us -> 1.67 us
  matrix products: 30.7 us -> 37.8 us
  waiting for transfers between devices: 34.2 us -> 37 us
  starting transfers between devices: 15.8 us -> 18.4 us
  local copies, waits for them, and re-layouts: 3.04 us -> 5.02 us
    all_gather x1 -> x0, waiting for transfers between devices: 18.5 us -> none  [per_device(): gathered = lax.all_gather(normed, 'tensor', axis=0, tiled=True)]
    ppermute x2, waiting for transfers between devices: 3.35 us -> 15.8 us  [per_device(): lax.ppermute(partials, 'tensor', [(i, i ^ step) for i in range(tensor_siz...]
    dot_general x1 -> x4, matrix products: 11.2 us -> 18.4 us  [per_device(): jnp.dot(token_block, qkv_weight, preferred_element_type=jnp.float32)]
    ppermute x1 -> x4, waiting for transfers between devices: 0.01 us -> 6.73 us  [the longest x1 6.72 us: per_device(): lax.ppermute(held_weight, 'tensor', route(k, 0))]
    ppermute x1 -> x4, starting transfers between devices: 0.48 us -> 3.23 us  [the longest x1 1.56 us: per_device(): lax.ppermute(held_weight, 'tensor', route(k, 0))]
    ppermute x3, starting transfers between devices: 0.05 us -> 2.14 us  [per_device(): pieces.append(lax.ppermute(outgoing, 'tensor', route(k, flip)))]
    broadcast_in_dim x0 -> x1, local copies, waits for them, and re-layouts: none -> 1.85 us  [per_device(): jnp.zeros((tensor_size * block, qkv_weight.shape[1]), jnp.bfloat16)]
  transfers between devices with their start and end apart: 15 -> 17, of which waited for: 10 -> 7; matrix products, arithmetic and copies ran while one was open for 27% -> 27% of each run, Pallas kernels for 21% -> 20%
where the time goes in v9:
time: 135 us; the launch traced here: 134 us
  matrix products  37.8 us (28%)
  waiting for transfers between devices  37 us (27%)
  Pallas kernels  27.2 us (20%)
  starting transfers between devices  18.4 us (14%)
  other arithmetic  7.05 us (5%)
  local copies, waits for them, and re-layouts  5.02 us (4%)
  between operations  1.67 us (1%)
    pallas_call x1, Pallas kernels, prefill_attention_kernel(): pl.pallas_call(functools.partial(_prefill_kernel, tq=tq), out_shape=jax.S...  27.2 us
    dot_general x4, matrix products, per_device(): jnp.dot(token_block, qkv_weight, preferred_element_type=jnp.float32)  18.4 us
    ppermute x2, waiting for transfers between devices, per_device(): lax.ppermute(partials, 'tensor', [(i, i ^ step) for i in range(tensor_siz...  15.8 us
    dot_general x3, matrix products, per_device(): summed = summed + jnp.dot(piece, weight, preferred_element_type=jnp.float32)  8.12 us
    ppermute x3, starting transfers between devices, per_device(): lax.ppermute(shifted_rows, 'dp', [(i, i ^ step) for i in range(dp_size)])  7.33 us
    ppermute x1, waiting for transfers between devices, per_device(): lax.ppermute(held_weight, 'tensor', route(k, 0))  6.72 us
    ppermute x3, waiting for transfers between devices, per_device(): lax.ppermute(returned, 'dp', [(i, i ^ step) for i in range(dp_size)])  5.56 us
    ppermute x3, waiting for transfers between devices, per_device(): pieces.append(lax.ppermute(outgoing, 'tensor', route(k, flip)))  4.67 us
  transfers between devices with their start and end apart: 17, of which 7 were waited for; matrix products, arithmetic and copies ran while one was open for 27% of the time, Pallas kernels for 20%

profile of v9, /device:TPU:0, one launch (start us, length us, event | category | flops | bytes accessed | tf_op | source)
XLA Modules:
  0.0 134.2 jit_solution(4696557662931402953)
XLA Ops:
  0.7 3.0 %collective-permute-start.3 = (bf16[2,2048]{1,0:T(2,128)(2,1)}, bf16[2,2048]{1,0:T(2,128)(2,1)S(1)}, u32[]{:S(2)}, u32[]{:S(2)}) collective-permute-start(bf16[2,2048]{1,0:T(2,128)(2,1)} %param.16), channel_id=1, source_target_pairs={{0,4},{4,0},{8,12},{12,8},{16,20},{20,16},{24,28},{28,24},{1,5},{5... | collective-permute-start | bytes 24584 | tf_op jit(solution)/shard_map/ppermute | solution.py:194
  3.7 0.7 subtract_convert_fusion
  4.4 0.7 iota_compare_fusion
  5.2 1.4 %convert_reduce_fusion = f32[256]{0:T(256)S(1)} fusion(bf16[256,2048]{1,0:T(8,128)(2,1)} %param.15), kind=kLoop, calls=%fused_computation.2 | loop fusion | flops 1048320 | bytes 1049600 | tf_op jit(solution)/shard_map/reduce_sum | solution.py:20
  6.7 1.6 %fusion.17 = f32[256]{0:T(256)S(1)} fusion(bf16[256,2048]{1,0:T(8,128)(2,1)} %param.15, f32[256]{0:T(256)S(1)} %broadcast_multiply_fusion), kind=kLoop, calls=%fused_computation.30 | loop fusion | flops 2096896 | bytes 1050624 | tf_op jit(solution)/shard_map/reduce_sum | solution.py:21
  8.3 0.2 fusion.61
  8.6 1.6 %collective-permute-start.4 = (bf16[4,2048]{1,0:T(4,128)(2,1)S(1)}, bf16[4,2048]{1,0:T(4,128)(2,1)S(1)}, u32[]{:S(2)}, u32[]{:S(2)}) collective-permute-start(bf16[4,2048]{1,0:T(4,128)(2,1)S(1)} %pad_maximum_fusion.4), channel_id=1, source_target_pairs={{0,8},{4,12},{8,0},{12,4},{16,24},{20,28},{24,16},{28,20},{1,9},{5... | collective-permute-start | bytes 49160 | tf_op jit(solution)/shard_map/ppermute | solution.py:194
  10.2 2.1 %collective-permute-done.4 = bf16[4,2048]{1,0:T(4,128)(2,1)S(1)} collective-permute-done((bf16[4,2048]{1,0:T(4,128)(2,1)S(1)}, bf16[4,2048]{1,0:T(4,128)(2,1)S(1)}, u32[]{:S(2)}, u32[]{:S(2)}) %collective-permute-start.4) | collective-permute-done | bytes 16416 | tf_op jit(solution)/shard_map/ppermute | solution.py:194
  12.4 2.7 %collective-permute-start.5 = (bf16[8,2048]{1,0:T(8,128)(2,1)S(1)}, bf16[8,2048]{1,0:T(8,128)(2,1)S(1)}, u32[]{:S(2)}, u32[]{:S(2)}) collective-permute-start(bf16[8,2048]{1,0:T(8,128)(2,1)S(1)} %pad_maximum_fusion.1), channel_id=1, source_target_pairs={{0,16},{4,20},{8,24},{12,28},{16,0},{20,4},{24,8},{28,12},{1,17},{... | collective-permute-start | bytes 98312 | tf_op jit(solution)/shard_map/ppermute | solution.py:194
  15.1 0.0 copy-start.8
  15.1 2.1 %collective-permute-done.5 = bf16[8,2048]{1,0:T(8,128)(2,1)S(1)} collective-permute-done((bf16[8,2048]{1,0:T(8,128)(2,1)S(1)}, bf16[8,2048]{1,0:T(8,128)(2,1)S(1)}, u32[]{:S(2)}, u32[]{:S(2)}) %collective-permute-start.5) | collective-permute-done | bytes 32800 | tf_op jit(solution)/shard_map/ppermute | solution.py:194
  17.3 0.3 fusion.74
  17.6 0.2 multiply_reduce_fusion
  17.8 3.8 %fusion.15 = bf16[2,1536]{1,0:T(2,128)(2,1)S(1)} fusion(bf16[2048,1536]{1,0:T(8,128)(2,1)} %param.19, f32[2,2048]{1,0:T(2,128)S(1)} %get-tuple-element.25, f32[2]{0:T(128)S(1)} %add_rsqrt_fusion.1, f32[2]{0:T(128)S(1)} %broadcast_multiply_fusion.1, f32[2048]{0:T(1024)S(1)} %convert_element_type.97, f32[2048]{0:T(1024)S(1)} %convert_element_type.96, ...), kind=kOutput, calls=%fused_computation.26 | convolution fusion | flops 12609536 | bytes 6336528 | tf_op jit(solution)/shard_map/dot_general | solution.py:208
  21.7 0.1 fusion.50
  21.8 3.6 %fusion.75 = (f32[2,4]{1,0:T(2,128)S(1)}, f32[2,4,2048]{2,1,0:T(4,128)S(1)}) fusion(f32[2,2048]{1,0:T(2,128)S(1)} %subtract_convert_fusion, f32[4]{0:T(128)S(1)} %multiply_exponential_fusion.slopes_ref, bf16[2,2048,512]{2,1,0:T(8,128)(2,1)} %param.25, pred[512,4]{0,1:T(4,128)(4,1)S(1)} %iota_compare_fusion.1, bf16[2,512]{1,0:T(2,128)(2,1)S(1)} %bitcast.51, ...), kind=kOutput, calls=%fused_computation.136 | convolution fusion | flops 16863224 | bytes 4284464 | tf_op jit(solution)/shard_map/vmap()/dot_general | solution.py:143
  25.4 0.2 fusion.37
  25.6 0.1 broadcast_bitcast_fusion
  25.7 0.7 fusion.21
  26.4 0.0 copy-start
  26.4 0.9 copy-done.1
  27.3 0.4 fusion.56
  27.7 0.0 collective-permute-start.6
  27.7 0.1 copy-done
  27.8 1.4 %fusion.20 = bf16[256,2048]{1,0:T(8,128)(2,1)} fusion(bf16[256,2048]{1,0:T(8,128)(2,1)S(1)} %copy-done, f32[2048]{0:T(1024)S(1)} %convert_element_type.97, f32[2048]{0:T(1024)S(1)} %convert_element_type.96, f32[256]{0:T(256)S(1)} %add_rsqrt_fusion, f32[256]{0:T(256)S(1)} %broadcast_multiply_fusion), kind=kLoop, calls=%fused_computation.33 | loop fusion | flops 3145728 | bytes 2115584 | tf_op jit(solution)/shard_map/convert_element_type | solution.py:23
  29.2 1.5 %collective-permute-start = (bf16[256,2048]{1,0:T(8,128)(2,1)}, bf16[256,2048]{1,0:T(8,128)(2,1)}, u32[]{:S(2)}, u32[]{:S(2)}) collective-permute-start(bf16[256,2048]{1,0:T(8,128)(2,1)} %fusion.20), channel_id=1, source_target_pairs={{0,2},{1,3},{2,0},{3,1},{4,6},{5,7},{6,4},{7,5},{8,10},{9,11},{10,... | collective-permute-start | bytes 3145736 | tf_op jit(solution)/shard_map/ppermute | solution.py:245
  30.7 0.1 collective-permute-start.1
  30.8 0.0 collective-permute-done.6
  30.8 0.6 collective-permute-start.7
  31.4 1.9 %broadcast_in_dim.54 = bf16[1024,1536]{1,0:T(8,128)(2,1)} broadcast(bf16[]{:T(256)} %constant.123.clone.1), dimensions={} | broadcast | bytes 3145730 | tf_op jit(solution)/shard_map/broadcast_in_dim | solution.py:252
  33.3 5.8 %fusion.3 = bf16[1024,1536]{1,0:T(8,128)(2,1)} fusion(bf16[1024,1536]{1,0:T(8,128)(2,1)} %broadcast_in_dim.54, s32[]{:T(128)S(6)} %select_n.124, bf16[256,2048]{1,0:T(8,128)(2,1)} %fusion.20, bf16[2048,1536]{1,0:T(8,128)(2,1)} %param.19, f32[1536]{0:T(1024)S(1)} %convert_element_type.99), kind=kOutput, calls=%fused_computation.12 | convolution fusion | flops 1611399168 | bytes 8132612 | tf_op jit(solution)/shard_map/dot_general | solution.py:257
  39.8 15.8 %collective-permute-done.7 = f32[4,2048]{1,0:T(4,128)S(1)} collective-permute-done((f32[4,2048]{1,0:T(4,128)S(1)}, f32[4,2048]{1,0:T(4,128)S(1)}, u32[]{:S(2)}, u32[]{:S(2)}) %collective-permute-start.7) | collective-permute-done | bytes 32800 | tf_op jit(solution)/shard_map/ppermute | solution.py:227
  55.7 0.0 collective-permute-done
  55.7 0.1 collective-permute-start.2
  55.7 0.0 slice-start
  55.8 0.0 slice-start.1
  55.8 1.6 %collective-permute-start.8 = (bf16[512,2048]{1,0:T(8,128)(2,1)S(1)}, bf16[512,2048]{1,0:T(8,128)(2,1)}, u32[]{:S(2)}, u32[]{:S(2)}) collective-permute-start(bf16[512,2048]{1,0:T(8,128)(2,1)S(1)} %copy-done.1), channel_id=1, source_target_pairs={{0,2},{1,3},{2,0},{3,1},{4,6},{5,7},{6,4},{7,5},{8,10},{9,11},{10,... | collective-permute-start | bytes 6291464 | tf_op jit(solution)/shard_map/ppermute | solution.py:250
  57.4 6.0 %fusion.5 = bf16[1024,1536]{1,0:T(8,128)(2,1)} fusion(bf16[1024,1536]{1,0:T(8,128)(2,1)} %fusion.3, s32[]{:T(128)S(6)} %select_n.126, bf16[256,2048]{1,0:T(8,128)(2,1)} %collective-permute-done, bf16[2048,1536]{1,0:T(8,128)(2,1)} %param.19, f32[1536]{0:T(1024)S(1)} %convert_element_type.99), kind=kOutput, calls=%fused_computation.14 | convolution fusion | flops 1611399168 | bytes 8132612 | tf_op jit(solution)/shard_map/dot_general | solution.py:257
  63.4 0.0 collective-permute-done.1
  63.4 0.0 collective-permute-done.2
  63.4 3.9 %fusion.7 = bf16[1024,1536]{1,0:T(8,128)(2,1)} fusion(bf16[1024,1536]{1,0:T(8,128)(2,1)} %fusion.5, s32[]{:T(128)S(6)} %select_n.138, bf16[256,2048]{1,0:T(8,128)(2,1)} %collective-permute-done.1, bf16[2048,1536]{1,0:T(8,128)(2,1)S(1)} %bitcast.49, f32[1536]{0:T(1024)S(1)} %convert_element_type.99), kind=kOutput, calls=%fused_computation.16 | convolution fusion | flops 1611399168 | bytes 8132612 | tf_op jit(solution)/shard_map/dot_general | solution.py:257
  67.3 2.7 %fusion.9.q_ref.kn_ref.vn_ref = bf16[1024,1536]{1,0:T(8,128)(2,1)} fusion(bf16[1024,1536]{1,0:T(8,128)(2,1)} %fusion.7, s32[]{:T(128)S(6)} %select_n.139, bf16[256,2048]{1,0:T(8,128)(2,1)S(1)} %collective-permute-done.2, bf16[2048,1536]{1,0:T(8,128)(2,1)S(1)} %bitcast.49, f32[1536]{0:T(1024)S(1)} %convert_element_type.99), kind=kOutput, calls=%fused_computation.18 | convolution fusion | flops 1611399168 | bytes 8132612 | tf_op jit(solution)/shard_map/dot_general | solution.py:257
  70.0 27.2 %shard_map.158 = bf16[1024,512]{1,0:T(8,128)(2,1)} custom-call(s32[1]{0:T(128)S(6)} %copy.39.prefix_ref, f32[4]{0:T(128)} %copy-done.8, bf16[1024,1536]{1,0:T(8,128)(2,1)} %fusion.9.q_ref.kn_ref.vn_ref, bf16[1024,1536]{1,0:T(8,128)(2,1)} %fusion.9.q_ref.kn_ref.vn_ref, bf16[1024,1536]{1,0:T(8,128)(2,1)} %fusion.9.q_ref.kn_ref.vn_ref, ...), custom_call_target="tpu_custom_call" | custom-call | flops 4294967296 | bytes 6291456 | tf_op jit(solution)/shard_map/pallas_call | solution.py:112
  97.3 6.7 %collective-permute-done.8 = bf16[512,2048]{1,0:T(8,128)(2,1)} collective-permute-done((bf16[512,2048]{1,0:T(8,128)(2,1)S(1)}, bf16[512,2048]{1,0:T(8,128)(2,1)}, u32[]{:S(2)}, u32[]{:S(2)}) %collective-permute-start.8) | collective-permute-done | bytes 2097184 | tf_op jit(solution)/shard_map/ppermute | solution.py:250
  104.0 0.5 collective-permute-start.11
  104.5 0.3 collective-permute-start.14
  104.8 3.4 %collective-permute-done.14 = bf16[2,2048]{1,0:T(2,128)(2,1)S(1)} collective-permute-done((bf16[2,2048]{1,0:T(2,128)(2,1)S(1)}, bf16[2,2048]{1,0:T(2,128)(2,1)S(1)}, u32[]{:S(2)}, u32[]{:S(2)}) %collective-permute-start.14) | collective-permute-done | bytes 8224 | tf_op jit(solution)/shard_map/ppermute | solution.py:283
  108.2 1.6 %collective-permute-start.15 = (bf16[4,2048]{1,0:T(4,128)(2,1)S(1)}, bf16[4,2048]{1,0:T(4,128)(2,1)S(1)}, u32[]{:S(2)}, u32[]{:S(2)}) collective-permute-start(bf16[4,2048]{1,0:T(4,128)(2,1)S(1)} %pad_maximum_fusion.5), channel_id=1, source_target_pairs={{0,8},{4,12},{8,0},{12,4},{16,24},{20,28},{24,16},{28,20},{1,9},{5... | collective-permute-start | bytes 49160 | tf_op jit(solution)/shard_map/ppermute | solution.py:283
  109.8 2.2 %collective-permute-done.15 = bf16[4,2048]{1,0:T(4,128)(2,1)S(1)} collective-permute-done((bf16[4,2048]{1,0:T(4,128)(2,1)S(1)}, bf16[4,2048]{1,0:T(4,128)(2,1)S(1)}, u32[]{:S(2)}, u32[]{:S(2)}) %collective-permute-start.15) | collective-permute-done | bytes 16416 | tf_op jit(solution)/shard_map/ppermute | solution.py:283
  112.0 2.7 %collective-permute-start.16 = (bf16[8,2048]{1,0:T(8,128)(2,1)S(1)}, bf16[8,2048]{1,0:T(8,128)(2,1)S(1)}, u32[]{:S(2)}, u32[]{:S(2)}) collective-permute-start(bf16[8,2048]{1,0:T(8,128)(2,1)S(1)} %pad_maximum_fusion.3), channel_id=1, source_target_pairs={{0,16},{4,20},{8,24},{12,28},{16,0},{20,4},{24,8},{28,12},{1,17},{... | collective-permute-start | bytes 98312 | tf_op jit(solution)/shard_map/ppermute | solution.py:283
  114.7 2.0 %constant_dynamic-slice_fusion = (bf16[256,512]{1,0:T(8,128)(2,1)S(1)}, bf16[256,512]{1,0:T(8,128)(2,1)}, bf16[256,512]{1,0:T(8,128)(2,1)}) fusion(bf16[1024,512]{1,0:T(8,128)(2,1)} %shard_map.158, s32[]{:T(128)S(6)} %select_n.138, s32[]{:T(128)S(6)} %select_n.143, s32[]{:T(128)S(6)} %select_n.142), kind=kLoop, calls=%fused_computation.89 | loop fusion | bytes 1572876 | tf_op jit(solution)/shard_map/dynamic_slice | solution.py:273
  116.6 1.5 %collective-permute-start.9 = (bf16[256,512]{1,0:T(8,128)(2,1)}, bf16[256,512]{1,0:T(8,128)(2,1)}, u32[]{:S(2)}, u32[]{:S(2)}) collective-permute-start(bf16[256,512]{1,0:T(8,128)(2,1)} %get-tuple-element.18), channel_id=1, source_target_pairs={{0,2},{1,3},{2,0},{3,1},{4,6},{5,7},{6,4},{7,5},{8,10},{9,11},{10,... | collective-permute-start | bytes 786440 | tf_op jit(solution)/shard_map/ppermute | solution.py:274
  118.1 0.1 fusion.65
  118.2 0.0 collective-permute-done.16
  118.2 0.8 convolution_convert_fusion
  119.0 0.0 collective-permute-start.12
  119.0 0.6 collective-permute-start.10
  119.7 4.7 %collective-permute-done.9 = bf16[256,512]{1,0:T(8,128)(2,1)} collective-permute-done((bf16[256,512]{1,0:T(8,128)(2,1)}, bf16[256,512]{1,0:T(8,128)(2,1)}, u32[]{:S(2)}, u32[]{:S(2)}) %collective-permute-start.9) | collective-permute-done | bytes 262176 | tf_op jit(solution)/shard_map/ppermute | solution.py:274
  124.3 2.4 %fusion.76 = f32[256,2048]{1,0:T(8,128)S(1)} fusion(bf16[256,512]{1,0:T(8,128)(2,1)} %collective-permute-done.9, bf16[512,2048]{1,0:T(8,128)(2,1)} %collective-permute-done.8), kind=kOutput, calls=%fused_computation.137 | convolution fusion | flops 536870912 | bytes 4456448 | tf_op jit(solution)/shard_map/dot_general | solution.py:277
  126.7 1.7 %convolution_add_fusion.1 = f32[256,2048]{1,0:T(8,128)S(1)} fusion(f32[256,2048]{1,0:T(8,128)S(1)} %fusion.76, bf16[512,2048]{1,0:T(8,128)(2,1)S(1)} %copy-done.1, bf16[1024,512]{1,0:T(8,128)(2,1)} %shard_map.158, s32[]{:T(128)S(6)} %select_n.140), kind=kOutput, calls=%fused_computation.5 | convolution fusion | flops 537395200 | bytes 6553604 | tf_op jit(solution)/shard_map/dot_general | solution.py:275
  128.5 0.0 collective-permute-done.12
  128.5 0.0 collective-permute-done.13
  128.5 2.3 %fusion.77 = f32[256,2048]{1,0:T(8,128)S(1)} fusion(bf16[256,512]{1,0:T(8,128)(2,1)S(1)} %collective-permute-done.12, bf16[512,2048]{1,0:T(8,128)(2,1)} %collective-permute-done.13), kind=kOutput, calls=%fused_computation.138 | convolution fusion | flops 536870912 | bytes 4456448 | tf_op jit(solution)/shard_map/dot_general | solution.py:277
  130.8 3.4 %fusion.10 = bf16[256,2048]{1,0:T(8,128)(2,1)} fusion(bf16[256,2048]{1,0:T(8,128)(2,1)S(1)} %copy-done, f32[256,2048]{1,0:T(8,128)S(1)} %fusion.77, f32[256,2048]{1,0:T(8,128)S(1)} %convolution_add_fusion.1, bf16[256,512]{1,0:T(8,128)(2,1)S(1)} %collective-permute-done.10, bf16[512,2048]{1,0:T(8,128)(2,1)} %collective-permute-done.11, ...), kind=kOutput, calls=%fused_computation.19 | convolution fusion | flops 540016640 | bytes 8658944 | tf_op jit(solution)/shard_map/dot_general | solution.py:277
  (51 shorter events, 0.5 us)
Async XLA Ops:
  0.6 7.9 %copy-start.3 = (bf16[2,2048]{1,0:T(2,128)(2,1)S(1)}, bf16[2,2048]{1,0:T(2,128)(2,1)}, u32[]{:S(2)}) copy-start(bf16[2,2048]{1,0:T(2,128)(2,1)} %param.16) | copy-start | bytes 24580
  0.6 7.7 %copy-start.9 = (s32[16]{0:T(128)S(1)}, s32[16]{0:T(128)}, u32[]{:S(2)}) copy-start(s32[16]{0:T(128)} %param.29) | copy-start | bytes 196
  0.7 14.4 %copy-start.4 = (bf16[2048]{0:T(1024)(128)(2,1)S(1)}, bf16[2048]{0:T(1024)(128)(2,1)}, u32[]{:S(2)}) copy-start(bf16[2048]{0:T(1024)(128)(2,1)} %param.18) | copy-start | bytes 12292
  0.7 14.4 %copy-start.5 = (bf16[2048]{0:T(1024)(128)(2,1)S(1)}, bf16[2048]{0:T(1024)(128)(2,1)}, u32[]{:S(2)}) copy-start(bf16[2048]{0:T(1024)(128)(2,1)} %param.17) | copy-start | bytes 12292
  0.7 14.5 %copy-start.6 = (bf16[1536]{0:T(1024)(128)(2,1)S(1)}, bf16[1536]{0:T(1024)(128)(2,1)}, u32[]{:S(2)}) copy-start(bf16[1536]{0:T(1024)(128)(2,1)} %param.20) | copy-start | bytes 9220
  0.7 7.8 %collective-permute-start.3 = (bf16[2,2048]{1,0:T(2,128)(2,1)}, bf16[2,2048]{1,0:T(2,128)(2,1)S(1)}, u32[]{:S(2)}, u32[]{:S(2)}) collective-permute-start(bf16[2,2048]{1,0:T(2,128)(2,1)} %param.16), channel_id=1, source_target_pairs={{0,4},{4,0},{8,12},{12,8},{16,20},{20,16},{24,28},{28,24},{1,5},{5... | collective-permute-start | bytes 24584 | tf_op jit(solution)/shard_map/ppermute | solution.py:194
  8.6 3.8 %collective-permute-start.4 = (bf16[4,2048]{1,0:T(4,128)(2,1)S(1)}, bf16[4,2048]{1,0:T(4,128)(2,1)S(1)}, u32[]{:S(2)}, u32[]{:S(2)}) collective-permute-start(bf16[4,2048]{1,0:T(4,128)(2,1)S(1)} %pad_maximum_fusion.4), channel_id=1, source_target_pairs={{0,8},{4,12},{8,0},{12,4},{16,24},{20,28},{24,16},{28,20},{1,9},{5... | collective-permute-start | bytes 49160 | tf_op jit(solution)/shard_map/ppermute | solution.py:194
  12.4 4.9 %collective-permute-start.5 = (bf16[8,2048]{1,0:T(8,128)(2,1)S(1)}, bf16[8,2048]{1,0:T(8,128)(2,1)S(1)}, u32[]{:S(2)}, u32[]{:S(2)}) collective-permute-start(bf16[8,2048]{1,0:T(8,128)(2,1)S(1)} %pad_maximum_fusion.1), channel_id=1, source_target_pairs={{0,16},{4,20},{8,24},{12,28},{16,0},{20,4},{24,8},{28,12},{1,17},{... | collective-permute-start | bytes 98312 | tf_op jit(solution)/shard_map/ppermute | solution.py:194
  15.1 6.7 %copy-start.8 = (f32[4]{0:T(128)}, f32[4]{0:T(128)S(1)}, u32[]{:S(2)}) copy-start(f32[4]{0:T(128)S(1)} %multiply_exponential_fusion.slopes_ref) | copy-start | bytes 52
  21.8 3.9 %copy-start.2 = (bf16[2,2048,512]{2,1,0:T(8,128)(2,1)S(1)}, bf16[2,2048,512]{2,1,0:T(8,128)(2,1)}, u32[]{:S(2)}) copy-start(bf16[2,2048,512]{2,1,0:T(8,128)(2,1)} %param.26) | copy-start | bytes 12582916
  25.7 1.6 %copy-start.1 = (bf16[512,2048]{1,0:T(8,128)(2,1)S(1)}, bf16[512,2048]{1,0:T(8,128)(2,1)}, u32[]{:S(2)}) copy-start(bf16[512,2048]{1,0:T(8,128)(2,1)} %param.21) | copy-start | bytes 6291460
  26.4 1.4 %copy-start = (bf16[256,2048]{1,0:T(8,128)(2,1)S(1)}, bf16[256,2048]{1,0:T(8,128)(2,1)}, u32[]{:S(2)}) copy-start(bf16[256,2048]{1,0:T(8,128)(2,1)} %param.15) | copy-start | bytes 3145732
  27.7 3.2 %collective-permute-start.6 = (f32[2,2048]{1,0:T(2,128)S(1)}, f32[2,2048]{1,0:T(2,128)S(1)}, u32[]{:S(2)}, u32[]{:S(2)}) collective-permute-start(f32[2,2048]{1,0:T(2,128)S(1)} %fusion.56), channel_id=1, source_target_pairs={{0,1},{1,0},{2,3},{3,2},{4,5},{5,4},{6,7},{7,6},{8,9},{9,8},{10,11... | collective-permute-start | bytes 49160 | tf_op jit(solution)/shard_map/ppermute | solution.py:227
  29.2 26.4 %collective-permute-start = (bf16[256,2048]{1,0:T(8,128)(2,1)}, bf16[256,2048]{1,0:T(8,128)(2,1)}, u32[]{:S(2)}, u32[]{:S(2)}) collective-permute-start(bf16[256,2048]{1,0:T(8,128)(2,1)} %fusion.20), channel_id=1, source_target_pairs={{0,2},{1,3},{2,0},{3,1},{4,6},{5,7},{6,4},{7,5},{8,10},{9,11},{10,... | collective-permute-start | bytes 3145736 | tf_op jit(solution)/shard_map/ppermute | solution.py:245
  30.7 32.7 %collective-permute-start.1 = (bf16[256,2048]{1,0:T(8,128)(2,1)}, bf16[256,2048]{1,0:T(8,128)(2,1)}, u32[]{:S(2)}, u32[]{:S(2)}) collective-permute-start(bf16[256,2048]{1,0:T(8,128)(2,1)} %fusion.20), channel_id=1, source_target_pairs={{0,1},{1,0},{2,3},{3,2},{4,5},{5,4},{6,7},{7,6},{8,9},{9,8},{10,11... | collective-permute-start | bytes 3145736 | tf_op jit(solution)/shard_map/ppermute | solution.py:248
  30.8 24.7 %collective-permute-start.7 = (f32[4,2048]{1,0:T(4,128)S(1)}, f32[4,2048]{1,0:T(4,128)S(1)}, u32[]{:S(2)}, u32[]{:S(2)}) collective-permute-start(f32[4,2048]{1,0:T(4,128)S(1)} %pad_maximum_fusion.2), channel_id=1, source_target_pairs={{0,2},{1,3},{2,0},{3,1},{4,6},{5,7},{6,4},{7,5},{8,10},{9,11},{10,... | collective-permute-start | bytes 98312 | tf_op jit(solution)/shard_map/ppermute | solution.py:227
  33.3 6.5 %copy-start.7 = (bf16[2048]{0:T(1024)(128)(2,1)S(1)}, bf16[2048]{0:T(1024)(128)(2,1)}, u32[]{:S(2)}) copy-start(bf16[2048]{0:T(1024)(128)(2,1)} %param.22) | copy-start | bytes 12292
  55.7 7.7 %collective-permute-start.2 = (bf16[256,2048]{1,0:T(8,128)(2,1)}, bf16[256,2048]{1,0:T(8,128)(2,1)S(1)}, u32[]{:S(2)}, u32[]{:S(2)}) collective-permute-start(bf16[256,2048]{1,0:T(8,128)(2,1)} %collective-permute-done), channel_id=1, source_target_pairs={{0,1},{1,0},{2,3},{3,2},{4,5},{5,4},{6,7},{7,6},{8,9},{9,8},{10,11... | collective-permute-start | bytes 3145736 | tf_op jit(solution)/shard_map/ppermute | solution.py:248
  55.7 7.7 %slice-start = ((s8[6291456]{0:T(1024)(128)(4,1)}), s8[4194304]{0:T(1024)(128)(4,1)S(1)}, s32[]{:S(2)}) async-start(s8[6291456]{0:T(1024)(128)(4,1)} %bitcast.48), calls=%async_computation | async-start | bytes 8388608
  55.8 7.6 %slice-start.1 = ((s8[6291456]{0:T(1024)(128)(4,1)}), s8[2097152]{0:T(1024)(128)(4,1)S(1)}, s32[]{:S(2)}) async-start(s8[6291456]{0:T(1024)(128)(4,1)} %bitcast.48), calls=%async_computation.1 | async-start | bytes 4194304
  55.8 48.2 %collective-permute-start.8 = (bf16[512,2048]{1,0:T(8,128)(2,1)S(1)}, bf16[512,2048]{1,0:T(8,128)(2,1)}, u32[]{:S(2)}, u32[]{:S(2)}) collective-permute-start(bf16[512,2048]{1,0:T(8,128)(2,1)S(1)} %copy-done.1), channel_id=1, source_target_pairs={{0,2},{1,3},{2,0},{3,1},{4,6},{5,7},{6,4},{7,5},{8,10},{9,11},{10,... | collective-permute-start | bytes 6291464 | tf_op jit(solution)/shard_map/ppermute | solution.py:250
  104.0 24.5 %collective-permute-start.13 = (bf16[512,2048]{1,0:T(8,128)(2,1)}, bf16[512,2048]{1,0:T(8,128)(2,1)}, u32[]{:S(2)}, u32[]{:S(2)}) collective-permute-start(bf16[512,2048]{1,0:T(8,128)(2,1)} %collective-permute-done.8), channel_id=1, source_target_pairs={{0,1},{1,0},{2,3},{3,2},{4,5},{5,4},{6,7},{7,6},{8,9},{9,8},{10,11... | collective-permute-start | bytes 6291464 | tf_op jit(solution)/shard_map/ppermute | solution.py:265
  104.0 26.8 %collective-permute-start.11 = (bf16[512,2048]{1,0:T(8,128)(2,1)S(1)}, bf16[512,2048]{1,0:T(8,128)(2,1)}, u32[]{:S(2)}, u32[]{:S(2)}) collective-permute-start(bf16[512,2048]{1,0:T(8,128)(2,1)S(1)} %copy-done.1), channel_id=1, source_target_pairs={{0,1},{1,0},{2,3},{3,2},{4,5},{5,4},{6,7},{7,6},{8,9},{9,8},{10,11... | collective-permute-start | bytes 6291464 | tf_op jit(solution)/shard_map/ppermute | solution.py:265
  104.5 3.7 %collective-permute-start.14 = (bf16[2,2048]{1,0:T(2,128)(2,1)S(1)}, bf16[2,2048]{1,0:T(2,128)(2,1)S(1)}, u32[]{:S(2)}, u32[]{:S(2)}) collective-permute-start(bf16[2,2048]{1,0:T(2,128)(2,1)S(1)} %fusion.41), channel_id=1, source_target_pairs={{0,4},{4,0},{8,12},{12,8},{16,20},{20,16},{24,28},{28,24},{1,5},{5... | collective-permute-start | bytes 24584 | tf_op jit(solution)/shard_map/ppermute | solution.py:283
  108.2 3.8 %collective-permute-start.15 = (bf16[4,2048]{1,0:T(4,128)(2,1)S(1)}, bf16[4,2048]{1,0:T(4,128)(2,1)S(1)}, u32[]{:S(2)}, u32[]{:S(2)}) collective-permute-start(bf16[4,2048]{1,0:T(4,128)(2,1)S(1)} %pad_maximum_fusion.5), channel_id=1, source_target_pairs={{0,8},{4,12},{8,0},{12,4},{16,24},{20,28},{24,16},{28,20},{1,9},{5... | collective-permute-start | bytes 49160 | tf_op jit(solution)/shard_map/ppermute | solution.py:283
  112.0 6.2 %collective-permute-start.16 = (bf16[8,2048]{1,0:T(8,128)(2,1)S(1)}, bf16[8,2048]{1,0:T(8,128)(2,1)S(1)}, u32[]{:S(2)}, u32[]{:S(2)}) collective-permute-start(bf16[8,2048]{1,0:T(8,128)(2,1)S(1)} %pad_maximum_fusion.3), channel_id=1, source_target_pairs={{0,16},{4,20},{8,24},{12,28},{16,0},{20,4},{24,8},{28,12},{1,17},{... | collective-permute-start | bytes 98312 | tf_op jit(solution)/shard_map/ppermute | solution.py:283
  116.6 7.7 %collective-permute-start.9 = (bf16[256,512]{1,0:T(8,128)(2,1)}, bf16[256,512]{1,0:T(8,128)(2,1)}, u32[]{:S(2)}, u32[]{:S(2)}) collective-permute-start(bf16[256,512]{1,0:T(8,128)(2,1)} %get-tuple-element.18), channel_id=1, source_target_pairs={{0,2},{1,3},{2,0},{3,1},{4,6},{5,7},{6,4},{7,5},{8,10},{9,11},{10,... | collective-permute-start | bytes 786440 | tf_op jit(solution)/shard_map/ppermute | solution.py:274
  119.0 9.4 %collective-permute-start.12 = (bf16[256,512]{1,0:T(8,128)(2,1)}, bf16[256,512]{1,0:T(8,128)(2,1)S(1)}, u32[]{:S(2)}, u32[]{:S(2)}) collective-permute-start(bf16[256,512]{1,0:T(8,128)(2,1)} %get-tuple-element.17), channel_id=1, source_target_pairs={{0,3},{1,2},{2,1},{3,0},{4,7},{5,6},{6,5},{7,4},{8,11},{9,10},{10,... | collective-permute-start | bytes 786440 | tf_op jit(solution)/shard_map/ppermute | solution.py:274
  119.0 11.8 %collective-permute-start.10 = (bf16[256,512]{1,0:T(8,128)(2,1)S(1)}, bf16[256,512]{1,0:T(8,128)(2,1)S(1)}, u32[]{:S(2)}, u32[]{:S(2)}) collective-permute-start(bf16[256,512]{1,0:T(8,128)(2,1)S(1)} %get-tuple-element.16), channel_id=1, source_target_pairs={{0,1},{1,0},{2,3},{3,2},{4,5},{5,4},{6,7},{7,6},{8,9},{9,8},{10,11... | collective-permute-start | bytes 786440 | tf_op jit(solution)/shard_map/ppermute | solution.py:274

commit v10 on v9

--- a/solution.py
+++ b/solution.py
@@ -181,6 +181,7 @@
     slopes = alibi_slopes(lax.axis_index("tensor") * local_heads, local_heads, H)
     bias_sum = out_bias.astype(jnp.float32)
     normed = normalize(pre_hidden, norm_gain, norm_shift)
+    normed, dec_hidden = lax.optimization_barrier((normed, dec_hidden))
     slot_count = dec_hidden.shape[0]
     dp_size = lax.axis_size("dp")
     tensor_size = lax.axis_size("tensor")
@@ -257,6 +258,18 @@
                 jnp.dot(token_block, qkv_weight, preferred_element_type=jnp.float32) + bias_row
             ).astype(jnp.bfloat16)
             merged_rows = lax.dynamic_update_slice_in_dim(merged_rows, projected, source * block, 0)
+    returned = slot_rows
+    step = 1
+    while step < dp_size:
+        returned = jnp.concatenate(
+            [returned, lax.ppermute(returned, "dp", [(i, i ^ step) for i in range(dp_size)])], axis=0
+        )
+        step *= 2
+    slot_wanted = lax.dynamic_slice_in_dim(slot_of, first_slot, slot_count)
+    back = ((slot_wanted // slot_count) ^ group) * slot_count + slot_wanted % slot_count
+    take = (back[:, None] == jnp.arange(returned.shape[0], dtype=jnp.int32)[None, :]).astype(jnp.bfloat16)
+    dec_output = jnp.dot(take, returned, preferred_element_type=jnp.float32).astype(jnp.bfloat16)
+    merged_rows, dec_output = lax.optimization_barrier((merged_rows, dec_output))
     context = prefill_attention_kernel(
         merged_rows, pre_keys[0], pre_values[0], prefix_lengths, slopes, head_size
     )
@@ -276,17 +289,6 @@
     for piece, weight in zip(pieces[1:], weight_blocks[1:]):
         summed = summed + jnp.dot(piece, weight, preferred_element_type=jnp.float32)
     pre_output = (summed + bias_sum + pre_hidden.astype(jnp.float32)).astype(jnp.bfloat16)
-    returned = slot_rows
-    step = 1
-    while step < dp_size:
-        returned = jnp.concatenate(
-            [returned, lax.ppermute(returned, "dp", [(i, i ^ step) for i in range(dp_size)])], axis=0
-        )
-        step *= 2
-    slot_wanted = lax.dynamic_slice_in_dim(slot_of, first_slot, slot_count)
-    back = ((slot_wanted // slot_count) ^ group) * slot_count + slot_wanted % slot_count
-    take = (back[:, None] == jnp.arange(returned.shape[0], dtype=jnp.int32)[None, :]).astype(jnp.bfloat16)
-    dec_output = jnp.dot(take, returned, preferred_element_type=jnp.float32).astype(jnp.bfloat16)
     return (pre_output, dec_output)
 
 

time: 135 us -> 115 us (0.85)
  waiting for transfers between devices: 37 us -> 15.4 us
  starting transfers between devices: 18.4 us -> 20.9 us
    ppermute x2, waiting for transfers between devices: 15.8 us -> 1.35 us  [per_device(): lax.ppermute(partials, 'tensor', [(i, i ^ step) for i in range(tensor_siz...]
    ppermute x1, waiting for transfers between devices: 6.72 us -> 0.01 us  [per_device(): lax.ppermute(held_weight, 'tensor', route(k, 0))]
    ppermute x3, waiting for transfers between devices: 5.56 us -> 0.01 us  [per_device(): lax.ppermute(returned, 'dp', [(i, i ^ step) for i in range(dp_size)])]
    ppermute x3, waiting for transfers between devices: 4.67 us -> 7.34 us  [per_device(): pieces.append(lax.ppermute(outgoing, 'tensor', route(k, flip)))]
    ppermute x3, waiting for transfers between devices: 4.29 us -> 6.02 us  [per_device(): lax.ppermute(shifted_rows, 'dp', [(i, i ^ step) for i in range(dp_size)])]
    ppermute x3, starting transfers between devices: 7.33 us -> 5.82 us  [per_device(): lax.ppermute(shifted_rows, 'dp', [(i, i ^ step) for i in range(dp_size)])]
    ppermute x1, starting transfers between devices: 1.52 us -> 2.94 us  [per_device(): lax.ppermute(normed, 'tensor', route(k, 0))]
  transfers between devices with their start and end apart: 17 -> 17, of which waited for: 7 -> 6; matrix products, arithmetic and copies ran while one was open for 27% -> 34% of each run, Pallas kernels for 20% -> 24%
where the time goes in v10:
time: 115 us; the launch traced here: 114 us
  matrix products  37 us (32%)
  Pallas kernels  27.3 us (24%)
  starting transfers between devices  20.9 us (18%)
  waiting for transfers between devices  15.4 us (13%)
  other arithmetic  7.25 us (6%)
  local copies, waits for them, and re-layouts  4.9 us (4%)
  between operations  1.63 us (1%)
    pallas_call x1, Pallas kernels, prefill_attention_kernel(): pl.pallas_call(functools.partial(_prefill_kernel, tq=tq), out_shape=jax.S...  27.3 us
    dot_general x4, matrix products, per_device(): jnp.dot(token_block, qkv_weight, preferred_element_type=jnp.float32)  17.6 us
    dot_general x3, matrix products, per_device(): summed = summed + jnp.dot(piece, weight, preferred_element_type=jnp.float32)  8.12 us
    ppermute x3, waiting for transfers between devices, per_device(): pieces.append(lax.ppermute(outgoing, 'tensor', route(k, flip)))  7.34 us
    ppermute x3, waiting for transfers between devices, per_device(): lax.ppermute(shifted_rows, 'dp', [(i, i ^ step) for i in range(dp_size)])  6.02 us
    ppermute x3, starting transfers between devices, per_device(): lax.ppermute(shifted_rows, 'dp', [(i, i ^ step) for i in range(dp_size)])  5.82 us
    ppermute x3, starting transfers between devices, per_device(): lax.ppermute(returned, 'dp', [(i, i ^ step) for i in range(dp_size)])  5.8 us
    dot_general x1, matrix products, per_device(): jnp.dot(normed_slots, qkv_weight, preferred_element_type=jnp.float32)  3.75 us
  transfers between devices with their start and end apart: 17, of which 6 were waited for; matrix products, arithmetic and copies ran while one was open for 34% of the time, Pallas kernels for 24%

profile of v10, /device:TPU:0, one launch (start us, length us, event | category | flops | bytes accessed | tf_op | source)
XLA Modules:
  0.0 114.3 jit_solution(17967062599340435427)
XLA Ops:
  0.6 0.0 copy-start
  0.6 0.8 convert_element_type.97
  1.4 0.7 convert_element_type.96
  2.1 1.5 %convert_reduce_fusion = f32[256]{0:T(256)S(1)} fusion(bf16[256,2048]{1,0:T(8,128)(2,1)} %param.15), kind=kLoop, calls=%fused_computation.2 | loop fusion | flops 1048320 | bytes 1049600 | tf_op jit(solution)/shard_map/reduce_sum | solution.py:20
  3.6 1.6 %fusion.17 = f32[256]{0:T(256)S(1)} fusion(bf16[256,2048]{1,0:T(8,128)(2,1)} %param.15, f32[256]{0:T(256)S(1)} %broadcast_multiply_fusion), kind=kLoop, calls=%fused_computation.30 | loop fusion | flops 2096896 | bytes 1050624 | tf_op jit(solution)/shard_map/reduce_sum | solution.py:21
  5.3 1.4 %fusion.20 = bf16[256,2048]{1,0:T(8,128)(2,1)} fusion(bf16[256,2048]{1,0:T(8,128)(2,1)S(1)} %copy-done, f32[2048]{0:T(1024)S(1)} %convert_element_type.97, f32[2048]{0:T(1024)S(1)} %convert_element_type.96, f32[256]{0:T(256)S(1)} %add_rsqrt_fusion, f32[256]{0:T(256)S(1)} %broadcast_multiply_fusion), kind=kLoop, calls=%fused_computation.33 | loop fusion | flops 3145728 | bytes 2115584 | tf_op jit(solution)/shard_map/convert_element_type | solution.py:23
  6.7 2.9 %collective-permute-start = (bf16[256,2048]{1,0:T(8,128)(2,1)}, bf16[256,2048]{1,0:T(8,128)(2,1)}, u32[]{:S(2)}, u32[]{:S(2)}) collective-permute-start(bf16[256,2048]{1,0:T(8,128)(2,1)} %fusion.20), channel_id=1, source_target_pairs={{0,2},{1,3},{2,0},{3,1},{4,6},{5,7},{6,4},{7,5},{8,10},{9,11},{10,... | collective-permute-start | bytes 3145736 | tf_op jit(solution)/shard_map/ppermute | solution.py:246
  9.7 0.0 collective-permute-start.1
  9.7 1.5 %collective-permute-start.3 = (bf16[2,2048]{1,0:T(2,128)(2,1)S(1)}, bf16[2,2048]{1,0:T(2,128)(2,1)S(1)}, u32[]{:S(2)}, u32[]{:S(2)}) collective-permute-start(bf16[2,2048]{1,0:T(2,128)(2,1)S(1)} %copy-done.4), channel_id=1, source_target_pairs={{0,4},{4,0},{8,12},{12,8},{16,20},{20,16},{24,28},{28,24},{1,5},{5... | collective-permute-start | bytes 24584 | tf_op jit(solution)/shard_map/ppermute | solution.py:195
  11.2 0.1 subtract_convert_fusion
  11.3 0.1 iota_compare_fusion
  11.4 0.2 fusion.61
  11.6 1.7 %collective-permute-done.3 = bf16[2,2048]{1,0:T(2,128)(2,1)S(1)} collective-permute-done((bf16[2,2048]{1,0:T(2,128)(2,1)S(1)}, bf16[2,2048]{1,0:T(2,128)(2,1)S(1)}, u32[]{:S(2)}, u32[]{:S(2)}) %collective-permute-start.3) | collective-permute-done | bytes 8224 | tf_op jit(solution)/shard_map/ppermute | solution.py:195
  13.3 1.6 %collective-permute-start.4 = (bf16[4,2048]{1,0:T(4,128)(2,1)S(1)}, bf16[4,2048]{1,0:T(4,128)(2,1)S(1)}, u32[]{:S(2)}, u32[]{:S(2)}) collective-permute-start(bf16[4,2048]{1,0:T(4,128)(2,1)S(1)} %pad_maximum_fusion.4), channel_id=1, source_target_pairs={{0,8},{4,12},{8,0},{12,4},{16,24},{20,28},{24,16},{28,20},{1,9},{5... | collective-permute-start | bytes 49160 | tf_op jit(solution)/shard_map/ppermute | solution.py:195
  15.0 2.1 %collective-permute-done.4 = bf16[4,2048]{1,0:T(4,128)(2,1)S(1)} collective-permute-done((bf16[4,2048]{1,0:T(4,128)(2,1)S(1)}, bf16[4,2048]{1,0:T(4,128)(2,1)S(1)}, u32[]{:S(2)}, u32[]{:S(2)}) %collective-permute-start.4) | collective-permute-done | bytes 16416 | tf_op jit(solution)/shard_map/ppermute | solution.py:195
  17.2 2.7 %collective-permute-start.5 = (bf16[8,2048]{1,0:T(8,128)(2,1)S(1)}, bf16[8,2048]{1,0:T(8,128)(2,1)S(1)}, u32[]{:S(2)}, u32[]{:S(2)}) collective-permute-start(bf16[8,2048]{1,0:T(8,128)(2,1)S(1)} %pad_maximum_fusion.1), channel_id=1, source_target_pairs={{0,16},{4,20},{8,24},{12,28},{16,0},{20,4},{24,8},{28,12},{1,17},{... | collective-permute-start | bytes 98312 | tf_op jit(solution)/shard_map/ppermute | solution.py:195
  19.9 2.1 %collective-permute-done.5 = bf16[8,2048]{1,0:T(8,128)(2,1)S(1)} collective-permute-done((bf16[8,2048]{1,0:T(8,128)(2,1)S(1)}, bf16[8,2048]{1,0:T(8,128)(2,1)S(1)}, u32[]{:S(2)}, u32[]{:S(2)}) %collective-permute-start.5) | collective-permute-done | bytes 32800 | tf_op jit(solution)/shard_map/ppermute | solution.py:195
  22.1 0.3 fusion.74
  22.4 0.2 multiply_reduce_fusion
  22.6 3.8 %fusion.15 = bf16[2,1536]{1,0:T(2,128)(2,1)S(1)} fusion(bf16[2048,1536]{1,0:T(8,128)(2,1)} %param.19, f32[2,2048]{1,0:T(2,128)S(1)} %get-tuple-element.33, f32[2]{0:T(128)S(1)} %add_rsqrt_fusion.1, f32[2]{0:T(128)S(1)} %broadcast_multiply_fusion.1, f32[2048]{0:T(1024)S(1)} %convert_element_type.97, f32[2048]{0:T(1024)S(1)} %convert_element_type.96, ...), kind=kOutput, calls=%fused_computation.26 | convolution fusion | flops 12609536 | bytes 6336528 | tf_op jit(solution)/shard_map/dot_general | solution.py:209
  26.4 0.1 fusion.50
  26.5 3.6 %fusion.75 = (f32[2,4]{1,0:T(2,128)S(1)}, f32[2,4,2048]{2,1,0:T(4,128)S(1)}) fusion(f32[2,2048]{1,0:T(2,128)S(1)} %subtract_convert_fusion, f32[4]{0:T(128)S(1)} %multiply_exponential_fusion.slopes_ref, bf16[2,2048,512]{2,1,0:T(8,128)(2,1)} %param.25, pred[512,4]{0,1:T(4,128)(4,1)S(1)} %iota_compare_fusion.1, bf16[2,512]{1,0:T(2,128)(2,1)S(1)} %bitcast.51, ...), kind=kOutput, calls=%fused_computation.136 | convolution fusion | flops 16863224 | bytes 4284464 | tf_op jit(solution)/shard_map/vmap()/dot_general | solution.py:143
  30.1 0.2 fusion.37
  30.4 0.1 broadcast_bitcast_fusion
  30.4 0.7 fusion.21
  31.2 0.9 copy-done.1
  32.0 0.4 fusion.56
  32.4 0.0 collective-permute-start.6
  32.4 0.7 collective-permute-done
  33.1 0.0 collective-permute-start.2
  33.1 1.9 %broadcast_in_dim.54 = bf16[1024,1536]{1,0:T(8,128)(2,1)} broadcast(bf16[]{:T(256)} %constant.123.clone.1), dimensions={} | broadcast | bytes 3145730 | tf_op jit(solution)/shard_map/broadcast_in_dim | solution.py:253
  35.0 3.9 %fusion.3 = bf16[1024,1536]{1,0:T(8,128)(2,1)} fusion(bf16[1024,1536]{1,0:T(8,128)(2,1)} %broadcast_in_dim.54, s32[]{:T(128)S(6)} %select_n.124, bf16[256,2048]{1,0:T(8,128)(2,1)} %fusion.20, bf16[2048,1536]{1,0:T(8,128)(2,1)S(1)} %copy-done.2, f32[1536]{0:T(1024)S(1)} %convert_element_type.99), kind=kOutput, calls=%fused_computation.12 | convolution fusion | flops 1611399168 | bytes 8132612 | tf_op jit(solution)/shard_map/dot_general | solution.py:258
  38.9 0.0 collective-permute-done.6
  39.0 1.8 %collective-permute-start.7 = (f32[4,2048]{1,0:T(4,128)S(1)}, f32[4,2048]{1,0:T(4,128)S(1)}, u32[]{:S(2)}, u32[]{:S(2)}) collective-permute-start(f32[4,2048]{1,0:T(4,128)S(1)} %pad_maximum_fusion.2), channel_id=1, source_target_pairs={{0,2},{1,3},{2,0},{3,1},{4,6},{5,7},{6,4},{7,5},{8,10},{9,11},{10,... | collective-permute-start | bytes 98312 | tf_op jit(solution)/shard_map/ppermute | solution.py:228
  40.8 0.1 fusion.65
  41.6 1.3 %collective-permute-done.7 = f32[4,2048]{1,0:T(4,128)S(1)} collective-permute-done((f32[4,2048]{1,0:T(4,128)S(1)}, f32[4,2048]{1,0:T(4,128)S(1)}, u32[]{:S(2)}, u32[]{:S(2)}) %collective-permute-start.7) | collective-permute-done | bytes 32800 | tf_op jit(solution)/shard_map/ppermute | solution.py:228
  43.0 0.0 slice-start
  43.1 0.0 slice-start.1
  43.1 1.8 %collective-permute-start.11 = (bf16[512,2048]{1,0:T(8,128)(2,1)S(1)}, bf16[512,2048]{1,0:T(8,128)(2,1)}, u32[]{:S(2)}, u32[]{:S(2)}) collective-permute-start(bf16[512,2048]{1,0:T(8,128)(2,1)S(1)} %copy-done.1), channel_id=1, source_target_pairs={{0,2},{1,3},{2,0},{3,1},{4,6},{5,7},{6,4},{7,5},{8,10},{9,11},{10,... | collective-permute-start | bytes 6291464 | tf_op jit(solution)/shard_map/ppermute | solution.py:251
  44.9 0.0 collective-permute-done.1
  44.9 0.0 collective-permute-done.2
  44.9 1.5 %collective-permute-start.8 = (bf16[2,2048]{1,0:T(2,128)(2,1)S(1)}, bf16[2,2048]{1,0:T(2,128)(2,1)S(1)}, u32[]{:S(2)}, u32[]{:S(2)}) collective-permute-start(bf16[2,2048]{1,0:T(2,128)(2,1)S(1)} %fusion.41), channel_id=1, source_target_pairs={{0,4},{4,0},{8,12},{12,8},{16,20},{20,16},{24,28},{28,24},{1,5},{5... | collective-permute-start | bytes 24584 | tf_op jit(solution)/shard_map/ppermute | solution.py:265
  46.5 5.8 %fusion.5 = bf16[1024,1536]{1,0:T(8,128)(2,1)} fusion(bf16[1024,1536]{1,0:T(8,128)(2,1)} %fusion.3, s32[]{:T(128)S(6)} %select_n.126, bf16[256,2048]{1,0:T(8,128)(2,1)} %collective-permute-done, bf16[2048,1536]{1,0:T(8,128)(2,1)} %param.19, f32[1536]{0:T(1024)S(1)} %convert_element_type.99), kind=kOutput, calls=%fused_computation.14 | convolution fusion | flops 1611399168 | bytes 8132612 | tf_op jit(solution)/shard_map/dot_general | solution.py:258
  52.3 1.6 %collective-permute-start.9 = (bf16[4,2048]{1,0:T(4,128)(2,1)S(1)}, bf16[4,2048]{1,0:T(4,128)(2,1)S(1)}, u32[]{:S(2)}, u32[]{:S(2)}) collective-permute-start(bf16[4,2048]{1,0:T(4,128)(2,1)S(1)} %pad_maximum_fusion.5), channel_id=1, source_target_pairs={{0,8},{4,12},{8,0},{12,4},{16,24},{20,28},{24,16},{28,20},{1,9},{5... | collective-permute-start | bytes 49160 | tf_op jit(solution)/shard_map/ppermute | solution.py:265
  54.0 3.9 %fusion.7 = bf16[1024,1536]{1,0:T(8,128)(2,1)} fusion(bf16[1024,1536]{1,0:T(8,128)(2,1)} %fusion.5, s32[]{:T(128)S(6)} %select_n.138, bf16[256,2048]{1,0:T(8,128)(2,1)} %collective-permute-done.1, bf16[2048,1536]{1,0:T(8,128)(2,1)S(1)} %bitcast.49, f32[1536]{0:T(1024)S(1)} %convert_element_type.99), kind=kOutput, calls=%fused_computation.16 | convolution fusion | flops 1611399168 | bytes 8132612 | tf_op jit(solution)/shard_map/dot_general | solution.py:258
  57.9 0.0 collective-permute-done.9
  57.9 2.6 %collective-permute-start.10 = (bf16[8,2048]{1,0:T(8,128)(2,1)S(1)}, bf16[8,2048]{1,0:T(8,128)(2,1)S(1)}, u32[]{:S(2)}, u32[]{:S(2)}) collective-permute-start(bf16[8,2048]{1,0:T(8,128)(2,1)S(1)} %pad_maximum_fusion.3), channel_id=1, source_target_pairs={{0,16},{4,20},{8,24},{12,28},{16,0},{20,4},{24,8},{28,12},{1,17},{... | collective-permute-start | bytes 98312 | tf_op jit(solution)/shard_map/ppermute | solution.py:265
  60.5 3.9 %fusion.9.q_ref.kn_ref.vn_ref = bf16[1024,1536]{1,0:T(8,128)(2,1)} fusion(bf16[1024,1536]{1,0:T(8,128)(2,1)} %fusion.7, s32[]{:T(128)S(6)} %select_n.139, bf16[256,2048]{1,0:T(8,128)(2,1)} %collective-permute-done.2, bf16[2048,1536]{1,0:T(8,128)(2,1)S(1)} %bitcast.49, f32[1536]{0:T(1024)S(1)} %convert_element_type.99), kind=kOutput, calls=%fused_computation.18 | convolution fusion | flops 1611399168 | bytes 8132612 | tf_op jit(solution)/shard_map/dot_general | solution.py:258
  64.4 0.8 convolution_convert_fusion
  65.2 27.3 %shard_map.158 = bf16[1024,512]{1,0:T(8,128)(2,1)} custom-call(s32[1]{0:T(128)S(6)} %copy.39.prefix_ref, f32[4]{0:T(128)} %copy-done.8, bf16[1024,1536]{1,0:T(8,128)(2,1)} %fusion.9.q_ref.kn_ref.vn_ref, bf16[1024,1536]{1,0:T(8,128)(2,1)} %fusion.9.q_ref.kn_ref.vn_ref, bf16[1024,1536]{1,0:T(8,128)(2,1)} %fusion.9.q_ref.kn_ref.vn_ref, ...), custom_call_target="tpu_custom_call" | custom-call | flops 4294967296 | bytes 6291456 | tf_op jit(solution)/shard_map/pallas_call | solution.py:112
  92.5 0.0 collective-permute-done.11
  92.5 0.0 collective-permute-start.16
  92.5 0.5 collective-permute-start.14
  93.0 2.0 %constant_dynamic-slice_fusion.2 = (bf16[256,512]{1,0:T(8,128)(2,1)S(1)}, bf16[256,512]{1,0:T(8,128)(2,1)}, bf16[256,512]{1,0:T(8,128)(2,1)}) fusion(bf16[1024,512]{1,0:T(8,128)(2,1)} %shard_map.158, s32[]{:T(128)S(6)} %select_n.138, s32[]{:T(128)S(6)} %select_n.146, s32[]{:T(128)S(6)} %select_n.145), kind=kLoop, calls=%fused_computation.92 | loop fusion | bytes 1572876 | tf_op jit(solution)/shard_map/dynamic_slice | solution.py:286
  95.0 0.5 collective-permute-start.12
  95.5 0.9 collective-permute-start.15
  96.4 0.7 collective-permute-start.13
  97.1 7.3 %collective-permute-done.12 = bf16[256,512]{1,0:T(8,128)(2,1)} collective-permute-done((bf16[256,512]{1,0:T(8,128)(2,1)}, bf16[256,512]{1,0:T(8,128)(2,1)}, u32[]{:S(2)}, u32[]{:S(2)}) %collective-permute-start.12) | collective-permute-done | bytes 262176 | tf_op jit(solution)/shard_map/ppermute | solution.py:287
  104.4 2.4 %fusion.76 = f32[256,2048]{1,0:T(8,128)S(1)} fusion(bf16[256,512]{1,0:T(8,128)(2,1)} %collective-permute-done.12, bf16[512,2048]{1,0:T(8,128)(2,1)} %collective-permute-done.11), kind=kOutput, calls=%fused_computation.137 | convolution fusion | flops 536870912 | bytes 4456448 | tf_op jit(solution)/shard_map/dot_general | solution.py:290
  106.8 1.7 %convolution_add_fusion.1 = f32[256,2048]{1,0:T(8,128)S(1)} fusion(f32[256,2048]{1,0:T(8,128)S(1)} %fusion.76, bf16[512,2048]{1,0:T(8,128)(2,1)S(1)} %copy-done.1, bf16[1024,512]{1,0:T(8,128)(2,1)} %shard_map.158, s32[]{:T(128)S(6)} %select_n.143), kind=kOutput, calls=%fused_computation.5 | convolution fusion | flops 537395200 | bytes 6553604 | tf_op jit(solution)/shard_map/dot_general | solution.py:288
  108.6 0.0 collective-permute-done.15
  108.6 0.0 collective-permute-done.16
  108.6 2.3 %fusion.77 = f32[256,2048]{1,0:T(8,128)S(1)} fusion(bf16[256,512]{1,0:T(8,128)(2,1)S(1)} %collective-permute-done.15, bf16[512,2048]{1,0:T(8,128)(2,1)} %collective-permute-done.16), kind=kOutput, calls=%fused_computation.138 | convolution fusion | flops 536870912 | bytes 4456448 | tf_op jit(solution)/shard_map/dot_general | solution.py:290
  110.9 3.4 %fusion.10 = bf16[256,2048]{1,0:T(8,128)(2,1)} fusion(bf16[256,2048]{1,0:T(8,128)(2,1)S(1)} %copy-done, f32[256,2048]{1,0:T(8,128)S(1)} %fusion.77, f32[256,2048]{1,0:T(8,128)S(1)} %convolution_add_fusion.1, bf16[256,512]{1,0:T(8,128)(2,1)S(1)} %collective-permute-done.13, bf16[512,2048]{1,0:T(8,128)(2,1)} %collective-permute-done.14, ...), kind=kOutput, calls=%fused_computation.19 | convolution fusion | flops 540016640 | bytes 8658944 | tf_op jit(solution)/shard_map/dot_general | solution.py:290
  (51 shorter events, 0.5 us)
Async XLA Ops:
  0.6 4.6 %copy-start = (bf16[256,2048]{1,0:T(8,128)(2,1)S(1)}, bf16[256,2048]{1,0:T(8,128)(2,1)}, u32[]{:S(2)}) copy-start(bf16[256,2048]{1,0:T(8,128)(2,1)} %param.15) | copy-start | bytes 3145732
  2.1 7.6 %copy-start.4 = (bf16[2,2048]{1,0:T(2,128)(2,1)S(1)}, bf16[2,2048]{1,0:T(2,128)(2,1)}, u32[]{:S(2)}) copy-start(bf16[2,2048]{1,0:T(2,128)(2,1)} %param.16) | copy-start | bytes 24580
  2.1 9.1 %copy-start.7 = (s32[2]{0:T(128)S(1)}, s32[2]{0:T(128)}, u32[]{:S(2)}) copy-start(s32[2]{0:T(128)} %param.28) | copy-start | bytes 28
  2.1 9.3 %copy-start.9 = (s32[16]{0:T(128)S(1)}, s32[16]{0:T(128)}, u32[]{:S(2)}) copy-start(s32[16]{0:T(128)} %param.29) | copy-start | bytes 196
  2.1 17.8 %copy-start.5 = (bf16[1536]{0:T(1024)(128)(2,1)S(1)}, bf16[1536]{0:T(1024)(128)(2,1)}, u32[]{:S(2)}) copy-start(bf16[1536]{0:T(1024)(128)(2,1)} %param.20) | copy-start | bytes 9220
  6.7 26.4 %collective-permute-start = (bf16[256,2048]{1,0:T(8,128)(2,1)}, bf16[256,2048]{1,0:T(8,128)(2,1)}, u32[]{:S(2)}, u32[]{:S(2)}) collective-permute-start(bf16[256,2048]{1,0:T(8,128)(2,1)} %fusion.20), channel_id=1, source_target_pairs={{0,2},{1,3},{2,0},{3,1},{4,6},{5,7},{6,4},{7,5},{8,10},{9,11},{10,... | collective-permute-start | bytes 3145736 | tf_op jit(solution)/shard_map/ppermute | solution.py:246
  9.7 35.3 %collective-permute-start.1 = (bf16[256,2048]{1,0:T(8,128)(2,1)}, bf16[256,2048]{1,0:T(8,128)(2,1)}, u32[]{:S(2)}, u32[]{:S(2)}) collective-permute-start(bf16[256,2048]{1,0:T(8,128)(2,1)} %fusion.20), channel_id=1, source_target_pairs={{0,1},{1,0},{2,3},{3,2},{4,5},{5,4},{6,7},{7,6},{8,9},{9,8},{10,11... | collective-permute-start | bytes 3145736 | tf_op jit(solution)/shard_map/ppermute | solution.py:249
  9.7 3.7 %collective-permute-start.3 = (bf16[2,2048]{1,0:T(2,128)(2,1)S(1)}, bf16[2,2048]{1,0:T(2,128)(2,1)S(1)}, u32[]{:S(2)}, u32[]{:S(2)}) collective-permute-start(bf16[2,2048]{1,0:T(2,128)(2,1)S(1)} %copy-done.4), channel_id=1, source_target_pairs={{0,4},{4,0},{8,12},{12,8},{16,20},{20,16},{24,28},{28,24},{1,5},{5... | collective-permute-start | bytes 24584 | tf_op jit(solution)/shard_map/ppermute | solution.py:195
  13.3 3.8 %collective-permute-start.4 = (bf16[4,2048]{1,0:T(4,128)(2,1)S(1)}, bf16[4,2048]{1,0:T(4,128)(2,1)S(1)}, u32[]{:S(2)}, u32[]{:S(2)}) collective-permute-start(bf16[4,2048]{1,0:T(4,128)(2,1)S(1)} %pad_maximum_fusion.4), channel_id=1, source_target_pairs={{0,8},{4,12},{8,0},{12,4},{16,24},{20,28},{24,16},{28,20},{1,9},{5... | collective-permute-start | bytes 49160 | tf_op jit(solution)/shard_map/ppermute | solution.py:195
  17.2 4.9 %collective-permute-start.5 = (bf16[8,2048]{1,0:T(8,128)(2,1)S(1)}, bf16[8,2048]{1,0:T(8,128)(2,1)S(1)}, u32[]{:S(2)}, u32[]{:S(2)}) collective-permute-start(bf16[8,2048]{1,0:T(8,128)(2,1)S(1)} %pad_maximum_fusion.1), channel_id=1, source_target_pairs={{0,16},{4,20},{8,24},{12,28},{16,0},{20,4},{24,8},{28,12},{1,17},{... | collective-permute-start | bytes 98312 | tf_op jit(solution)/shard_map/ppermute | solution.py:195
  19.8 6.7 %copy-start.8 = (f32[4]{0:T(128)}, f32[4]{0:T(128)S(1)}, u32[]{:S(2)}) copy-start(f32[4]{0:T(128)S(1)} %multiply_exponential_fusion.slopes_ref) | copy-start | bytes 52
  26.5 3.9 %copy-start.3 = (bf16[2,2048,512]{2,1,0:T(8,128)(2,1)S(1)}, bf16[2,2048,512]{2,1,0:T(8,128)(2,1)}, u32[]{:S(2)}) copy-start(bf16[2,2048,512]{2,1,0:T(8,128)(2,1)} %param.26) | copy-start | bytes 12582916
  30.4 1.6 %copy-start.1 = (bf16[512,2048]{1,0:T(8,128)(2,1)S(1)}, bf16[512,2048]{1,0:T(8,128)(2,1)}, u32[]{:S(2)}) copy-start(bf16[512,2048]{1,0:T(8,128)(2,1)} %param.21) | copy-start | bytes 6291460
  30.4 4.6 %copy-start.2 = (bf16[2048,1536]{1,0:T(8,128)(2,1)S(1)}, bf16[2048,1536]{1,0:T(8,128)(2,1)}, u32[]{:S(2)}) copy-start(bf16[2048,1536]{1,0:T(8,128)(2,1)} %param.19) | copy-start | bytes 18874372
  32.4 6.5 %collective-permute-start.6 = (f32[2,2048]{1,0:T(2,128)S(1)}, f32[2,2048]{1,0:T(2,128)S(1)}, u32[]{:S(2)}, u32[]{:S(2)}) collective-permute-start(f32[2,2048]{1,0:T(2,128)S(1)} %fusion.56), channel_id=1, source_target_pairs={{0,1},{1,0},{2,3},{3,2},{4,5},{5,4},{6,7},{7,6},{8,9},{9,8},{10,11... | collective-permute-start | bytes 49160 | tf_op jit(solution)/shard_map/ppermute | solution.py:228
  33.1 11.8 %collective-permute-start.2 = (bf16[256,2048]{1,0:T(8,128)(2,1)}, bf16[256,2048]{1,0:T(8,128)(2,1)}, u32[]{:S(2)}, u32[]{:S(2)}) collective-permute-start(bf16[256,2048]{1,0:T(8,128)(2,1)} %collective-permute-done), channel_id=1, source_target_pairs={{0,1},{1,0},{2,3},{3,2},{4,5},{5,4},{6,7},{7,6},{8,9},{9,8},{10,11... | collective-permute-start | bytes 3145736 | tf_op jit(solution)/shard_map/ppermute | solution.py:249
  35.0 6.6 %copy-start.6 = (bf16[2048]{0:T(1024)(128)(2,1)S(1)}, bf16[2048]{0:T(1024)(128)(2,1)}, u32[]{:S(2)}) copy-start(bf16[2048]{0:T(1024)(128)(2,1)} %param.22) | copy-start | bytes 12292
  39.0 4.0 %collective-permute-start.7 = (f32[4,2048]{1,0:T(4,128)S(1)}, f32[4,2048]{1,0:T(4,128)S(1)}, u32[]{:S(2)}, u32[]{:S(2)}) collective-permute-start(f32[4,2048]{1,0:T(4,128)S(1)} %pad_maximum_fusion.2), channel_id=1, source_target_pairs={{0,2},{1,3},{2,0},{3,1},{4,6},{5,7},{6,4},{7,5},{8,10},{9,11},{10,... | collective-permute-start | bytes 98312 | tf_op jit(solution)/shard_map/ppermute | solution.py:228
  43.0 10.9 %slice-start = ((s8[6291456]{0:T(1024)(128)(4,1)}), s8[4194304]{0:T(1024)(128)(4,1)S(1)}, s32[]{:S(2)}) async-start(s8[6291456]{0:T(1024)(128)(4,1)} %bitcast.48), calls=%async_computation | async-start | bytes 8388608
  43.1 10.9 %slice-start.1 = ((s8[6291456]{0:T(1024)(128)(4,1)}), s8[2097152]{0:T(1024)(128)(4,1)S(1)}, s32[]{:S(2)}) async-start(s8[6291456]{0:T(1024)(128)(4,1)} %bitcast.48), calls=%async_computation.1 | async-start | bytes 4194304
  43.1 49.4 %collective-permute-start.11 = (bf16[512,2048]{1,0:T(8,128)(2,1)S(1)}, bf16[512,2048]{1,0:T(8,128)(2,1)}, u32[]{:S(2)}, u32[]{:S(2)}) collective-permute-start(bf16[512,2048]{1,0:T(8,128)(2,1)S(1)} %copy-done.1), channel_id=1, source_target_pairs={{0,2},{1,3},{2,0},{3,1},{4,6},{5,7},{6,4},{7,5},{8,10},{9,11},{10,... | collective-permute-start | bytes 6291464 | tf_op jit(solution)/shard_map/ppermute | solution.py:251
  44.9 7.3 %collective-permute-start.8 = (bf16[2,2048]{1,0:T(2,128)(2,1)S(1)}, bf16[2,2048]{1,0:T(2,128)(2,1)S(1)}, u32[]{:S(2)}, u32[]{:S(2)}) collective-permute-start(bf16[2,2048]{1,0:T(2,128)(2,1)S(1)} %fusion.41), channel_id=1, source_target_pairs={{0,4},{4,0},{8,12},{12,8},{16,20},{20,16},{24,28},{28,24},{1,5},{5... | collective-permute-start | bytes 24584 | tf_op jit(solution)/shard_map/ppermute | solution.py:265
  52.3 5.6 %collective-permute-start.9 = (bf16[4,2048]{1,0:T(4,128)(2,1)S(1)}, bf16[4,2048]{1,0:T(4,128)(2,1)S(1)}, u32[]{:S(2)}, u32[]{:S(2)}) collective-permute-start(bf16[4,2048]{1,0:T(4,128)(2,1)S(1)} %pad_maximum_fusion.5), channel_id=1, source_target_pairs={{0,8},{4,12},{8,0},{12,4},{16,24},{20,28},{24,16},{28,20},{1,9},{5... | collective-permute-start | bytes 49160 | tf_op jit(solution)/shard_map/ppermute | solution.py:265
  57.9 6.5 %collective-permute-start.10 = (bf16[8,2048]{1,0:T(8,128)(2,1)S(1)}, bf16[8,2048]{1,0:T(8,128)(2,1)S(1)}, u32[]{:S(2)}, u32[]{:S(2)}) collective-permute-start(bf16[8,2048]{1,0:T(8,128)(2,1)S(1)} %pad_maximum_fusion.3), channel_id=1, source_target_pairs={{0,16},{4,20},{8,24},{12,28},{16,0},{20,4},{24,8},{28,12},{1,17},{... | collective-permute-start | bytes 98312 | tf_op jit(solution)/shard_map/ppermute | solution.py:265
  92.5 16.1 %collective-permute-start.16 = (bf16[512,2048]{1,0:T(8,128)(2,1)}, bf16[512,2048]{1,0:T(8,128)(2,1)}, u32[]{:S(2)}, u32[]{:S(2)}) collective-permute-start(bf16[512,2048]{1,0:T(8,128)(2,1)} %collective-permute-done.11), channel_id=1, source_target_pairs={{0,1},{1,0},{2,3},{3,2},{4,5},{5,4},{6,7},{7,6},{8,9},{9,8},{10,11... | collective-permute-start | bytes 6291464 | tf_op jit(solution)/shard_map/ppermute | solution.py:278
  92.5 18.4 %collective-permute-start.14 = (bf16[512,2048]{1,0:T(8,128)(2,1)S(1)}, bf16[512,2048]{1,0:T(8,128)(2,1)}, u32[]{:S(2)}, u32[]{:S(2)}) collective-permute-start(bf16[512,2048]{1,0:T(8,128)(2,1)S(1)} %copy-done.1), channel_id=1, source_target_pairs={{0,1},{1,0},{2,3},{3,2},{4,5},{5,4},{6,7},{7,6},{8,9},{9,8},{10,11... | collective-permute-start | bytes 6291464 | tf_op jit(solution)/shard_map/ppermute | solution.py:278
  95.0 9.5 %collective-permute-start.12 = (bf16[256,512]{1,0:T(8,128)(2,1)}, bf16[256,512]{1,0:T(8,128)(2,1)}, u32[]{:S(2)}, u32[]{:S(2)}) collective-permute-start(bf16[256,512]{1,0:T(8,128)(2,1)} %get-tuple-element.26), channel_id=1, source_target_pairs={{0,2},{1,3},{2,0},{3,1},{4,6},{5,7},{6,4},{7,5},{8,10},{9,11},{10,... | collective-permute-start | bytes 786440 | tf_op jit(solution)/shard_map/ppermute | solution.py:287
  95.5 13.1 %collective-permute-start.15 = (bf16[256,512]{1,0:T(8,128)(2,1)}, bf16[256,512]{1,0:T(8,128)(2,1)S(1)}, u32[]{:S(2)}, u32[]{:S(2)}) collective-permute-start(bf16[256,512]{1,0:T(8,128)(2,1)} %get-tuple-element.25), channel_id=1, source_target_pairs={{0,3},{1,2},{2,1},{3,0},{4,7},{5,6},{6,5},{7,4},{8,11},{9,10},{10,... | collective-permute-start | bytes 786440 | tf_op jit(solution)/shard_map/ppermute | solution.py:287
  96.4 14.6 %collective-permute-start.13 = (bf16[256,512]{1,0:T(8,128)(2,1)S(1)}, bf16[256,512]{1,0:T(8,128)(2,1)S(1)}, u32[]{:S(2)}, u32[]{:S(2)}) collective-permute-start(bf16[256,512]{1,0:T(8,128)(2,1)S(1)} %get-tuple-element.24), channel_id=1, source_target_pairs={{0,1},{1,0},{2,3},{3,2},{4,5},{5,4},{6,7},{7,6},{8,9},{9,8},{10,11... | collective-permute-start | bytes 786440 | tf_op jit(solution)/shard_map/ppermute | solution.py:287

commit v11 on v10

--- a/solution.py
+++ b/solution.py
@@ -74,9 +74,9 @@
     return context.astype(jnp.bfloat16).reshape(group_size, -1)
 
 
-def _prefill_kernel(prefix_ref, slopes_ref, q_ref, kn_ref, vn_ref, kc_ref, vc_ref, o_ref, *, tq):
+def _prefill_kernel(prefix_ref, slopes_ref, tile_ref, q_ref, kn_ref, vn_ref, kc_ref, vc_ref, o_ref, *, tq):
     h = pl.program_id(0)
-    i = pl.program_id(1)
+    i = tile_ref[0]
     prefix = prefix_ref[0]
     slope = slopes_ref[h]
     factor = 1.0 / math.sqrt(q_ref.shape[-1])
@@ -104,32 +104,33 @@
     ctx = ctx + jnp.dot(p_n, vn_ref[...], preferred_element_type=jnp.float32)
     o_ref[...] = ctx.astype(o_ref.dtype)
 
-def prefill_attention_kernel(merged, cache_keys, cache_values, prefix, slopes, head_size, tq=256):
+
+def prefill_attention_tile(merged, cache_keys, cache_values, prefix, slopes, tile, head_size, tq):
     group = merged.shape[0]
     heads = merged.shape[1] // (3 * head_size)
     cache_size = cache_keys.shape[0]
-    col = lambda c: (lambda h, i, *_: (0, h * 3 + c))
+    col = lambda c: (lambda h, *_: (0, h * 3 + c))
     return pl.pallas_call(
         functools.partial(_prefill_kernel, tq=tq),
-        out_shape=jax.ShapeDtypeStruct((group, heads * head_size), jnp.bfloat16),
+        out_shape=jax.ShapeDtypeStruct((tq, heads * head_size), jnp.bfloat16),
         grid_spec=pltpu.PrefetchScalarGridSpec(
-            num_scalar_prefetch=2,
-            grid=(heads, group // tq),
+            num_scalar_prefetch=3,
+            grid=(heads,),
             in_specs=[
-                pl.BlockSpec((tq, head_size), lambda h, i, *_: (i, h * 3)),
+                pl.BlockSpec((tq, head_size), lambda h, p, s, t: (t[0], h * 3)),
                 pl.BlockSpec((group, head_size), col(1)),
                 pl.BlockSpec((group, head_size), col(2)),
-                pl.BlockSpec((cache_size, head_size), lambda h, i, *_: (0, h)),
-                pl.BlockSpec((cache_size, head_size), lambda h, i, *_: (0, h)),
+                pl.BlockSpec((cache_size, head_size), lambda h, *_: (0, h)),
+                pl.BlockSpec((cache_size, head_size), lambda h, *_: (0, h)),
             ],
-            out_specs=pl.BlockSpec((tq, head_size), lambda h, i, *_: (i, h)),
+            out_specs=pl.BlockSpec((tq, head_size), lambda h, *_: (0, h)),
         ),
         cost_estimate=pl.CostEstimate(
-            flops=4 * heads * group * (group + cache_size) * head_size,
-            transcendentals=heads * group * (group + cache_size),
-            bytes_accessed=2 * (group * heads * 3 * head_size + 2 * cache_size * heads * head_size + group * heads * head_size),
+            flops=4 * heads * tq * (group + cache_size) * head_size,
+            transcendentals=heads * tq * (group + cache_size),
+            bytes_accessed=2 * (4 * group * heads * head_size + 2 * tq * heads * head_size),
         ),
-    )(prefix, slopes, merged, merged, merged, cache_keys, cache_values)
+    )(prefix, slopes, tile, merged, merged, merged, cache_keys, cache_values)
 
 
 def decode_attention(query_row, new_key, new_value, cache_keys, cache_values, length, slopes):
@@ -270,21 +271,20 @@
     take = (back[:, None] == jnp.arange(returned.shape[0], dtype=jnp.int32)[None, :]).astype(jnp.bfloat16)
     dec_output = jnp.dot(take, returned, preferred_element_type=jnp.float32).astype(jnp.bfloat16)
     merged_rows, dec_output = lax.optimization_barrier((merged_rows, dec_output))
-    context = prefill_attention_kernel(
-        merged_rows, pre_keys[0], pre_values[0], prefix_lengths, slopes, head_size
-    )
-    context, across_chips = lax.optimization_barrier((context, across_chips))
+    order = [(k, flip) for flip in (0, 1) for k in range(chips)]
+    pieces = [None] * len(order)
+    for position in sorted(range(len(order)), key=lambda n: (order[n] == (0, 0), -order[n][0], -order[n][1])):
+        k, flip = order[position]
+        target = ((chip + k) % chips) * 2 + (core ^ flip)
+        context = prefill_attention_tile(
+            merged_rows, pre_keys[0], pre_values[0], prefix_lengths, slopes,
+            target.reshape(1).astype(jnp.int32), head_size, block,
+        )
+        pieces[position] = context if (k, flip) == (0, 0) else lax.ppermute(context, "tensor", route(k, flip))
+    across_chips = list(across_chips)
+    pieces[0], across_chips = lax.optimization_barrier((pieces[0], across_chips))
     same_core = [out_weight] + list(across_chips)
     weight_blocks = same_core + [lax.ppermute(w, "tensor", route(0, 1)) for w in same_core]
-    pieces = []
-    for flip in (0, 1):
-        for k in range(chips):
-            if k == 0 and flip == 0:
-                pieces.append(lax.dynamic_slice_in_dim(context, member * block, block))
-                continue
-            target = ((chip + k) % chips) * 2 + (core ^ flip)
-            outgoing = lax.dynamic_slice_in_dim(context, target * block, block)
-            pieces.append(lax.ppermute(outgoing, "tensor", route(k, flip)))
     summed = jnp.dot(pieces[0], weight_blocks[0], preferred_element_type=jnp.float32)
     for piece, weight in zip(pieces[1:], weight_blocks[1:]):
         summed = summed + jnp.dot(piece, weight, preferred_element_type=jnp.float32)

time: 115 us -> 129 us (1.12)
  waiting for transfers between devices: 15.4 us -> 30.6 us
  Pallas kernels: 27.3 us -> 34.5 us
  local copies, waits for them, and re-layouts: 4.9 us -> 1.07 us
  matrix products: 37 us -> 34.5 us
  starting transfers between devices: 20.9 us -> 19.1 us
    ppermute x1, waiting for transfers between devices: 0.01 us -> 18.6 us  [per_device(): lax.ppermute(held_weight, 'tensor', route(k, 0))]
    pallas_call x1 -> x4, Pallas kernels: 27.3 us -> 34.5 us  [prefill_attention_tile(): pl.pallas_call(functools.partial(_prefill_kernel, tq=tq), out_shape=jax.S...]
    dot_general x4, matrix products: 17.6 us -> 14 us  [per_device(): jnp.dot(token_block, qkv_weight, preferred_element_type=jnp.float32)]
    ppermute x3, waiting for transfers between devices: 7.34 us -> 4.06 us  [per_device(): lax.ppermute(context, 'tensor', route(k, flip))]
    dot_general x3, matrix products: 8.12 us -> 5.3 us  [per_device(): summed = summed + jnp.dot(piece, weight, preferred_element_type=jnp.float32)]
    dynamic_slice x1 -> x0, local copies, waits for them, and re-layouts: 1.95 us -> none  [per_device(): outgoing = lax.dynamic_slice_in_dim(context, target * block, block)]
    dot_general x1, matrix products: 0.38 us -> 2.28 us  [per_device(): jnp.dot(slot_context, out_weight, preferred_element_type=jnp.float32)]
    dot_general x1, matrix products: 1.72 us -> 3.52 us  [per_device(): jnp.dot(pieces[0], weight_blocks[0], preferred_element_type=jnp.float32)]
  transfers between devices with their start and end apart: 17 -> 17, of which waited for: 6 -> 6; matrix products, arithmetic and copies ran while one was open for 34% -> 25% of each run, Pallas kernels for 24% -> 27%
where the time goes in v11:
time: 129 us
  matrix products  34.5 us (27%)
  Pallas kernels  34.5 us (27%)
  waiting for transfers between devices  30.6 us (24%)
  starting transfers between devices  19.1 us (15%)
  other arithmetic  7.26 us (6%)
  between operations  1.77 us (1%)
    pallas_call x4, Pallas kernels, prefill_attention_tile(): pl.pallas_call(functools.partial(_prefill_kernel, tq=tq), out_shape=jax.S...  34.5 us
    ppermute x1, waiting for transfers between devices, per_device(): lax.ppermute(held_weight, 'tensor', route(k, 0))  18.6 us
    dot_general x4, matrix products, per_device(): jnp.dot(token_block, qkv_weight, preferred_element_type=jnp.float32)  14 us
    ppermute x3, starting transfers between devices, per_device(): lax.ppermute(shifted_rows, 'dp', [(i, i ^ step) for i in range(dp_size)])  5.82 us
    ppermute x3, starting transfers between devices, per_device(): lax.ppermute(returned, 'dp', [(i, i ^ step) for i in range(dp_size)])  5.81 us
    ppermute x3, waiting for transfers between devices, per_device(): lax.ppermute(shifted_rows, 'dp', [(i, i ^ step) for i in range(dp_size)])  5.78 us
    dot_general x3, matrix products, per_device(): summed = summed + jnp.dot(piece, weight, preferred_element_type=jnp.float32)  5.3 us
    ppermute x3, waiting for transfers between devices, per_device(): lax.ppermute(context, 'tensor', route(k, flip))  4.06 us
  transfers between devices with their start and end apart: 17, of which 6 were waited for; matrix products, arithmetic and copies ran while one was open for 25% of the time, Pallas kernels for 27%

profile of v11, /device:TPU:0, one launch (start us, length us, event | category | flops | bytes accessed | tf_op | source)
XLA Modules:
  0.0 128.9 jit_solution(8413557537885744685)
XLA Ops:
  0.6 0.0 copy-start.1
  0.6 0.8 convert_element_type.96
  1.4 0.7 convert_element_type.97
  2.1 1.5 %convert_reduce_fusion = f32[256]{0:T(256)S(1)} fusion(bf16[256,2048]{1,0:T(8,128)(2,1)} %param.15), kind=kLoop, calls=%fused_computation.2 | loop fusion | flops 1048320 | bytes 1049600 | tf_op jit(solution)/shard_map/reduce_sum | solution.py:20
  3.6 1.6 %fusion.18 = f32[256]{0:T(256)S(1)} fusion(bf16[256,2048]{1,0:T(8,128)(2,1)} %param.15, f32[256]{0:T(256)S(1)} %broadcast_multiply_fusion), kind=kLoop, calls=%fused_computation.30 | loop fusion | flops 2096896 | bytes 1050624 | tf_op jit(solution)/shard_map/reduce_sum | solution.py:21
  5.3 1.4 %fusion.21 = bf16[256,2048]{1,0:T(8,128)(2,1)} fusion(bf16[256,2048]{1,0:T(8,128)(2,1)S(1)} %copy-done.1, f32[2048]{0:T(1024)S(1)} %convert_element_type.97, f32[2048]{0:T(1024)S(1)} %convert_element_type.96, f32[256]{0:T(256)S(1)} %add_rsqrt_fusion, f32[256]{0:T(256)S(1)} %broadcast_multiply_fusion), kind=kLoop, calls=%fused_computation.33 | loop fusion | flops 3145728 | bytes 2115584 | tf_op jit(solution)/shard_map/convert_element_type | solution.py:23
  6.7 2.9 %collective-permute-start = (bf16[256,2048]{1,0:T(8,128)(2,1)}, bf16[256,2048]{1,0:T(8,128)(2,1)}, u32[]{:S(2)}, u32[]{:S(2)}) collective-permute-start(bf16[256,2048]{1,0:T(8,128)(2,1)} %fusion.21), channel_id=1, source_target_pairs={{0,2},{1,3},{2,0},{3,1},{4,6},{5,7},{6,4},{7,5},{8,10},{9,11},{10,... | collective-permute-start | bytes 3145736 | tf_op jit(solution)/shard_map/ppermute | solution.py:247
  9.7 0.0 collective-permute-start.1
  9.7 1.5 %collective-permute-start.3 = (bf16[2,2048]{1,0:T(2,128)(2,1)S(1)}, bf16[2,2048]{1,0:T(2,128)(2,1)S(1)}, u32[]{:S(2)}, u32[]{:S(2)}) collective-permute-start(bf16[2,2048]{1,0:T(2,128)(2,1)S(1)} %copy-done.5), channel_id=1, source_target_pairs={{0,4},{4,0},{8,12},{12,8},{16,20},{20,16},{24,28},{28,24},{1,5},{5... | collective-permute-start | bytes 24584 | tf_op jit(solution)/shard_map/ppermute | solution.py:196
  11.2 0.2 collective-permute-start.14
  11.4 0.1 subtract_convert_fusion
  11.5 0.1 iota_compare_fusion
  11.6 0.2 fusion.60
  11.8 1.5 %collective-permute-done.3 = bf16[2,2048]{1,0:T(2,128)(2,1)S(1)} collective-permute-done((bf16[2,2048]{1,0:T(2,128)(2,1)S(1)}, bf16[2,2048]{1,0:T(2,128)(2,1)S(1)}, u32[]{:S(2)}, u32[]{:S(2)}) %collective-permute-start.3) | collective-permute-done | bytes 8224 | tf_op jit(solution)/shard_map/ppermute | solution.py:196
  13.3 1.6 %collective-permute-start.4 = (bf16[4,2048]{1,0:T(4,128)(2,1)S(1)}, bf16[4,2048]{1,0:T(4,128)(2,1)S(1)}, u32[]{:S(2)}, u32[]{:S(2)}) collective-permute-start(bf16[4,2048]{1,0:T(4,128)(2,1)S(1)} %pad_maximum_fusion.4), channel_id=1, source_target_pairs={{0,8},{4,12},{8,0},{12,4},{16,24},{20,28},{24,16},{28,20},{1,9},{5... | collective-permute-start | bytes 49160 | tf_op jit(solution)/shard_map/ppermute | solution.py:196
  15.0 2.1 %collective-permute-done.4 = bf16[4,2048]{1,0:T(4,128)(2,1)S(1)} collective-permute-done((bf16[4,2048]{1,0:T(4,128)(2,1)S(1)}, bf16[4,2048]{1,0:T(4,128)(2,1)S(1)}, u32[]{:S(2)}, u32[]{:S(2)}) %collective-permute-start.4) | collective-permute-done | bytes 16416 | tf_op jit(solution)/shard_map/ppermute | solution.py:196
  17.2 2.7 %collective-permute-start.5 = (bf16[8,2048]{1,0:T(8,128)(2,1)S(1)}, bf16[8,2048]{1,0:T(8,128)(2,1)S(1)}, u32[]{:S(2)}, u32[]{:S(2)}) collective-permute-start(bf16[8,2048]{1,0:T(8,128)(2,1)S(1)} %pad_maximum_fusion.1), channel_id=1, source_target_pairs={{0,16},{4,20},{8,24},{12,28},{16,0},{20,4},{24,8},{28,12},{1,17},{... | collective-permute-start | bytes 98312 | tf_op jit(solution)/shard_map/ppermute | solution.py:196
  19.9 2.1 %collective-permute-done.5 = bf16[8,2048]{1,0:T(8,128)(2,1)S(1)} collective-permute-done((bf16[8,2048]{1,0:T(8,128)(2,1)S(1)}, bf16[8,2048]{1,0:T(8,128)(2,1)S(1)}, u32[]{:S(2)}, u32[]{:S(2)}) %collective-permute-start.5) | collective-permute-done | bytes 32800 | tf_op jit(solution)/shard_map/ppermute | solution.py:196
  22.1 0.3 fusion.73
  22.4 0.2 multiply_reduce_fusion
  22.6 3.8 %fusion.16 = bf16[2,1536]{1,0:T(2,128)(2,1)S(1)} fusion(bf16[2048,1536]{1,0:T(8,128)(2,1)} %param.19, f32[2,2048]{1,0:T(2,128)S(1)} %get-tuple-element.30, f32[2]{0:T(128)S(1)} %add_rsqrt_fusion.1, f32[2]{0:T(128)S(1)} %broadcast_multiply_fusion.1, f32[2048]{0:T(1024)S(1)} %convert_element_type.97, f32[2048]{0:T(1024)S(1)} %convert_element_type.96, ...), kind=kOutput, calls=%fused_computation.26 | convolution fusion | flops 12609536 | bytes 6336528 | tf_op jit(solution)/shard_map/dot_general | solution.py:210
  26.4 0.0 copy-start.3
  26.4 0.1 fusion.50
  26.5 3.6 %fusion.74 = (f32[2,4]{1,0:T(2,128)S(1)}, f32[2,4,2048]{2,1,0:T(4,128)S(1)}) fusion(f32[2,2048]{1,0:T(2,128)S(1)} %subtract_convert_fusion, f32[4]{0:T(128)S(1)} %multiply_exponential_fusion.slopes_ref, bf16[2,2048,512]{2,1,0:T(8,128)(2,1)} %param.25, pred[512,4]{0,1:T(4,128)(4,1)S(1)} %iota_compare_fusion.1, bf16[2,512]{1,0:T(2,128)(2,1)S(1)} %bitcast.66, ...), kind=kOutput, calls=%fused_computation.131 | convolution fusion | flops 16863224 | bytes 4284464 | tf_op jit(solution)/shard_map/vmap()/dot_general | solution.py:144
  30.2 0.2 fusion.37
  30.4 0.1 broadcast_bitcast_fusion
  30.4 0.7 fusion.22
  31.2 2.3 %fusion.55 = f32[2,2048]{1,0:T(2,128)S(1)} fusion(bf16[512,2048]{1,0:T(8,128)(2,1)} %param.21, f32[2,512]{1,0:T(2,128)S(1)} %fusion.22, f32[1,2,4,128]{3,2,1,0:T(4,128)S(1)} %bitcast.65, f32[1,2,4,128]{3,2,1,0:T(4,128)S(1)} %broadcast_bitcast_fusion), kind=kOutput, calls=%fused_computation.90 | convolution fusion | flops 4197376 | bytes 2125824 | tf_op jit(solution)/shard_map/dot_general | solution.py:224
  33.5 0.0 collective-permute-start.6
  33.5 0.0 collective-permute-done
  33.5 0.5 collective-permute-start.2
  34.0 0.2 broadcast_in_dim.54
  34.2 0.0 copy-start.8
  34.2 3.1 %fusion.5 = bf16[1024,1536]{1,0:T(8,128)(2,1)S(1)} fusion(bf16[1024,1536]{1,0:T(8,128)(2,1)S(1)} %broadcast_in_dim.54, s32[]{:T(128)S(6)} %select_n.116, bf16[256,2048]{1,0:T(8,128)(2,1)} %fusion.21, bf16[2048,1536]{1,0:T(8,128)(2,1)S(1)} %bitcast.62, f32[1536]{0:T(1024)S(1)} %convert_element_type.99), kind=kOutput, calls=%fused_computation.13 | convolution fusion | flops 1611399168 | bytes 8134660 | tf_op jit(solution)/shard_map/dot_general | solution.py:259
  37.3 0.0 collective-permute-done.6
  37.3 1.0 collective-permute-start.7
  38.3 0.1 fusion.64
  39.1 2.2 %collective-permute-done.7 = f32[4,2048]{1,0:T(4,128)S(1)} collective-permute-done((f32[4,2048]{1,0:T(4,128)S(1)}, f32[4,2048]{1,0:T(4,128)S(1)}, u32[]{:S(2)}, u32[]{:S(2)}) %collective-permute-start.7) | collective-permute-done | bytes 32800 | tf_op jit(solution)/shard_map/ppermute | solution.py:229
  41.4 0.0 slice-start.2
  41.4 0.0 slice-start.3
  41.4 1.0 collective-permute-start.11
  42.4 0.0 collective-permute-done.1
  42.4 1.5 %collective-permute-start.8 = (bf16[2,2048]{1,0:T(2,128)(2,1)S(1)}, bf16[2,2048]{1,0:T(2,128)(2,1)S(1)}, u32[]{:S(2)}, u32[]{:S(2)}) collective-permute-start(bf16[2,2048]{1,0:T(2,128)(2,1)S(1)} %fusion.41), channel_id=1, source_target_pairs={{0,4},{4,0},{8,12},{12,8},{16,20},{20,16},{24,28},{28,24},{1,5},{5... | collective-permute-start | bytes 24584 | tf_op jit(solution)/shard_map/ppermute | solution.py:266
  44.0 4.9 %fusion.7 = bf16[1024,1536]{1,0:T(8,128)(2,1)S(1)} fusion(bf16[1024,1536]{1,0:T(8,128)(2,1)S(1)} %fusion.5, s32[]{:T(128)S(6)} %select_n.118, bf16[256,2048]{1,0:T(8,128)(2,1)} %collective-permute-done, bf16[2048,1536]{1,0:T(8,128)(2,1)} %param.19, f32[1536]{0:T(1024)S(1)} %convert_element_type.99), kind=kOutput, calls=%fused_computation.15 | convolution fusion | flops 1611399168 | bytes 8134660 | tf_op jit(solution)/shard_map/dot_general | solution.py:259
  48.9 1.6 %collective-permute-start.9 = (bf16[4,2048]{1,0:T(4,128)(2,1)S(1)}, bf16[4,2048]{1,0:T(4,128)(2,1)S(1)}, u32[]{:S(2)}, u32[]{:S(2)}) collective-permute-start(bf16[4,2048]{1,0:T(4,128)(2,1)S(1)} %pad_maximum_fusion.5), channel_id=1, source_target_pairs={{0,8},{4,12},{8,0},{12,4},{16,24},{20,28},{24,16},{28,20},{1,9},{5... | collective-permute-start | bytes 49160 | tf_op jit(solution)/shard_map/ppermute | solution.py:266
  50.6 3.0 %fusion.9 = bf16[1024,1536]{1,0:T(8,128)(2,1)S(1)} fusion(bf16[1024,1536]{1,0:T(8,128)(2,1)S(1)} %fusion.7, s32[]{:T(128)S(6)} %select_n.130, bf16[256,2048]{1,0:T(8,128)(2,1)} %collective-permute-done.1, bf16[2048,1536]{1,0:T(8,128)(2,1)S(1)} %bitcast.64, f32[1536]{0:T(1024)S(1)} %convert_element_type.99), kind=kOutput, calls=%fused_computation.17 | convolution fusion | flops 1611399168 | bytes 8134660 | tf_op jit(solution)/shard_map/dot_general | solution.py:259
  53.6 2.6 %collective-permute-start.10 = (bf16[8,2048]{1,0:T(8,128)(2,1)S(1)}, bf16[8,2048]{1,0:T(8,128)(2,1)S(1)}, u32[]{:S(2)}, u32[]{:S(2)}) collective-permute-start(bf16[8,2048]{1,0:T(8,128)(2,1)S(1)} %pad_maximum_fusion.3), channel_id=1, source_target_pairs={{0,16},{4,20},{8,24},{12,28},{16,0},{20,4},{24,8},{28,12},{1,17},{... | collective-permute-start | bytes 98312 | tf_op jit(solution)/shard_map/ppermute | solution.py:266
  56.3 3.0 %fusion.11.q_ref.kn_ref.vn_ref = bf16[1024,1536]{1,0:T(8,128)(2,1)S(1)} fusion(bf16[1024,1536]{1,0:T(8,128)(2,1)S(1)} %fusion.9, s32[]{:T(128)S(6)} %select_n.131, bf16[256,2048]{1,0:T(8,128)(2,1)} %collective-permute-done.2, bf16[2048,1536]{1,0:T(8,128)(2,1)S(1)} %bitcast.64, f32[1536]{0:T(1024)S(1)} %convert_element_type.99), kind=kOutput, calls=%fused_computation.19 | convolution fusion | flops 1611399168 | bytes 8134660 | tf_op jit(solution)/shard_map/dot_general | solution.py:259
  59.3 1.0 convolution_convert_fusion
  60.3 0.6 copy-done
  60.9 8.8 %shard_map.158 = bf16[256,512]{1,0:T(8,128)(2,1)} custom-call(s32[1]{0:T(128)S(6)} %copy.39.prefix_ref, f32[4]{0:T(128)} %copy-done.6, s32[1]{0:T(128)} %bitcast.tile_ref, bf16[1024,1536]{1,0:T(8,128)(2,1)} %copy-done, bf16[1024,1536]{1,0:T(8,128)(2,1)} %copy-done, bf16[1024,1536]{1,0:T(8,128)(2,1)} %copy-done, bf16[1024,512]{1,0:T(8,128)(2,1)} %bitcast.53, ...), custom_call_target="tpu_custom_call" | custom-call | flops 1073741824 | bytes 4718592 | tf_op jit(solution)/shard_map/pallas_call | solution.py:113
  69.7 18.6 %collective-permute-done.11 = bf16[512,2048]{1,0:T(8,128)(2,1)} collective-permute-done((bf16[512,2048]{1,0:T(8,128)(2,1)}, bf16[512,2048]{1,0:T(8,128)(2,1)}, u32[]{:S(2)}, u32[]{:S(2)}) %collective-permute-start.11) | collective-permute-done | bytes 2097184 | tf_op jit(solution)/shard_map/ppermute | solution.py:252
  88.3 8.6 %shard_map.160 = bf16[256,512]{1,0:T(8,128)(2,1)} custom-call(s32[1]{0:T(128)S(6)} %copy.39.prefix_ref, f32[4]{0:T(128)} %copy-done.6, s32[1]{0:T(128)} %bitcast.5.tile_ref, bf16[1024,1536]{1,0:T(8,128)(2,1)} %copy-done, bf16[1024,1536]{1,0:T(8,128)(2,1)} %copy-done, bf16[1024,1536]{1,0:T(8,128)(2,1)} %copy-done, bf16[1024,512]{1,0:T(8,128)(2,1)} %bitcast.54, ...), custom_call_target="tpu_custom_call" | custom-call | flops 1073741824 | bytes 4718592 | tf_op jit(solution)/shard_map/pallas_call | solution.py:113
  96.9 0.5 collective-permute-start.13
  97.4 8.6 %shard_map.159 = bf16[256,512]{1,0:T(8,128)(2,1)} custom-call(s32[1]{0:T(128)S(6)} %copy.39.prefix_ref, f32[4]{0:T(128)} %copy-done.6, s32[1]{0:T(128)} %bitcast.4.tile_ref, bf16[1024,1536]{1,0:T(8,128)(2,1)} %copy-done, bf16[1024,1536]{1,0:T(8,128)(2,1)} %copy-done, bf16[1024,1536]{1,0:T(8,128)(2,1)} %copy-done, bf16[1024,512]{1,0:T(8,128)(2,1)} %bitcast.55, ...), custom_call_target="tpu_custom_call" | custom-call | flops 1073741824 | bytes 4718592 | tf_op jit(solution)/shard_map/pallas_call | solution.py:113
  105.9 1.3 %collective-permute-start.12 = (bf16[256,512]{1,0:T(8,128)(2,1)}, bf16[256,512]{1,0:T(8,128)(2,1)S(1)}, u32[]{:S(2)}, u32[]{:S(2)}) collective-permute-start(bf16[256,512]{1,0:T(8,128)(2,1)} %shard_map.159), channel_id=1, source_target_pairs={{0,2},{1,3},{2,0},{3,1},{4,6},{5,7},{6,4},{7,5},{8,10},{9,11},{10,... | collective-permute-start | bytes 786440 | tf_op jit(solution)/shard_map/ppermute | solution.py:283
  107.3 8.6 %shard_map.161 = bf16[256,512]{1,0:T(8,128)(2,1)} custom-call(s32[1]{0:T(128)S(6)} %copy.39.prefix_ref, f32[4]{0:T(128)} %copy-done.6, s32[1]{0:T(128)} %bitcast.6.tile_ref, bf16[1024,1536]{1,0:T(8,128)(2,1)} %copy-done, bf16[1024,1536]{1,0:T(8,128)(2,1)} %copy-done, bf16[1024,1536]{1,0:T(8,128)(2,1)} %copy-done, bf16[1024,512]{1,0:T(8,128)(2,1)} %bitcast.56, ...), custom_call_target="tpu_custom_call" | custom-call | flops 1073741824 | bytes 4718592 | tf_op jit(solution)/shard_map/pallas_call | solution.py:113
  115.9 0.0 collective-permute-start.15
  115.9 2.3 %fusion.76 = f32[256,2048]{1,0:T(8,128)S(1)} fusion(bf16[256,512]{1,0:T(8,128)(2,1)S(1)} %collective-permute-done.13, bf16[512,2048]{1,0:T(8,128)(2,1)} %collective-permute-done.14), kind=kOutput, calls=%fused_computation.133 | convolution fusion | flops 536870912 | bytes 4456448 | tf_op jit(solution)/shard_map/dot_general | solution.py:290
  118.2 2.3 %fusion.75 = f32[256,2048]{1,0:T(8,128)S(1)} fusion(bf16[256,512]{1,0:T(8,128)(2,1)S(1)} %collective-permute-done.12, bf16[512,2048]{1,0:T(8,128)(2,1)} %collective-permute-done.11), kind=kOutput, calls=%fused_computation.132 | convolution fusion | flops 536870912 | bytes 4456448 | tf_op jit(solution)/shard_map/dot_general | solution.py:290
  120.5 0.0 copy-start.2
  120.5 4.1 %collective-permute-done.15 = bf16[256,512]{1,0:T(8,128)(2,1)S(1)} collective-permute-done((bf16[256,512]{1,0:T(8,128)(2,1)}, bf16[256,512]{1,0:T(8,128)(2,1)S(1)}, u32[]{:S(2)}, u32[]{:S(2)}) %collective-permute-start.15) | collective-permute-done | bytes 262176 | tf_op jit(solution)/shard_map/ppermute | solution.py:283
  124.6 0.7 fusion.77
  125.3 3.5 %fusion.3 = bf16[256,2048]{1,0:T(8,128)(2,1)} fusion(bf16[256,2048]{1,0:T(8,128)(2,1)S(1)} %copy-done.2, f32[256,2048]{1,0:T(8,128)S(1)} %fusion.77, f32[256,2048]{1,0:T(8,128)S(1)} %fusion.76, f32[256,2048]{1,0:T(8,128)S(1)} %fusion.75, bf16[256,512]{1,0:T(8,128)(2,1)S(1)} %copy-done.4, bf16[512,2048]{1,0:T(8,128)(2,1)} %param.21, ...), kind=kOutput, calls=%fused_computation.11 | convolution fusion | flops 540540928 | bytes 10756096 | tf_op jit(solution)/shard_map/dot_general | solution.py:288
  (60 shorter events, 0.5 us)
Async XLA Ops:
  0.6 4.6 %copy-start.1 = (bf16[256,2048]{1,0:T(8,128)(2,1)S(1)}, bf16[256,2048]{1,0:T(8,128)(2,1)}, u32[]{:S(2)}) copy-start(bf16[256,2048]{1,0:T(8,128)(2,1)} %param.15) | copy-start | bytes 3145732
  2.1 7.6 %copy-start.5 = (bf16[2,2048]{1,0:T(2,128)(2,1)S(1)}, bf16[2,2048]{1,0:T(2,128)(2,1)}, u32[]{:S(2)}) copy-start(bf16[2,2048]{1,0:T(2,128)(2,1)} %param.16) | copy-start | bytes 24580
  2.1 9.3 %copy-start.9 = (s32[2]{0:T(128)S(1)}, s32[2]{0:T(128)}, u32[]{:S(2)}) copy-start(s32[2]{0:T(128)} %param.28) | copy-start | bytes 28
  2.1 9.5 %copy-start.10 = (s32[16]{0:T(128)S(1)}, s32[16]{0:T(128)}, u32[]{:S(2)}) copy-start(s32[16]{0:T(128)} %param.29) | copy-start | bytes 196
  2.1 17.8 %copy-start.7 = (bf16[1536]{0:T(1024)(128)(2,1)S(1)}, bf16[1536]{0:T(1024)(128)(2,1)}, u32[]{:S(2)}) copy-start(bf16[1536]{0:T(1024)(128)(2,1)} %param.20) | copy-start | bytes 9220
  6.7 26.7 %collective-permute-start = (bf16[256,2048]{1,0:T(8,128)(2,1)}, bf16[256,2048]{1,0:T(8,128)(2,1)}, u32[]{:S(2)}, u32[]{:S(2)}) collective-permute-start(bf16[256,2048]{1,0:T(8,128)(2,1)} %fusion.21), channel_id=1, source_target_pairs={{0,2},{1,3},{2,0},{3,1},{4,6},{5,7},{6,4},{7,5},{8,10},{9,11},{10,... | collective-permute-start | bytes 3145736 | tf_op jit(solution)/shard_map/ppermute | solution.py:247
  9.7 32.8 %collective-permute-start.1 = (bf16[256,2048]{1,0:T(8,128)(2,1)}, bf16[256,2048]{1,0:T(8,128)(2,1)}, u32[]{:S(2)}, u32[]{:S(2)}) collective-permute-start(bf16[256,2048]{1,0:T(8,128)(2,1)} %fusion.21), channel_id=1, source_target_pairs={{0,1},{1,0},{2,3},{3,2},{4,5},{5,4},{6,7},{7,6},{8,9},{9,8},{10,11... | collective-permute-start | bytes 3145736 | tf_op jit(solution)/shard_map/ppermute | solution.py:250
  9.7 3.7 %collective-permute-start.3 = (bf16[2,2048]{1,0:T(2,128)(2,1)S(1)}, bf16[2,2048]{1,0:T(2,128)(2,1)S(1)}, u32[]{:S(2)}, u32[]{:S(2)}) collective-permute-start(bf16[2,2048]{1,0:T(2,128)(2,1)S(1)} %copy-done.5), channel_id=1, source_target_pairs={{0,4},{4,0},{8,12},{12,8},{16,20},{20,16},{24,28},{28,24},{1,5},{5... | collective-permute-start | bytes 24584 | tf_op jit(solution)/shard_map/ppermute | solution.py:196
  11.2 104.7 %collective-permute-start.14 = (bf16[512,2048]{1,0:T(8,128)(2,1)}, bf16[512,2048]{1,0:T(8,128)(2,1)}, u32[]{:S(2)}, u32[]{:S(2)}) collective-permute-start(bf16[512,2048]{1,0:T(8,128)(2,1)} %param.21), channel_id=1, source_target_pairs={{0,1},{1,0},{2,3},{3,2},{4,5},{5,4},{6,7},{7,6},{8,9},{9,8},{10,11... | collective-permute-start | bytes 6291464 | tf_op jit(solution)/shard_map/ppermute | solution.py:287
  13.3 3.8 %collective-permute-start.4 = (bf16[4,2048]{1,0:T(4,128)(2,1)S(1)}, bf16[4,2048]{1,0:T(4,128)(2,1)S(1)}, u32[]{:S(2)}, u32[]{:S(2)}) collective-permute-start(bf16[4,2048]{1,0:T(4,128)(2,1)S(1)} %pad_maximum_fusion.4), channel_id=1, source_target_pairs={{0,8},{4,12},{8,0},{12,4},{16,24},{20,28},{24,16},{28,20},{1,9},{5... | collective-permute-start | bytes 49160 | tf_op jit(solution)/shard_map/ppermute | solution.py:196
  17.2 4.9 %collective-permute-start.5 = (bf16[8,2048]{1,0:T(8,128)(2,1)S(1)}, bf16[8,2048]{1,0:T(8,128)(2,1)S(1)}, u32[]{:S(2)}, u32[]{:S(2)}) collective-permute-start(bf16[8,2048]{1,0:T(8,128)(2,1)S(1)} %pad_maximum_fusion.1), channel_id=1, source_target_pairs={{0,16},{4,20},{8,24},{12,28},{16,0},{20,4},{24,8},{28,12},{1,17},{... | collective-permute-start | bytes 98312 | tf_op jit(solution)/shard_map/ppermute | solution.py:196
  19.8 6.7 %copy-start.6 = (f32[4]{0:T(128)}, f32[4]{0:T(128)S(1)}, u32[]{:S(2)}) copy-start(f32[4]{0:T(128)S(1)} %multiply_exponential_fusion.slopes_ref) | copy-start | bytes 52
  26.4 4.1 %copy-start.3 = (bf16[2,2048,512]{2,1,0:T(8,128)(2,1)S(1)}, bf16[2,2048,512]{2,1,0:T(8,128)(2,1)}, u32[]{:S(2)}) copy-start(bf16[2,2048,512]{2,1,0:T(8,128)(2,1)} %param.26) | copy-start | bytes 12582916
  26.5 7.6 %slice-start = ((s8[6291456]{0:T(1024)(128)(4,1)}), s8[2097152]{0:T(1024)(128)(4,1)S(1)}, s32[]{:S(2)}) async-start(s8[6291456]{0:T(1024)(128)(4,1)} %bitcast.61), calls=%async_computation | async-start | bytes 4194304
  30.4 3.8 %slice-start.1 = ((s8[6291456]{0:T(1024)(128)(4,1)}), s8[4194304]{0:T(1024)(128)(4,1)S(1)}, s32[]{:S(2)}) async-start(s8[6291456]{0:T(1024)(128)(4,1)} %bitcast.61), calls=%async_computation.1 | async-start | bytes 8388608
  33.5 3.8 %collective-permute-start.6 = (f32[2,2048]{1,0:T(2,128)S(1)}, f32[2,2048]{1,0:T(2,128)S(1)}, u32[]{:S(2)}, u32[]{:S(2)}) collective-permute-start(f32[2,2048]{1,0:T(2,128)S(1)} %fusion.55), channel_id=1, source_target_pairs={{0,1},{1,0},{2,3},{3,2},{4,5},{5,4},{6,7},{7,6},{8,9},{9,8},{10,11... | collective-permute-start | bytes 49160 | tf_op jit(solution)/shard_map/ppermute | solution.py:229
  33.5 9.0 %collective-permute-start.2 = (bf16[256,2048]{1,0:T(8,128)(2,1)}, bf16[256,2048]{1,0:T(8,128)(2,1)}, u32[]{:S(2)}, u32[]{:S(2)}) collective-permute-start(bf16[256,2048]{1,0:T(8,128)(2,1)} %collective-permute-done), channel_id=1, source_target_pairs={{0,1},{1,0},{2,3},{3,2},{4,5},{5,4},{6,7},{7,6},{8,9},{9,8},{10,11... | collective-permute-start | bytes 3145736 | tf_op jit(solution)/shard_map/ppermute | solution.py:250
  34.2 4.2 %copy-start.8 = (bf16[2048]{0:T(1024)(128)(2,1)S(1)}, bf16[2048]{0:T(1024)(128)(2,1)}, u32[]{:S(2)}) copy-start(bf16[2048]{0:T(1024)(128)(2,1)} %param.22) | copy-start | bytes 12292
  37.3 4.0 %collective-permute-start.7 = (f32[4,2048]{1,0:T(4,128)S(1)}, f32[4,2048]{1,0:T(4,128)S(1)}, u32[]{:S(2)}, u32[]{:S(2)}) collective-permute-start(f32[4,2048]{1,0:T(4,128)S(1)} %pad_maximum_fusion.2), channel_id=1, source_target_pairs={{0,2},{1,3},{2,0},{3,1},{4,6},{5,7},{6,4},{7,5},{8,10},{9,11},{10,... | collective-permute-start | bytes 98312 | tf_op jit(solution)/shard_map/ppermute | solution.py:229
  41.4 9.2 %slice-start.2 = ((s8[6291456]{0:T(1024)(128)(4,1)}), s8[4194304]{0:T(1024)(128)(4,1)S(1)}, s32[]{:S(2)}) async-start(s8[6291456]{0:T(1024)(128)(4,1)} %bitcast.63), calls=%async_computation.2 | async-start | bytes 8388608
  41.4 9.1 %slice-start.3 = ((s8[6291456]{0:T(1024)(128)(4,1)}), s8[2097152]{0:T(1024)(128)(4,1)S(1)}, s32[]{:S(2)}) async-start(s8[6291456]{0:T(1024)(128)(4,1)} %bitcast.63), calls=%async_computation.3 | async-start | bytes 4194304
  41.4 46.8 %collective-permute-start.11 = (bf16[512,2048]{1,0:T(8,128)(2,1)}, bf16[512,2048]{1,0:T(8,128)(2,1)}, u32[]{:S(2)}, u32[]{:S(2)}) collective-permute-start(bf16[512,2048]{1,0:T(8,128)(2,1)} %param.21), channel_id=1, source_target_pairs={{0,2},{1,3},{2,0},{3,1},{4,6},{5,7},{6,4},{7,5},{8,10},{9,11},{10,... | collective-permute-start | bytes 6291464 | tf_op jit(solution)/shard_map/ppermute | solution.py:252
  42.4 6.4 %collective-permute-start.8 = (bf16[2,2048]{1,0:T(2,128)(2,1)S(1)}, bf16[2,2048]{1,0:T(2,128)(2,1)S(1)}, u32[]{:S(2)}, u32[]{:S(2)}) collective-permute-start(bf16[2,2048]{1,0:T(2,128)(2,1)S(1)} %fusion.41), channel_id=1, source_target_pairs={{0,4},{4,0},{8,12},{12,8},{16,20},{20,16},{24,28},{28,24},{1,5},{5... | collective-permute-start | bytes 24584 | tf_op jit(solution)/shard_map/ppermute | solution.py:266
  48.9 4.7 %collective-permute-start.9 = (bf16[4,2048]{1,0:T(4,128)(2,1)S(1)}, bf16[4,2048]{1,0:T(4,128)(2,1)S(1)}, u32[]{:S(2)}, u32[]{:S(2)}) collective-permute-start(bf16[4,2048]{1,0:T(4,128)(2,1)S(1)} %pad_maximum_fusion.5), channel_id=1, source_target_pairs={{0,8},{4,12},{8,0},{12,4},{16,24},{20,28},{24,16},{28,20},{1,9},{5... | collective-permute-start | bytes 49160 | tf_op jit(solution)/shard_map/ppermute | solution.py:266
  53.6 5.7 %collective-permute-start.10 = (bf16[8,2048]{1,0:T(8,128)(2,1)S(1)}, bf16[8,2048]{1,0:T(8,128)(2,1)S(1)}, u32[]{:S(2)}, u32[]{:S(2)}) collective-permute-start(bf16[8,2048]{1,0:T(8,128)(2,1)S(1)} %pad_maximum_fusion.3), channel_id=1, source_target_pairs={{0,16},{4,20},{8,24},{12,28},{16,0},{20,4},{24,8},{28,12},{1,17},{... | collective-permute-start | bytes 98312 | tf_op jit(solution)/shard_map/ppermute | solution.py:266
  59.3 1.6 %copy-start = (bf16[1024,1536]{1,0:T(8,128)(2,1)}, bf16[1024,1536]{1,0:T(8,128)(2,1)S(1)}, u32[]{:S(2)}) copy-start(bf16[1024,1536]{1,0:T(8,128)(2,1)S(1)} %fusion.11.q_ref.kn_ref.vn_ref) | copy-start | bytes 9437188
  88.3 36.3 %collective-permute-start.16 = (bf16[512,2048]{1,0:T(8,128)(2,1)}, bf16[512,2048]{1,0:T(8,128)(2,1)S(1)}, u32[]{:S(2)}, u32[]{:S(2)}) collective-permute-start(bf16[512,2048]{1,0:T(8,128)(2,1)} %collective-permute-done.11), channel_id=1, source_target_pairs={{0,1},{1,0},{2,3},{3,2},{4,5},{5,4},{6,7},{7,6},{8,9},{9,8},{10,11... | collective-permute-start | bytes 6291464 | tf_op jit(solution)/shard_map/ppermute | solution.py:287
  96.9 19.0 %collective-permute-start.13 = (bf16[256,512]{1,0:T(8,128)(2,1)}, bf16[256,512]{1,0:T(8,128)(2,1)S(1)}, u32[]{:S(2)}, u32[]{:S(2)}) collective-permute-start(bf16[256,512]{1,0:T(8,128)(2,1)} %shard_map.160), channel_id=1, source_target_pairs={{0,1},{1,0},{2,3},{3,2},{4,5},{5,4},{6,7},{7,6},{8,9},{9,8},{10,11... | collective-permute-start | bytes 786440 | tf_op jit(solution)/shard_map/ppermute | solution.py:283
  105.9 12.3 %collective-permute-start.12 = (bf16[256,512]{1,0:T(8,128)(2,1)}, bf16[256,512]{1,0:T(8,128)(2,1)S(1)}, u32[]{:S(2)}, u32[]{:S(2)}) collective-permute-start(bf16[256,512]{1,0:T(8,128)(2,1)} %shard_map.159), channel_id=1, source_target_pairs={{0,2},{1,3},{2,0},{3,1},{4,6},{5,7},{6,4},{7,5},{8,10},{9,11},{10,... | collective-permute-start | bytes 786440 | tf_op jit(solution)/shard_map/ppermute | solution.py:283
  115.9 8.7 %collective-permute-start.15 = (bf16[256,512]{1,0:T(8,128)(2,1)}, bf16[256,512]{1,0:T(8,128)(2,1)S(1)}, u32[]{:S(2)}, u32[]{:S(2)}) collective-permute-start(bf16[256,512]{1,0:T(8,128)(2,1)} %shard_map.161), channel_id=1, source_target_pairs={{0,3},{1,2},{2,1},{3,0},{4,7},{5,6},{6,5},{7,4},{8,11},{9,10},{10,... | collective-permute-start | bytes 786440 | tf_op jit(solution)/shard_map/ppermute | solution.py:283
  120.5 4.8 %copy-start.2 = (bf16[256,2048]{1,0:T(8,128)(2,1)S(1)}, bf16[256,2048]{1,0:T(8,128)(2,1)}, u32[]{:S(2)}) copy-start(bf16[256,2048]{1,0:T(8,128)(2,1)} %param.15) | copy-start | bytes 3145732
  120.5 4.8 %copy-start.4 = (bf16[256,512]{1,0:T(8,128)(2,1)S(1)}, bf16[256,512]{1,0:T(8,128)(2,1)}, u32[]{:S(2)}) copy-start(bf16[256,512]{1,0:T(8,128)(2,1)} %shard_map.158) | copy-start | bytes 786436

commit v12 on v10

--- a/solution.py
+++ b/solution.py
@@ -80,29 +80,34 @@
     prefix = prefix_ref[0]
     slope = slopes_ref[h]
     factor = 1.0 / math.sqrt(q_ref.shape[-1])
-    q = q_ref[...]
     dims = (((1,), (1,)), ((), ()))
     cache_size = kc_ref.shape[0]
-    group = kn_ref.shape[0]
-    q_tok = i * tq + lax.broadcasted_iota(jnp.int32, (tq, 1), 0)
-    q_pos = prefix + q_tok
-    c_pos = lax.broadcasted_iota(jnp.int32, (1, cache_size), 1)
-    k_tok = lax.broadcasted_iota(jnp.int32, (1, group), 1)
-    s_c = lax.dot_general(q, kc_ref[...], dims, preferred_element_type=jnp.float32) * factor
-    s_c = s_c - slope * (q_pos - c_pos).astype(jnp.float32)
-    s_c = jnp.where(c_pos < prefix, s_c, -jnp.inf)
-    s_n = lax.dot_general(q, kn_ref[...], dims, preferred_element_type=jnp.float32) * factor
-    s_n = s_n - slope * (q_tok - k_tok).astype(jnp.float32)
-    s_n = jnp.where(k_tok <= q_tok, s_n, -jnp.inf)
-    m = jnp.maximum(jnp.max(s_c, axis=-1, keepdims=True), jnp.max(s_n, axis=-1, keepdims=True))
-    e_c = jnp.exp(s_c - m)
-    e_n = jnp.exp(s_n - m)
-    l = jnp.sum(e_c, axis=-1, keepdims=True) + jnp.sum(e_n, axis=-1, keepdims=True)
-    p_c = (e_c / l).astype(jnp.bfloat16)
-    p_n = (e_n / l).astype(jnp.bfloat16)
-    ctx = jnp.dot(p_c, vc_ref[...], preferred_element_type=jnp.float32)
-    ctx = ctx + jnp.dot(p_n, vn_ref[...], preferred_element_type=jnp.float32)
-    o_ref[...] = ctx.astype(o_ref.dtype)
+
+    def tile(last, width):
+        q = q_ref[...]
+        q_tok = last * tq + lax.broadcasted_iota(jnp.int32, (tq, 1), 0)
+        q_pos = prefix + q_tok
+        c_pos = lax.broadcasted_iota(jnp.int32, (1, cache_size), 1)
+        k_tok = lax.broadcasted_iota(jnp.int32, (1, width), 1)
+        s_c = lax.dot_general(q, kc_ref[...], dims, preferred_element_type=jnp.float32) * factor
+        s_c = s_c - slope * (q_pos - c_pos).astype(jnp.float32)
+        s_c = jnp.where(c_pos < prefix, s_c, -jnp.inf)
+        s_n = lax.dot_general(q, kn_ref[:width, :], dims, preferred_element_type=jnp.float32) * factor
+        s_n = s_n - slope * (q_tok - k_tok).astype(jnp.float32)
+        s_n = jnp.where(k_tok <= q_tok, s_n, -jnp.inf)
+        m = jnp.maximum(jnp.max(s_c, axis=-1, keepdims=True), jnp.max(s_n, axis=-1, keepdims=True))
+        e_c = jnp.exp(s_c - m)
+        e_n = jnp.exp(s_n - m)
+        l = jnp.sum(e_c, axis=-1, keepdims=True) + jnp.sum(e_n, axis=-1, keepdims=True)
+        p_c = (e_c / l).astype(jnp.bfloat16)
+        p_n = (e_n / l).astype(jnp.bfloat16)
+        ctx = jnp.dot(p_c, vc_ref[...], preferred_element_type=jnp.float32)
+        ctx = ctx + jnp.dot(p_n, vn_ref[:width, :], preferred_element_type=jnp.float32)
+        o_ref[...] = ctx.astype(o_ref.dtype)
+
+    for last in range(kn_ref.shape[0] // tq):
+        pl.when(i == last)(functools.partial(tile, last, (last + 1) * tq))
+
 
 def prefill_attention_kernel(merged, cache_keys, cache_values, prefix, slopes, head_size, tq=256):
     group = merged.shape[0]
@@ -249,15 +254,13 @@
     sibling_tokens = [lax.ppermute(t, "tensor", route(0, 1)) for t in same_core_tokens]
     sibling_tokens, slot_rows = lax.optimization_barrier((sibling_tokens, slot_rows))
     across_chips = [lax.ppermute(held_weight, "tensor", route(k, 0)) for k in range(1, chips)]
-    bias_row = qkv_bias.astype(jnp.float32)
-    merged_rows = jnp.zeros((tensor_size * block, qkv_weight.shape[1]), jnp.bfloat16)
+    tokens = jnp.zeros((tensor_size * block, normed.shape[1]), normed.dtype)
     for flip, token_blocks in ((0, same_core_tokens), (1, sibling_tokens)):
         for k, token_block in enumerate(token_blocks):
             source = ((chip - k) % chips) * 2 + (core ^ flip)
-            projected = (
-                jnp.dot(token_block, qkv_weight, preferred_element_type=jnp.float32) + bias_row
-            ).astype(jnp.bfloat16)
-            merged_rows = lax.dynamic_update_slice_in_dim(merged_rows, projected, source * block, 0)
+            tokens = lax.dynamic_update_slice_in_dim(tokens, token_block, source * block, 0)
+    product = jnp.dot(tokens, qkv_weight, preferred_element_type=jnp.float32)
+    merged_rows = (product + qkv_bias.astype(jnp.float32)).astype(jnp.bfloat16)
     returned = slot_rows
     step = 1
     while step < dp_size:

time: 115 us -> 113 us (0.983)
  local copies, waits for them, and re-layouts: 4.9 us -> 14.8 us
  matrix products: 37 us -> 30.6 us
  Pallas kernels: 27.3 us -> 23.2 us
  starting transfers between devices: 20.9 us -> 18.8 us
    dynamic_update_slice x0 -> x4, local copies, waits for them, and re-layouts: none -> 9.34 us  [per_device(): lax.dynamic_update_slice_in_dim(tokens, token_block, source * block, 0)]
    dot_general x4 -> x1, matrix products: 17.6 us -> 11.2 us  [per_device(): product = jnp.dot(tokens, qkv_weight, preferred_element_type=jnp.float32)]
    pallas_call x1, Pallas kernels: 27.3 us -> 23.2 us  [prefill_attention_kernel(): pl.pallas_call(functools.partial(_prefill_kernel, tq=tq), out_shape=jax.S...]
    ppermute x2, waiting for transfers between devices: 1.35 us -> 2.97 us  [per_device(): lax.ppermute(partials, 'tensor', [(i, i ^ step) for i in range(tensor_siz...]
    ppermute x2, starting transfers between devices: 1.84 us -> 0.22 us  [per_device(): lax.ppermute(partials, 'tensor', [(i, i ^ step) for i in range(tensor_siz...]
    ppermute x1, starting transfers between devices: 1.84 us -> 0.22 us  [per_device(): lax.ppermute(held_weight, 'tensor', route(k, 0))]
  transfers between devices with their start and end apart: 17 -> 17, of which waited for: 6 -> 5; matrix products, arithmetic and copies ran while one was open for 34% -> 38% of each run, Pallas kernels for 24% -> 21%
where the time goes in v12:
time: 113 us
  matrix products  30.6 us (27%)
  Pallas kernels  23.2 us (21%)
  starting transfers between devices  18.8 us (17%)
  waiting for transfers between devices  16.4 us (15%)
  local copies, waits for them, and re-layouts  14.8 us (13%)
  other arithmetic  7.25 us (6%)
  between operations  1.62 us (1%)
    pallas_call x1, Pallas kernels, prefill_attention_kernel(): pl.pallas_call(functools.partial(_prefill_kernel, tq=tq), out_shape=jax.S...  23.2 us
    dot_general x1, matrix products, per_device(): product = jnp.dot(tokens, qkv_weight, preferred_element_type=jnp.float32)  11.2 us
    dynamic_update_slice x4, local copies, waits for them, and re-layouts, per_device(): lax.dynamic_update_slice_in_dim(tokens, token_block, source * block, 0)  9.34 us
    dot_general x3, matrix products, per_device(): summed = summed + jnp.dot(piece, weight, preferred_element_type=jnp.float32)  8.12 us
    ppermute x3, waiting for transfers between devices, per_device(): pieces.append(lax.ppermute(outgoing, 'tensor', route(k, flip)))  7.34 us
    ppermute x3, starting transfers between devices, per_device(): lax.ppermute(returned, 'dp', [(i, i ^ step) for i in range(dp_size)])  6.38 us
    ppermute x3, waiting for transfers between devices, per_device(): lax.ppermute(shifted_rows, 'dp', [(i, i ^ step) for i in range(dp_size)])  6.02 us
    ppermute x3, starting transfers between devices, per_device(): lax.ppermute(shifted_rows, 'dp', [(i, i ^ step) for i in range(dp_size)])  5.82 us
  transfers between devices with their start and end apart: 17, of which 5 were waited for; matrix products, arithmetic and copies ran while one was open for 38% of the time, Pallas kernels for 21%

profile of v12, /device:TPU:0, one launch (start us, length us, event | category | flops | bytes accessed | tf_op | source)
XLA Modules:
  0.0 112.6 jit_solution(9703877777690806206)
XLA Ops:
  0.6 0.0 copy-start
  0.6 0.8 convert_element_type.88
  1.4 0.7 convert_element_type.87
  2.1 1.5 %convert_reduce_fusion = f32[256]{0:T(256)S(1)} fusion(bf16[256,2048]{1,0:T(8,128)(2,1)} %param.15), kind=kLoop, calls=%fused_computation.3 | loop fusion | flops 1048320 | bytes 1049600 | tf_op jit(solution)/shard_map/reduce_sum | solution.py:20
  3.6 1.6 %fusion.9 = f32[256]{0:T(256)S(1)} fusion(bf16[256,2048]{1,0:T(8,128)(2,1)} %param.15, f32[256]{0:T(256)S(1)} %broadcast_multiply_fusion), kind=kLoop, calls=%fused_computation.19 | loop fusion | flops 2096896 | bytes 1050624 | tf_op jit(solution)/shard_map/reduce_sum | solution.py:21
  5.3 1.4 %fusion.12 = bf16[256,2048]{1,0:T(8,128)(2,1)} fusion(bf16[256,2048]{1,0:T(8,128)(2,1)S(1)} %copy-done, f32[2048]{0:T(1024)S(1)} %convert_element_type.88, f32[2048]{0:T(1024)S(1)} %convert_element_type.87, f32[256]{0:T(256)S(1)} %add_rsqrt_fusion, f32[256]{0:T(256)S(1)} %broadcast_multiply_fusion), kind=kLoop, calls=%fused_computation.22 | loop fusion | flops 3145728 | bytes 2115584 | tf_op jit(solution)/shard_map/convert_element_type | solution.py:23
  6.7 2.9 %collective-permute-start = (bf16[256,2048]{1,0:T(8,128)(2,1)}, bf16[256,2048]{1,0:T(8,128)(2,1)}, u32[]{:S(2)}, u32[]{:S(2)}) collective-permute-start(bf16[256,2048]{1,0:T(8,128)(2,1)} %fusion.12), channel_id=1, source_target_pairs={{0,2},{1,3},{2,0},{3,1},{4,6},{5,7},{6,4},{7,5},{8,10},{9,11},{10,... | collective-permute-start | bytes 3145736 | tf_op jit(solution)/shard_map/ppermute | solution.py:251
  9.7 0.0 collective-permute-start.1
  9.7 1.5 %collective-permute-start.3 = (bf16[2,2048]{1,0:T(2,128)(2,1)S(1)}, bf16[2,2048]{1,0:T(2,128)(2,1)S(1)}, u32[]{:S(2)}, u32[]{:S(2)}) collective-permute-start(bf16[2,2048]{1,0:T(2,128)(2,1)S(1)} %copy-done.3), channel_id=1, source_target_pairs={{0,4},{4,0},{8,12},{12,8},{16,20},{20,16},{24,28},{28,24},{1,5},{5... | collective-permute-start | bytes 24584 | tf_op jit(solution)/shard_map/ppermute | solution.py:200
  11.2 0.1 subtract_convert_fusion
  11.3 0.1 iota_compare_fusion
  11.4 0.2 fusion.53
  11.6 1.7 %collective-permute-done.3 = bf16[2,2048]{1,0:T(2,128)(2,1)S(1)} collective-permute-done((bf16[2,2048]{1,0:T(2,128)(2,1)S(1)}, bf16[2,2048]{1,0:T(2,128)(2,1)S(1)}, u32[]{:S(2)}, u32[]{:S(2)}) %collective-permute-start.3) | collective-permute-done | bytes 8224 | tf_op jit(solution)/shard_map/ppermute | solution.py:200
  13.3 1.6 %collective-permute-start.4 = (bf16[4,2048]{1,0:T(4,128)(2,1)S(1)}, bf16[4,2048]{1,0:T(4,128)(2,1)S(1)}, u32[]{:S(2)}, u32[]{:S(2)}) collective-permute-start(bf16[4,2048]{1,0:T(4,128)(2,1)S(1)} %pad_maximum_fusion.4), channel_id=1, source_target_pairs={{0,8},{4,12},{8,0},{12,4},{16,24},{20,28},{24,16},{28,20},{1,9},{5... | collective-permute-start | bytes 49160 | tf_op jit(solution)/shard_map/ppermute | solution.py:200
  15.0 2.1 %collective-permute-done.4 = bf16[4,2048]{1,0:T(4,128)(2,1)S(1)} collective-permute-done((bf16[4,2048]{1,0:T(4,128)(2,1)S(1)}, bf16[4,2048]{1,0:T(4,128)(2,1)S(1)}, u32[]{:S(2)}, u32[]{:S(2)}) %collective-permute-start.4) | collective-permute-done | bytes 16416 | tf_op jit(solution)/shard_map/ppermute | solution.py:200
  17.2 2.7 %collective-permute-start.5 = (bf16[8,2048]{1,0:T(8,128)(2,1)S(1)}, bf16[8,2048]{1,0:T(8,128)(2,1)S(1)}, u32[]{:S(2)}, u32[]{:S(2)}) collective-permute-start(bf16[8,2048]{1,0:T(8,128)(2,1)S(1)} %pad_maximum_fusion.1), channel_id=1, source_target_pairs={{0,16},{4,20},{8,24},{12,28},{16,0},{20,4},{24,8},{28,12},{1,17},{... | collective-permute-start | bytes 98312 | tf_op jit(solution)/shard_map/ppermute | solution.py:200
  19.9 2.1 %collective-permute-done.5 = bf16[8,2048]{1,0:T(8,128)(2,1)S(1)} collective-permute-done((bf16[8,2048]{1,0:T(8,128)(2,1)S(1)}, bf16[8,2048]{1,0:T(8,128)(2,1)S(1)}, u32[]{:S(2)}, u32[]{:S(2)}) %collective-permute-start.5) | collective-permute-done | bytes 32800 | tf_op jit(solution)/shard_map/ppermute | solution.py:200
  22.1 0.3 fusion.66
  22.4 0.2 multiply_reduce_fusion
  22.6 3.8 %fusion.7 = bf16[2,1536]{1,0:T(2,128)(2,1)S(1)} fusion(bf16[2048,1536]{1,0:T(8,128)(2,1)} %param.19, f32[2,2048]{1,0:T(2,128)S(1)} %get-tuple-element.33, f32[2]{0:T(128)S(1)} %add_rsqrt_fusion.1, f32[2]{0:T(128)S(1)} %broadcast_multiply_fusion.1, f32[2048]{0:T(1024)S(1)} %convert_element_type.88, f32[2048]{0:T(1024)S(1)} %convert_element_type.87, ...), kind=kOutput, calls=%fused_computation.15 | convolution fusion | flops 12609536 | bytes 6336528 | tf_op jit(solution)/shard_map/dot_general | solution.py:214
  26.4 0.1 fusion.42
  26.5 3.6 %fusion.67 = (f32[2,4]{1,0:T(2,128)S(1)}, f32[2,4,2048]{2,1,0:T(4,128)S(1)}) fusion(f32[2,2048]{1,0:T(2,128)S(1)} %subtract_convert_fusion, f32[4]{0:T(128)S(1)} %multiply_exponential_fusion.slopes_ref, bf16[2,2048,512]{2,1,0:T(8,128)(2,1)} %param.25, pred[512,4]{0,1:T(4,128)(4,1)S(1)} %iota_compare_fusion.1, bf16[2,512]{1,0:T(2,128)(2,1)S(1)} %bitcast.43, ...), kind=kOutput, calls=%fused_computation.129 | convolution fusion | flops 16863224 | bytes 4284464 | tf_op jit(solution)/shard_map/vmap()/dot_general | solution.py:148
  30.1 0.2 fusion.29
  30.4 0.1 broadcast_bitcast_fusion
  30.4 0.7 fusion.13
  31.2 0.9 copy-done.1
  32.0 0.4 fusion.48
  32.4 0.0 collective-permute-start.6
  32.4 2.5 %broadcast_in_dim.54 = bf16[1024,2048]{1,0:T(8,128)(2,1)} broadcast(bf16[]{:T(256)} %constant.123.clone.1), dimensions={} | broadcast | bytes 4194306 | tf_op jit(solution)/shard_map/broadcast_in_dim | solution.py:257
  34.9 2.3 %constant_dynamic-update-slice_fusion.3 = bf16[1024,2048]{1,0:T(8,128)(2,1)} fusion(bf16[1024,2048]{1,0:T(8,128)(2,1)} %broadcast_in_dim.54, bf16[256,2048]{1,0:T(8,128)(2,1)} %fusion.12, s32[]{:T(128)S(6)} %select_n.124), kind=kLoop, calls=%fused_computation.85 | loop fusion | bytes 2097156 | tf_op jit(solution)/shard_map/dynamic_update_slice | solution.py:261
  37.2 0.0 collective-permute-done
  37.2 0.6 collective-permute-start.2
  37.8 0.0 collective-permute-done.6
  37.8 0.2 collective-permute-start.7
  38.0 0.1 fusion.57
  38.8 3.0 %collective-permute-done.7 = f32[4,2048]{1,0:T(4,128)S(1)} collective-permute-done((f32[4,2048]{1,0:T(4,128)S(1)}, f32[4,2048]{1,0:T(4,128)S(1)}, u32[]{:S(2)}, u32[]{:S(2)}) %collective-permute-start.7) | collective-permute-done | bytes 32800 | tf_op jit(solution)/shard_map/ppermute | solution.py:233
  41.9 0.2 collective-permute-start.11
  42.1 2.3 %constant_dynamic-update-slice_fusion.2 = bf16[1024,2048]{1,0:T(8,128)(2,1)} fusion(bf16[1024,2048]{1,0:T(8,128)(2,1)} %constant_dynamic-update-slice_fusion.3, bf16[256,2048]{1,0:T(8,128)(2,1)} %collective-permute-done, s32[]{:T(128)S(6)} %select_n.126), kind=kLoop, calls=%fused_computation.84 | loop fusion | bytes 2097156 | tf_op jit(solution)/shard_map/dynamic_update_slice | solution.py:261
  44.4 0.0 collective-permute-done.1
  44.4 0.0 collective-permute-done.2
  44.4 1.9 %collective-permute-start.8 = (bf16[2,2048]{1,0:T(2,128)(2,1)S(1)}, bf16[2,2048]{1,0:T(2,128)(2,1)S(1)}, u32[]{:S(2)}, u32[]{:S(2)}) collective-permute-start(bf16[2,2048]{1,0:T(2,128)(2,1)S(1)} %fusion.33), channel_id=1, source_target_pairs={{0,4},{4,0},{8,12},{12,8},{16,20},{20,16},{24,28},{28,24},{1,5},{5... | collective-permute-start | bytes 24584 | tf_op jit(solution)/shard_map/ppermute | solution.py:268
  46.3 2.4 %constant_dynamic-update-slice_fusion.1 = bf16[1024,2048]{1,0:T(8,128)(2,1)} fusion(bf16[1024,2048]{1,0:T(8,128)(2,1)} %constant_dynamic-update-slice_fusion.2, bf16[256,2048]{1,0:T(8,128)(2,1)} %collective-permute-done.1, s32[]{:T(128)S(6)} %select_n.138), kind=kLoop, calls=%fused_computation.81 | loop fusion | bytes 2097156 | tf_op jit(solution)/shard_map/dynamic_update_slice | solution.py:261
  48.7 0.0 collective-permute-done.8
  48.7 1.6 %collective-permute-start.9 = (bf16[4,2048]{1,0:T(4,128)(2,1)S(1)}, bf16[4,2048]{1,0:T(4,128)(2,1)S(1)}, u32[]{:S(2)}, u32[]{:S(2)}) collective-permute-start(bf16[4,2048]{1,0:T(4,128)(2,1)S(1)} %pad_maximum_fusion.5), channel_id=1, source_target_pairs={{0,8},{4,12},{8,0},{12,4},{16,24},{20,28},{24,16},{28,20},{1,9},{5... | collective-permute-start | bytes 49160 | tf_op jit(solution)/shard_map/ppermute | solution.py:268
  50.3 2.3 %constant_dynamic-update-slice_fusion = bf16[1024,2048]{1,0:T(8,128)(2,1)} fusion(bf16[1024,2048]{1,0:T(8,128)(2,1)} %constant_dynamic-update-slice_fusion.1, bf16[256,2048]{1,0:T(8,128)(2,1)} %collective-permute-done.2, s32[]{:T(128)S(6)} %select_n.139), kind=kLoop, calls=%fused_computation.80 | loop fusion | bytes 2097156 | tf_op jit(solution)/shard_map/dynamic_update_slice | solution.py:261
  52.6 0.0 collective-permute-done.9
  52.7 2.9 %collective-permute-start.10 = (bf16[8,2048]{1,0:T(8,128)(2,1)S(1)}, bf16[8,2048]{1,0:T(8,128)(2,1)S(1)}, u32[]{:S(2)}, u32[]{:S(2)}) collective-permute-start(bf16[8,2048]{1,0:T(8,128)(2,1)S(1)} %pad_maximum_fusion.3), channel_id=1, source_target_pairs={{0,16},{4,20},{8,24},{12,28},{16,0},{20,4},{24,8},{28,12},{1,17},{... | collective-permute-start | bytes 98312 | tf_op jit(solution)/shard_map/ppermute | solution.py:268
  55.6 11.2 %add_convert_fusion.q_ref.kn_ref.vn_ref = bf16[1024,1536]{1,0:T(8,128)(2,1)} fusion(bf16[1024,2048]{1,0:T(8,128)(2,1)} %constant_dynamic-update-slice_fusion, bf16[2048,1536]{1,0:T(8,128)(2,1)} %param.19, f32[1536]{0:T(1024)S(1)} %convert_element_type.93), kind=kOutput, calls=%fused_computation | convolution fusion | flops 6445596672 | bytes 13637632 | tf_op jit(solution)/shard_map/dot_general | solution.py:262
  66.8 0.8 convolution_convert_fusion
  67.6 23.2 %shard_map.158 = bf16[1024,512]{1,0:T(8,128)(2,1)} custom-call(s32[1]{0:T(128)S(6)} %copy.39.prefix_ref, f32[4]{0:T(128)} %copy-done.7, bf16[1024,1536]{1,0:T(8,128)(2,1)} %add_convert_fusion.q_ref.kn_ref.vn_ref, bf16[1024,1536]{1,0:T(8,128)(2,1)} %add_convert_fusion.q_ref.kn_ref.vn_ref, bf16[1024,1536]{1,0:T(8,128)(2,1)} %add_convert_fusion.q_ref.kn_ref.vn_ref, ...), custom_call_target="tpu_custom_call" | custom-call | flops 4294967296 | bytes 6291456 | tf_op jit(solution)/shard_map/pallas_call | solution.py:117
  90.7 0.0 collective-permute-done.11
  90.7 0.0 collective-permute-start.16
  90.7 0.5 collective-permute-start.14
  91.2 2.0 %constant_dynamic-slice_fusion.2 = (bf16[256,512]{1,0:T(8,128)(2,1)S(1)}, bf16[256,512]{1,0:T(8,128)(2,1)}, bf16[256,512]{1,0:T(8,128)(2,1)}) fusion(bf16[1024,512]{1,0:T(8,128)(2,1)} %shard_map.158, s32[]{:T(128)S(6)} %select_n.138, s32[]{:T(128)S(6)} %select_n.146, s32[]{:T(128)S(6)} %select_n.145), kind=kLoop, calls=%fused_computation.83 | loop fusion | bytes 1572876 | tf_op jit(solution)/shard_map/dynamic_slice | solution.py:289
  93.2 1.6 %collective-permute-start.12 = (bf16[256,512]{1,0:T(8,128)(2,1)}, bf16[256,512]{1,0:T(8,128)(2,1)}, u32[]{:S(2)}, u32[]{:S(2)}) collective-permute-start(bf16[256,512]{1,0:T(8,128)(2,1)} %get-tuple-element.26), channel_id=1, source_target_pairs={{0,2},{1,3},{2,0},{3,1},{4,6},{5,7},{6,4},{7,5},{8,10},{9,11},{10,... | collective-permute-start | bytes 786440 | tf_op jit(solution)/shard_map/ppermute | solution.py:290
  94.8 0.0 collective-permute-start.15
  94.8 0.6 collective-permute-start.13
  95.3 7.3 %collective-permute-done.12 = bf16[256,512]{1,0:T(8,128)(2,1)} collective-permute-done((bf16[256,512]{1,0:T(8,128)(2,1)}, bf16[256,512]{1,0:T(8,128)(2,1)}, u32[]{:S(2)}, u32[]{:S(2)}) %collective-permute-start.12) | collective-permute-done | bytes 262176 | tf_op jit(solution)/shard_map/ppermute | solution.py:290
  102.7 2.4 %fusion.68 = f32[256,2048]{1,0:T(8,128)S(1)} fusion(bf16[256,512]{1,0:T(8,128)(2,1)} %collective-permute-done.12, bf16[512,2048]{1,0:T(8,128)(2,1)} %collective-permute-done.11), kind=kOutput, calls=%fused_computation.130 | convolution fusion | flops 536870912 | bytes 4456448 | tf_op jit(solution)/shard_map/dot_general | solution.py:293
  105.1 1.7 %convolution_add_fusion.1 = f32[256,2048]{1,0:T(8,128)S(1)} fusion(f32[256,2048]{1,0:T(8,128)S(1)} %fusion.68, bf16[512,2048]{1,0:T(8,128)(2,1)S(1)} %copy-done.1, bf16[1024,512]{1,0:T(8,128)(2,1)} %shard_map.158, s32[]{:T(128)S(6)} %select_n.143), kind=kOutput, calls=%fused_computation.6 | convolution fusion | flops 537395200 | bytes 6553604 | tf_op jit(solution)/shard_map/dot_general | solution.py:291
  106.8 2.3 %fusion.69 = f32[256,2048]{1,0:T(8,128)S(1)} fusion(bf16[256,512]{1,0:T(8,128)(2,1)S(1)} %collective-permute-done.15, bf16[512,2048]{1,0:T(8,128)(2,1)} %collective-permute-done.16), kind=kOutput, calls=%fused_computation.131 | convolution fusion | flops 536870912 | bytes 4456448 | tf_op jit(solution)/shard_map/dot_general | solution.py:293
  109.2 0.0 collective-permute-done.14
  109.2 0.0 collective-permute-done.13
  109.2 3.4 %fusion.2 = bf16[256,2048]{1,0:T(8,128)(2,1)} fusion(bf16[256,2048]{1,0:T(8,128)(2,1)S(1)} %copy-done, f32[256,2048]{1,0:T(8,128)S(1)} %fusion.69, f32[256,2048]{1,0:T(8,128)S(1)} %convolution_add_fusion.1, bf16[256,512]{1,0:T(8,128)(2,1)S(1)} %collective-permute-done.13, bf16[512,2048]{1,0:T(8,128)(2,1)} %collective-permute-done.14, ...), kind=kOutput, calls=%fused_computation.8 | convolution fusion | flops 540016640 | bytes 8658944 | tf_op jit(solution)/shard_map/dot_general | solution.py:293
  (45 shorter events, 0.4 us)
Async XLA Ops:
  0.6 4.6 %copy-start = (bf16[256,2048]{1,0:T(8,128)(2,1)S(1)}, bf16[256,2048]{1,0:T(8,128)(2,1)}, u32[]{:S(2)}) copy-start(bf16[256,2048]{1,0:T(8,128)(2,1)} %param.15) | copy-start | bytes 3145732
  2.1 7.6 %copy-start.3 = (bf16[2,2048]{1,0:T(2,128)(2,1)S(1)}, bf16[2,2048]{1,0:T(2,128)(2,1)}, u32[]{:S(2)}) copy-start(bf16[2,2048]{1,0:T(2,128)(2,1)} %param.16) | copy-start | bytes 24580
  2.1 9.1 %copy-start.6 = (s32[2]{0:T(128)S(1)}, s32[2]{0:T(128)}, u32[]{:S(2)}) copy-start(s32[2]{0:T(128)} %param.28) | copy-start | bytes 28
  2.1 9.3 %copy-start.8 = (s32[16]{0:T(128)S(1)}, s32[16]{0:T(128)}, u32[]{:S(2)}) copy-start(s32[16]{0:T(128)} %param.29) | copy-start | bytes 196
  2.1 17.8 %copy-start.4 = (bf16[1536]{0:T(1024)(128)(2,1)S(1)}, bf16[1536]{0:T(1024)(128)(2,1)}, u32[]{:S(2)}) copy-start(bf16[1536]{0:T(1024)(128)(2,1)} %param.20) | copy-start | bytes 9220
  6.7 30.5 %collective-permute-start = (bf16[256,2048]{1,0:T(8,128)(2,1)}, bf16[256,2048]{1,0:T(8,128)(2,1)}, u32[]{:S(2)}, u32[]{:S(2)}) collective-permute-start(bf16[256,2048]{1,0:T(8,128)(2,1)} %fusion.12), channel_id=1, source_target_pairs={{0,2},{1,3},{2,0},{3,1},{4,6},{5,7},{6,4},{7,5},{8,10},{9,11},{10,... | collective-permute-start | bytes 3145736 | tf_op jit(solution)/shard_map/ppermute | solution.py:251
  9.7 34.8 %collective-permute-start.1 = (bf16[256,2048]{1,0:T(8,128)(2,1)}, bf16[256,2048]{1,0:T(8,128)(2,1)}, u32[]{:S(2)}, u32[]{:S(2)}) collective-permute-start(bf16[256,2048]{1,0:T(8,128)(2,1)} %fusion.12), channel_id=1, source_target_pairs={{0,1},{1,0},{2,3},{3,2},{4,5},{5,4},{6,7},{7,6},{8,9},{9,8},{10,11... | collective-permute-start | bytes 3145736 | tf_op jit(solution)/shard_map/ppermute | solution.py:254
  9.7 3.7 %collective-permute-start.3 = (bf16[2,2048]{1,0:T(2,128)(2,1)S(1)}, bf16[2,2048]{1,0:T(2,128)(2,1)S(1)}, u32[]{:S(2)}, u32[]{:S(2)}) collective-permute-start(bf16[2,2048]{1,0:T(2,128)(2,1)S(1)} %copy-done.3), channel_id=1, source_target_pairs={{0,4},{4,0},{8,12},{12,8},{16,20},{20,16},{24,28},{28,24},{1,5},{5... | collective-permute-start | bytes 24584 | tf_op jit(solution)/shard_map/ppermute | solution.py:200
  13.3 3.8 %collective-permute-start.4 = (bf16[4,2048]{1,0:T(4,128)(2,1)S(1)}, bf16[4,2048]{1,0:T(4,128)(2,1)S(1)}, u32[]{:S(2)}, u32[]{:S(2)}) collective-permute-start(bf16[4,2048]{1,0:T(4,128)(2,1)S(1)} %pad_maximum_fusion.4), channel_id=1, source_target_pairs={{0,8},{4,12},{8,0},{12,4},{16,24},{20,28},{24,16},{28,20},{1,9},{5... | collective-permute-start | bytes 49160 | tf_op jit(solution)/shard_map/ppermute | solution.py:200
  17.2 4.9 %collective-permute-start.5 = (bf16[8,2048]{1,0:T(8,128)(2,1)S(1)}, bf16[8,2048]{1,0:T(8,128)(2,1)S(1)}, u32[]{:S(2)}, u32[]{:S(2)}) collective-permute-start(bf16[8,2048]{1,0:T(8,128)(2,1)S(1)} %pad_maximum_fusion.1), channel_id=1, source_target_pairs={{0,16},{4,20},{8,24},{12,28},{16,0},{20,4},{24,8},{28,12},{1,17},{... | collective-permute-start | bytes 98312 | tf_op jit(solution)/shard_map/ppermute | solution.py:200
  19.8 6.7 %copy-start.7 = (f32[4]{0:T(128)}, f32[4]{0:T(128)S(1)}, u32[]{:S(2)}) copy-start(f32[4]{0:T(128)S(1)} %multiply_exponential_fusion.slopes_ref) | copy-start | bytes 52
  26.5 3.9 %copy-start.2 = (bf16[2,2048,512]{2,1,0:T(8,128)(2,1)S(1)}, bf16[2,2048,512]{2,1,0:T(8,128)(2,1)}, u32[]{:S(2)}) copy-start(bf16[2,2048,512]{2,1,0:T(8,128)(2,1)} %param.26) | copy-start | bytes 12582916
  30.4 1.6 %copy-start.1 = (bf16[512,2048]{1,0:T(8,128)(2,1)S(1)}, bf16[512,2048]{1,0:T(8,128)(2,1)}, u32[]{:S(2)}) copy-start(bf16[512,2048]{1,0:T(8,128)(2,1)} %param.21) | copy-start | bytes 6291460
  32.4 5.4 %collective-permute-start.6 = (f32[2,2048]{1,0:T(2,128)S(1)}, f32[2,2048]{1,0:T(2,128)S(1)}, u32[]{:S(2)}, u32[]{:S(2)}) collective-permute-start(f32[2,2048]{1,0:T(2,128)S(1)} %fusion.48), channel_id=1, source_target_pairs={{0,1},{1,0},{2,3},{3,2},{4,5},{5,4},{6,7},{7,6},{8,9},{9,8},{10,11... | collective-permute-start | bytes 49160 | tf_op jit(solution)/shard_map/ppermute | solution.py:233
  34.9 3.9 %copy-start.5 = (bf16[2048]{0:T(1024)(128)(2,1)S(1)}, bf16[2048]{0:T(1024)(128)(2,1)}, u32[]{:S(2)}) copy-start(bf16[2048]{0:T(1024)(128)(2,1)} %param.22) | copy-start | bytes 12292
  37.2 7.2 %collective-permute-start.2 = (bf16[256,2048]{1,0:T(8,128)(2,1)}, bf16[256,2048]{1,0:T(8,128)(2,1)}, u32[]{:S(2)}, u32[]{:S(2)}) collective-permute-start(bf16[256,2048]{1,0:T(8,128)(2,1)} %collective-permute-done), channel_id=1, source_target_pairs={{0,1},{1,0},{2,3},{3,2},{4,5},{5,4},{6,7},{7,6},{8,9},{9,8},{10,11... | collective-permute-start | bytes 3145736 | tf_op jit(solution)/shard_map/ppermute | solution.py:254
  37.8 4.0 %collective-permute-start.7 = (f32[4,2048]{1,0:T(4,128)S(1)}, f32[4,2048]{1,0:T(4,128)S(1)}, u32[]{:S(2)}, u32[]{:S(2)}) collective-permute-start(f32[4,2048]{1,0:T(4,128)S(1)} %pad_maximum_fusion.2), channel_id=1, source_target_pairs={{0,2},{1,3},{2,0},{3,1},{4,6},{5,7},{6,4},{7,5},{8,10},{9,11},{10,... | collective-permute-start | bytes 98312 | tf_op jit(solution)/shard_map/ppermute | solution.py:233
  41.9 48.8 %collective-permute-start.11 = (bf16[512,2048]{1,0:T(8,128)(2,1)S(1)}, bf16[512,2048]{1,0:T(8,128)(2,1)}, u32[]{:S(2)}, u32[]{:S(2)}) collective-permute-start(bf16[512,2048]{1,0:T(8,128)(2,1)S(1)} %copy-done.1), channel_id=1, source_target_pairs={{0,2},{1,3},{2,0},{3,1},{4,6},{5,7},{6,4},{7,5},{8,10},{9,11},{10,... | collective-permute-start | bytes 6291464 | tf_op jit(solution)/shard_map/ppermute | solution.py:256
  44.4 4.2 %collective-permute-start.8 = (bf16[2,2048]{1,0:T(2,128)(2,1)S(1)}, bf16[2,2048]{1,0:T(2,128)(2,1)S(1)}, u32[]{:S(2)}, u32[]{:S(2)}) collective-permute-start(bf16[2,2048]{1,0:T(2,128)(2,1)S(1)} %fusion.33), channel_id=1, source_target_pairs={{0,4},{4,0},{8,12},{12,8},{16,20},{20,16},{24,28},{28,24},{1,5},{5... | collective-permute-start | bytes 24584 | tf_op jit(solution)/shard_map/ppermute | solution.py:268
  48.7 4.0 %collective-permute-start.9 = (bf16[4,2048]{1,0:T(4,128)(2,1)S(1)}, bf16[4,2048]{1,0:T(4,128)(2,1)S(1)}, u32[]{:S(2)}, u32[]{:S(2)}) collective-permute-start(bf16[4,2048]{1,0:T(4,128)(2,1)S(1)} %pad_maximum_fusion.5), channel_id=1, source_target_pairs={{0,8},{4,12},{8,0},{12,4},{16,24},{20,28},{24,16},{28,20},{1,9},{5... | collective-permute-start | bytes 49160 | tf_op jit(solution)/shard_map/ppermute | solution.py:268
  52.7 14.1 %collective-permute-start.10 = (bf16[8,2048]{1,0:T(8,128)(2,1)S(1)}, bf16[8,2048]{1,0:T(8,128)(2,1)S(1)}, u32[]{:S(2)}, u32[]{:S(2)}) collective-permute-start(bf16[8,2048]{1,0:T(8,128)(2,1)S(1)} %pad_maximum_fusion.3), channel_id=1, source_target_pairs={{0,16},{4,20},{8,24},{12,28},{16,0},{20,4},{24,8},{28,12},{1,17},{... | collective-permute-start | bytes 98312 | tf_op jit(solution)/shard_map/ppermute | solution.py:268
  90.7 16.1 %collective-permute-start.16 = (bf16[512,2048]{1,0:T(8,128)(2,1)}, bf16[512,2048]{1,0:T(8,128)(2,1)}, u32[]{:S(2)}, u32[]{:S(2)}) collective-permute-start(bf16[512,2048]{1,0:T(8,128)(2,1)} %collective-permute-done.11), channel_id=1, source_target_pairs={{0,1},{1,0},{2,3},{3,2},{4,5},{5,4},{6,7},{7,6},{8,9},{9,8},{10,11... | collective-permute-start | bytes 6291464 | tf_op jit(solution)/shard_map/ppermute | solution.py:281
  90.7 18.4 %collective-permute-start.14 = (bf16[512,2048]{1,0:T(8,128)(2,1)S(1)}, bf16[512,2048]{1,0:T(8,128)(2,1)}, u32[]{:S(2)}, u32[]{:S(2)}) collective-permute-start(bf16[512,2048]{1,0:T(8,128)(2,1)S(1)} %copy-done.1), channel_id=1, source_target_pairs={{0,1},{1,0},{2,3},{3,2},{4,5},{5,4},{6,7},{7,6},{8,9},{9,8},{10,11... | collective-permute-start | bytes 6291464 | tf_op jit(solution)/shard_map/ppermute | solution.py:281
  93.2 9.5 %collective-permute-start.12 = (bf16[256,512]{1,0:T(8,128)(2,1)}, bf16[256,512]{1,0:T(8,128)(2,1)}, u32[]{:S(2)}, u32[]{:S(2)}) collective-permute-start(bf16[256,512]{1,0:T(8,128)(2,1)} %get-tuple-element.26), channel_id=1, source_target_pairs={{0,2},{1,3},{2,0},{3,1},{4,6},{5,7},{6,4},{7,5},{8,10},{9,11},{10,... | collective-permute-start | bytes 786440 | tf_op jit(solution)/shard_map/ppermute | solution.py:290
  94.8 12.0 %collective-permute-start.15 = (bf16[256,512]{1,0:T(8,128)(2,1)}, bf16[256,512]{1,0:T(8,128)(2,1)S(1)}, u32[]{:S(2)}, u32[]{:S(2)}) collective-permute-start(bf16[256,512]{1,0:T(8,128)(2,1)} %get-tuple-element.25), channel_id=1, source_target_pairs={{0,3},{1,2},{2,1},{3,0},{4,7},{5,6},{6,5},{7,4},{8,11},{9,10},{10,... | collective-permute-start | bytes 786440 | tf_op jit(solution)/shard_map/ppermute | solution.py:290
  94.8 14.4 %collective-permute-start.13 = (bf16[256,512]{1,0:T(8,128)(2,1)S(1)}, bf16[256,512]{1,0:T(8,128)(2,1)S(1)}, u32[]{:S(2)}, u32[]{:S(2)}) collective-permute-start(bf16[256,512]{1,0:T(8,128)(2,1)S(1)} %get-tuple-element.24), channel_id=1, source_target_pairs={{0,1},{1,0},{2,3},{3,2},{4,5},{5,4},{6,7},{7,6},{8,9},{9,8},{10,11... | collective-permute-start | bytes 786440 | tf_op jit(solution)/shard_map/ppermute | solution.py:290

commit v13 on v12

--- a/solution.py
+++ b/solution.py
@@ -254,11 +254,10 @@
     sibling_tokens = [lax.ppermute(t, "tensor", route(0, 1)) for t in same_core_tokens]
     sibling_tokens, slot_rows = lax.optimization_barrier((sibling_tokens, slot_rows))
     across_chips = [lax.ppermute(held_weight, "tensor", route(k, 0)) for k in range(1, chips)]
-    tokens = jnp.zeros((tensor_size * block, normed.shape[1]), normed.dtype)
-    for flip, token_blocks in ((0, same_core_tokens), (1, sibling_tokens)):
-        for k, token_block in enumerate(token_blocks):
-            source = ((chip - k) % chips) * 2 + (core ^ flip)
-            tokens = lax.dynamic_update_slice_in_dim(tokens, token_block, source * block, 0)
+    members = jnp.arange(tensor_size, dtype=jnp.int32)
+    arrival_of = ((members % 2) ^ core) * chips + (chip - members // 2) % chips
+    tokens = jnp.take(jnp.stack(list(same_core_tokens) + list(sibling_tokens)), arrival_of, axis=0)
+    tokens = tokens.reshape(tensor_size * block, normed.shape[1])
     product = jnp.dot(tokens, qkv_weight, preferred_element_type=jnp.float32)
     merged_rows = (product + qkv_bias.astype(jnp.float32)).astype(jnp.bfloat16)
     returned = slot_rows

time: 113 us -> 113 us (level)
  local copies, waits for them, and re-layouts: 14.8 us -> 8.08 us
  other arithmetic: 7.25 us -> 13.7 us
  matrix products: 30.6 us -> 29.3 us
    dynamic_update_slice x4 -> x0, local copies, waits for them, and re-layouts: 9.34 us -> none  [per_device(): lax.dynamic_update_slice_in_dim(tokens, token_block, source * block, 0)]
    gather x0 -> x1, local copies, waits for them, and re-layouts: none -> 4.97 us  [per_device(): jnp.take(jnp.stack(list(same_core_tokens) + list(sibling_tokens)), arriva...]
    another operation x0 -> x1, other arithmetic: none -> 3.74 us  [per_device(): jnp.stack(list(same_core_tokens) + list(sibling_tokens))]
    select_n x0 -> x2, other arithmetic: none -> 2.65 us  [per_device(): jnp.take(jnp.stack(list(same_core_tokens) + list(sibling_tokens)), arriva...]
    broadcast_in_dim x1 -> x2, local copies, waits for them, and re-layouts: 2.46 us -> 0.09 us  [per_device(): jnp.take(jnp.stack(list(same_core_tokens) + list(sibling_tokens)), arriva...]
    dot_general x1, matrix products: 11.2 us -> 9.93 us  [per_device(): product = jnp.dot(tokens, qkv_weight, preferred_element_type=jnp.float32)]
    ppermute x2, starting transfers between devices: 0.22 us -> 1.37 us  [per_device(): lax.ppermute(partials, 'tensor', [(i, i ^ step) for i in range(tensor_siz...]
    ppermute x1, starting transfers between devices: 0.22 us -> 1.36 us  [per_device(): lax.ppermute(held_weight, 'tensor', route(k, 0))]
  transfers between devices with their start and end apart: 17 -> 17, of which waited for: 5 -> 7; matrix products, arithmetic and copies ran while one was open for 38% -> 36% of each run, Pallas kernels for 21% -> 21%
where the time goes in v13:
time: 113 us; the launch traced here: 112 us
  matrix products  29.3 us (26%)
  Pallas kernels  23.2 us (21%)
  starting transfers between devices  19.9 us (18%)
  waiting for transfers between devices  16.3 us (14%)
  other arithmetic  13.7 us (12%)
  local copies, waits for them, and re-layouts  8.08 us (7%)
  between operations  1.59 us (1%)
    pallas_call x1, Pallas kernels, prefill_attention_kernel(): pl.pallas_call(functools.partial(_prefill_kernel, tq=tq), out_shape=jax.S...  23.2 us
    dot_general x1, matrix products, per_device(): product = jnp.dot(tokens, qkv_weight, preferred_element_type=jnp.float32)  9.93 us
    dot_general x3, matrix products, per_device(): summed = summed + jnp.dot(piece, weight, preferred_element_type=jnp.float32)  8.12 us
    ppermute x3, waiting for transfers between devices, per_device(): pieces.append(lax.ppermute(outgoing, 'tensor', route(k, flip)))  7.34 us
    ppermute x3, waiting for transfers between devices, per_device(): lax.ppermute(shifted_rows, 'dp', [(i, i ^ step) for i in range(dp_size)])  6.01 us
    ppermute x3, starting transfers between devices, per_device(): lax.ppermute(returned, 'dp', [(i, i ^ step) for i in range(dp_size)])  5.82 us
    ppermute x3, starting transfers between devices, per_device(): lax.ppermute(shifted_rows, 'dp', [(i, i ^ step) for i in range(dp_size)])  5.82 us
    gather x1, local copies, waits for them, and re-layouts, per_device(): jnp.take(jnp.stack(list(same_core_tokens) + list(sibling_tokens)), arriva...  4.97 us
  transfers between devices with their start and end apart: 17, of which 7 were waited for; matrix products, arithmetic and copies ran while one was open for 36% of the time, Pallas kernels for 21%

profile of v13, /device:TPU:0, one launch (start us, length us, event | category | flops | bytes accessed | tf_op | source)
XLA Modules:
  0.0 112.1 jit_solution(11933390796431042918)
XLA Ops:
  0.6 0.0 copy-start
  0.6 0.8 convert_element_type.87
  1.4 0.7 convert_element_type.88
  2.1 1.5 %convert_reduce_fusion = f32[256]{0:T(256)S(1)} fusion(bf16[256,2048]{1,0:T(8,128)(2,1)} %param.15), kind=kLoop, calls=%fused_computation.6 | loop fusion | flops 1048320 | bytes 1049600 | tf_op jit(solution)/shard_map/reduce_sum | solution.py:20
  3.6 1.6 %fusion.9 = f32[256]{0:T(256)S(1)} fusion(bf16[256,2048]{1,0:T(8,128)(2,1)} %param.15, f32[256]{0:T(256)S(1)} %broadcast_multiply_fusion), kind=kLoop, calls=%fused_computation.22 | loop fusion | flops 2096896 | bytes 1050624 | tf_op jit(solution)/shard_map/reduce_sum | solution.py:21
  5.3 1.4 %fusion.12 = bf16[256,2048]{1,0:T(8,128)(2,1)} fusion(bf16[256,2048]{1,0:T(8,128)(2,1)S(1)} %copy-done, f32[2048]{0:T(1024)S(1)} %convert_element_type.88, f32[2048]{0:T(1024)S(1)} %convert_element_type.87, f32[256]{0:T(256)S(1)} %add_rsqrt_fusion, f32[256]{0:T(256)S(1)} %broadcast_multiply_fusion), kind=kLoop, calls=%fused_computation.25 | loop fusion | flops 3145728 | bytes 2115584 | tf_op jit(solution)/shard_map/convert_element_type | solution.py:23
  6.7 2.9 %collective-permute-start = (bf16[256,2048]{1,0:T(8,128)(2,1)}, bf16[256,2048]{1,0:T(8,128)(2,1)}, u32[]{:S(2)}, u32[]{:S(2)}) collective-permute-start(bf16[256,2048]{1,0:T(8,128)(2,1)} %fusion.12), channel_id=1, source_target_pairs={{0,2},{1,3},{2,0},{3,1},{4,6},{5,7},{6,4},{7,5},{8,10},{9,11},{10,... | collective-permute-start | bytes 3145736 | tf_op jit(solution)/shard_map/ppermute | solution.py:251
  9.7 0.0 collective-permute-start.1
  9.7 1.5 %collective-permute-start.3 = (bf16[2,2048]{1,0:T(2,128)(2,1)S(1)}, bf16[2,2048]{1,0:T(2,128)(2,1)S(1)}, u32[]{:S(2)}, u32[]{:S(2)}) collective-permute-start(bf16[2,2048]{1,0:T(2,128)(2,1)S(1)} %copy-done.3), channel_id=1, source_target_pairs={{0,4},{4,0},{8,12},{12,8},{16,20},{20,16},{24,28},{28,24},{1,5},{5... | collective-permute-start | bytes 24584 | tf_op jit(solution)/shard_map/ppermute | solution.py:200
  11.2 0.1 subtract_convert_fusion
  11.3 0.1 iota_compare_fusion
  11.4 0.2 fusion.53
  11.6 1.7 %collective-permute-done.3 = bf16[2,2048]{1,0:T(2,128)(2,1)S(1)} collective-permute-done((bf16[2,2048]{1,0:T(2,128)(2,1)S(1)}, bf16[2,2048]{1,0:T(2,128)(2,1)S(1)}, u32[]{:S(2)}, u32[]{:S(2)}) %collective-permute-start.3) | collective-permute-done | bytes 8224 | tf_op jit(solution)/shard_map/ppermute | solution.py:200
  13.3 1.6 %collective-permute-start.4 = (bf16[4,2048]{1,0:T(4,128)(2,1)S(1)}, bf16[4,2048]{1,0:T(4,128)(2,1)S(1)}, u32[]{:S(2)}, u32[]{:S(2)}) collective-permute-start(bf16[4,2048]{1,0:T(4,128)(2,1)S(1)} %pad_maximum_fusion.5), channel_id=1, source_target_pairs={{0,8},{4,12},{8,0},{12,4},{16,24},{20,28},{24,16},{28,20},{1,9},{5... | collective-permute-start | bytes 49160 | tf_op jit(solution)/shard_map/ppermute | solution.py:200
  15.0 2.2 %collective-permute-done.4 = bf16[4,2048]{1,0:T(4,128)(2,1)S(1)} collective-permute-done((bf16[4,2048]{1,0:T(4,128)(2,1)S(1)}, bf16[4,2048]{1,0:T(4,128)(2,1)S(1)}, u32[]{:S(2)}, u32[]{:S(2)}) %collective-permute-start.4) | collective-permute-done | bytes 16416 | tf_op jit(solution)/shard_map/ppermute | solution.py:200
  17.2 2.7 %collective-permute-start.5 = (bf16[8,2048]{1,0:T(8,128)(2,1)S(1)}, bf16[8,2048]{1,0:T(8,128)(2,1)S(1)}, u32[]{:S(2)}, u32[]{:S(2)}) collective-permute-start(bf16[8,2048]{1,0:T(8,128)(2,1)S(1)} %pad_maximum_fusion.2), channel_id=1, source_target_pairs={{0,16},{4,20},{8,24},{12,28},{16,0},{20,4},{24,8},{28,12},{1,17},{... | collective-permute-start | bytes 98312 | tf_op jit(solution)/shard_map/ppermute | solution.py:200
  19.9 2.2 %collective-permute-done.5 = bf16[8,2048]{1,0:T(8,128)(2,1)S(1)} collective-permute-done((bf16[8,2048]{1,0:T(8,128)(2,1)S(1)}, bf16[8,2048]{1,0:T(8,128)(2,1)S(1)}, u32[]{:S(2)}, u32[]{:S(2)}) %collective-permute-start.5) | collective-permute-done | bytes 32800 | tf_op jit(solution)/shard_map/ppermute | solution.py:200
  22.1 0.3 fusion.77
  22.4 0.2 multiply_reduce_fusion
  22.6 3.8 %fusion.7 = bf16[2,1536]{1,0:T(2,128)(2,1)S(1)} fusion(bf16[2048,1536]{1,0:T(8,128)(2,1)} %param.19, f32[2,2048]{1,0:T(2,128)S(1)} %get-tuple-element.33, f32[2]{0:T(128)S(1)} %add_rsqrt_fusion.1, f32[2]{0:T(128)S(1)} %broadcast_multiply_fusion.1, f32[2048]{0:T(1024)S(1)} %convert_element_type.88, f32[2048]{0:T(1024)S(1)} %convert_element_type.87, ...), kind=kOutput, calls=%fused_computation.18 | convolution fusion | flops 12609536 | bytes 6336528 | tf_op jit(solution)/shard_map/dot_general | solution.py:214
  26.4 0.1 fusion.42
  26.5 3.6 %fusion.78 = (f32[2,4]{1,0:T(2,128)S(1)}, f32[2,4,2048]{2,1,0:T(4,128)S(1)}) fusion(f32[2,2048]{1,0:T(2,128)S(1)} %subtract_convert_fusion, f32[4]{0:T(128)S(1)} %multiply_exponential_fusion.slopes_ref, bf16[2,2048,512]{2,1,0:T(8,128)(2,1)} %param.25, pred[512,4]{0,1:T(4,128)(4,1)S(1)} %iota_compare_fusion.1, bf16[2,512]{1,0:T(2,128)(2,1)S(1)} %bitcast.51, ...), kind=kOutput, calls=%fused_computation.157 | convolution fusion | flops 16863224 | bytes 4284464 | tf_op jit(solution)/shard_map/vmap()/dot_general | solution.py:148
  30.1 0.2 fusion.29
  30.4 0.1 broadcast_bitcast_fusion
  30.4 0.7 fusion.13
  31.2 0.0 copy-start.5
  31.2 0.9 copy-done.1
  32.0 0.4 fusion.47
  32.4 0.0 collective-permute-start.6
  32.4 0.7 collective-permute-done
  33.1 0.0 collective-permute-start.2
  33.1 0.5 collective-permute-done.6
  33.6 1.4 %collective-permute-start.7 = (f32[4,2048]{1,0:T(4,128)S(1)}, f32[4,2048]{1,0:T(4,128)S(1)}, u32[]{:S(2)}, u32[]{:S(2)}) collective-permute-start(f32[4,2048]{1,0:T(4,128)S(1)} %pad_maximum_fusion.3), channel_id=1, source_target_pairs={{0,2},{1,3},{2,0},{3,1},{4,6},{5,7},{6,4},{7,5},{8,10},{9,11},{10,... | collective-permute-start | bytes 98312 | tf_op jit(solution)/shard_map/ppermute | solution.py:233
  35.0 0.1 fusion.59
  35.1 0.1 broadcast_in_dim.99
  35.8 1.8 %collective-permute-done.7 = f32[4,2048]{1,0:T(4,128)S(1)} collective-permute-done((f32[4,2048]{1,0:T(4,128)S(1)}, f32[4,2048]{1,0:T(4,128)S(1)}, u32[]{:S(2)}, u32[]{:S(2)}) %collective-permute-start.7) | collective-permute-done | bytes 32800 | tf_op jit(solution)/shard_map/ppermute | solution.py:233
  37.7 1.4 %collective-permute-start.11 = (bf16[512,2048]{1,0:T(8,128)(2,1)S(1)}, bf16[512,2048]{1,0:T(8,128)(2,1)}, u32[]{:S(2)}, u32[]{:S(2)}) collective-permute-start(bf16[512,2048]{1,0:T(8,128)(2,1)S(1)} %copy-done.1), channel_id=1, source_target_pairs={{0,2},{1,3},{2,0},{3,1},{4,6},{5,7},{6,4},{7,5},{8,10},{9,11},{10,... | collective-permute-start | bytes 6291464 | tf_op jit(solution)/shard_map/ppermute | solution.py:256
  39.1 0.0 collective-permute-done.1
  39.1 0.0 collective-permute-done.2
  39.1 1.5 %collective-permute-start.8 = (bf16[2,2048]{1,0:T(2,128)(2,1)S(1)}, bf16[2,2048]{1,0:T(2,128)(2,1)S(1)}, u32[]{:S(2)}, u32[]{:S(2)}) collective-permute-start(bf16[2,2048]{1,0:T(2,128)(2,1)S(1)} %fusion.33), channel_id=1, source_target_pairs={{0,4},{4,0},{8,12},{12,8},{16,20},{20,16},{24,28},{28,24},{1,5},{5... | collective-permute-start | bytes 24584 | tf_op jit(solution)/shard_map/ppermute | solution.py:267
  40.6 3.7 %pad_maximum_fusion = bf16[4,256,2048]{2,1,0:T(8,128)(2,1)} fusion(bf16[1,256,2048]{2,1,0:T(8,128)(2,1)} %bitcast.4, bf16[1,256,2048]{2,1,0:T(8,128)(2,1)} %bitcast.3, bf16[1,256,2048]{2,1,0:T(8,128)(2,1)} %bitcast.1, bf16[1,256,2048]{2,1,0:T(8,128)(2,1)} %bitcast), kind=kLoop, calls=%fused_computation.2 | loop fusion | flops 6291456 | bytes 8388608 | tf_op jit(solution)/shard_map/stack | solution.py:259
  44.4 5.0 %gather_fusion = bf16[4,256,2048]{2,1,0:T(8,128)(2,1)} fusion(bf16[4,256,2048]{2,1,0:T(8,128)(2,1)} %pad_maximum_fusion, s32[1024]{0:T(1024)S(1)} %pad_clamp_fusion), kind=kCustom, calls=%fused_computation | custom fusion | bytes 8388624 | tf_op jit(solution)/shard_map/jit(_take)/gather | solution.py:259
  49.3 0.0 collective-permute-done.8
  49.4 1.6 %collective-permute-start.9 = (bf16[4,2048]{1,0:T(4,128)(2,1)S(1)}, bf16[4,2048]{1,0:T(4,128)(2,1)S(1)}, u32[]{:S(2)}, u32[]{:S(2)}) collective-permute-start(bf16[4,2048]{1,0:T(4,128)(2,1)S(1)} %pad_maximum_fusion.6), channel_id=1, source_target_pairs={{0,8},{4,12},{8,0},{12,4},{16,24},{20,28},{24,16},{28,20},{1,9},{5... | collective-permute-start | bytes 49160 | tf_op jit(solution)/shard_map/ppermute | solution.py:267
  51.0 2.6 %bitcast_select_fusion = bf16[1024,2048]{1,0:T(8,128)(2,1)S(1)} fusion(bf16[4,256,2048]{2,1,0:T(8,128)(2,1)} %gather_fusion, pred[1024]{0:T(1024)(128)(4,1)S(1)} %broadcast_in_dim.100), kind=kLoop, calls=%fused_computation.3 | loop fusion | flops 2097152 | bytes 8389632 | tf_op jit(solution)/shard_map/jit(_take)/select_n | solution.py:259
  53.7 2.7 %collective-permute-start.10 = (bf16[8,2048]{1,0:T(8,128)(2,1)S(1)}, bf16[8,2048]{1,0:T(8,128)(2,1)S(1)}, u32[]{:S(2)}, u32[]{:S(2)}) collective-permute-start(bf16[8,2048]{1,0:T(8,128)(2,1)S(1)} %pad_maximum_fusion.4), channel_id=1, source_target_pairs={{0,16},{4,20},{8,24},{12,28},{16,0},{20,4},{24,8},{28,12},{1,17},{... | collective-permute-start | bytes 98312 | tf_op jit(solution)/shard_map/ppermute | solution.py:267
  56.3 9.9 %add_convert_fusion.q_ref.kn_ref.vn_ref = bf16[1024,1536]{1,0:T(8,128)(2,1)} fusion(bf16[1024,2048]{1,0:T(8,128)(2,1)S(1)} %bitcast_select_fusion, bf16[2048,1536]{1,0:T(8,128)(2,1)} %param.19, f32[1536]{0:T(1024)S(1)} %convert_element_type.93), kind=kOutput, calls=%fused_computation.1 | convolution fusion | flops 6445596672 | bytes 13637632 | tf_op jit(solution)/shard_map/dot_general | solution.py:261
  66.3 0.0 collective-permute-done.10
  66.3 0.8 convolution_convert_fusion
  67.1 23.2 %shard_map.158 = bf16[1024,512]{1,0:T(8,128)(2,1)} custom-call(s32[1]{0:T(128)S(6)} %copy.35.prefix_ref, f32[4]{0:T(128)} %copy-done.7, bf16[1024,1536]{1,0:T(8,128)(2,1)} %add_convert_fusion.q_ref.kn_ref.vn_ref, bf16[1024,1536]{1,0:T(8,128)(2,1)} %add_convert_fusion.q_ref.kn_ref.vn_ref, bf16[1024,1536]{1,0:T(8,128)(2,1)} %add_convert_fusion.q_ref.kn_ref.vn_ref, ...), custom_call_target="tpu_custom_call" | custom-call | flops 4294967296 | bytes 6291456 | tf_op jit(solution)/shard_map/pallas_call | solution.py:117
  90.2 0.0 collective-permute-done.11
  90.2 0.0 collective-permute-start.16
  90.2 0.5 collective-permute-start.14
  90.7 2.0 %constant_dynamic-slice_fusion.2 = (bf16[256,512]{1,0:T(8,128)(2,1)S(1)}, bf16[256,512]{1,0:T(8,128)(2,1)}, bf16[256,512]{1,0:T(8,128)(2,1)}) fusion(bf16[1024,512]{1,0:T(8,128)(2,1)} %shard_map.158, s32[]{:T(128)S(6)} %select_n.198, s32[]{:T(128)S(6)} %select_n.199, s32[]{:T(128)S(6)} %select_n.196), kind=kLoop, calls=%fused_computation.96 | loop fusion | bytes 1572876 | tf_op jit(solution)/shard_map/dynamic_slice | solution.py:288
  92.7 1.0 collective-permute-start.12
  93.7 0.5 collective-permute-start.15
  94.1 0.7 collective-permute-start.13
  94.8 7.3 %collective-permute-done.12 = bf16[256,512]{1,0:T(8,128)(2,1)} collective-permute-done((bf16[256,512]{1,0:T(8,128)(2,1)}, bf16[256,512]{1,0:T(8,128)(2,1)}, u32[]{:S(2)}, u32[]{:S(2)}) %collective-permute-start.12) | collective-permute-done | bytes 262176 | tf_op jit(solution)/shard_map/ppermute | solution.py:289
  102.2 2.4 %fusion.79 = f32[256,2048]{1,0:T(8,128)S(1)} fusion(bf16[256,512]{1,0:T(8,128)(2,1)} %collective-permute-done.12, bf16[512,2048]{1,0:T(8,128)(2,1)} %collective-permute-done.11), kind=kOutput, calls=%fused_computation.158 | convolution fusion | flops 536870912 | bytes 4456448 | tf_op jit(solution)/shard_map/dot_general | solution.py:292
  104.6 1.7 %convolution_add_fusion.1 = f32[256,2048]{1,0:T(8,128)S(1)} fusion(f32[256,2048]{1,0:T(8,128)S(1)} %fusion.79, bf16[512,2048]{1,0:T(8,128)(2,1)S(1)} %copy-done.1, bf16[1024,512]{1,0:T(8,128)(2,1)} %shard_map.158, s32[]{:T(128)S(6)} %select_n.194), kind=kOutput, calls=%fused_computation.9 | convolution fusion | flops 537395200 | bytes 6553604 | tf_op jit(solution)/shard_map/dot_general | solution.py:290
  106.3 0.0 collective-permute-done.16
  106.3 2.3 %fusion.80 = f32[256,2048]{1,0:T(8,128)S(1)} fusion(bf16[256,512]{1,0:T(8,128)(2,1)S(1)} %collective-permute-done.15, bf16[512,2048]{1,0:T(8,128)(2,1)} %collective-permute-done.16), kind=kOutput, calls=%fused_computation.159 | convolution fusion | flops 536870912 | bytes 4456448 | tf_op jit(solution)/shard_map/dot_general | solution.py:292
  108.7 0.0 collective-permute-done.14
  108.7 3.4 %fusion.2 = bf16[256,2048]{1,0:T(8,128)(2,1)} fusion(bf16[256,2048]{1,0:T(8,128)(2,1)S(1)} %copy-done, f32[256,2048]{1,0:T(8,128)S(1)} %fusion.80, f32[256,2048]{1,0:T(8,128)S(1)} %convolution_add_fusion.1, bf16[256,512]{1,0:T(8,128)(2,1)S(1)} %collective-permute-done.13, bf16[512,2048]{1,0:T(8,128)(2,1)} %collective-permute-done.14, ...), kind=kOutput, calls=%fused_computation.11 | convolution fusion | flops 540016640 | bytes 8658944 | tf_op jit(solution)/shard_map/dot_general | solution.py:292
  (48 shorter events, 0.5 us)
Async XLA Ops:
  0.6 4.6 %copy-start = (bf16[256,2048]{1,0:T(8,128)(2,1)S(1)}, bf16[256,2048]{1,0:T(8,128)(2,1)}, u32[]{:S(2)}) copy-start(bf16[256,2048]{1,0:T(8,128)(2,1)} %param.15) | copy-start | bytes 3145732
  2.1 7.6 %copy-start.3 = (bf16[2,2048]{1,0:T(2,128)(2,1)S(1)}, bf16[2,2048]{1,0:T(2,128)(2,1)}, u32[]{:S(2)}) copy-start(bf16[2,2048]{1,0:T(2,128)(2,1)} %param.16) | copy-start | bytes 24580
  2.1 9.1 %copy-start.6 = (s32[2]{0:T(128)S(1)}, s32[2]{0:T(128)}, u32[]{:S(2)}) copy-start(s32[2]{0:T(128)} %param.28) | copy-start | bytes 28
  2.1 9.3 %copy-start.8 = (s32[16]{0:T(128)S(1)}, s32[16]{0:T(128)}, u32[]{:S(2)}) copy-start(s32[16]{0:T(128)} %param.29) | copy-start | bytes 196
  2.1 17.7 %copy-start.4 = (bf16[1536]{0:T(1024)(128)(2,1)S(1)}, bf16[1536]{0:T(1024)(128)(2,1)}, u32[]{:S(2)}) copy-start(bf16[1536]{0:T(1024)(128)(2,1)} %param.20) | copy-start | bytes 9220
  6.7 26.4 %collective-permute-start = (bf16[256,2048]{1,0:T(8,128)(2,1)}, bf16[256,2048]{1,0:T(8,128)(2,1)}, u32[]{:S(2)}, u32[]{:S(2)}) collective-permute-start(bf16[256,2048]{1,0:T(8,128)(2,1)} %fusion.12), channel_id=1, source_target_pairs={{0,2},{1,3},{2,0},{3,1},{4,6},{5,7},{6,4},{7,5},{8,10},{9,11},{10,... | collective-permute-start | bytes 3145736 | tf_op jit(solution)/shard_map/ppermute | solution.py:251
  9.7 29.4 %collective-permute-start.1 = (bf16[256,2048]{1,0:T(8,128)(2,1)}, bf16[256,2048]{1,0:T(8,128)(2,1)}, u32[]{:S(2)}, u32[]{:S(2)}) collective-permute-start(bf16[256,2048]{1,0:T(8,128)(2,1)} %fusion.12), channel_id=1, source_target_pairs={{0,1},{1,0},{2,3},{3,2},{4,5},{5,4},{6,7},{7,6},{8,9},{9,8},{10,11... | collective-permute-start | bytes 3145736 | tf_op jit(solution)/shard_map/ppermute | solution.py:254
  9.7 3.7 %collective-permute-start.3 = (bf16[2,2048]{1,0:T(2,128)(2,1)S(1)}, bf16[2,2048]{1,0:T(2,128)(2,1)S(1)}, u32[]{:S(2)}, u32[]{:S(2)}) collective-permute-start(bf16[2,2048]{1,0:T(2,128)(2,1)S(1)} %copy-done.3), channel_id=1, source_target_pairs={{0,4},{4,0},{8,12},{12,8},{16,20},{20,16},{24,28},{28,24},{1,5},{5... | collective-permute-start | bytes 24584 | tf_op jit(solution)/shard_map/ppermute | solution.py:200
  13.3 3.8 %collective-permute-start.4 = (bf16[4,2048]{1,0:T(4,128)(2,1)S(1)}, bf16[4,2048]{1,0:T(4,128)(2,1)S(1)}, u32[]{:S(2)}, u32[]{:S(2)}) collective-permute-start(bf16[4,2048]{1,0:T(4,128)(2,1)S(1)} %pad_maximum_fusion.5), channel_id=1, source_target_pairs={{0,8},{4,12},{8,0},{12,4},{16,24},{20,28},{24,16},{28,20},{1,9},{5... | collective-permute-start | bytes 49160 | tf_op jit(solution)/shard_map/ppermute | solution.py:200
  17.2 4.9 %collective-permute-start.5 = (bf16[8,2048]{1,0:T(8,128)(2,1)S(1)}, bf16[8,2048]{1,0:T(8,128)(2,1)S(1)}, u32[]{:S(2)}, u32[]{:S(2)}) collective-permute-start(bf16[8,2048]{1,0:T(8,128)(2,1)S(1)} %pad_maximum_fusion.2), channel_id=1, source_target_pairs={{0,16},{4,20},{8,24},{12,28},{16,0},{20,4},{24,8},{28,12},{1,17},{... | collective-permute-start | bytes 98312 | tf_op jit(solution)/shard_map/ppermute | solution.py:200
  19.8 6.7 %copy-start.7 = (f32[4]{0:T(128)}, f32[4]{0:T(128)S(1)}, u32[]{:S(2)}) copy-start(f32[4]{0:T(128)S(1)} %multiply_exponential_fusion.slopes_ref) | copy-start | bytes 52
  26.5 3.9 %copy-start.2 = (bf16[2,2048,512]{2,1,0:T(8,128)(2,1)S(1)}, bf16[2,2048,512]{2,1,0:T(8,128)(2,1)}, u32[]{:S(2)}) copy-start(bf16[2,2048,512]{2,1,0:T(8,128)(2,1)} %param.26) | copy-start | bytes 12582916
  30.4 1.6 %copy-start.1 = (bf16[512,2048]{1,0:T(8,128)(2,1)S(1)}, bf16[512,2048]{1,0:T(8,128)(2,1)}, u32[]{:S(2)}) copy-start(bf16[512,2048]{1,0:T(8,128)(2,1)} %param.21) | copy-start | bytes 6291460
  31.2 3.9 %copy-start.5 = (bf16[2048]{0:T(1024)(128)(2,1)S(1)}, bf16[2048]{0:T(1024)(128)(2,1)}, u32[]{:S(2)}) copy-start(bf16[2048]{0:T(1024)(128)(2,1)} %param.22) | copy-start | bytes 12292
  32.4 1.2 %collective-permute-start.6 = (f32[2,2048]{1,0:T(2,128)S(1)}, f32[2,2048]{1,0:T(2,128)S(1)}, u32[]{:S(2)}, u32[]{:S(2)}) collective-permute-start(f32[2,2048]{1,0:T(2,128)S(1)} %fusion.47), channel_id=1, source_target_pairs={{0,1},{1,0},{2,3},{3,2},{4,5},{5,4},{6,7},{7,6},{8,9},{9,8},{10,11... | collective-permute-start | bytes 49160 | tf_op jit(solution)/shard_map/ppermute | solution.py:233
  33.1 6.0 %collective-permute-start.2 = (bf16[256,2048]{1,0:T(8,128)(2,1)}, bf16[256,2048]{1,0:T(8,128)(2,1)}, u32[]{:S(2)}, u32[]{:S(2)}) collective-permute-start(bf16[256,2048]{1,0:T(8,128)(2,1)} %collective-permute-done), channel_id=1, source_target_pairs={{0,1},{1,0},{2,3},{3,2},{4,5},{5,4},{6,7},{7,6},{8,9},{9,8},{10,11... | collective-permute-start | bytes 3145736 | tf_op jit(solution)/shard_map/ppermute | solution.py:254
  33.6 4.0 %collective-permute-start.7 = (f32[4,2048]{1,0:T(4,128)S(1)}, f32[4,2048]{1,0:T(4,128)S(1)}, u32[]{:S(2)}, u32[]{:S(2)}) collective-permute-start(f32[4,2048]{1,0:T(4,128)S(1)} %pad_maximum_fusion.3), channel_id=1, source_target_pairs={{0,2},{1,3},{2,0},{3,1},{4,6},{5,7},{6,4},{7,5},{8,10},{9,11},{10,... | collective-permute-start | bytes 98312 | tf_op jit(solution)/shard_map/ppermute | solution.py:233
  37.7 52.5 %collective-permute-start.11 = (bf16[512,2048]{1,0:T(8,128)(2,1)S(1)}, bf16[512,2048]{1,0:T(8,128)(2,1)}, u32[]{:S(2)}, u32[]{:S(2)}) collective-permute-start(bf16[512,2048]{1,0:T(8,128)(2,1)S(1)} %copy-done.1), channel_id=1, source_target_pairs={{0,2},{1,3},{2,0},{3,1},{4,6},{5,7},{6,4},{7,5},{8,10},{9,11},{10,... | collective-permute-start | bytes 6291464 | tf_op jit(solution)/shard_map/ppermute | solution.py:256
  39.1 10.2 %collective-permute-start.8 = (bf16[2,2048]{1,0:T(2,128)(2,1)S(1)}, bf16[2,2048]{1,0:T(2,128)(2,1)S(1)}, u32[]{:S(2)}, u32[]{:S(2)}) collective-permute-start(bf16[2,2048]{1,0:T(2,128)(2,1)S(1)} %fusion.33), channel_id=1, source_target_pairs={{0,4},{4,0},{8,12},{12,8},{16,20},{20,16},{24,28},{28,24},{1,5},{5... | collective-permute-start | bytes 24584 | tf_op jit(solution)/shard_map/ppermute | solution.py:267
  49.4 4.3 %collective-permute-start.9 = (bf16[4,2048]{1,0:T(4,128)(2,1)S(1)}, bf16[4,2048]{1,0:T(4,128)(2,1)S(1)}, u32[]{:S(2)}, u32[]{:S(2)}) collective-permute-start(bf16[4,2048]{1,0:T(4,128)(2,1)S(1)} %pad_maximum_fusion.6), channel_id=1, source_target_pairs={{0,8},{4,12},{8,0},{12,4},{16,24},{20,28},{24,16},{28,20},{1,9},{5... | collective-permute-start | bytes 49160 | tf_op jit(solution)/shard_map/ppermute | solution.py:267
  53.7 12.6 %collective-permute-start.10 = (bf16[8,2048]{1,0:T(8,128)(2,1)S(1)}, bf16[8,2048]{1,0:T(8,128)(2,1)S(1)}, u32[]{:S(2)}, u32[]{:S(2)}) collective-permute-start(bf16[8,2048]{1,0:T(8,128)(2,1)S(1)} %pad_maximum_fusion.4), channel_id=1, source_target_pairs={{0,16},{4,20},{8,24},{12,28},{16,0},{20,4},{24,8},{28,12},{1,17},{... | collective-permute-start | bytes 98312 | tf_op jit(solution)/shard_map/ppermute | solution.py:267
  90.2 16.1 %collective-permute-start.16 = (bf16[512,2048]{1,0:T(8,128)(2,1)}, bf16[512,2048]{1,0:T(8,128)(2,1)}, u32[]{:S(2)}, u32[]{:S(2)}) collective-permute-start(bf16[512,2048]{1,0:T(8,128)(2,1)} %collective-permute-done.11), channel_id=1, source_target_pairs={{0,1},{1,0},{2,3},{3,2},{4,5},{5,4},{6,7},{7,6},{8,9},{9,8},{10,11... | collective-permute-start | bytes 6291464 | tf_op jit(solution)/shard_map/ppermute | solution.py:280
  90.2 18.4 %collective-permute-start.14 = (bf16[512,2048]{1,0:T(8,128)(2,1)S(1)}, bf16[512,2048]{1,0:T(8,128)(2,1)}, u32[]{:S(2)}, u32[]{:S(2)}) collective-permute-start(bf16[512,2048]{1,0:T(8,128)(2,1)S(1)} %copy-done.1), channel_id=1, source_target_pairs={{0,1},{1,0},{2,3},{3,2},{4,5},{5,4},{6,7},{7,6},{8,9},{9,8},{10,11... | collective-permute-start | bytes 6291464 | tf_op jit(solution)/shard_map/ppermute | solution.py:280
  92.7 9.5 %collective-permute-start.12 = (bf16[256,512]{1,0:T(8,128)(2,1)}, bf16[256,512]{1,0:T(8,128)(2,1)}, u32[]{:S(2)}, u32[]{:S(2)}) collective-permute-start(bf16[256,512]{1,0:T(8,128)(2,1)} %get-tuple-element.26), channel_id=1, source_target_pairs={{0,2},{1,3},{2,0},{3,1},{4,6},{5,7},{6,4},{7,5},{8,10},{9,11},{10,... | collective-permute-start | bytes 786440 | tf_op jit(solution)/shard_map/ppermute | solution.py:289
  93.7 12.6 %collective-permute-start.15 = (bf16[256,512]{1,0:T(8,128)(2,1)}, bf16[256,512]{1,0:T(8,128)(2,1)S(1)}, u32[]{:S(2)}, u32[]{:S(2)}) collective-permute-start(bf16[256,512]{1,0:T(8,128)(2,1)} %get-tuple-element.25), channel_id=1, source_target_pairs={{0,3},{1,2},{2,1},{3,0},{4,7},{5,6},{6,5},{7,4},{8,11},{9,10},{10,... | collective-permute-start | bytes 786440 | tf_op jit(solution)/shard_map/ppermute | solution.py:289
  94.1 14.6 %collective-permute-start.13 = (bf16[256,512]{1,0:T(8,128)(2,1)S(1)}, bf16[256,512]{1,0:T(8,128)(2,1)S(1)}, u32[]{:S(2)}, u32[]{:S(2)}) collective-permute-start(bf16[256,512]{1,0:T(8,128)(2,1)S(1)} %get-tuple-element.24), channel_id=1, source_target_pairs={{0,1},{1,0},{2,3},{3,2},{4,5},{5,4},{6,7},{7,6},{8,9},{9,8},{10,11... | collective-permute-start | bytes 786440 | tf_op jit(solution)/shard_map/ppermute | solution.py:289

commit v14 on v12

--- a/solution.py
+++ b/solution.py
@@ -254,13 +254,15 @@
     sibling_tokens = [lax.ppermute(t, "tensor", route(0, 1)) for t in same_core_tokens]
     sibling_tokens, slot_rows = lax.optimization_barrier((sibling_tokens, slot_rows))
     across_chips = [lax.ppermute(held_weight, "tensor", route(k, 0)) for k in range(1, chips)]
-    tokens = jnp.zeros((tensor_size * block, normed.shape[1]), normed.dtype)
+    bias_row = qkv_bias.astype(jnp.float32)
+    merged_rows = jnp.zeros((tensor_size * block, qkv_weight.shape[1]), jnp.bfloat16)
     for flip, token_blocks in ((0, same_core_tokens), (1, sibling_tokens)):
         for k, token_block in enumerate(token_blocks):
             source = ((chip - k) % chips) * 2 + (core ^ flip)
-            tokens = lax.dynamic_update_slice_in_dim(tokens, token_block, source * block, 0)
-    product = jnp.dot(tokens, qkv_weight, preferred_element_type=jnp.float32)
-    merged_rows = (product + qkv_bias.astype(jnp.float32)).astype(jnp.bfloat16)
+            projected = (
+                jnp.dot(token_block, qkv_weight, preferred_element_type=jnp.float32) + bias_row
+            ).astype(jnp.bfloat16)
+            merged_rows = lax.dynamic_update_slice_in_dim(merged_rows, projected, source * block, 0)
     returned = slot_rows
     step = 1
     while step < dp_size:

time: 113 us -> 113 us (level)
  local copies, waits for them, and re-layouts: 14.8 us -> 4.9 us
  matrix products: 30.6 us -> 37 us
  starting transfers between devices: 18.8 us -> 20.9 us
    dynamic_update_slice x4 -> x0, local copies, waits for them, and re-layouts: 9.34 us -> none  [per_device(): lax.dynamic_update_slice_in_dim(tokens, token_block, source * block, 0)]
    dot_general x1 -> x4, matrix products: 11.2 us -> 17.6 us  [per_device(): jnp.dot(token_block, qkv_weight, preferred_element_type=jnp.float32)]
    ppermute x2, waiting for transfers between devices: 2.97 us -> 1.35 us  [per_device(): lax.ppermute(partials, 'tensor', [(i, i ^ step) for i in range(tensor_siz...]
    ppermute x2, starting transfers between devices: 0.22 us -> 1.84 us  [per_device(): lax.ppermute(partials, 'tensor', [(i, i ^ step) for i in range(tensor_siz...]
    ppermute x1, starting transfers between devices: 0.22 us -> 1.84 us  [per_device(): lax.ppermute(held_weight, 'tensor', route(k, 0))]
    ppermute x1, waiting for transfers between devices: 0.01 us -> 1.57 us  [per_device(): lax.ppermute(held_weight, 'tensor', route(k, 0))]
  transfers between devices with their start and end apart: 17 -> 17, of which waited for: 5 -> 7; matrix products, arithmetic and copies ran while one was open for 38% -> 35% of each run, Pallas kernels for 21% -> 21%
where the time goes in v14:
time: 113 us; the launch traced here: 112 us
  matrix products  37 us (33%)
  Pallas kernels  23.4 us (21%)
  starting transfers between devices  20.9 us (18%)
  waiting for transfers between devices  17 us (15%)
  other arithmetic  7.25 us (6%)
  local copies, waits for them, and re-layouts  4.9 us (4%)
  between operations  1.63 us (1%)
    pallas_call x1, Pallas kernels, prefill_attention_kernel(): pl.pallas_call(functools.partial(_prefill_kernel, tq=tq), out_shape=jax.S...  23.4 us
    dot_general x4, matrix products, per_device(): jnp.dot(token_block, qkv_weight, preferred_element_type=jnp.float32)  17.6 us
    dot_general x3, matrix products, per_device(): summed = summed + jnp.dot(piece, weight, preferred_element_type=jnp.float32)  8.12 us
    ppermute x3, waiting for transfers between devices, per_device(): pieces.append(lax.ppermute(outgoing, 'tensor', route(k, flip)))  7.35 us
    ppermute x3, waiting for transfers between devices, per_device(): lax.ppermute(shifted_rows, 'dp', [(i, i ^ step) for i in range(dp_size)])  6.02 us
    ppermute x3, starting transfers between devices, per_device(): lax.ppermute(shifted_rows, 'dp', [(i, i ^ step) for i in range(dp_size)])  5.82 us
    ppermute x3, starting transfers between devices, per_device(): lax.ppermute(returned, 'dp', [(i, i ^ step) for i in range(dp_size)])  5.8 us
    dot_general x1, matrix products, per_device(): jnp.dot(normed_slots, qkv_weight, preferred_element_type=jnp.float32)  3.75 us
  transfers between devices with their start and end apart: 17, of which 7 were waited for; matrix products, arithmetic and copies ran while one was open for 35% of the time, Pallas kernels for 21%

profile of v14, /device:TPU:0, one launch (start us, length us, event | category | flops | bytes accessed | tf_op | source)
XLA Modules:
  0.0 112.0 jit_solution(16435826424081757748)
XLA Ops:
  0.6 0.0 copy-start
  0.6 0.8 convert_element_type.97
  1.4 0.7 convert_element_type.96
  2.1 1.5 %convert_reduce_fusion = f32[256]{0:T(256)S(1)} fusion(bf16[256,2048]{1,0:T(8,128)(2,1)} %param.15), kind=kLoop, calls=%fused_computation.2 | loop fusion | flops 1048320 | bytes 1049600 | tf_op jit(solution)/shard_map/reduce_sum | solution.py:20
  3.6 1.6 %fusion.17 = f32[256]{0:T(256)S(1)} fusion(bf16[256,2048]{1,0:T(8,128)(2,1)} %param.15, f32[256]{0:T(256)S(1)} %broadcast_multiply_fusion), kind=kLoop, calls=%fused_computation.30 | loop fusion | flops 2096896 | bytes 1050624 | tf_op jit(solution)/shard_map/reduce_sum | solution.py:21
  5.3 1.4 %fusion.20 = bf16[256,2048]{1,0:T(8,128)(2,1)} fusion(bf16[256,2048]{1,0:T(8,128)(2,1)S(1)} %copy-done, f32[2048]{0:T(1024)S(1)} %convert_element_type.97, f32[2048]{0:T(1024)S(1)} %convert_element_type.96, f32[256]{0:T(256)S(1)} %add_rsqrt_fusion, f32[256]{0:T(256)S(1)} %broadcast_multiply_fusion), kind=kLoop, calls=%fused_computation.33 | loop fusion | flops 3145728 | bytes 2115584 | tf_op jit(solution)/shard_map/convert_element_type | solution.py:23
  6.7 2.9 %collective-permute-start = (bf16[256,2048]{1,0:T(8,128)(2,1)}, bf16[256,2048]{1,0:T(8,128)(2,1)}, u32[]{:S(2)}, u32[]{:S(2)}) collective-permute-start(bf16[256,2048]{1,0:T(8,128)(2,1)} %fusion.20), channel_id=1, source_target_pairs={{0,2},{1,3},{2,0},{3,1},{4,6},{5,7},{6,4},{7,5},{8,10},{9,11},{10,... | collective-permute-start | bytes 3145736 | tf_op jit(solution)/shard_map/ppermute | solution.py:251
  9.7 0.0 collective-permute-start.1
  9.7 1.5 %collective-permute-start.3 = (bf16[2,2048]{1,0:T(2,128)(2,1)S(1)}, bf16[2,2048]{1,0:T(2,128)(2,1)S(1)}, u32[]{:S(2)}, u32[]{:S(2)}) collective-permute-start(bf16[2,2048]{1,0:T(2,128)(2,1)S(1)} %copy-done.4), channel_id=1, source_target_pairs={{0,4},{4,0},{8,12},{12,8},{16,20},{20,16},{24,28},{28,24},{1,5},{5... | collective-permute-start | bytes 24584 | tf_op jit(solution)/shard_map/ppermute | solution.py:200
  11.2 0.1 subtract_convert_fusion
  11.3 0.1 iota_compare_fusion
  11.4 0.2 fusion.61
  11.6 1.7 %collective-permute-done.3 = bf16[2,2048]{1,0:T(2,128)(2,1)S(1)} collective-permute-done((bf16[2,2048]{1,0:T(2,128)(2,1)S(1)}, bf16[2,2048]{1,0:T(2,128)(2,1)S(1)}, u32[]{:S(2)}, u32[]{:S(2)}) %collective-permute-start.3) | collective-permute-done | bytes 8224 | tf_op jit(solution)/shard_map/ppermute | solution.py:200
  13.3 1.6 %collective-permute-start.4 = (bf16[4,2048]{1,0:T(4,128)(2,1)S(1)}, bf16[4,2048]{1,0:T(4,128)(2,1)S(1)}, u32[]{:S(2)}, u32[]{:S(2)}) collective-permute-start(bf16[4,2048]{1,0:T(4,128)(2,1)S(1)} %pad_maximum_fusion.4), channel_id=1, source_target_pairs={{0,8},{4,12},{8,0},{12,4},{16,24},{20,28},{24,16},{28,20},{1,9},{5... | collective-permute-start | bytes 49160 | tf_op jit(solution)/shard_map/ppermute | solution.py:200
  15.0 2.1 %collective-permute-done.4 = bf16[4,2048]{1,0:T(4,128)(2,1)S(1)} collective-permute-done((bf16[4,2048]{1,0:T(4,128)(2,1)S(1)}, bf16[4,2048]{1,0:T(4,128)(2,1)S(1)}, u32[]{:S(2)}, u32[]{:S(2)}) %collective-permute-start.4) | collective-permute-done | bytes 16416 | tf_op jit(solution)/shard_map/ppermute | solution.py:200
  17.2 2.7 %collective-permute-start.5 = (bf16[8,2048]{1,0:T(8,128)(2,1)S(1)}, bf16[8,2048]{1,0:T(8,128)(2,1)S(1)}, u32[]{:S(2)}, u32[]{:S(2)}) collective-permute-start(bf16[8,2048]{1,0:T(8,128)(2,1)S(1)} %pad_maximum_fusion.1), channel_id=1, source_target_pairs={{0,16},{4,20},{8,24},{12,28},{16,0},{20,4},{24,8},{28,12},{1,17},{... | collective-permute-start | bytes 98312 | tf_op jit(solution)/shard_map/ppermute | solution.py:200
  19.9 2.1 %collective-permute-done.5 = bf16[8,2048]{1,0:T(8,128)(2,1)S(1)} collective-permute-done((bf16[8,2048]{1,0:T(8,128)(2,1)S(1)}, bf16[8,2048]{1,0:T(8,128)(2,1)S(1)}, u32[]{:S(2)}, u32[]{:S(2)}) %collective-permute-start.5) | collective-permute-done | bytes 32800 | tf_op jit(solution)/shard_map/ppermute | solution.py:200
  22.1 0.3 fusion.74
  22.4 0.2 multiply_reduce_fusion
  22.6 3.8 %fusion.15 = bf16[2,1536]{1,0:T(2,128)(2,1)S(1)} fusion(bf16[2048,1536]{1,0:T(8,128)(2,1)} %param.19, f32[2,2048]{1,0:T(2,128)S(1)} %get-tuple-element.33, f32[2]{0:T(128)S(1)} %add_rsqrt_fusion.1, f32[2]{0:T(128)S(1)} %broadcast_multiply_fusion.1, f32[2048]{0:T(1024)S(1)} %convert_element_type.97, f32[2048]{0:T(1024)S(1)} %convert_element_type.96, ...), kind=kOutput, calls=%fused_computation.26 | convolution fusion | flops 12609536 | bytes 6336528 | tf_op jit(solution)/shard_map/dot_general | solution.py:214
  26.4 0.1 fusion.50
  26.5 3.6 %fusion.75 = (f32[2,4]{1,0:T(2,128)S(1)}, f32[2,4,2048]{2,1,0:T(4,128)S(1)}) fusion(f32[2,2048]{1,0:T(2,128)S(1)} %subtract_convert_fusion, f32[4]{0:T(128)S(1)} %multiply_exponential_fusion.slopes_ref, bf16[2,2048,512]{2,1,0:T(8,128)(2,1)} %param.25, pred[512,4]{0,1:T(4,128)(4,1)S(1)} %iota_compare_fusion.1, bf16[2,512]{1,0:T(2,128)(2,1)S(1)} %bitcast.51, ...), kind=kOutput, calls=%fused_computation.136 | convolution fusion | flops 16863224 | bytes 4284464 | tf_op jit(solution)/shard_map/vmap()/dot_general | solution.py:148
  30.1 0.2 fusion.37
  30.4 0.1 broadcast_bitcast_fusion
  30.4 0.7 fusion.21
  31.2 0.9 copy-done.1
  32.0 0.4 fusion.56
  32.4 0.0 collective-permute-start.6
  32.4 0.7 collective-permute-done
  33.1 0.0 collective-permute-start.2
  33.1 1.9 %broadcast_in_dim.54 = bf16[1024,1536]{1,0:T(8,128)(2,1)} broadcast(bf16[]{:T(256)} %constant.123.clone.1), dimensions={} | broadcast | bytes 3145730 | tf_op jit(solution)/shard_map/broadcast_in_dim | solution.py:258
  35.0 3.9 %fusion.3 = bf16[1024,1536]{1,0:T(8,128)(2,1)} fusion(bf16[1024,1536]{1,0:T(8,128)(2,1)} %broadcast_in_dim.54, s32[]{:T(128)S(6)} %select_n.124, bf16[256,2048]{1,0:T(8,128)(2,1)} %fusion.20, bf16[2048,1536]{1,0:T(8,128)(2,1)S(1)} %copy-done.2, f32[1536]{0:T(1024)S(1)} %convert_element_type.99), kind=kOutput, calls=%fused_computation.12 | convolution fusion | flops 1611399168 | bytes 8132612 | tf_op jit(solution)/shard_map/dot_general | solution.py:263
  38.9 0.0 collective-permute-done.6
  39.0 1.8 %collective-permute-start.7 = (f32[4,2048]{1,0:T(4,128)S(1)}, f32[4,2048]{1,0:T(4,128)S(1)}, u32[]{:S(2)}, u32[]{:S(2)}) collective-permute-start(f32[4,2048]{1,0:T(4,128)S(1)} %pad_maximum_fusion.2), channel_id=1, source_target_pairs={{0,2},{1,3},{2,0},{3,1},{4,6},{5,7},{6,4},{7,5},{8,10},{9,11},{10,... | collective-permute-start | bytes 98312 | tf_op jit(solution)/shard_map/ppermute | solution.py:233
  40.8 0.1 fusion.65
  41.6 1.3 %collective-permute-done.7 = f32[4,2048]{1,0:T(4,128)S(1)} collective-permute-done((f32[4,2048]{1,0:T(4,128)S(1)}, f32[4,2048]{1,0:T(4,128)S(1)}, u32[]{:S(2)}, u32[]{:S(2)}) %collective-permute-start.7) | collective-permute-done | bytes 32800 | tf_op jit(solution)/shard_map/ppermute | solution.py:233
  43.0 0.0 slice-start
  43.1 0.0 slice-start.1
  43.1 1.8 %collective-permute-start.11 = (bf16[512,2048]{1,0:T(8,128)(2,1)S(1)}, bf16[512,2048]{1,0:T(8,128)(2,1)}, u32[]{:S(2)}, u32[]{:S(2)}) collective-permute-start(bf16[512,2048]{1,0:T(8,128)(2,1)S(1)} %copy-done.1), channel_id=1, source_target_pairs={{0,2},{1,3},{2,0},{3,1},{4,6},{5,7},{6,4},{7,5},{8,10},{9,11},{10,... | collective-permute-start | bytes 6291464 | tf_op jit(solution)/shard_map/ppermute | solution.py:256
  44.9 0.0 collective-permute-done.1
  44.9 0.0 collective-permute-done.2
  44.9 1.5 %collective-permute-start.8 = (bf16[2,2048]{1,0:T(2,128)(2,1)S(1)}, bf16[2,2048]{1,0:T(2,128)(2,1)S(1)}, u32[]{:S(2)}, u32[]{:S(2)}) collective-permute-start(bf16[2,2048]{1,0:T(2,128)(2,1)S(1)} %fusion.41), channel_id=1, source_target_pairs={{0,4},{4,0},{8,12},{12,8},{16,20},{20,16},{24,28},{28,24},{1,5},{5... | collective-permute-start | bytes 24584 | tf_op jit(solution)/shard_map/ppermute | solution.py:270
  46.5 5.8 %fusion.5 = bf16[1024,1536]{1,0:T(8,128)(2,1)} fusion(bf16[1024,1536]{1,0:T(8,128)(2,1)} %fusion.3, s32[]{:T(128)S(6)} %select_n.126, bf16[256,2048]{1,0:T(8,128)(2,1)} %collective-permute-done, bf16[2048,1536]{1,0:T(8,128)(2,1)} %param.19, f32[1536]{0:T(1024)S(1)} %convert_element_type.99), kind=kOutput, calls=%fused_computation.14 | convolution fusion | flops 1611399168 | bytes 8132612 | tf_op jit(solution)/shard_map/dot_general | solution.py:263
  52.3 0.0 collective-permute-done.8
  52.3 1.6 %collective-permute-start.9 = (bf16[4,2048]{1,0:T(4,128)(2,1)S(1)}, bf16[4,2048]{1,0:T(4,128)(2,1)S(1)}, u32[]{:S(2)}, u32[]{:S(2)}) collective-permute-start(bf16[4,2048]{1,0:T(4,128)(2,1)S(1)} %pad_maximum_fusion.5), channel_id=1, source_target_pairs={{0,8},{4,12},{8,0},{12,4},{16,24},{20,28},{24,16},{28,20},{1,9},{5... | collective-permute-start | bytes 49160 | tf_op jit(solution)/shard_map/ppermute | solution.py:270
  54.0 3.9 %fusion.7 = bf16[1024,1536]{1,0:T(8,128)(2,1)} fusion(bf16[1024,1536]{1,0:T(8,128)(2,1)} %fusion.5, s32[]{:T(128)S(6)} %select_n.138, bf16[256,2048]{1,0:T(8,128)(2,1)} %collective-permute-done.1, bf16[2048,1536]{1,0:T(8,128)(2,1)S(1)} %bitcast.49, f32[1536]{0:T(1024)S(1)} %convert_element_type.99), kind=kOutput, calls=%fused_computation.16 | convolution fusion | flops 1611399168 | bytes 8132612 | tf_op jit(solution)/shard_map/dot_general | solution.py:263
  57.9 0.0 collective-permute-done.9
  57.9 2.6 %collective-permute-start.10 = (bf16[8,2048]{1,0:T(8,128)(2,1)S(1)}, bf16[8,2048]{1,0:T(8,128)(2,1)S(1)}, u32[]{:S(2)}, u32[]{:S(2)}) collective-permute-start(bf16[8,2048]{1,0:T(8,128)(2,1)S(1)} %pad_maximum_fusion.3), channel_id=1, source_target_pairs={{0,16},{4,20},{8,24},{12,28},{16,0},{20,4},{24,8},{28,12},{1,17},{... | collective-permute-start | bytes 98312 | tf_op jit(solution)/shard_map/ppermute | solution.py:270
  60.5 3.9 %fusion.9.q_ref.kn_ref.vn_ref = bf16[1024,1536]{1,0:T(8,128)(2,1)} fusion(bf16[1024,1536]{1,0:T(8,128)(2,1)} %fusion.7, s32[]{:T(128)S(6)} %select_n.139, bf16[256,2048]{1,0:T(8,128)(2,1)} %collective-permute-done.2, bf16[2048,1536]{1,0:T(8,128)(2,1)S(1)} %bitcast.49, f32[1536]{0:T(1024)S(1)} %convert_element_type.99), kind=kOutput, calls=%fused_computation.18 | convolution fusion | flops 1611399168 | bytes 8132612 | tf_op jit(solution)/shard_map/dot_general | solution.py:263
  64.4 0.8 convolution_convert_fusion
  65.2 23.4 %shard_map.158 = bf16[1024,512]{1,0:T(8,128)(2,1)} custom-call(s32[1]{0:T(128)S(6)} %copy.39.prefix_ref, f32[4]{0:T(128)} %copy-done.8, bf16[1024,1536]{1,0:T(8,128)(2,1)} %fusion.9.q_ref.kn_ref.vn_ref, bf16[1024,1536]{1,0:T(8,128)(2,1)} %fusion.9.q_ref.kn_ref.vn_ref, bf16[1024,1536]{1,0:T(8,128)(2,1)} %fusion.9.q_ref.kn_ref.vn_ref, ...), custom_call_target="tpu_custom_call" | custom-call | flops 4294967296 | bytes 6291456 | tf_op jit(solution)/shard_map/pallas_call | solution.py:117
  88.6 1.6 %collective-permute-done.11 = bf16[512,2048]{1,0:T(8,128)(2,1)} collective-permute-done((bf16[512,2048]{1,0:T(8,128)(2,1)S(1)}, bf16[512,2048]{1,0:T(8,128)(2,1)}, u32[]{:S(2)}, u32[]{:S(2)}) %collective-permute-start.11) | collective-permute-done | bytes 2097184 | tf_op jit(solution)/shard_map/ppermute | solution.py:256
  90.2 0.5 collective-permute-start.14
  90.7 2.0 %constant_dynamic-slice_fusion.2 = (bf16[256,512]{1,0:T(8,128)(2,1)S(1)}, bf16[256,512]{1,0:T(8,128)(2,1)}, bf16[256,512]{1,0:T(8,128)(2,1)}) fusion(bf16[1024,512]{1,0:T(8,128)(2,1)} %shard_map.158, s32[]{:T(128)S(6)} %select_n.138, s32[]{:T(128)S(6)} %select_n.146, s32[]{:T(128)S(6)} %select_n.145), kind=kLoop, calls=%fused_computation.92 | loop fusion | bytes 1572876 | tf_op jit(solution)/shard_map/dynamic_slice | solution.py:291
  92.6 1.7 %collective-permute-start.12 = (bf16[256,512]{1,0:T(8,128)(2,1)}, bf16[256,512]{1,0:T(8,128)(2,1)}, u32[]{:S(2)}, u32[]{:S(2)}) collective-permute-start(bf16[256,512]{1,0:T(8,128)(2,1)} %get-tuple-element.26), channel_id=1, source_target_pairs={{0,2},{1,3},{2,0},{3,1},{4,6},{5,7},{6,4},{7,5},{8,10},{9,11},{10,... | collective-permute-start | bytes 786440 | tf_op jit(solution)/shard_map/ppermute | solution.py:292
  94.4 0.0 collective-permute-start.15
  94.4 0.4 collective-permute-start.13
  94.8 7.3 %collective-permute-done.12 = bf16[256,512]{1,0:T(8,128)(2,1)} collective-permute-done((bf16[256,512]{1,0:T(8,128)(2,1)}, bf16[256,512]{1,0:T(8,128)(2,1)}, u32[]{:S(2)}, u32[]{:S(2)}) %collective-permute-start.12) | collective-permute-done | bytes 262176 | tf_op jit(solution)/shard_map/ppermute | solution.py:292
  102.1 2.4 %fusion.76 = f32[256,2048]{1,0:T(8,128)S(1)} fusion(bf16[256,512]{1,0:T(8,128)(2,1)} %collective-permute-done.12, bf16[512,2048]{1,0:T(8,128)(2,1)} %collective-permute-done.11), kind=kOutput, calls=%fused_computation.137 | convolution fusion | flops 536870912 | bytes 4456448 | tf_op jit(solution)/shard_map/dot_general | solution.py:295
  104.5 1.7 %convolution_add_fusion.1 = f32[256,2048]{1,0:T(8,128)S(1)} fusion(f32[256,2048]{1,0:T(8,128)S(1)} %fusion.76, bf16[512,2048]{1,0:T(8,128)(2,1)S(1)} %copy-done.1, bf16[1024,512]{1,0:T(8,128)(2,1)} %shard_map.158, s32[]{:T(128)S(6)} %select_n.143), kind=kOutput, calls=%fused_computation.5 | convolution fusion | flops 537395200 | bytes 6553604 | tf_op jit(solution)/shard_map/dot_general | solution.py:293
  106.2 0.0 collective-permute-done.15
  106.3 2.3 %fusion.77 = f32[256,2048]{1,0:T(8,128)S(1)} fusion(bf16[256,512]{1,0:T(8,128)(2,1)S(1)} %collective-permute-done.15, bf16[512,2048]{1,0:T(8,128)(2,1)} %collective-permute-done.16), kind=kOutput, calls=%fused_computation.138 | convolution fusion | flops 536870912 | bytes 4456448 | tf_op jit(solution)/shard_map/dot_general | solution.py:295
  108.6 0.0 collective-permute-done.14
  108.6 3.4 %fusion.10 = bf16[256,2048]{1,0:T(8,128)(2,1)} fusion(bf16[256,2048]{1,0:T(8,128)(2,1)S(1)} %copy-done, f32[256,2048]{1,0:T(8,128)S(1)} %fusion.77, f32[256,2048]{1,0:T(8,128)S(1)} %convolution_add_fusion.1, bf16[256,512]{1,0:T(8,128)(2,1)S(1)} %collective-permute-done.13, bf16[512,2048]{1,0:T(8,128)(2,1)} %collective-permute-done.14, ...), kind=kOutput, calls=%fused_computation.19 | convolution fusion | flops 540016640 | bytes 8658944 | tf_op jit(solution)/shard_map/dot_general | solution.py:295
  (51 shorter events, 0.5 us)
Async XLA Ops:
  0.6 4.6 %copy-start = (bf16[256,2048]{1,0:T(8,128)(2,1)S(1)}, bf16[256,2048]{1,0:T(8,128)(2,1)}, u32[]{:S(2)}) copy-start(bf16[256,2048]{1,0:T(8,128)(2,1)} %param.15) | copy-start | bytes 3145732
  2.1 7.6 %copy-start.4 = (bf16[2,2048]{1,0:T(2,128)(2,1)S(1)}, bf16[2,2048]{1,0:T(2,128)(2,1)}, u32[]{:S(2)}) copy-start(bf16[2,2048]{1,0:T(2,128)(2,1)} %param.16) | copy-start | bytes 24580
  2.1 9.1 %copy-start.7 = (s32[2]{0:T(128)S(1)}, s32[2]{0:T(128)}, u32[]{:S(2)}) copy-start(s32[2]{0:T(128)} %param.28) | copy-start | bytes 28
  2.1 9.3 %copy-start.9 = (s32[16]{0:T(128)S(1)}, s32[16]{0:T(128)}, u32[]{:S(2)}) copy-start(s32[16]{0:T(128)} %param.29) | copy-start | bytes 196
  2.1 17.8 %copy-start.5 = (bf16[1536]{0:T(1024)(128)(2,1)S(1)}, bf16[1536]{0:T(1024)(128)(2,1)}, u32[]{:S(2)}) copy-start(bf16[1536]{0:T(1024)(128)(2,1)} %param.20) | copy-start | bytes 9220
  6.7 26.4 %collective-permute-start = (bf16[256,2048]{1,0:T(8,128)(2,1)}, bf16[256,2048]{1,0:T(8,128)(2,1)}, u32[]{:S(2)}, u32[]{:S(2)}) collective-permute-start(bf16[256,2048]{1,0:T(8,128)(2,1)} %fusion.20), channel_id=1, source_target_pairs={{0,2},{1,3},{2,0},{3,1},{4,6},{5,7},{6,4},{7,5},{8,10},{9,11},{10,... | collective-permute-start | bytes 3145736 | tf_op jit(solution)/shard_map/ppermute | solution.py:251
  9.7 35.3 %collective-permute-start.1 = (bf16[256,2048]{1,0:T(8,128)(2,1)}, bf16[256,2048]{1,0:T(8,128)(2,1)}, u32[]{:S(2)}, u32[]{:S(2)}) collective-permute-start(bf16[256,2048]{1,0:T(8,128)(2,1)} %fusion.20), channel_id=1, source_target_pairs={{0,1},{1,0},{2,3},{3,2},{4,5},{5,4},{6,7},{7,6},{8,9},{9,8},{10,11... | collective-permute-start | bytes 3145736 | tf_op jit(solution)/shard_map/ppermute | solution.py:254
  9.7 3.7 %collective-permute-start.3 = (bf16[2,2048]{1,0:T(2,128)(2,1)S(1)}, bf16[2,2048]{1,0:T(2,128)(2,1)S(1)}, u32[]{:S(2)}, u32[]{:S(2)}) collective-permute-start(bf16[2,2048]{1,0:T(2,128)(2,1)S(1)} %copy-done.4), channel_id=1, source_target_pairs={{0,4},{4,0},{8,12},{12,8},{16,20},{20,16},{24,28},{28,24},{1,5},{5... | collective-permute-start | bytes 24584 | tf_op jit(solution)/shard_map/ppermute | solution.py:200
  13.3 3.8 %collective-permute-start.4 = (bf16[4,2048]{1,0:T(4,128)(2,1)S(1)}, bf16[4,2048]{1,0:T(4,128)(2,1)S(1)}, u32[]{:S(2)}, u32[]{:S(2)}) collective-permute-start(bf16[4,2048]{1,0:T(4,128)(2,1)S(1)} %pad_maximum_fusion.4), channel_id=1, source_target_pairs={{0,8},{4,12},{8,0},{12,4},{16,24},{20,28},{24,16},{28,20},{1,9},{5... | collective-permute-start | bytes 49160 | tf_op jit(solution)/shard_map/ppermute | solution.py:200
  17.2 4.9 %collective-permute-start.5 = (bf16[8,2048]{1,0:T(8,128)(2,1)S(1)}, bf16[8,2048]{1,0:T(8,128)(2,1)S(1)}, u32[]{:S(2)}, u32[]{:S(2)}) collective-permute-start(bf16[8,2048]{1,0:T(8,128)(2,1)S(1)} %pad_maximum_fusion.1), channel_id=1, source_target_pairs={{0,16},{4,20},{8,24},{12,28},{16,0},{20,4},{24,8},{28,12},{1,17},{... | collective-permute-start | bytes 98312 | tf_op jit(solution)/shard_map/ppermute | solution.py:200
  19.8 6.7 %copy-start.8 = (f32[4]{0:T(128)}, f32[4]{0:T(128)S(1)}, u32[]{:S(2)}) copy-start(f32[4]{0:T(128)S(1)} %multiply_exponential_fusion.slopes_ref) | copy-start | bytes 52
  26.5 3.9 %copy-start.3 = (bf16[2,2048,512]{2,1,0:T(8,128)(2,1)S(1)}, bf16[2,2048,512]{2,1,0:T(8,128)(2,1)}, u32[]{:S(2)}) copy-start(bf16[2,2048,512]{2,1,0:T(8,128)(2,1)} %param.26) | copy-start | bytes 12582916
  30.4 1.6 %copy-start.1 = (bf16[512,2048]{1,0:T(8,128)(2,1)S(1)}, bf16[512,2048]{1,0:T(8,128)(2,1)}, u32[]{:S(2)}) copy-start(bf16[512,2048]{1,0:T(8,128)(2,1)} %param.21) | copy-start | bytes 6291460
  30.4 4.6 %copy-start.2 = (bf16[2048,1536]{1,0:T(8,128)(2,1)S(1)}, bf16[2048,1536]{1,0:T(8,128)(2,1)}, u32[]{:S(2)}) copy-start(bf16[2048,1536]{1,0:T(8,128)(2,1)} %param.19) | copy-start | bytes 18874372
  32.4 6.5 %collective-permute-start.6 = (f32[2,2048]{1,0:T(2,128)S(1)}, f32[2,2048]{1,0:T(2,128)S(1)}, u32[]{:S(2)}, u32[]{:S(2)}) collective-permute-start(f32[2,2048]{1,0:T(2,128)S(1)} %fusion.56), channel_id=1, source_target_pairs={{0,1},{1,0},{2,3},{3,2},{4,5},{5,4},{6,7},{7,6},{8,9},{9,8},{10,11... | collective-permute-start | bytes 49160 | tf_op jit(solution)/shard_map/ppermute | solution.py:233
  33.1 11.8 %collective-permute-start.2 = (bf16[256,2048]{1,0:T(8,128)(2,1)}, bf16[256,2048]{1,0:T(8,128)(2,1)}, u32[]{:S(2)}, u32[]{:S(2)}) collective-permute-start(bf16[256,2048]{1,0:T(8,128)(2,1)} %collective-permute-done), channel_id=1, source_target_pairs={{0,1},{1,0},{2,3},{3,2},{4,5},{5,4},{6,7},{7,6},{8,9},{9,8},{10,11... | collective-permute-start | bytes 3145736 | tf_op jit(solution)/shard_map/ppermute | solution.py:254
  35.0 6.6 %copy-start.6 = (bf16[2048]{0:T(1024)(128)(2,1)S(1)}, bf16[2048]{0:T(1024)(128)(2,1)}, u32[]{:S(2)}) copy-start(bf16[2048]{0:T(1024)(128)(2,1)} %param.22) | copy-start | bytes 12292
  39.0 4.0 %collective-permute-start.7 = (f32[4,2048]{1,0:T(4,128)S(1)}, f32[4,2048]{1,0:T(4,128)S(1)}, u32[]{:S(2)}, u32[]{:S(2)}) collective-permute-start(f32[4,2048]{1,0:T(4,128)S(1)} %pad_maximum_fusion.2), channel_id=1, source_target_pairs={{0,2},{1,3},{2,0},{3,1},{4,6},{5,7},{6,4},{7,5},{8,10},{9,11},{10,... | collective-permute-start | bytes 98312 | tf_op jit(solution)/shard_map/ppermute | solution.py:233
  43.0 10.9 %slice-start = ((s8[6291456]{0:T(1024)(128)(4,1)}), s8[4194304]{0:T(1024)(128)(4,1)S(1)}, s32[]{:S(2)}) async-start(s8[6291456]{0:T(1024)(128)(4,1)} %bitcast.48), calls=%async_computation | async-start | bytes 8388608
  43.1 10.9 %slice-start.1 = ((s8[6291456]{0:T(1024)(128)(4,1)}), s8[2097152]{0:T(1024)(128)(4,1)S(1)}, s32[]{:S(2)}) async-start(s8[6291456]{0:T(1024)(128)(4,1)} %bitcast.48), calls=%async_computation.1 | async-start | bytes 4194304
  43.1 47.1 %collective-permute-start.11 = (bf16[512,2048]{1,0:T(8,128)(2,1)S(1)}, bf16[512,2048]{1,0:T(8,128)(2,1)}, u32[]{:S(2)}, u32[]{:S(2)}) collective-permute-start(bf16[512,2048]{1,0:T(8,128)(2,1)S(1)} %copy-done.1), channel_id=1, source_target_pairs={{0,2},{1,3},{2,0},{3,1},{4,6},{5,7},{6,4},{7,5},{8,10},{9,11},{10,... | collective-permute-start | bytes 6291464 | tf_op jit(solution)/shard_map/ppermute | solution.py:256
  44.9 7.3 %collective-permute-start.8 = (bf16[2,2048]{1,0:T(2,128)(2,1)S(1)}, bf16[2,2048]{1,0:T(2,128)(2,1)S(1)}, u32[]{:S(2)}, u32[]{:S(2)}) collective-permute-start(bf16[2,2048]{1,0:T(2,128)(2,1)S(1)} %fusion.41), channel_id=1, source_target_pairs={{0,4},{4,0},{8,12},{12,8},{16,20},{20,16},{24,28},{28,24},{1,5},{5... | collective-permute-start | bytes 24584 | tf_op jit(solution)/shard_map/ppermute | solution.py:270
  52.3 5.6 %collective-permute-start.9 = (bf16[4,2048]{1,0:T(4,128)(2,1)S(1)}, bf16[4,2048]{1,0:T(4,128)(2,1)S(1)}, u32[]{:S(2)}, u32[]{:S(2)}) collective-permute-start(bf16[4,2048]{1,0:T(4,128)(2,1)S(1)} %pad_maximum_fusion.5), channel_id=1, source_target_pairs={{0,8},{4,12},{8,0},{12,4},{16,24},{20,28},{24,16},{28,20},{1,9},{5... | collective-permute-start | bytes 49160 | tf_op jit(solution)/shard_map/ppermute | solution.py:270
  57.9 6.5 %collective-permute-start.10 = (bf16[8,2048]{1,0:T(8,128)(2,1)S(1)}, bf16[8,2048]{1,0:T(8,128)(2,1)S(1)}, u32[]{:S(2)}, u32[]{:S(2)}) collective-permute-start(bf16[8,2048]{1,0:T(8,128)(2,1)S(1)} %pad_maximum_fusion.3), channel_id=1, source_target_pairs={{0,16},{4,20},{8,24},{12,28},{16,0},{20,4},{24,8},{28,12},{1,17},{... | collective-permute-start | bytes 98312 | tf_op jit(solution)/shard_map/ppermute | solution.py:270
  90.2 16.1 %collective-permute-start.16 = (bf16[512,2048]{1,0:T(8,128)(2,1)}, bf16[512,2048]{1,0:T(8,128)(2,1)}, u32[]{:S(2)}, u32[]{:S(2)}) collective-permute-start(bf16[512,2048]{1,0:T(8,128)(2,1)} %collective-permute-done.11), channel_id=1, source_target_pairs={{0,1},{1,0},{2,3},{3,2},{4,5},{5,4},{6,7},{7,6},{8,9},{9,8},{10,11... | collective-permute-start | bytes 6291464 | tf_op jit(solution)/shard_map/ppermute | solution.py:283
  90.2 18.4 %collective-permute-start.14 = (bf16[512,2048]{1,0:T(8,128)(2,1)S(1)}, bf16[512,2048]{1,0:T(8,128)(2,1)}, u32[]{:S(2)}, u32[]{:S(2)}) collective-permute-start(bf16[512,2048]{1,0:T(8,128)(2,1)S(1)} %copy-done.1), channel_id=1, source_target_pairs={{0,1},{1,0},{2,3},{3,2},{4,5},{5,4},{6,7},{7,6},{8,9},{9,8},{10,11... | collective-permute-start | bytes 6291464 | tf_op jit(solution)/shard_map/ppermute | solution.py:283
  92.6 9.5 %collective-permute-start.12 = (bf16[256,512]{1,0:T(8,128)(2,1)}, bf16[256,512]{1,0:T(8,128)(2,1)}, u32[]{:S(2)}, u32[]{:S(2)}) collective-permute-start(bf16[256,512]{1,0:T(8,128)(2,1)} %get-tuple-element.26), channel_id=1, source_target_pairs={{0,2},{1,3},{2,0},{3,1},{4,6},{5,7},{6,4},{7,5},{8,10},{9,11},{10,... | collective-permute-start | bytes 786440 | tf_op jit(solution)/shard_map/ppermute | solution.py:292
  94.4 11.9 %collective-permute-start.15 = (bf16[256,512]{1,0:T(8,128)(2,1)}, bf16[256,512]{1,0:T(8,128)(2,1)S(1)}, u32[]{:S(2)}, u32[]{:S(2)}) collective-permute-start(bf16[256,512]{1,0:T(8,128)(2,1)} %get-tuple-element.25), channel_id=1, source_target_pairs={{0,3},{1,2},{2,1},{3,0},{4,7},{5,6},{6,5},{7,4},{8,11},{9,10},{10,... | collective-permute-start | bytes 786440 | tf_op jit(solution)/shard_map/ppermute | solution.py:292
  94.4 14.2 %collective-permute-start.13 = (bf16[256,512]{1,0:T(8,128)(2,1)S(1)}, bf16[256,512]{1,0:T(8,128)(2,1)S(1)}, u32[]{:S(2)}, u32[]{:S(2)}) collective-permute-start(bf16[256,512]{1,0:T(8,128)(2,1)S(1)} %get-tuple-element.24), channel_id=1, source_target_pairs={{0,1},{1,0},{2,3},{3,2},{4,5},{5,4},{6,7},{7,6},{8,9},{9,8},{10,11... | collective-permute-start | bytes 786440 | tf_op jit(solution)/shard_map/ppermute | solution.py:292

commit v15 on v14

--- a/solution.py
+++ b/solution.py
@@ -99,8 +99,9 @@
         e_c = jnp.exp(s_c - m)
         e_n = jnp.exp(s_n - m)
         l = jnp.sum(e_c, axis=-1, keepdims=True) + jnp.sum(e_n, axis=-1, keepdims=True)
-        p_c = (e_c / l).astype(jnp.bfloat16)
-        p_n = (e_n / l).astype(jnp.bfloat16)
+        inverse = 1.0 / l
+        p_c = (e_c * inverse).astype(jnp.bfloat16)
+        p_n = (e_n * inverse).astype(jnp.bfloat16)
         ctx = jnp.dot(p_c, vc_ref[...], preferred_element_type=jnp.float32)
         ctx = ctx + jnp.dot(p_n, vn_ref[:width, :], preferred_element_type=jnp.float32)
         o_ref[...] = ctx.astype(o_ref.dtype)

time: 113 us -> 113 us (level)
  no operation moved by 1% of the time
where the time goes in v15:
time: 113 us; the launch traced here: 112 us
  matrix products  37 us (33%)
  Pallas kernels  23.4 us (21%)
  starting transfers between devices  20.9 us (18%)
  waiting for transfers between devices  17 us (15%)
  other arithmetic  7.25 us (6%)
  local copies, waits for them, and re-layouts  4.9 us (4%)
  between operations  1.63 us (1%)
    pallas_call x1, Pallas kernels, prefill_attention_kernel(): pl.pallas_call(functools.partial(_prefill_kernel, tq=tq), out_shape=jax.S...  23.4 us
    dot_general x4, matrix products, per_device(): jnp.dot(token_block, qkv_weight, preferred_element_type=jnp.float32)  17.6 us
    dot_general x3, matrix products, per_device(): summed = summed + jnp.dot(piece, weight, preferred_element_type=jnp.float32)  8.12 us
    ppermute x3, waiting for transfers between devices, per_device(): pieces.append(lax.ppermute(outgoing, 'tensor', route(k, flip)))  7.35 us
    ppermute x3, waiting for transfers between devices, per_device(): lax.ppermute(shifted_rows, 'dp', [(i, i ^ step) for i in range(dp_size)])  6.02 us
    ppermute x3, starting transfers between devices, per_device(): lax.ppermute(shifted_rows, 'dp', [(i, i ^ step) for i in range(dp_size)])  5.82 us
    ppermute x3, starting transfers between devices, per_device(): lax.ppermute(returned, 'dp', [(i, i ^ step) for i in range(dp_size)])  5.8 us
    dot_general x1, matrix products, per_device(): jnp.dot(normed_slots, qkv_weight, preferred_element_type=jnp.float32)  3.75 us
  transfers between devices with their start and end apart: 17, of which 7 were waited for; matrix products, arithmetic and copies ran while one was open for 35% of the time, Pallas kernels for 21%

profile of v15, /device:TPU:0, one launch (start us, length us, event | category | flops | bytes accessed | tf_op | source)
XLA Modules:
  0.0 112.0 jit_solution(16435826424081757748)
XLA Ops:
  0.6 0.0 copy-start
  0.6 0.8 convert_element_type.97
  1.4 0.7 convert_element_type.96
  2.1 1.5 %convert_reduce_fusion = f32[256]{0:T(256)S(1)} fusion(bf16[256,2048]{1,0:T(8,128)(2,1)} %param.15), kind=kLoop, calls=%fused_computation.2 | loop fusion | flops 1048320 | bytes 1049600 | tf_op jit(solution)/shard_map/reduce_sum | solution.py:20
  3.6 1.6 %fusion.17 = f32[256]{0:T(256)S(1)} fusion(bf16[256,2048]{1,0:T(8,128)(2,1)} %param.15, f32[256]{0:T(256)S(1)} %broadcast_multiply_fusion), kind=kLoop, calls=%fused_computation.30 | loop fusion | flops 2096896 | bytes 1050624 | tf_op jit(solution)/shard_map/reduce_sum | solution.py:21
  5.3 1.4 %fusion.20 = bf16[256,2048]{1,0:T(8,128)(2,1)} fusion(bf16[256,2048]{1,0:T(8,128)(2,1)S(1)} %copy-done, f32[2048]{0:T(1024)S(1)} %convert_element_type.97, f32[2048]{0:T(1024)S(1)} %convert_element_type.96, f32[256]{0:T(256)S(1)} %add_rsqrt_fusion, f32[256]{0:T(256)S(1)} %broadcast_multiply_fusion), kind=kLoop, calls=%fused_computation.33 | loop fusion | flops 3145728 | bytes 2115584 | tf_op jit(solution)/shard_map/convert_element_type | solution.py:23
  6.7 2.9 %collective-permute-start = (bf16[256,2048]{1,0:T(8,128)(2,1)}, bf16[256,2048]{1,0:T(8,128)(2,1)}, u32[]{:S(2)}, u32[]{:S(2)}) collective-permute-start(bf16[256,2048]{1,0:T(8,128)(2,1)} %fusion.20), channel_id=1, source_target_pairs={{0,2},{1,3},{2,0},{3,1},{4,6},{5,7},{6,4},{7,5},{8,10},{9,11},{10,... | collective-permute-start | bytes 3145736 | tf_op jit(solution)/shard_map/ppermute | solution.py:252
  9.7 0.0 collective-permute-start.1
  9.7 1.5 %collective-permute-start.3 = (bf16[2,2048]{1,0:T(2,128)(2,1)S(1)}, bf16[2,2048]{1,0:T(2,128)(2,1)S(1)}, u32[]{:S(2)}, u32[]{:S(2)}) collective-permute-start(bf16[2,2048]{1,0:T(2,128)(2,1)S(1)} %copy-done.4), channel_id=1, source_target_pairs={{0,4},{4,0},{8,12},{12,8},{16,20},{20,16},{24,28},{28,24},{1,5},{5... | collective-permute-start | bytes 24584 | tf_op jit(solution)/shard_map/ppermute | solution.py:201
  11.2 0.1 subtract_convert_fusion
  11.3 0.1 iota_compare_fusion
  11.4 0.2 fusion.61
  11.6 1.7 %collective-permute-done.3 = bf16[2,2048]{1,0:T(2,128)(2,1)S(1)} collective-permute-done((bf16[2,2048]{1,0:T(2,128)(2,1)S(1)}, bf16[2,2048]{1,0:T(2,128)(2,1)S(1)}, u32[]{:S(2)}, u32[]{:S(2)}) %collective-permute-start.3) | collective-permute-done | bytes 8224 | tf_op jit(solution)/shard_map/ppermute | solution.py:201
  13.3 1.6 %collective-permute-start.4 = (bf16[4,2048]{1,0:T(4,128)(2,1)S(1)}, bf16[4,2048]{1,0:T(4,128)(2,1)S(1)}, u32[]{:S(2)}, u32[]{:S(2)}) collective-permute-start(bf16[4,2048]{1,0:T(4,128)(2,1)S(1)} %pad_maximum_fusion.4), channel_id=1, source_target_pairs={{0,8},{4,12},{8,0},{12,4},{16,24},{20,28},{24,16},{28,20},{1,9},{5... | collective-permute-start | bytes 49160 | tf_op jit(solution)/shard_map/ppermute | solution.py:201
  15.0 2.1 %collective-permute-done.4 = bf16[4,2048]{1,0:T(4,128)(2,1)S(1)} collective-permute-done((bf16[4,2048]{1,0:T(4,128)(2,1)S(1)}, bf16[4,2048]{1,0:T(4,128)(2,1)S(1)}, u32[]{:S(2)}, u32[]{:S(2)}) %collective-permute-start.4) | collective-permute-done | bytes 16416 | tf_op jit(solution)/shard_map/ppermute | solution.py:201
  17.2 2.7 %collective-permute-start.5 = (bf16[8,2048]{1,0:T(8,128)(2,1)S(1)}, bf16[8,2048]{1,0:T(8,128)(2,1)S(1)}, u32[]{:S(2)}, u32[]{:S(2)}) collective-permute-start(bf16[8,2048]{1,0:T(8,128)(2,1)S(1)} %pad_maximum_fusion.1), channel_id=1, source_target_pairs={{0,16},{4,20},{8,24},{12,28},{16,0},{20,4},{24,8},{28,12},{1,17},{... | collective-permute-start | bytes 98312 | tf_op jit(solution)/shard_map/ppermute | solution.py:201
  19.9 2.1 %collective-permute-done.5 = bf16[8,2048]{1,0:T(8,128)(2,1)S(1)} collective-permute-done((bf16[8,2048]{1,0:T(8,128)(2,1)S(1)}, bf16[8,2048]{1,0:T(8,128)(2,1)S(1)}, u32[]{:S(2)}, u32[]{:S(2)}) %collective-permute-start.5) | collective-permute-done | bytes 32800 | tf_op jit(solution)/shard_map/ppermute | solution.py:201
  22.1 0.3 fusion.74
  22.4 0.2 multiply_reduce_fusion
  22.6 3.8 %fusion.15 = bf16[2,1536]{1,0:T(2,128)(2,1)S(1)} fusion(bf16[2048,1536]{1,0:T(8,128)(2,1)} %param.19, f32[2,2048]{1,0:T(2,128)S(1)} %get-tuple-element.33, f32[2]{0:T(128)S(1)} %add_rsqrt_fusion.1, f32[2]{0:T(128)S(1)} %broadcast_multiply_fusion.1, f32[2048]{0:T(1024)S(1)} %convert_element_type.97, f32[2048]{0:T(1024)S(1)} %convert_element_type.96, ...), kind=kOutput, calls=%fused_computation.26 | convolution fusion | flops 12609536 | bytes 6336528 | tf_op jit(solution)/shard_map/dot_general | solution.py:215
  26.4 0.1 fusion.50
  26.5 3.6 %fusion.75 = (f32[2,4]{1,0:T(2,128)S(1)}, f32[2,4,2048]{2,1,0:T(4,128)S(1)}) fusion(f32[2,2048]{1,0:T(2,128)S(1)} %subtract_convert_fusion, f32[4]{0:T(128)S(1)} %multiply_exponential_fusion.slopes_ref, bf16[2,2048,512]{2,1,0:T(8,128)(2,1)} %param.25, pred[512,4]{0,1:T(4,128)(4,1)S(1)} %iota_compare_fusion.1, bf16[2,512]{1,0:T(2,128)(2,1)S(1)} %bitcast.51, ...), kind=kOutput, calls=%fused_computation.136 | convolution fusion | flops 16863224 | bytes 4284464 | tf_op jit(solution)/shard_map/vmap()/dot_general | solution.py:149
  30.1 0.2 fusion.37
  30.4 0.1 broadcast_bitcast_fusion
  30.4 0.7 fusion.21
  31.2 0.9 copy-done.1
  32.0 0.4 fusion.56
  32.4 0.0 collective-permute-start.6
  32.4 0.7 collective-permute-done
  33.1 0.0 collective-permute-start.2
  33.1 1.9 %broadcast_in_dim.54 = bf16[1024,1536]{1,0:T(8,128)(2,1)} broadcast(bf16[]{:T(256)} %constant.123.clone.1), dimensions={} | broadcast | bytes 3145730 | tf_op jit(solution)/shard_map/broadcast_in_dim | solution.py:259
  35.0 3.9 %fusion.3 = bf16[1024,1536]{1,0:T(8,128)(2,1)} fusion(bf16[1024,1536]{1,0:T(8,128)(2,1)} %broadcast_in_dim.54, s32[]{:T(128)S(6)} %select_n.124, bf16[256,2048]{1,0:T(8,128)(2,1)} %fusion.20, bf16[2048,1536]{1,0:T(8,128)(2,1)S(1)} %copy-done.2, f32[1536]{0:T(1024)S(1)} %convert_element_type.99), kind=kOutput, calls=%fused_computation.12 | convolution fusion | flops 1611399168 | bytes 8132612 | tf_op jit(solution)/shard_map/dot_general | solution.py:264
  38.9 0.0 collective-permute-done.6
  39.0 1.8 %collective-permute-start.7 = (f32[4,2048]{1,0:T(4,128)S(1)}, f32[4,2048]{1,0:T(4,128)S(1)}, u32[]{:S(2)}, u32[]{:S(2)}) collective-permute-start(f32[4,2048]{1,0:T(4,128)S(1)} %pad_maximum_fusion.2), channel_id=1, source_target_pairs={{0,2},{1,3},{2,0},{3,1},{4,6},{5,7},{6,4},{7,5},{8,10},{9,11},{10,... | collective-permute-start | bytes 98312 | tf_op jit(solution)/shard_map/ppermute | solution.py:234
  40.8 0.1 fusion.65
  41.6 1.3 %collective-permute-done.7 = f32[4,2048]{1,0:T(4,128)S(1)} collective-permute-done((f32[4,2048]{1,0:T(4,128)S(1)}, f32[4,2048]{1,0:T(4,128)S(1)}, u32[]{:S(2)}, u32[]{:S(2)}) %collective-permute-start.7) | collective-permute-done | bytes 32800 | tf_op jit(solution)/shard_map/ppermute | solution.py:234
  43.0 0.0 slice-start
  43.1 0.0 slice-start.1
  43.1 1.8 %collective-permute-start.11 = (bf16[512,2048]{1,0:T(8,128)(2,1)S(1)}, bf16[512,2048]{1,0:T(8,128)(2,1)}, u32[]{:S(2)}, u32[]{:S(2)}) collective-permute-start(bf16[512,2048]{1,0:T(8,128)(2,1)S(1)} %copy-done.1), channel_id=1, source_target_pairs={{0,2},{1,3},{2,0},{3,1},{4,6},{5,7},{6,4},{7,5},{8,10},{9,11},{10,... | collective-permute-start | bytes 6291464 | tf_op jit(solution)/shard_map/ppermute | solution.py:257
  44.9 0.0 collective-permute-done.1
  44.9 0.0 collective-permute-done.2
  44.9 1.5 %collective-permute-start.8 = (bf16[2,2048]{1,0:T(2,128)(2,1)S(1)}, bf16[2,2048]{1,0:T(2,128)(2,1)S(1)}, u32[]{:S(2)}, u32[]{:S(2)}) collective-permute-start(bf16[2,2048]{1,0:T(2,128)(2,1)S(1)} %fusion.41), channel_id=1, source_target_pairs={{0,4},{4,0},{8,12},{12,8},{16,20},{20,16},{24,28},{28,24},{1,5},{5... | collective-permute-start | bytes 24584 | tf_op jit(solution)/shard_map/ppermute | solution.py:271
  46.5 5.8 %fusion.5 = bf16[1024,1536]{1,0:T(8,128)(2,1)} fusion(bf16[1024,1536]{1,0:T(8,128)(2,1)} %fusion.3, s32[]{:T(128)S(6)} %select_n.126, bf16[256,2048]{1,0:T(8,128)(2,1)} %collective-permute-done, bf16[2048,1536]{1,0:T(8,128)(2,1)} %param.19, f32[1536]{0:T(1024)S(1)} %convert_element_type.99), kind=kOutput, calls=%fused_computation.14 | convolution fusion | flops 1611399168 | bytes 8132612 | tf_op jit(solution)/shard_map/dot_general | solution.py:264
  52.3 0.0 collective-permute-done.8
  52.3 1.6 %collective-permute-start.9 = (bf16[4,2048]{1,0:T(4,128)(2,1)S(1)}, bf16[4,2048]{1,0:T(4,128)(2,1)S(1)}, u32[]{:S(2)}, u32[]{:S(2)}) collective-permute-start(bf16[4,2048]{1,0:T(4,128)(2,1)S(1)} %pad_maximum_fusion.5), channel_id=1, source_target_pairs={{0,8},{4,12},{8,0},{12,4},{16,24},{20,28},{24,16},{28,20},{1,9},{5... | collective-permute-start | bytes 49160 | tf_op jit(solution)/shard_map/ppermute | solution.py:271
  54.0 3.9 %fusion.7 = bf16[1024,1536]{1,0:T(8,128)(2,1)} fusion(bf16[1024,1536]{1,0:T(8,128)(2,1)} %fusion.5, s32[]{:T(128)S(6)} %select_n.138, bf16[256,2048]{1,0:T(8,128)(2,1)} %collective-permute-done.1, bf16[2048,1536]{1,0:T(8,128)(2,1)S(1)} %bitcast.49, f32[1536]{0:T(1024)S(1)} %convert_element_type.99), kind=kOutput, calls=%fused_computation.16 | convolution fusion | flops 1611399168 | bytes 8132612 | tf_op jit(solution)/shard_map/dot_general | solution.py:264
  57.9 0.0 collective-permute-done.9
  57.9 2.6 %collective-permute-start.10 = (bf16[8,2048]{1,0:T(8,128)(2,1)S(1)}, bf16[8,2048]{1,0:T(8,128)(2,1)S(1)}, u32[]{:S(2)}, u32[]{:S(2)}) collective-permute-start(bf16[8,2048]{1,0:T(8,128)(2,1)S(1)} %pad_maximum_fusion.3), channel_id=1, source_target_pairs={{0,16},{4,20},{8,24},{12,28},{16,0},{20,4},{24,8},{28,12},{1,17},{... | collective-permute-start | bytes 98312 | tf_op jit(solution)/shard_map/ppermute | solution.py:271
  60.5 3.9 %fusion.9.q_ref.kn_ref.vn_ref = bf16[1024,1536]{1,0:T(8,128)(2,1)} fusion(bf16[1024,1536]{1,0:T(8,128)(2,1)} %fusion.7, s32[]{:T(128)S(6)} %select_n.139, bf16[256,2048]{1,0:T(8,128)(2,1)} %collective-permute-done.2, bf16[2048,1536]{1,0:T(8,128)(2,1)S(1)} %bitcast.49, f32[1536]{0:T(1024)S(1)} %convert_element_type.99), kind=kOutput, calls=%fused_computation.18 | convolution fusion | flops 1611399168 | bytes 8132612 | tf_op jit(solution)/shard_map/dot_general | solution.py:264
  64.4 0.8 convolution_convert_fusion
  65.2 23.4 %shard_map.158 = bf16[1024,512]{1,0:T(8,128)(2,1)} custom-call(s32[1]{0:T(128)S(6)} %copy.39.prefix_ref, f32[4]{0:T(128)} %copy-done.8, bf16[1024,1536]{1,0:T(8,128)(2,1)} %fusion.9.q_ref.kn_ref.vn_ref, bf16[1024,1536]{1,0:T(8,128)(2,1)} %fusion.9.q_ref.kn_ref.vn_ref, bf16[1024,1536]{1,0:T(8,128)(2,1)} %fusion.9.q_ref.kn_ref.vn_ref, ...), custom_call_target="tpu_custom_call" | custom-call | flops 4294967296 | bytes 6291456 | tf_op jit(solution)/shard_map/pallas_call | solution.py:118
  88.6 1.6 %collective-permute-done.11 = bf16[512,2048]{1,0:T(8,128)(2,1)} collective-permute-done((bf16[512,2048]{1,0:T(8,128)(2,1)S(1)}, bf16[512,2048]{1,0:T(8,128)(2,1)}, u32[]{:S(2)}, u32[]{:S(2)}) %collective-permute-start.11) | collective-permute-done | bytes 2097184 | tf_op jit(solution)/shard_map/ppermute | solution.py:257
  90.2 0.5 collective-permute-start.14
  90.7 2.0 %constant_dynamic-slice_fusion.2 = (bf16[256,512]{1,0:T(8,128)(2,1)S(1)}, bf16[256,512]{1,0:T(8,128)(2,1)}, bf16[256,512]{1,0:T(8,128)(2,1)}) fusion(bf16[1024,512]{1,0:T(8,128)(2,1)} %shard_map.158, s32[]{:T(128)S(6)} %select_n.138, s32[]{:T(128)S(6)} %select_n.146, s32[]{:T(128)S(6)} %select_n.145), kind=kLoop, calls=%fused_computation.92 | loop fusion | bytes 1572876 | tf_op jit(solution)/shard_map/dynamic_slice | solution.py:292
  92.6 1.7 %collective-permute-start.12 = (bf16[256,512]{1,0:T(8,128)(2,1)}, bf16[256,512]{1,0:T(8,128)(2,1)}, u32[]{:S(2)}, u32[]{:S(2)}) collective-permute-start(bf16[256,512]{1,0:T(8,128)(2,1)} %get-tuple-element.26), channel_id=1, source_target_pairs={{0,2},{1,3},{2,0},{3,1},{4,6},{5,7},{6,4},{7,5},{8,10},{9,11},{10,... | collective-permute-start | bytes 786440 | tf_op jit(solution)/shard_map/ppermute | solution.py:293
  94.4 0.0 collective-permute-start.15
  94.4 0.4 collective-permute-start.13
  94.8 7.3 %collective-permute-done.12 = bf16[256,512]{1,0:T(8,128)(2,1)} collective-permute-done((bf16[256,512]{1,0:T(8,128)(2,1)}, bf16[256,512]{1,0:T(8,128)(2,1)}, u32[]{:S(2)}, u32[]{:S(2)}) %collective-permute-start.12) | collective-permute-done | bytes 262176 | tf_op jit(solution)/shard_map/ppermute | solution.py:293
  102.1 2.4 %fusion.76 = f32[256,2048]{1,0:T(8,128)S(1)} fusion(bf16[256,512]{1,0:T(8,128)(2,1)} %collective-permute-done.12, bf16[512,2048]{1,0:T(8,128)(2,1)} %collective-permute-done.11), kind=kOutput, calls=%fused_computation.137 | convolution fusion | flops 536870912 | bytes 4456448 | tf_op jit(solution)/shard_map/dot_general | solution.py:296
  104.5 1.7 %convolution_add_fusion.1 = f32[256,2048]{1,0:T(8,128)S(1)} fusion(f32[256,2048]{1,0:T(8,128)S(1)} %fusion.76, bf16[512,2048]{1,0:T(8,128)(2,1)S(1)} %copy-done.1, bf16[1024,512]{1,0:T(8,128)(2,1)} %shard_map.158, s32[]{:T(128)S(6)} %select_n.143), kind=kOutput, calls=%fused_computation.5 | convolution fusion | flops 537395200 | bytes 6553604 | tf_op jit(solution)/shard_map/dot_general | solution.py:294
  106.2 0.0 collective-permute-done.15
  106.3 2.3 %fusion.77 = f32[256,2048]{1,0:T(8,128)S(1)} fusion(bf16[256,512]{1,0:T(8,128)(2,1)S(1)} %collective-permute-done.15, bf16[512,2048]{1,0:T(8,128)(2,1)} %collective-permute-done.16), kind=kOutput, calls=%fused_computation.138 | convolution fusion | flops 536870912 | bytes 4456448 | tf_op jit(solution)/shard_map/dot_general | solution.py:296
  108.6 0.0 collective-permute-done.14
  108.6 3.4 %fusion.10 = bf16[256,2048]{1,0:T(8,128)(2,1)} fusion(bf16[256,2048]{1,0:T(8,128)(2,1)S(1)} %copy-done, f32[256,2048]{1,0:T(8,128)S(1)} %fusion.77, f32[256,2048]{1,0:T(8,128)S(1)} %convolution_add_fusion.1, bf16[256,512]{1,0:T(8,128)(2,1)S(1)} %collective-permute-done.13, bf16[512,2048]{1,0:T(8,128)(2,1)} %collective-permute-done.14, ...), kind=kOutput, calls=%fused_computation.19 | convolution fusion | flops 540016640 | bytes 8658944 | tf_op jit(solution)/shard_map/dot_general | solution.py:296
  (51 shorter events, 0.5 us)
Async XLA Ops:
  0.6 4.6 %copy-start = (bf16[256,2048]{1,0:T(8,128)(2,1)S(1)}, bf16[256,2048]{1,0:T(8,128)(2,1)}, u32[]{:S(2)}) copy-start(bf16[256,2048]{1,0:T(8,128)(2,1)} %param.15) | copy-start | bytes 3145732
  2.1 7.6 %copy-start.4 = (bf16[2,2048]{1,0:T(2,128)(2,1)S(1)}, bf16[2,2048]{1,0:T(2,128)(2,1)}, u32[]{:S(2)}) copy-start(bf16[2,2048]{1,0:T(2,128)(2,1)} %param.16) | copy-start | bytes 24580
  2.1 9.1 %copy-start.7 = (s32[2]{0:T(128)S(1)}, s32[2]{0:T(128)}, u32[]{:S(2)}) copy-start(s32[2]{0:T(128)} %param.28) | copy-start | bytes 28
  2.1 9.3 %copy-start.9 = (s32[16]{0:T(128)S(1)}, s32[16]{0:T(128)}, u32[]{:S(2)}) copy-start(s32[16]{0:T(128)} %param.29) | copy-start | bytes 196
  2.1 17.8 %copy-start.5 = (bf16[1536]{0:T(1024)(128)(2,1)S(1)}, bf16[1536]{0:T(1024)(128)(2,1)}, u32[]{:S(2)}) copy-start(bf16[1536]{0:T(1024)(128)(2,1)} %param.20) | copy-start | bytes 9220
  6.7 26.4 %collective-permute-start = (bf16[256,2048]{1,0:T(8,128)(2,1)}, bf16[256,2048]{1,0:T(8,128)(2,1)}, u32[]{:S(2)}, u32[]{:S(2)}) collective-permute-start(bf16[256,2048]{1,0:T(8,128)(2,1)} %fusion.20), channel_id=1, source_target_pairs={{0,2},{1,3},{2,0},{3,1},{4,6},{5,7},{6,4},{7,5},{8,10},{9,11},{10,... | collective-permute-start | bytes 3145736 | tf_op jit(solution)/shard_map/ppermute | solution.py:252
  9.7 35.3 %collective-permute-start.1 = (bf16[256,2048]{1,0:T(8,128)(2,1)}, bf16[256,2048]{1,0:T(8,128)(2,1)}, u32[]{:S(2)}, u32[]{:S(2)}) collective-permute-start(bf16[256,2048]{1,0:T(8,128)(2,1)} %fusion.20), channel_id=1, source_target_pairs={{0,1},{1,0},{2,3},{3,2},{4,5},{5,4},{6,7},{7,6},{8,9},{9,8},{10,11... | collective-permute-start | bytes 3145736 | tf_op jit(solution)/shard_map/ppermute | solution.py:255
  9.7 3.7 %collective-permute-start.3 = (bf16[2,2048]{1,0:T(2,128)(2,1)S(1)}, bf16[2,2048]{1,0:T(2,128)(2,1)S(1)}, u32[]{:S(2)}, u32[]{:S(2)}) collective-permute-start(bf16[2,2048]{1,0:T(2,128)(2,1)S(1)} %copy-done.4), channel_id=1, source_target_pairs={{0,4},{4,0},{8,12},{12,8},{16,20},{20,16},{24,28},{28,24},{1,5},{5... | collective-permute-start | bytes 24584 | tf_op jit(solution)/shard_map/ppermute | solution.py:201
  13.3 3.8 %collective-permute-start.4 = (bf16[4,2048]{1,0:T(4,128)(2,1)S(1)}, bf16[4,2048]{1,0:T(4,128)(2,1)S(1)}, u32[]{:S(2)}, u32[]{:S(2)}) collective-permute-start(bf16[4,2048]{1,0:T(4,128)(2,1)S(1)} %pad_maximum_fusion.4), channel_id=1, source_target_pairs={{0,8},{4,12},{8,0},{12,4},{16,24},{20,28},{24,16},{28,20},{1,9},{5... | collective-permute-start | bytes 49160 | tf_op jit(solution)/shard_map/ppermute | solution.py:201
  17.2 4.9 %collective-permute-start.5 = (bf16[8,2048]{1,0:T(8,128)(2,1)S(1)}, bf16[8,2048]{1,0:T(8,128)(2,1)S(1)}, u32[]{:S(2)}, u32[]{:S(2)}) collective-permute-start(bf16[8,2048]{1,0:T(8,128)(2,1)S(1)} %pad_maximum_fusion.1), channel_id=1, source_target_pairs={{0,16},{4,20},{8,24},{12,28},{16,0},{20,4},{24,8},{28,12},{1,17},{... | collective-permute-start | bytes 98312 | tf_op jit(solution)/shard_map/ppermute | solution.py:201
  19.8 6.7 %copy-start.8 = (f32[4]{0:T(128)}, f32[4]{0:T(128)S(1)}, u32[]{:S(2)}) copy-start(f32[4]{0:T(128)S(1)} %multiply_exponential_fusion.slopes_ref) | copy-start | bytes 52
  26.5 3.9 %copy-start.3 = (bf16[2,2048,512]{2,1,0:T(8,128)(2,1)S(1)}, bf16[2,2048,512]{2,1,0:T(8,128)(2,1)}, u32[]{:S(2)}) copy-start(bf16[2,2048,512]{2,1,0:T(8,128)(2,1)} %param.26) | copy-start | bytes 12582916
  30.4 1.6 %copy-start.1 = (bf16[512,2048]{1,0:T(8,128)(2,1)S(1)}, bf16[512,2048]{1,0:T(8,128)(2,1)}, u32[]{:S(2)}) copy-start(bf16[512,2048]{1,0:T(8,128)(2,1)} %param.21) | copy-start | bytes 6291460
  30.4 4.6 %copy-start.2 = (bf16[2048,1536]{1,0:T(8,128)(2,1)S(1)}, bf16[2048,1536]{1,0:T(8,128)(2,1)}, u32[]{:S(2)}) copy-start(bf16[2048,1536]{1,0:T(8,128)(2,1)} %param.19) | copy-start | bytes 18874372
  32.4 6.5 %collective-permute-start.6 = (f32[2,2048]{1,0:T(2,128)S(1)}, f32[2,2048]{1,0:T(2,128)S(1)}, u32[]{:S(2)}, u32[]{:S(2)}) collective-permute-start(f32[2,2048]{1,0:T(2,128)S(1)} %fusion.56), channel_id=1, source_target_pairs={{0,1},{1,0},{2,3},{3,2},{4,5},{5,4},{6,7},{7,6},{8,9},{9,8},{10,11... | collective-permute-start | bytes 49160 | tf_op jit(solution)/shard_map/ppermute | solution.py:234
  33.1 11.8 %collective-permute-start.2 = (bf16[256,2048]{1,0:T(8,128)(2,1)}, bf16[256,2048]{1,0:T(8,128)(2,1)}, u32[]{:S(2)}, u32[]{:S(2)}) collective-permute-start(bf16[256,2048]{1,0:T(8,128)(2,1)} %collective-permute-done), channel_id=1, source_target_pairs={{0,1},{1,0},{2,3},{3,2},{4,5},{5,4},{6,7},{7,6},{8,9},{9,8},{10,11... | collective-permute-start | bytes 3145736 | tf_op jit(solution)/shard_map/ppermute | solution.py:255
  35.0 6.6 %copy-start.6 = (bf16[2048]{0:T(1024)(128)(2,1)S(1)}, bf16[2048]{0:T(1024)(128)(2,1)}, u32[]{:S(2)}) copy-start(bf16[2048]{0:T(1024)(128)(2,1)} %param.22) | copy-start | bytes 12292
  39.0 4.0 %collective-permute-start.7 = (f32[4,2048]{1,0:T(4,128)S(1)}, f32[4,2048]{1,0:T(4,128)S(1)}, u32[]{:S(2)}, u32[]{:S(2)}) collective-permute-start(f32[4,2048]{1,0:T(4,128)S(1)} %pad_maximum_fusion.2), channel_id=1, source_target_pairs={{0,2},{1,3},{2,0},{3,1},{4,6},{5,7},{6,4},{7,5},{8,10},{9,11},{10,... | collective-permute-start | bytes 98312 | tf_op jit(solution)/shard_map/ppermute | solution.py:234
  43.0 10.9 %slice-start = ((s8[6291456]{0:T(1024)(128)(4,1)}), s8[4194304]{0:T(1024)(128)(4,1)S(1)}, s32[]{:S(2)}) async-start(s8[6291456]{0:T(1024)(128)(4,1)} %bitcast.48), calls=%async_computation | async-start | bytes 8388608
  43.1 10.9 %slice-start.1 = ((s8[6291456]{0:T(1024)(128)(4,1)}), s8[2097152]{0:T(1024)(128)(4,1)S(1)}, s32[]{:S(2)}) async-start(s8[6291456]{0:T(1024)(128)(4,1)} %bitcast.48), calls=%async_computation.1 | async-start | bytes 4194304
  43.1 47.1 %collective-permute-start.11 = (bf16[512,2048]{1,0:T(8,128)(2,1)S(1)}, bf16[512,2048]{1,0:T(8,128)(2,1)}, u32[]{:S(2)}, u32[]{:S(2)}) collective-permute-start(bf16[512,2048]{1,0:T(8,128)(2,1)S(1)} %copy-done.1), channel_id=1, source_target_pairs={{0,2},{1,3},{2,0},{3,1},{4,6},{5,7},{6,4},{7,5},{8,10},{9,11},{10,... | collective-permute-start | bytes 6291464 | tf_op jit(solution)/shard_map/ppermute | solution.py:257
  44.9 7.3 %collective-permute-start.8 = (bf16[2,2048]{1,0:T(2,128)(2,1)S(1)}, bf16[2,2048]{1,0:T(2,128)(2,1)S(1)}, u32[]{:S(2)}, u32[]{:S(2)}) collective-permute-start(bf16[2,2048]{1,0:T(2,128)(2,1)S(1)} %fusion.41), channel_id=1, source_target_pairs={{0,4},{4,0},{8,12},{12,8},{16,20},{20,16},{24,28},{28,24},{1,5},{5... | collective-permute-start | bytes 24584 | tf_op jit(solution)/shard_map/ppermute | solution.py:271
  52.3 5.6 %collective-permute-start.9 = (bf16[4,2048]{1,0:T(4,128)(2,1)S(1)}, bf16[4,2048]{1,0:T(4,128)(2,1)S(1)}, u32[]{:S(2)}, u32[]{:S(2)}) collective-permute-start(bf16[4,2048]{1,0:T(4,128)(2,1)S(1)} %pad_maximum_fusion.5), channel_id=1, source_target_pairs={{0,8},{4,12},{8,0},{12,4},{16,24},{20,28},{24,16},{28,20},{1,9},{5... | collective-permute-start | bytes 49160 | tf_op jit(solution)/shard_map/ppermute | solution.py:271
  57.9 6.5 %collective-permute-start.10 = (bf16[8,2048]{1,0:T(8,128)(2,1)S(1)}, bf16[8,2048]{1,0:T(8,128)(2,1)S(1)}, u32[]{:S(2)}, u32[]{:S(2)}) collective-permute-start(bf16[8,2048]{1,0:T(8,128)(2,1)S(1)} %pad_maximum_fusion.3), channel_id=1, source_target_pairs={{0,16},{4,20},{8,24},{12,28},{16,0},{20,4},{24,8},{28,12},{1,17},{... | collective-permute-start | bytes 98312 | tf_op jit(solution)/shard_map/ppermute | solution.py:271
  90.2 16.1 %collective-permute-start.16 = (bf16[512,2048]{1,0:T(8,128)(2,1)}, bf16[512,2048]{1,0:T(8,128)(2,1)}, u32[]{:S(2)}, u32[]{:S(2)}) collective-permute-start(bf16[512,2048]{1,0:T(8,128)(2,1)} %collective-permute-done.11), channel_id=1, source_target_pairs={{0,1},{1,0},{2,3},{3,2},{4,5},{5,4},{6,7},{7,6},{8,9},{9,8},{10,11... | collective-permute-start | bytes 6291464 | tf_op jit(solution)/shard_map/ppermute | solution.py:284
  90.2 18.4 %collective-permute-start.14 = (bf16[512,2048]{1,0:T(8,128)(2,1)S(1)}, bf16[512,2048]{1,0:T(8,128)(2,1)}, u32[]{:S(2)}, u32[]{:S(2)}) collective-permute-start(bf16[512,2048]{1,0:T(8,128)(2,1)S(1)} %copy-done.1), channel_id=1, source_target_pairs={{0,1},{1,0},{2,3},{3,2},{4,5},{5,4},{6,7},{7,6},{8,9},{9,8},{10,11... | collective-permute-start | bytes 6291464 | tf_op jit(solution)/shard_map/ppermute | solution.py:284
  92.6 9.5 %collective-permute-start.12 = (bf16[256,512]{1,0:T(8,128)(2,1)}, bf16[256,512]{1,0:T(8,128)(2,1)}, u32[]{:S(2)}, u32[]{:S(2)}) collective-permute-start(bf16[256,512]{1,0:T(8,128)(2,1)} %get-tuple-element.26), channel_id=1, source_target_pairs={{0,2},{1,3},{2,0},{3,1},{4,6},{5,7},{6,4},{7,5},{8,10},{9,11},{10,... | collective-permute-start | bytes 786440 | tf_op jit(solution)/shard_map/ppermute | solution.py:293
  94.4 11.9 %collective-permute-start.15 = (bf16[256,512]{1,0:T(8,128)(2,1)}, bf16[256,512]{1,0:T(8,128)(2,1)S(1)}, u32[]{:S(2)}, u32[]{:S(2)}) collective-permute-start(bf16[256,512]{1,0:T(8,128)(2,1)} %get-tuple-element.25), channel_id=1, source_target_pairs={{0,3},{1,2},{2,1},{3,0},{4,7},{5,6},{6,5},{7,4},{8,11},{9,10},{10,... | collective-permute-start | bytes 786440 | tf_op jit(solution)/shard_map/ppermute | solution.py:293
  94.4 14.2 %collective-permute-start.13 = (bf16[256,512]{1,0:T(8,128)(2,1)S(1)}, bf16[256,512]{1,0:T(8,128)(2,1)S(1)}, u32[]{:S(2)}, u32[]{:S(2)}) collective-permute-start(bf16[256,512]{1,0:T(8,128)(2,1)S(1)} %get-tuple-element.24), channel_id=1, source_target_pairs={{0,1},{1,0},{2,3},{3,2},{4,5},{5,4},{6,7},{7,6},{8,9},{9,8},{10,11... | collective-permute-start | bytes 786440 | tf_op jit(solution)/shard_map/ppermute | solution.py:293

commit v16 on v14

--- a/solution.py
+++ b/solution.py
@@ -109,7 +109,7 @@
         pl.when(i == last)(functools.partial(tile, last, (last + 1) * tq))
 
 
-def prefill_attention_kernel(merged, cache_keys, cache_values, prefix, slopes, head_size, tq=256):
+def prefill_attention_kernel(merged, cache_keys, cache_values, prefix, slopes, head_size, tq=512):
     group = merged.shape[0]
     heads = merged.shape[1] // (3 * head_size)
     cache_size = cache_keys.shape[0]

time: 113 us -> 113 us (level)
  transfers between devices with their start and end apart: 17 -> 17, of which waited for: 7 -> 7; matrix products, arithmetic and copies ran while one was open for 35% -> 35% of each run, Pallas kernels for 21% -> 22%
where the time goes in v16:
time: 113 us; the launch traced here: 112 us
  matrix products  37 us (33%)
  Pallas kernels  24.3 us (22%)
  starting transfers between devices  20.9 us (18%)
  waiting for transfers between devices  16.1 us (14%)
  other arithmetic  7.25 us (6%)
  local copies, waits for them, and re-layouts  4.9 us (4%)
  between operations  1.63 us (1%)
    pallas_call x1, Pallas kernels, prefill_attention_kernel(): pl.pallas_call(functools.partial(_prefill_kernel, tq=tq), out_shape=jax.S...  24.3 us
    dot_general x4, matrix products, per_device(): jnp.dot(token_block, qkv_weight, preferred_element_type=jnp.float32)  17.6 us
    dot_general x3, matrix products, per_device(): summed = summed + jnp.dot(piece, weight, preferred_element_type=jnp.float32)  8.12 us
    ppermute x3, waiting for transfers between devices, per_device(): pieces.append(lax.ppermute(outgoing, 'tensor', route(k, flip)))  7.35 us
    ppermute x3, waiting for transfers between devices, per_device(): lax.ppermute(shifted_rows, 'dp', [(i, i ^ step) for i in range(dp_size)])  6.02 us
    ppermute x3, starting transfers between devices, per_device(): lax.ppermute(shifted_rows, 'dp', [(i, i ^ step) for i in range(dp_size)])  5.82 us
    ppermute x3, starting transfers between devices, per_device(): lax.ppermute(returned, 'dp', [(i, i ^ step) for i in range(dp_size)])  5.8 us
    dot_general x1, matrix products, per_device(): jnp.dot(normed_slots, qkv_weight, preferred_element_type=jnp.float32)  3.75 us
  transfers between devices with their start and end apart: 17, of which 7 were waited for; matrix products, arithmetic and copies ran while one was open for 35% of the time, Pallas kernels for 22%

profile of v16, /device:TPU:0, one launch (start us, length us, event | category | flops | bytes accessed | tf_op | source)
XLA Modules:
  0.0 112.0 jit_solution(11127186745709581265)
XLA Ops:
  0.6 0.0 copy-start
  0.6 0.8 convert_element_type.97
  1.4 0.7 convert_element_type.96
  2.1 1.5 %convert_reduce_fusion = f32[256]{0:T(256)S(1)} fusion(bf16[256,2048]{1,0:T(8,128)(2,1)} %param.15), kind=kLoop, calls=%fused_computation.2 | loop fusion | flops 1048320 | bytes 1049600 | tf_op jit(solution)/shard_map/reduce_sum | solution.py:20
  3.6 1.6 %fusion.17 = f32[256]{0:T(256)S(1)} fusion(bf16[256,2048]{1,0:T(8,128)(2,1)} %param.15, f32[256]{0:T(256)S(1)} %broadcast_multiply_fusion), kind=kLoop, calls=%fused_computation.30 | loop fusion | flops 2096896 | bytes 1050624 | tf_op jit(solution)/shard_map/reduce_sum | solution.py:21
  5.3 1.4 %fusion.20 = bf16[256,2048]{1,0:T(8,128)(2,1)} fusion(bf16[256,2048]{1,0:T(8,128)(2,1)S(1)} %copy-done, f32[2048]{0:T(1024)S(1)} %convert_element_type.97, f32[2048]{0:T(1024)S(1)} %convert_element_type.96, f32[256]{0:T(256)S(1)} %add_rsqrt_fusion, f32[256]{0:T(256)S(1)} %broadcast_multiply_fusion), kind=kLoop, calls=%fused_computation.33 | loop fusion | flops 3145728 | bytes 2115584 | tf_op jit(solution)/shard_map/convert_element_type | solution.py:23
  6.7 2.9 %collective-permute-start = (bf16[256,2048]{1,0:T(8,128)(2,1)}, bf16[256,2048]{1,0:T(8,128)(2,1)}, u32[]{:S(2)}, u32[]{:S(2)}) collective-permute-start(bf16[256,2048]{1,0:T(8,128)(2,1)} %fusion.20), channel_id=1, source_target_pairs={{0,2},{1,3},{2,0},{3,1},{4,6},{5,7},{6,4},{7,5},{8,10},{9,11},{10,... | collective-permute-start | bytes 3145736 | tf_op jit(solution)/shard_map/ppermute | solution.py:251
  9.7 0.0 collective-permute-start.1
  9.7 1.5 %collective-permute-start.3 = (bf16[2,2048]{1,0:T(2,128)(2,1)S(1)}, bf16[2,2048]{1,0:T(2,128)(2,1)S(1)}, u32[]{:S(2)}, u32[]{:S(2)}) collective-permute-start(bf16[2,2048]{1,0:T(2,128)(2,1)S(1)} %copy-done.4), channel_id=1, source_target_pairs={{0,4},{4,0},{8,12},{12,8},{16,20},{20,16},{24,28},{28,24},{1,5},{5... | collective-permute-start | bytes 24584 | tf_op jit(solution)/shard_map/ppermute | solution.py:200
  11.2 0.1 subtract_convert_fusion
  11.3 0.1 iota_compare_fusion
  11.4 0.2 fusion.61
  11.6 1.7 %collective-permute-done.3 = bf16[2,2048]{1,0:T(2,128)(2,1)S(1)} collective-permute-done((bf16[2,2048]{1,0:T(2,128)(2,1)S(1)}, bf16[2,2048]{1,0:T(2,128)(2,1)S(1)}, u32[]{:S(2)}, u32[]{:S(2)}) %collective-permute-start.3) | collective-permute-done | bytes 8224 | tf_op jit(solution)/shard_map/ppermute | solution.py:200
  13.3 1.6 %collective-permute-start.4 = (bf16[4,2048]{1,0:T(4,128)(2,1)S(1)}, bf16[4,2048]{1,0:T(4,128)(2,1)S(1)}, u32[]{:S(2)}, u32[]{:S(2)}) collective-permute-start(bf16[4,2048]{1,0:T(4,128)(2,1)S(1)} %pad_maximum_fusion.4), channel_id=1, source_target_pairs={{0,8},{4,12},{8,0},{12,4},{16,24},{20,28},{24,16},{28,20},{1,9},{5... | collective-permute-start | bytes 49160 | tf_op jit(solution)/shard_map/ppermute | solution.py:200
  15.0 2.1 %collective-permute-done.4 = bf16[4,2048]{1,0:T(4,128)(2,1)S(1)} collective-permute-done((bf16[4,2048]{1,0:T(4,128)(2,1)S(1)}, bf16[4,2048]{1,0:T(4,128)(2,1)S(1)}, u32[]{:S(2)}, u32[]{:S(2)}) %collective-permute-start.4) | collective-permute-done | bytes 16416 | tf_op jit(solution)/shard_map/ppermute | solution.py:200
  17.2 2.7 %collective-permute-start.5 = (bf16[8,2048]{1,0:T(8,128)(2,1)S(1)}, bf16[8,2048]{1,0:T(8,128)(2,1)S(1)}, u32[]{:S(2)}, u32[]{:S(2)}) collective-permute-start(bf16[8,2048]{1,0:T(8,128)(2,1)S(1)} %pad_maximum_fusion.1), channel_id=1, source_target_pairs={{0,16},{4,20},{8,24},{12,28},{16,0},{20,4},{24,8},{28,12},{1,17},{... | collective-permute-start | bytes 98312 | tf_op jit(solution)/shard_map/ppermute | solution.py:200
  19.9 2.1 %collective-permute-done.5 = bf16[8,2048]{1,0:T(8,128)(2,1)S(1)} collective-permute-done((bf16[8,2048]{1,0:T(8,128)(2,1)S(1)}, bf16[8,2048]{1,0:T(8,128)(2,1)S(1)}, u32[]{:S(2)}, u32[]{:S(2)}) %collective-permute-start.5) | collective-permute-done | bytes 32800 | tf_op jit(solution)/shard_map/ppermute | solution.py:200
  22.1 0.3 fusion.74
  22.4 0.2 multiply_reduce_fusion
  22.6 3.8 %fusion.15 = bf16[2,1536]{1,0:T(2,128)(2,1)S(1)} fusion(bf16[2048,1536]{1,0:T(8,128)(2,1)} %param.19, f32[2,2048]{1,0:T(2,128)S(1)} %get-tuple-element.33, f32[2]{0:T(128)S(1)} %add_rsqrt_fusion.1, f32[2]{0:T(128)S(1)} %broadcast_multiply_fusion.1, f32[2048]{0:T(1024)S(1)} %convert_element_type.97, f32[2048]{0:T(1024)S(1)} %convert_element_type.96, ...), kind=kOutput, calls=%fused_computation.26 | convolution fusion | flops 12609536 | bytes 6336528 | tf_op jit(solution)/shard_map/dot_general | solution.py:214
  26.4 0.1 fusion.50
  26.5 3.6 %fusion.75 = (f32[2,4]{1,0:T(2,128)S(1)}, f32[2,4,2048]{2,1,0:T(4,128)S(1)}) fusion(f32[2,2048]{1,0:T(2,128)S(1)} %subtract_convert_fusion, f32[4]{0:T(128)S(1)} %multiply_exponential_fusion.slopes_ref, bf16[2,2048,512]{2,1,0:T(8,128)(2,1)} %param.25, pred[512,4]{0,1:T(4,128)(4,1)S(1)} %iota_compare_fusion.1, bf16[2,512]{1,0:T(2,128)(2,1)S(1)} %bitcast.51, ...), kind=kOutput, calls=%fused_computation.136 | convolution fusion | flops 16863224 | bytes 4284464 | tf_op jit(solution)/shard_map/vmap()/dot_general | solution.py:148
  30.1 0.2 fusion.37
  30.4 0.1 broadcast_bitcast_fusion
  30.4 0.7 fusion.21
  31.2 0.9 copy-done.1
  32.0 0.4 fusion.56
  32.4 0.0 collective-permute-start.6
  32.4 0.7 collective-permute-done
  33.1 0.0 collective-permute-start.2
  33.1 1.9 %broadcast_in_dim.54 = bf16[1024,1536]{1,0:T(8,128)(2,1)} broadcast(bf16[]{:T(256)} %constant.123.clone.1), dimensions={} | broadcast | bytes 3145730 | tf_op jit(solution)/shard_map/broadcast_in_dim | solution.py:258
  35.0 3.9 %fusion.3 = bf16[1024,1536]{1,0:T(8,128)(2,1)} fusion(bf16[1024,1536]{1,0:T(8,128)(2,1)} %broadcast_in_dim.54, s32[]{:T(128)S(6)} %select_n.124, bf16[256,2048]{1,0:T(8,128)(2,1)} %fusion.20, bf16[2048,1536]{1,0:T(8,128)(2,1)S(1)} %copy-done.2, f32[1536]{0:T(1024)S(1)} %convert_element_type.99), kind=kOutput, calls=%fused_computation.12 | convolution fusion | flops 1611399168 | bytes 8132612 | tf_op jit(solution)/shard_map/dot_general | solution.py:263
  38.9 0.0 collective-permute-done.6
  39.0 1.8 %collective-permute-start.7 = (f32[4,2048]{1,0:T(4,128)S(1)}, f32[4,2048]{1,0:T(4,128)S(1)}, u32[]{:S(2)}, u32[]{:S(2)}) collective-permute-start(f32[4,2048]{1,0:T(4,128)S(1)} %pad_maximum_fusion.2), channel_id=1, source_target_pairs={{0,2},{1,3},{2,0},{3,1},{4,6},{5,7},{6,4},{7,5},{8,10},{9,11},{10,... | collective-permute-start | bytes 98312 | tf_op jit(solution)/shard_map/ppermute | solution.py:233
  40.8 0.1 fusion.65
  41.6 1.3 %collective-permute-done.7 = f32[4,2048]{1,0:T(4,128)S(1)} collective-permute-done((f32[4,2048]{1,0:T(4,128)S(1)}, f32[4,2048]{1,0:T(4,128)S(1)}, u32[]{:S(2)}, u32[]{:S(2)}) %collective-permute-start.7) | collective-permute-done | bytes 32800 | tf_op jit(solution)/shard_map/ppermute | solution.py:233
  43.0 0.0 slice-start
  43.1 0.0 slice-start.1
  43.1 1.8 %collective-permute-start.11 = (bf16[512,2048]{1,0:T(8,128)(2,1)S(1)}, bf16[512,2048]{1,0:T(8,128)(2,1)}, u32[]{:S(2)}, u32[]{:S(2)}) collective-permute-start(bf16[512,2048]{1,0:T(8,128)(2,1)S(1)} %copy-done.1), channel_id=1, source_target_pairs={{0,2},{1,3},{2,0},{3,1},{4,6},{5,7},{6,4},{7,5},{8,10},{9,11},{10,... | collective-permute-start | bytes 6291464 | tf_op jit(solution)/shard_map/ppermute | solution.py:256
  44.9 0.0 collective-permute-done.1
  44.9 0.0 collective-permute-done.2
  44.9 1.5 %collective-permute-start.8 = (bf16[2,2048]{1,0:T(2,128)(2,1)S(1)}, bf16[2,2048]{1,0:T(2,128)(2,1)S(1)}, u32[]{:S(2)}, u32[]{:S(2)}) collective-permute-start(bf16[2,2048]{1,0:T(2,128)(2,1)S(1)} %fusion.41), channel_id=1, source_target_pairs={{0,4},{4,0},{8,12},{12,8},{16,20},{20,16},{24,28},{28,24},{1,5},{5... | collective-permute-start | bytes 24584 | tf_op jit(solution)/shard_map/ppermute | solution.py:270
  46.5 5.8 %fusion.5 = bf16[1024,1536]{1,0:T(8,128)(2,1)} fusion(bf16[1024,1536]{1,0:T(8,128)(2,1)} %fusion.3, s32[]{:T(128)S(6)} %select_n.126, bf16[256,2048]{1,0:T(8,128)(2,1)} %collective-permute-done, bf16[2048,1536]{1,0:T(8,128)(2,1)} %param.19, f32[1536]{0:T(1024)S(1)} %convert_element_type.99), kind=kOutput, calls=%fused_computation.14 | convolution fusion | flops 1611399168 | bytes 8132612 | tf_op jit(solution)/shard_map/dot_general | solution.py:263
  52.3 0.0 collective-permute-done.8
  52.3 1.6 %collective-permute-start.9 = (bf16[4,2048]{1,0:T(4,128)(2,1)S(1)}, bf16[4,2048]{1,0:T(4,128)(2,1)S(1)}, u32[]{:S(2)}, u32[]{:S(2)}) collective-permute-start(bf16[4,2048]{1,0:T(4,128)(2,1)S(1)} %pad_maximum_fusion.5), channel_id=1, source_target_pairs={{0,8},{4,12},{8,0},{12,4},{16,24},{20,28},{24,16},{28,20},{1,9},{5... | collective-permute-start | bytes 49160 | tf_op jit(solution)/shard_map/ppermute | solution.py:270
  54.0 3.9 %fusion.7 = bf16[1024,1536]{1,0:T(8,128)(2,1)} fusion(bf16[1024,1536]{1,0:T(8,128)(2,1)} %fusion.5, s32[]{:T(128)S(6)} %select_n.138, bf16[256,2048]{1,0:T(8,128)(2,1)} %collective-permute-done.1, bf16[2048,1536]{1,0:T(8,128)(2,1)S(1)} %bitcast.49, f32[1536]{0:T(1024)S(1)} %convert_element_type.99), kind=kOutput, calls=%fused_computation.16 | convolution fusion | flops 1611399168 | bytes 8132612 | tf_op jit(solution)/shard_map/dot_general | solution.py:263
  57.9 0.0 collective-permute-done.9
  57.9 2.6 %collective-permute-start.10 = (bf16[8,2048]{1,0:T(8,128)(2,1)S(1)}, bf16[8,2048]{1,0:T(8,128)(2,1)S(1)}, u32[]{:S(2)}, u32[]{:S(2)}) collective-permute-start(bf16[8,2048]{1,0:T(8,128)(2,1)S(1)} %pad_maximum_fusion.3), channel_id=1, source_target_pairs={{0,16},{4,20},{8,24},{12,28},{16,0},{20,4},{24,8},{28,12},{1,17},{... | collective-permute-start | bytes 98312 | tf_op jit(solution)/shard_map/ppermute | solution.py:270
  60.5 3.9 %fusion.9.q_ref.kn_ref.vn_ref = bf16[1024,1536]{1,0:T(8,128)(2,1)} fusion(bf16[1024,1536]{1,0:T(8,128)(2,1)} %fusion.7, s32[]{:T(128)S(6)} %select_n.139, bf16[256,2048]{1,0:T(8,128)(2,1)} %collective-permute-done.2, bf16[2048,1536]{1,0:T(8,128)(2,1)S(1)} %bitcast.49, f32[1536]{0:T(1024)S(1)} %convert_element_type.99), kind=kOutput, calls=%fused_computation.18 | convolution fusion | flops 1611399168 | bytes 8132612 | tf_op jit(solution)/shard_map/dot_general | solution.py:263
  64.4 0.8 convolution_convert_fusion
  65.2 24.3 %shard_map.158 = bf16[1024,512]{1,0:T(8,128)(2,1)} custom-call(s32[1]{0:T(128)S(6)} %copy.39.prefix_ref, f32[4]{0:T(128)} %copy-done.8, bf16[1024,1536]{1,0:T(8,128)(2,1)} %fusion.9.q_ref.kn_ref.vn_ref, bf16[1024,1536]{1,0:T(8,128)(2,1)} %fusion.9.q_ref.kn_ref.vn_ref, bf16[1024,1536]{1,0:T(8,128)(2,1)} %fusion.9.q_ref.kn_ref.vn_ref, ...), custom_call_target="tpu_custom_call" | custom-call | flops 4294967296 | bytes 6291456 | tf_op jit(solution)/shard_map/pallas_call | solution.py:117
  89.5 0.7 collective-permute-done.11
  90.2 0.5 collective-permute-start.14
  90.7 2.0 %constant_dynamic-slice_fusion.2 = (bf16[256,512]{1,0:T(8,128)(2,1)S(1)}, bf16[256,512]{1,0:T(8,128)(2,1)}, bf16[256,512]{1,0:T(8,128)(2,1)}) fusion(bf16[1024,512]{1,0:T(8,128)(2,1)} %shard_map.158, s32[]{:T(128)S(6)} %select_n.138, s32[]{:T(128)S(6)} %select_n.146, s32[]{:T(128)S(6)} %select_n.145), kind=kLoop, calls=%fused_computation.92 | loop fusion | bytes 1572876 | tf_op jit(solution)/shard_map/dynamic_slice | solution.py:291
  92.6 1.7 %collective-permute-start.12 = (bf16[256,512]{1,0:T(8,128)(2,1)}, bf16[256,512]{1,0:T(8,128)(2,1)}, u32[]{:S(2)}, u32[]{:S(2)}) collective-permute-start(bf16[256,512]{1,0:T(8,128)(2,1)} %get-tuple-element.26), channel_id=1, source_target_pairs={{0,2},{1,3},{2,0},{3,1},{4,6},{5,7},{6,4},{7,5},{8,10},{9,11},{10,... | collective-permute-start | bytes 786440 | tf_op jit(solution)/shard_map/ppermute | solution.py:292
  94.4 0.0 collective-permute-start.15
  94.4 0.4 collective-permute-start.13
  94.8 7.3 %collective-permute-done.12 = bf16[256,512]{1,0:T(8,128)(2,1)} collective-permute-done((bf16[256,512]{1,0:T(8,128)(2,1)}, bf16[256,512]{1,0:T(8,128)(2,1)}, u32[]{:S(2)}, u32[]{:S(2)}) %collective-permute-start.12) | collective-permute-done | bytes 262176 | tf_op jit(solution)/shard_map/ppermute | solution.py:292
  102.1 2.4 %fusion.76 = f32[256,2048]{1,0:T(8,128)S(1)} fusion(bf16[256,512]{1,0:T(8,128)(2,1)} %collective-permute-done.12, bf16[512,2048]{1,0:T(8,128)(2,1)} %collective-permute-done.11), kind=kOutput, calls=%fused_computation.137 | convolution fusion | flops 536870912 | bytes 4456448 | tf_op jit(solution)/shard_map/dot_general | solution.py:295
  104.5 1.7 %convolution_add_fusion.1 = f32[256,2048]{1,0:T(8,128)S(1)} fusion(f32[256,2048]{1,0:T(8,128)S(1)} %fusion.76, bf16[512,2048]{1,0:T(8,128)(2,1)S(1)} %copy-done.1, bf16[1024,512]{1,0:T(8,128)(2,1)} %shard_map.158, s32[]{:T(128)S(6)} %select_n.143), kind=kOutput, calls=%fused_computation.5 | convolution fusion | flops 537395200 | bytes 6553604 | tf_op jit(solution)/shard_map/dot_general | solution.py:293
  106.2 0.0 collective-permute-done.15
  106.3 2.3 %fusion.77 = f32[256,2048]{1,0:T(8,128)S(1)} fusion(bf16[256,512]{1,0:T(8,128)(2,1)S(1)} %collective-permute-done.15, bf16[512,2048]{1,0:T(8,128)(2,1)} %collective-permute-done.16), kind=kOutput, calls=%fused_computation.138 | convolution fusion | flops 536870912 | bytes 4456448 | tf_op jit(solution)/shard_map/dot_general | solution.py:295
  108.6 0.0 collective-permute-done.14
  108.6 3.4 %fusion.10 = bf16[256,2048]{1,0:T(8,128)(2,1)} fusion(bf16[256,2048]{1,0:T(8,128)(2,1)S(1)} %copy-done, f32[256,2048]{1,0:T(8,128)S(1)} %fusion.77, f32[256,2048]{1,0:T(8,128)S(1)} %convolution_add_fusion.1, bf16[256,512]{1,0:T(8,128)(2,1)S(1)} %collective-permute-done.13, bf16[512,2048]{1,0:T(8,128)(2,1)} %collective-permute-done.14, ...), kind=kOutput, calls=%fused_computation.19 | convolution fusion | flops 540016640 | bytes 8658944 | tf_op jit(solution)/shard_map/dot_general | solution.py:295
  (51 shorter events, 0.5 us)
Async XLA Ops:
  0.6 4.6 %copy-start = (bf16[256,2048]{1,0:T(8,128)(2,1)S(1)}, bf16[256,2048]{1,0:T(8,128)(2,1)}, u32[]{:S(2)}) copy-start(bf16[256,2048]{1,0:T(8,128)(2,1)} %param.15) | copy-start | bytes 3145732
  2.1 7.6 %copy-start.4 = (bf16[2,2048]{1,0:T(2,128)(2,1)S(1)}, bf16[2,2048]{1,0:T(2,128)(2,1)}, u32[]{:S(2)}) copy-start(bf16[2,2048]{1,0:T(2,128)(2,1)} %param.16) | copy-start | bytes 24580
  2.1 9.1 %copy-start.7 = (s32[2]{0:T(128)S(1)}, s32[2]{0:T(128)}, u32[]{:S(2)}) copy-start(s32[2]{0:T(128)} %param.28) | copy-start | bytes 28
  2.1 9.3 %copy-start.9 = (s32[16]{0:T(128)S(1)}, s32[16]{0:T(128)}, u32[]{:S(2)}) copy-start(s32[16]{0:T(128)} %param.29) | copy-start | bytes 196
  2.1 17.8 %copy-start.5 = (bf16[1536]{0:T(1024)(128)(2,1)S(1)}, bf16[1536]{0:T(1024)(128)(2,1)}, u32[]{:S(2)}) copy-start(bf16[1536]{0:T(1024)(128)(2,1)} %param.20) | copy-start | bytes 9220
  6.7 26.4 %collective-permute-start = (bf16[256,2048]{1,0:T(8,128)(2,1)}, bf16[256,2048]{1,0:T(8,128)(2,1)}, u32[]{:S(2)}, u32[]{:S(2)}) collective-permute-start(bf16[256,2048]{1,0:T(8,128)(2,1)} %fusion.20), channel_id=1, source_target_pairs={{0,2},{1,3},{2,0},{3,1},{4,6},{5,7},{6,4},{7,5},{8,10},{9,11},{10,... | collective-permute-start | bytes 3145736 | tf_op jit(solution)/shard_map/ppermute | solution.py:251
  9.7 35.3 %collective-permute-start.1 = (bf16[256,2048]{1,0:T(8,128)(2,1)}, bf16[256,2048]{1,0:T(8,128)(2,1)}, u32[]{:S(2)}, u32[]{:S(2)}) collective-permute-start(bf16[256,2048]{1,0:T(8,128)(2,1)} %fusion.20), channel_id=1, source_target_pairs={{0,1},{1,0},{2,3},{3,2},{4,5},{5,4},{6,7},{7,6},{8,9},{9,8},{10,11... | collective-permute-start | bytes 3145736 | tf_op jit(solution)/shard_map/ppermute | solution.py:254
  9.7 3.7 %collective-permute-start.3 = (bf16[2,2048]{1,0:T(2,128)(2,1)S(1)}, bf16[2,2048]{1,0:T(2,128)(2,1)S(1)}, u32[]{:S(2)}, u32[]{:S(2)}) collective-permute-start(bf16[2,2048]{1,0:T(2,128)(2,1)S(1)} %copy-done.4), channel_id=1, source_target_pairs={{0,4},{4,0},{8,12},{12,8},{16,20},{20,16},{24,28},{28,24},{1,5},{5... | collective-permute-start | bytes 24584 | tf_op jit(solution)/shard_map/ppermute | solution.py:200
  13.3 3.8 %collective-permute-start.4 = (bf16[4,2048]{1,0:T(4,128)(2,1)S(1)}, bf16[4,2048]{1,0:T(4,128)(2,1)S(1)}, u32[]{:S(2)}, u32[]{:S(2)}) collective-permute-start(bf16[4,2048]{1,0:T(4,128)(2,1)S(1)} %pad_maximum_fusion.4), channel_id=1, source_target_pairs={{0,8},{4,12},{8,0},{12,4},{16,24},{20,28},{24,16},{28,20},{1,9},{5... | collective-permute-start | bytes 49160 | tf_op jit(solution)/shard_map/ppermute | solution.py:200
  17.2 4.9 %collective-permute-start.5 = (bf16[8,2048]{1,0:T(8,128)(2,1)S(1)}, bf16[8,2048]{1,0:T(8,128)(2,1)S(1)}, u32[]{:S(2)}, u32[]{:S(2)}) collective-permute-start(bf16[8,2048]{1,0:T(8,128)(2,1)S(1)} %pad_maximum_fusion.1), channel_id=1, source_target_pairs={{0,16},{4,20},{8,24},{12,28},{16,0},{20,4},{24,8},{28,12},{1,17},{... | collective-permute-start | bytes 98312 | tf_op jit(solution)/shard_map/ppermute | solution.py:200
  19.8 6.7 %copy-start.8 = (f32[4]{0:T(128)}, f32[4]{0:T(128)S(1)}, u32[]{:S(2)}) copy-start(f32[4]{0:T(128)S(1)} %multiply_exponential_fusion.slopes_ref) | copy-start | bytes 52
  26.5 3.9 %copy-start.3 = (bf16[2,2048,512]{2,1,0:T(8,128)(2,1)S(1)}, bf16[2,2048,512]{2,1,0:T(8,128)(2,1)}, u32[]{:S(2)}) copy-start(bf16[2,2048,512]{2,1,0:T(8,128)(2,1)} %param.26) | copy-start | bytes 12582916
  30.4 1.6 %copy-start.1 = (bf16[512,2048]{1,0:T(8,128)(2,1)S(1)}, bf16[512,2048]{1,0:T(8,128)(2,1)}, u32[]{:S(2)}) copy-start(bf16[512,2048]{1,0:T(8,128)(2,1)} %param.21) | copy-start | bytes 6291460
  30.4 4.6 %copy-start.2 = (bf16[2048,1536]{1,0:T(8,128)(2,1)S(1)}, bf16[2048,1536]{1,0:T(8,128)(2,1)}, u32[]{:S(2)}) copy-start(bf16[2048,1536]{1,0:T(8,128)(2,1)} %param.19) | copy-start | bytes 18874372
  32.4 6.5 %collective-permute-start.6 = (f32[2,2048]{1,0:T(2,128)S(1)}, f32[2,2048]{1,0:T(2,128)S(1)}, u32[]{:S(2)}, u32[]{:S(2)}) collective-permute-start(f32[2,2048]{1,0:T(2,128)S(1)} %fusion.56), channel_id=1, source_target_pairs={{0,1},{1,0},{2,3},{3,2},{4,5},{5,4},{6,7},{7,6},{8,9},{9,8},{10,11... | collective-permute-start | bytes 49160 | tf_op jit(solution)/shard_map/ppermute | solution.py:233
  33.1 11.8 %collective-permute-start.2 = (bf16[256,2048]{1,0:T(8,128)(2,1)}, bf16[256,2048]{1,0:T(8,128)(2,1)}, u32[]{:S(2)}, u32[]{:S(2)}) collective-permute-start(bf16[256,2048]{1,0:T(8,128)(2,1)} %collective-permute-done), channel_id=1, source_target_pairs={{0,1},{1,0},{2,3},{3,2},{4,5},{5,4},{6,7},{7,6},{8,9},{9,8},{10,11... | collective-permute-start | bytes 3145736 | tf_op jit(solution)/shard_map/ppermute | solution.py:254
  35.0 6.6 %copy-start.6 = (bf16[2048]{0:T(1024)(128)(2,1)S(1)}, bf16[2048]{0:T(1024)(128)(2,1)}, u32[]{:S(2)}) copy-start(bf16[2048]{0:T(1024)(128)(2,1)} %param.22) | copy-start | bytes 12292
  39.0 4.0 %collective-permute-start.7 = (f32[4,2048]{1,0:T(4,128)S(1)}, f32[4,2048]{1,0:T(4,128)S(1)}, u32[]{:S(2)}, u32[]{:S(2)}) collective-permute-start(f32[4,2048]{1,0:T(4,128)S(1)} %pad_maximum_fusion.2), channel_id=1, source_target_pairs={{0,2},{1,3},{2,0},{3,1},{4,6},{5,7},{6,4},{7,5},{8,10},{9,11},{10,... | collective-permute-start | bytes 98312 | tf_op jit(solution)/shard_map/ppermute | solution.py:233
  43.0 10.9 %slice-start = ((s8[6291456]{0:T(1024)(128)(4,1)}), s8[4194304]{0:T(1024)(128)(4,1)S(1)}, s32[]{:S(2)}) async-start(s8[6291456]{0:T(1024)(128)(4,1)} %bitcast.48), calls=%async_computation | async-start | bytes 8388608
  43.1 10.9 %slice-start.1 = ((s8[6291456]{0:T(1024)(128)(4,1)}), s8[2097152]{0:T(1024)(128)(4,1)S(1)}, s32[]{:S(2)}) async-start(s8[6291456]{0:T(1024)(128)(4,1)} %bitcast.48), calls=%async_computation.1 | async-start | bytes 4194304
  43.1 47.1 %collective-permute-start.11 = (bf16[512,2048]{1,0:T(8,128)(2,1)S(1)}, bf16[512,2048]{1,0:T(8,128)(2,1)}, u32[]{:S(2)}, u32[]{:S(2)}) collective-permute-start(bf16[512,2048]{1,0:T(8,128)(2,1)S(1)} %copy-done.1), channel_id=1, source_target_pairs={{0,2},{1,3},{2,0},{3,1},{4,6},{5,7},{6,4},{7,5},{8,10},{9,11},{10,... | collective-permute-start | bytes 6291464 | tf_op jit(solution)/shard_map/ppermute | solution.py:256
  44.9 7.3 %collective-permute-start.8 = (bf16[2,2048]{1,0:T(2,128)(2,1)S(1)}, bf16[2,2048]{1,0:T(2,128)(2,1)S(1)}, u32[]{:S(2)}, u32[]{:S(2)}) collective-permute-start(bf16[2,2048]{1,0:T(2,128)(2,1)S(1)} %fusion.41), channel_id=1, source_target_pairs={{0,4},{4,0},{8,12},{12,8},{16,20},{20,16},{24,28},{28,24},{1,5},{5... | collective-permute-start | bytes 24584 | tf_op jit(solution)/shard_map/ppermute | solution.py:270
  52.3 5.6 %collective-permute-start.9 = (bf16[4,2048]{1,0:T(4,128)(2,1)S(1)}, bf16[4,2048]{1,0:T(4,128)(2,1)S(1)}, u32[]{:S(2)}, u32[]{:S(2)}) collective-permute-start(bf16[4,2048]{1,0:T(4,128)(2,1)S(1)} %pad_maximum_fusion.5), channel_id=1, source_target_pairs={{0,8},{4,12},{8,0},{12,4},{16,24},{20,28},{24,16},{28,20},{1,9},{5... | collective-permute-start | bytes 49160 | tf_op jit(solution)/shard_map/ppermute | solution.py:270
  57.9 6.5 %collective-permute-start.10 = (bf16[8,2048]{1,0:T(8,128)(2,1)S(1)}, bf16[8,2048]{1,0:T(8,128)(2,1)S(1)}, u32[]{:S(2)}, u32[]{:S(2)}) collective-permute-start(bf16[8,2048]{1,0:T(8,128)(2,1)S(1)} %pad_maximum_fusion.3), channel_id=1, source_target_pairs={{0,16},{4,20},{8,24},{12,28},{16,0},{20,4},{24,8},{28,12},{1,17},{... | collective-permute-start | bytes 98312 | tf_op jit(solution)/shard_map/ppermute | solution.py:270
  90.2 16.1 %collective-permute-start.16 = (bf16[512,2048]{1,0:T(8,128)(2,1)}, bf16[512,2048]{1,0:T(8,128)(2,1)}, u32[]{:S(2)}, u32[]{:S(2)}) collective-permute-start(bf16[512,2048]{1,0:T(8,128)(2,1)} %collective-permute-done.11), channel_id=1, source_target_pairs={{0,1},{1,0},{2,3},{3,2},{4,5},{5,4},{6,7},{7,6},{8,9},{9,8},{10,11... | collective-permute-start | bytes 6291464 | tf_op jit(solution)/shard_map/ppermute | solution.py:283
  90.2 18.4 %collective-permute-start.14 = (bf16[512,2048]{1,0:T(8,128)(2,1)S(1)}, bf16[512,2048]{1,0:T(8,128)(2,1)}, u32[]{:S(2)}, u32[]{:S(2)}) collective-permute-start(bf16[512,2048]{1,0:T(8,128)(2,1)S(1)} %copy-done.1), channel_id=1, source_target_pairs={{0,1},{1,0},{2,3},{3,2},{4,5},{5,4},{6,7},{7,6},{8,9},{9,8},{10,11... | collective-permute-start | bytes 6291464 | tf_op jit(solution)/shard_map/ppermute | solution.py:283
  92.6 9.5 %collective-permute-start.12 = (bf16[256,512]{1,0:T(8,128)(2,1)}, bf16[256,512]{1,0:T(8,128)(2,1)}, u32[]{:S(2)}, u32[]{:S(2)}) collective-permute-start(bf16[256,512]{1,0:T(8,128)(2,1)} %get-tuple-element.26), channel_id=1, source_target_pairs={{0,2},{1,3},{2,0},{3,1},{4,6},{5,7},{6,4},{7,5},{8,10},{9,11},{10,... | collective-permute-start | bytes 786440 | tf_op jit(solution)/shard_map/ppermute | solution.py:292
  94.4 11.9 %collective-permute-start.15 = (bf16[256,512]{1,0:T(8,128)(2,1)}, bf16[256,512]{1,0:T(8,128)(2,1)S(1)}, u32[]{:S(2)}, u32[]{:S(2)}) collective-permute-start(bf16[256,512]{1,0:T(8,128)(2,1)} %get-tuple-element.25), channel_id=1, source_target_pairs={{0,3},{1,2},{2,1},{3,0},{4,7},{5,6},{6,5},{7,4},{8,11},{9,10},{10,... | collective-permute-start | bytes 786440 | tf_op jit(solution)/shard_map/ppermute | solution.py:292
  94.4 14.2 %collective-permute-start.13 = (bf16[256,512]{1,0:T(8,128)(2,1)S(1)}, bf16[256,512]{1,0:T(8,128)(2,1)S(1)}, u32[]{:S(2)}, u32[]{:S(2)}) collective-permute-start(bf16[256,512]{1,0:T(8,128)(2,1)S(1)} %get-tuple-element.24), channel_id=1, source_target_pairs={{0,1},{1,0},{2,3},{3,2},{4,5},{5,4},{6,7},{7,6},{8,9},{9,8},{10,11... | collective-permute-start | bytes 786440 | tf_op jit(solution)/shard_map/ppermute | solution.py:292

commit v17 on v14

--- a/solution.py
+++ b/solution.py
@@ -290,10 +290,10 @@
             target = ((chip + k) % chips) * 2 + (core ^ flip)
             outgoing = lax.dynamic_slice_in_dim(context, target * block, block)
             pieces.append(lax.ppermute(outgoing, "tensor", route(k, flip)))
-    summed = jnp.dot(pieces[0], weight_blocks[0], preferred_element_type=jnp.float32)
-    for piece, weight in zip(pieces[1:], weight_blocks[1:]):
+    summed = pre_hidden.astype(jnp.float32) + bias_sum
+    for piece, weight in zip(pieces, weight_blocks):
         summed = summed + jnp.dot(piece, weight, preferred_element_type=jnp.float32)
-    pre_output = (summed + bias_sum + pre_hidden.astype(jnp.float32)).astype(jnp.bfloat16)
+    pre_output = summed.astype(jnp.bfloat16)
     return (pre_output, dec_output)
 
 

time: 113 us -> 110 us (0.973)
  local copies, waits for them, and re-layouts: 4.9 us -> 3.24 us
    dot_general x1 -> x0, matrix products: 1.72 us -> none  [per_device(): jnp.dot(pieces[0], weight_blocks[0], preferred_element_type=jnp.float32)]
    ppermute x3, waiting for transfers between devices: 7.35 us -> 5.68 us  [per_device(): pieces.append(lax.ppermute(outgoing, 'tensor', route(k, flip)))]
    dot_general x3 -> x4, matrix products: 8.12 us -> 9.77 us  [per_device(): summed = summed + jnp.dot(piece, weight, preferred_element_type=jnp.float32)]
  transfers between devices with their start and end apart: 17 -> 17, of which waited for: 7 -> 8; matrix products, arithmetic and copies ran while one was open for 35% -> 35% of each run, Pallas kernels for 21% -> 21%
where the time goes in v17:
time: 110 us; the launch traced here: 109 us
  matrix products  36.9 us (34%)
  Pallas kernels  23.3 us (21%)
  starting transfers between devices  20.8 us (19%)
  waiting for transfers between devices  16 us (15%)
  other arithmetic  7.35 us (7%)
  local copies, waits for them, and re-layouts  3.24 us (3%)
  between operations  1.64 us (1%)
    pallas_call x1, Pallas kernels, prefill_attention_kernel(): pl.pallas_call(functools.partial(_prefill_kernel, tq=tq), out_shape=jax.S...  23.3 us
    dot_general x4, matrix products, per_device(): jnp.dot(token_block, qkv_weight, preferred_element_type=jnp.float32)  17.6 us
    dot_general x4, matrix products, per_device(): summed = summed + jnp.dot(piece, weight, preferred_element_type=jnp.float32)  9.77 us
    ppermute x3, starting transfers between devices, per_device(): lax.ppermute(returned, 'dp', [(i, i ^ step) for i in range(dp_size)])  5.82 us
    ppermute x3, starting transfers between devices, per_device(): lax.ppermute(shifted_rows, 'dp', [(i, i ^ step) for i in range(dp_size)])  5.82 us
    ppermute x3, waiting for transfers between devices, per_device(): lax.ppermute(shifted_rows, 'dp', [(i, i ^ step) for i in range(dp_size)])  5.79 us
    ppermute x3, waiting for transfers between devices, per_device(): pieces.append(lax.ppermute(outgoing, 'tensor', route(k, flip)))  5.68 us
    dot_general x1, matrix products, per_device(): jnp.dot(normed_slots, qkv_weight, preferred_element_type=jnp.float32)  3.75 us
  transfers between devices with their start and end apart: 17, of which 8 were waited for; matrix products, arithmetic and copies ran while one was open for 35% of the time, Pallas kernels for 21%

profile of v17, /device:TPU:0, one launch (start us, length us, event | category | flops | bytes accessed | tf_op | source)
XLA Modules:
  0.0 109.3 jit_solution(798899284771110420)
XLA Ops:
  0.6 0.0 copy-start
  0.6 0.8 convert_element_type.98
  1.4 0.7 convert_element_type.97
  2.1 0.0 copy-start.4
  2.1 1.6 %convert_reduce_fusion = f32[256]{0:T(256)S(1)} fusion(bf16[256,2048]{1,0:T(8,128)(2,1)} %param.15), kind=kLoop, calls=%fused_computation.1 | loop fusion | flops 1048320 | bytes 1049600 | tf_op jit(solution)/shard_map/reduce_sum | solution.py:20
  3.7 1.6 %fusion.17 = f32[256]{0:T(256)S(1)} fusion(bf16[256,2048]{1,0:T(8,128)(2,1)} %param.15, f32[256]{0:T(256)S(1)} %broadcast_multiply_fusion), kind=kLoop, calls=%fused_computation.30 | loop fusion | flops 2096896 | bytes 1050624 | tf_op jit(solution)/shard_map/reduce_sum | solution.py:21
  5.4 1.4 %fusion.20 = bf16[256,2048]{1,0:T(8,128)(2,1)} fusion(bf16[256,2048]{1,0:T(8,128)(2,1)S(1)} %copy-done, f32[2048]{0:T(1024)S(1)} %convert_element_type.98, f32[2048]{0:T(1024)S(1)} %convert_element_type.97, f32[256]{0:T(256)S(1)} %add_rsqrt_fusion, f32[256]{0:T(256)S(1)} %broadcast_multiply_fusion), kind=kLoop, calls=%fused_computation.33 | loop fusion | flops 3145728 | bytes 2115584 | tf_op jit(solution)/shard_map/convert_element_type | solution.py:23
  6.8 2.9 %collective-permute-start = (bf16[256,2048]{1,0:T(8,128)(2,1)}, bf16[256,2048]{1,0:T(8,128)(2,1)}, u32[]{:S(2)}, u32[]{:S(2)}) collective-permute-start(bf16[256,2048]{1,0:T(8,128)(2,1)} %fusion.20), channel_id=1, source_target_pairs={{0,2},{1,3},{2,0},{3,1},{4,6},{5,7},{6,4},{7,5},{8,10},{9,11},{10,... | collective-permute-start | bytes 3145736 | tf_op jit(solution)/shard_map/ppermute | solution.py:251
  9.8 0.0 collective-permute-start.1
  9.8 1.5 %collective-permute-start.3 = (bf16[2,2048]{1,0:T(2,128)(2,1)S(1)}, bf16[2,2048]{1,0:T(2,128)(2,1)S(1)}, u32[]{:S(2)}, u32[]{:S(2)}) collective-permute-start(bf16[2,2048]{1,0:T(2,128)(2,1)S(1)} %copy-done.3), channel_id=1, source_target_pairs={{0,4},{4,0},{8,12},{12,8},{16,20},{20,16},{24,28},{28,24},{1,5},{5... | collective-permute-start | bytes 24584 | tf_op jit(solution)/shard_map/ppermute | solution.py:200
  11.3 0.2 collective-permute-start.14
  11.5 0.1 subtract_convert_fusion
  11.6 0.1 iota_compare_fusion
  11.7 0.2 fusion.61
  11.9 1.5 %collective-permute-done.3 = bf16[2,2048]{1,0:T(2,128)(2,1)S(1)} collective-permute-done((bf16[2,2048]{1,0:T(2,128)(2,1)S(1)}, bf16[2,2048]{1,0:T(2,128)(2,1)S(1)}, u32[]{:S(2)}, u32[]{:S(2)}) %collective-permute-start.3) | collective-permute-done | bytes 8224 | tf_op jit(solution)/shard_map/ppermute | solution.py:200
  13.5 1.6 %collective-permute-start.4 = (bf16[4,2048]{1,0:T(4,128)(2,1)S(1)}, bf16[4,2048]{1,0:T(4,128)(2,1)S(1)}, u32[]{:S(2)}, u32[]{:S(2)}) collective-permute-start(bf16[4,2048]{1,0:T(4,128)(2,1)S(1)} %pad_maximum_fusion.4), channel_id=1, source_target_pairs={{0,8},{4,12},{8,0},{12,4},{16,24},{20,28},{24,16},{28,20},{1,9},{5... | collective-permute-start | bytes 49160 | tf_op jit(solution)/shard_map/ppermute | solution.py:200
  15.1 2.1 %collective-permute-done.4 = bf16[4,2048]{1,0:T(4,128)(2,1)S(1)} collective-permute-done((bf16[4,2048]{1,0:T(4,128)(2,1)S(1)}, bf16[4,2048]{1,0:T(4,128)(2,1)S(1)}, u32[]{:S(2)}, u32[]{:S(2)}) %collective-permute-start.4) | collective-permute-done | bytes 16416 | tf_op jit(solution)/shard_map/ppermute | solution.py:200
  17.3 2.7 %collective-permute-start.5 = (bf16[8,2048]{1,0:T(8,128)(2,1)S(1)}, bf16[8,2048]{1,0:T(8,128)(2,1)S(1)}, u32[]{:S(2)}, u32[]{:S(2)}) collective-permute-start(bf16[8,2048]{1,0:T(8,128)(2,1)S(1)} %pad_maximum_fusion.1), channel_id=1, source_target_pairs={{0,16},{4,20},{8,24},{12,28},{16,0},{20,4},{24,8},{28,12},{1,17},{... | collective-permute-start | bytes 98312 | tf_op jit(solution)/shard_map/ppermute | solution.py:200
  20.0 2.1 %collective-permute-done.5 = bf16[8,2048]{1,0:T(8,128)(2,1)S(1)} collective-permute-done((bf16[8,2048]{1,0:T(8,128)(2,1)S(1)}, bf16[8,2048]{1,0:T(8,128)(2,1)S(1)}, u32[]{:S(2)}, u32[]{:S(2)}) %collective-permute-start.5) | collective-permute-done | bytes 32800 | tf_op jit(solution)/shard_map/ppermute | solution.py:200
  22.2 0.3 fusion.74
  22.5 0.2 multiply_reduce_fusion
  22.7 3.8 %fusion.15 = bf16[2,1536]{1,0:T(2,128)(2,1)S(1)} fusion(bf16[2048,1536]{1,0:T(8,128)(2,1)} %param.19, f32[2,2048]{1,0:T(2,128)S(1)} %get-tuple-element.33, f32[2]{0:T(128)S(1)} %add_rsqrt_fusion.1, f32[2]{0:T(128)S(1)} %broadcast_multiply_fusion.1, f32[2048]{0:T(1024)S(1)} %convert_element_type.98, f32[2048]{0:T(1024)S(1)} %convert_element_type.97, ...), kind=kOutput, calls=%fused_computation.26 | convolution fusion | flops 12609536 | bytes 6336528 | tf_op jit(solution)/shard_map/dot_general | solution.py:214
  26.5 0.0 copy-start.2
  26.6 0.1 fusion.50
  26.6 3.6 %fusion.75 = (f32[2,4]{1,0:T(2,128)S(1)}, f32[2,4,2048]{2,1,0:T(4,128)S(1)}) fusion(f32[2,2048]{1,0:T(2,128)S(1)} %subtract_convert_fusion, f32[4]{0:T(128)S(1)} %multiply_exponential_fusion.slopes_ref, bf16[2,2048,512]{2,1,0:T(8,128)(2,1)} %param.25, pred[512,4]{0,1:T(4,128)(4,1)S(1)} %iota_compare_fusion.1, bf16[2,512]{1,0:T(2,128)(2,1)S(1)} %bitcast.53, ...), kind=kOutput, calls=%fused_computation.136 | convolution fusion | flops 16863224 | bytes 4284464 | tf_op jit(solution)/shard_map/vmap()/dot_general | solution.py:148
  30.3 0.2 fusion.37
  30.5 0.1 broadcast_bitcast_fusion
  30.6 0.7 fusion.21
  31.3 0.4 fusion.56
  31.7 1.6 %collective-permute-done = bf16[256,2048]{1,0:T(8,128)(2,1)} collective-permute-done((bf16[256,2048]{1,0:T(8,128)(2,1)}, bf16[256,2048]{1,0:T(8,128)(2,1)}, u32[]{:S(2)}, u32[]{:S(2)}) %collective-permute-start) | collective-permute-done | bytes 1048608 | tf_op jit(solution)/shard_map/ppermute | solution.py:251
  33.2 0.0 collective-permute-start.2
  33.2 1.9 %broadcast_in_dim.54 = bf16[1024,1536]{1,0:T(8,128)(2,1)} broadcast(bf16[]{:T(256)} %constant.123.clone.1), dimensions={} | broadcast | bytes 3145730 | tf_op jit(solution)/shard_map/broadcast_in_dim | solution.py:258
  35.1 4.0 %fusion.3 = bf16[1024,1536]{1,0:T(8,128)(2,1)} fusion(bf16[1024,1536]{1,0:T(8,128)(2,1)} %broadcast_in_dim.54, s32[]{:T(128)S(6)} %select_n.124, bf16[256,2048]{1,0:T(8,128)(2,1)} %fusion.20, bf16[2048,1536]{1,0:T(8,128)(2,1)S(1)} %bitcast.49, f32[1536]{0:T(1024)S(1)} %convert_element_type.100), kind=kOutput, calls=%fused_computation.12 | convolution fusion | flops 1611399168 | bytes 8132612 | tf_op jit(solution)/shard_map/dot_general | solution.py:263
  39.1 1.8 %collective-permute-start.7 = (f32[4,2048]{1,0:T(4,128)S(1)}, f32[4,2048]{1,0:T(4,128)S(1)}, u32[]{:S(2)}, u32[]{:S(2)}) collective-permute-start(f32[4,2048]{1,0:T(4,128)S(1)} %pad_maximum_fusion.2), channel_id=1, source_target_pairs={{0,2},{1,3},{2,0},{3,1},{4,6},{5,7},{6,4},{7,5},{8,10},{9,11},{10,... | collective-permute-start | bytes 98312 | tf_op jit(solution)/shard_map/ppermute | solution.py:233
  40.9 0.1 fusion.65
  41.7 1.4 %collective-permute-done.7 = f32[4,2048]{1,0:T(4,128)S(1)} collective-permute-done((f32[4,2048]{1,0:T(4,128)S(1)}, f32[4,2048]{1,0:T(4,128)S(1)}, u32[]{:S(2)}, u32[]{:S(2)}) %collective-permute-start.7) | collective-permute-done | bytes 32800 | tf_op jit(solution)/shard_map/ppermute | solution.py:233
  43.2 0.0 slice-start.2
  43.2 0.0 slice-start.3
  43.2 1.8 %collective-permute-start.11 = (bf16[512,2048]{1,0:T(8,128)(2,1)S(1)}, bf16[512,2048]{1,0:T(8,128)(2,1)}, u32[]{:S(2)}, u32[]{:S(2)}) collective-permute-start(bf16[512,2048]{1,0:T(8,128)(2,1)S(1)} %copy-done.1), channel_id=1, source_target_pairs={{0,2},{1,3},{2,0},{3,1},{4,6},{5,7},{6,4},{7,5},{8,10},{9,11},{10,... | collective-permute-start | bytes 6291464 | tf_op jit(solution)/shard_map/ppermute | solution.py:256
  45.0 0.0 collective-permute-done.1
  45.0 0.0 collective-permute-done.2
  45.0 1.5 %collective-permute-start.8 = (bf16[2,2048]{1,0:T(2,128)(2,1)S(1)}, bf16[2,2048]{1,0:T(2,128)(2,1)S(1)}, u32[]{:S(2)}, u32[]{:S(2)}) collective-permute-start(bf16[2,2048]{1,0:T(2,128)(2,1)S(1)} %fusion.41), channel_id=1, source_target_pairs={{0,4},{4,0},{8,12},{12,8},{16,20},{20,16},{24,28},{28,24},{1,5},{5... | collective-permute-start | bytes 24584 | tf_op jit(solution)/shard_map/ppermute | solution.py:270
  46.6 5.8 %fusion.5 = bf16[1024,1536]{1,0:T(8,128)(2,1)} fusion(bf16[1024,1536]{1,0:T(8,128)(2,1)} %fusion.3, s32[]{:T(128)S(6)} %select_n.126, bf16[256,2048]{1,0:T(8,128)(2,1)} %collective-permute-done, bf16[2048,1536]{1,0:T(8,128)(2,1)} %param.19, f32[1536]{0:T(1024)S(1)} %convert_element_type.100), kind=kOutput, calls=%fused_computation.14 | convolution fusion | flops 1611399168 | bytes 8132612 | tf_op jit(solution)/shard_map/dot_general | solution.py:263
  52.4 0.0 collective-permute-done.8
  52.4 1.6 %collective-permute-start.9 = (bf16[4,2048]{1,0:T(4,128)(2,1)S(1)}, bf16[4,2048]{1,0:T(4,128)(2,1)S(1)}, u32[]{:S(2)}, u32[]{:S(2)}) collective-permute-start(bf16[4,2048]{1,0:T(4,128)(2,1)S(1)} %pad_maximum_fusion.5), channel_id=1, source_target_pairs={{0,8},{4,12},{8,0},{12,4},{16,24},{20,28},{24,16},{28,20},{1,9},{5... | collective-permute-start | bytes 49160 | tf_op jit(solution)/shard_map/ppermute | solution.py:270
  54.0 3.9 %fusion.7 = bf16[1024,1536]{1,0:T(8,128)(2,1)} fusion(bf16[1024,1536]{1,0:T(8,128)(2,1)} %fusion.5, s32[]{:T(128)S(6)} %select_n.138, bf16[256,2048]{1,0:T(8,128)(2,1)} %collective-permute-done.1, bf16[2048,1536]{1,0:T(8,128)(2,1)S(1)} %bitcast.51, f32[1536]{0:T(1024)S(1)} %convert_element_type.100), kind=kOutput, calls=%fused_computation.16 | convolution fusion | flops 1611399168 | bytes 8132612 | tf_op jit(solution)/shard_map/dot_general | solution.py:263
  58.0 2.7 %collective-permute-start.10 = (bf16[8,2048]{1,0:T(8,128)(2,1)S(1)}, bf16[8,2048]{1,0:T(8,128)(2,1)S(1)}, u32[]{:S(2)}, u32[]{:S(2)}) collective-permute-start(bf16[8,2048]{1,0:T(8,128)(2,1)S(1)} %pad_maximum_fusion.3), channel_id=1, source_target_pairs={{0,16},{4,20},{8,24},{12,28},{16,0},{20,4},{24,8},{28,12},{1,17},{... | collective-permute-start | bytes 98312 | tf_op jit(solution)/shard_map/ppermute | solution.py:270
  60.6 3.9 %fusion.9.q_ref.kn_ref.vn_ref = bf16[1024,1536]{1,0:T(8,128)(2,1)} fusion(bf16[1024,1536]{1,0:T(8,128)(2,1)} %fusion.7, s32[]{:T(128)S(6)} %select_n.139, bf16[256,2048]{1,0:T(8,128)(2,1)} %collective-permute-done.2, bf16[2048,1536]{1,0:T(8,128)(2,1)S(1)} %bitcast.51, f32[1536]{0:T(1024)S(1)} %convert_element_type.100), kind=kOutput, calls=%fused_computation.18 | convolution fusion | flops 1611399168 | bytes 8132612 | tf_op jit(solution)/shard_map/dot_general | solution.py:263
  64.5 0.0 collective-permute-done.10
  64.5 0.8 convolution_convert_fusion
  65.3 23.3 %shard_map.158 = bf16[1024,512]{1,0:T(8,128)(2,1)} custom-call(s32[1]{0:T(128)S(6)} %copy.39.prefix_ref, f32[4]{0:T(128)} %copy-done.7, bf16[1024,1536]{1,0:T(8,128)(2,1)} %fusion.9.q_ref.kn_ref.vn_ref, bf16[1024,1536]{1,0:T(8,128)(2,1)} %fusion.9.q_ref.kn_ref.vn_ref, bf16[1024,1536]{1,0:T(8,128)(2,1)} %fusion.9.q_ref.kn_ref.vn_ref, ...), custom_call_target="tpu_custom_call" | custom-call | flops 4294967296 | bytes 6291456 | tf_op jit(solution)/shard_map/pallas_call | solution.py:117
  88.7 1.6 %collective-permute-done.11 = bf16[512,2048]{1,0:T(8,128)(2,1)} collective-permute-done((bf16[512,2048]{1,0:T(8,128)(2,1)S(1)}, bf16[512,2048]{1,0:T(8,128)(2,1)}, u32[]{:S(2)}, u32[]{:S(2)}) %collective-permute-start.11) | collective-permute-done | bytes 2097184 | tf_op jit(solution)/shard_map/ppermute | solution.py:256
  90.3 0.0 collective-permute-start.16
  90.3 1.2 %constant_dynamic-slice_fusion = (bf16[256,512]{1,0:T(8,128)(2,1)S(1)}, bf16[256,512]{1,0:T(8,128)(2,1)S(1)}, bf16[256,512]{1,0:T(8,128)(2,1)S(1)}) fusion(bf16[1024,512]{1,0:T(8,128)(2,1)} %shard_map.158, s32[]{:T(128)S(6)} %select_n.145, s32[]{:T(128)S(6)} %select_n.146, s32[]{:T(128)S(6)} %select_n.138), kind=kLoop, calls=%fused_computation.89 | loop fusion | bytes 1572876 | tf_op jit(solution)/shard_map/dynamic_slice | solution.py:291
  91.4 1.9 %collective-permute-start.15 = (bf16[256,512]{1,0:T(8,128)(2,1)S(1)}, bf16[256,512]{1,0:T(8,128)(2,1)S(1)}, u32[]{:S(2)}, u32[]{:S(2)}) collective-permute-start(bf16[256,512]{1,0:T(8,128)(2,1)S(1)} %get-tuple-element.25), channel_id=1, source_target_pairs={{0,3},{1,2},{2,1},{3,0},{4,7},{5,6},{6,5},{7,4},{8,11},{9,10},{10,... | collective-permute-start | bytes 786440 | tf_op jit(solution)/shard_map/ppermute | solution.py:292
  93.4 0.0 collective-permute-start.13
  93.4 0.5 collective-permute-start.12
  93.8 1.7 %convolution_add_fusion.1 = f32[256,2048]{1,0:T(8,128)S(1)} fusion(bf16[512,2048]{1,0:T(8,128)(2,1)S(1)} %copy-done.1, bf16[256,2048]{1,0:T(8,128)(2,1)S(1)} %copy-done, f32[2048]{0:T(1024)S(1)} %convert_element_type.95, bf16[1024,512]{1,0:T(8,128)(2,1)} %shard_map.158, s32[]{:T(128)S(6)} %select_n.143), kind=kOutput, calls=%fused_computation.5 | convolution fusion | flops 538443776 | bytes 5513220 | tf_op jit(solution)/shard_map/dot_general | solution.py:295
  95.5 0.0 collective-permute-done.14
  95.5 2.3 %fusion.76 = f32[256,2048]{1,0:T(8,128)S(1)} fusion(bf16[256,512]{1,0:T(8,128)(2,1)S(1)} %collective-permute-done.13, bf16[512,2048]{1,0:T(8,128)(2,1)} %collective-permute-done.14), kind=kOutput, calls=%fused_computation.137 | convolution fusion | flops 536870912 | bytes 4456448 | tf_op jit(solution)/shard_map/dot_general | solution.py:295
  97.8 2.2 %collective-permute-done.15 = bf16[256,512]{1,0:T(8,128)(2,1)S(1)} collective-permute-done((bf16[256,512]{1,0:T(8,128)(2,1)S(1)}, bf16[256,512]{1,0:T(8,128)(2,1)S(1)}, u32[]{:S(2)}, u32[]{:S(2)}) %collective-permute-start.15) | collective-permute-done | bytes 262176 | tf_op jit(solution)/shard_map/ppermute | solution.py:292
  100.0 2.3 %fusion.77 = f32[256,2048]{1,0:T(8,128)S(1)} fusion(bf16[256,512]{1,0:T(8,128)(2,1)S(1)} %collective-permute-done.15, bf16[512,2048]{1,0:T(8,128)(2,1)} %collective-permute-done.16), kind=kOutput, calls=%fused_computation.138 | convolution fusion | flops 536870912 | bytes 4456448 | tf_op jit(solution)/shard_map/dot_general | solution.py:295
  102.4 3.5 %collective-permute-done.12 = bf16[256,512]{1,0:T(8,128)(2,1)S(1)} collective-permute-done((bf16[256,512]{1,0:T(8,128)(2,1)S(1)}, bf16[256,512]{1,0:T(8,128)(2,1)S(1)}, u32[]{:S(2)}, u32[]{:S(2)}) %collective-permute-start.12) | collective-permute-done | bytes 262176 | tf_op jit(solution)/shard_map/ppermute | solution.py:292
  105.8 3.5 %fusion.10 = bf16[256,2048]{1,0:T(8,128)(2,1)} fusion(f32[256,2048]{1,0:T(8,128)S(1)} %fusion.77, f32[256,2048]{1,0:T(8,128)S(1)} %fusion.76, f32[256,2048]{1,0:T(8,128)S(1)} %convolution_add_fusion.1, bf16[256,512]{1,0:T(8,128)(2,1)S(1)} %collective-permute-done.12, bf16[512,2048]{1,0:T(8,128)(2,1)} %collective-permute-done.11), kind=kOutput, calls=%fused_computation.19 | convolution fusion | flops 538968064 | bytes 9699328 | tf_op jit(solution)/shard_map/dot_general | solution.py:295
  (54 shorter events, 0.5 us)
Async XLA Ops:
  0.6 4.8 %copy-start = (bf16[256,2048]{1,0:T(8,128)(2,1)S(1)}, bf16[256,2048]{1,0:T(8,128)(2,1)}, u32[]{:S(2)}) copy-start(bf16[256,2048]{1,0:T(8,128)(2,1)} %param.15) | copy-start | bytes 3145732
  2.1 7.7 %copy-start.3 = (bf16[2,2048]{1,0:T(2,128)(2,1)S(1)}, bf16[2,2048]{1,0:T(2,128)(2,1)}, u32[]{:S(2)}) copy-start(bf16[2,2048]{1,0:T(2,128)(2,1)} %param.16) | copy-start | bytes 24580
  2.1 9.2 %copy-start.1 = (bf16[512,2048]{1,0:T(8,128)(2,1)S(1)}, bf16[512,2048]{1,0:T(8,128)(2,1)}, u32[]{:S(2)}) copy-start(bf16[512,2048]{1,0:T(8,128)(2,1)} %param.21) | copy-start | bytes 6291460
  2.1 9.4 %copy-start.6 = (s32[2]{0:T(128)S(1)}, s32[2]{0:T(128)}, u32[]{:S(2)}) copy-start(s32[2]{0:T(128)} %param.28) | copy-start | bytes 28
  2.1 9.6 %copy-start.8 = (s32[16]{0:T(128)S(1)}, s32[16]{0:T(128)}, u32[]{:S(2)}) copy-start(s32[16]{0:T(128)} %param.29) | copy-start | bytes 196
  2.1 17.9 %copy-start.4 = (bf16[1536]{0:T(1024)(128)(2,1)S(1)}, bf16[1536]{0:T(1024)(128)(2,1)}, u32[]{:S(2)}) copy-start(bf16[1536]{0:T(1024)(128)(2,1)} %param.20) | copy-start | bytes 9220
  6.8 26.4 %collective-permute-start = (bf16[256,2048]{1,0:T(8,128)(2,1)}, bf16[256,2048]{1,0:T(8,128)(2,1)}, u32[]{:S(2)}, u32[]{:S(2)}) collective-permute-start(bf16[256,2048]{1,0:T(8,128)(2,1)} %fusion.20), channel_id=1, source_target_pairs={{0,2},{1,3},{2,0},{3,1},{4,6},{5,7},{6,4},{7,5},{8,10},{9,11},{10,... | collective-permute-start | bytes 3145736 | tf_op jit(solution)/shard_map/ppermute | solution.py:251
  9.8 35.3 %collective-permute-start.1 = (bf16[256,2048]{1,0:T(8,128)(2,1)}, bf16[256,2048]{1,0:T(8,128)(2,1)}, u32[]{:S(2)}, u32[]{:S(2)}) collective-permute-start(bf16[256,2048]{1,0:T(8,128)(2,1)} %fusion.20), channel_id=1, source_target_pairs={{0,1},{1,0},{2,3},{3,2},{4,5},{5,4},{6,7},{7,6},{8,9},{9,8},{10,11... | collective-permute-start | bytes 3145736 | tf_op jit(solution)/shard_map/ppermute | solution.py:254
  9.8 3.7 %collective-permute-start.3 = (bf16[2,2048]{1,0:T(2,128)(2,1)S(1)}, bf16[2,2048]{1,0:T(2,128)(2,1)S(1)}, u32[]{:S(2)}, u32[]{:S(2)}) collective-permute-start(bf16[2,2048]{1,0:T(2,128)(2,1)S(1)} %copy-done.3), channel_id=1, source_target_pairs={{0,4},{4,0},{8,12},{12,8},{16,20},{20,16},{24,28},{28,24},{1,5},{5... | collective-permute-start | bytes 24584 | tf_op jit(solution)/shard_map/ppermute | solution.py:200
  11.3 84.2 %collective-permute-start.14 = (bf16[512,2048]{1,0:T(8,128)(2,1)S(1)}, bf16[512,2048]{1,0:T(8,128)(2,1)}, u32[]{:S(2)}, u32[]{:S(2)}) collective-permute-start(bf16[512,2048]{1,0:T(8,128)(2,1)S(1)} %copy-done.1), channel_id=1, source_target_pairs={{0,1},{1,0},{2,3},{3,2},{4,5},{5,4},{6,7},{7,6},{8,9},{9,8},{10,11... | collective-permute-start | bytes 6291464 | tf_op jit(solution)/shard_map/ppermute | solution.py:283
  13.5 3.8 %collective-permute-start.4 = (bf16[4,2048]{1,0:T(4,128)(2,1)S(1)}, bf16[4,2048]{1,0:T(4,128)(2,1)S(1)}, u32[]{:S(2)}, u32[]{:S(2)}) collective-permute-start(bf16[4,2048]{1,0:T(4,128)(2,1)S(1)} %pad_maximum_fusion.4), channel_id=1, source_target_pairs={{0,8},{4,12},{8,0},{12,4},{16,24},{20,28},{24,16},{28,20},{1,9},{5... | collective-permute-start | bytes 49160 | tf_op jit(solution)/shard_map/ppermute | solution.py:200
  17.3 4.9 %collective-permute-start.5 = (bf16[8,2048]{1,0:T(8,128)(2,1)S(1)}, bf16[8,2048]{1,0:T(8,128)(2,1)S(1)}, u32[]{:S(2)}, u32[]{:S(2)}) collective-permute-start(bf16[8,2048]{1,0:T(8,128)(2,1)S(1)} %pad_maximum_fusion.1), channel_id=1, source_target_pairs={{0,16},{4,20},{8,24},{12,28},{16,0},{20,4},{24,8},{28,12},{1,17},{... | collective-permute-start | bytes 98312 | tf_op jit(solution)/shard_map/ppermute | solution.py:200
  20.0 6.7 %copy-start.7 = (f32[4]{0:T(128)}, f32[4]{0:T(128)S(1)}, u32[]{:S(2)}) copy-start(f32[4]{0:T(128)S(1)} %multiply_exponential_fusion.slopes_ref) | copy-start | bytes 52
  26.5 4.1 %copy-start.2 = (bf16[2,2048,512]{2,1,0:T(8,128)(2,1)S(1)}, bf16[2,2048,512]{2,1,0:T(8,128)(2,1)}, u32[]{:S(2)}) copy-start(bf16[2,2048,512]{2,1,0:T(8,128)(2,1)} %param.26) | copy-start | bytes 12582916
  26.6 8.5 %slice-start = ((s8[6291456]{0:T(1024)(128)(4,1)}), s8[2097152]{0:T(1024)(128)(4,1)S(1)}, s32[]{:S(2)}) async-start(s8[6291456]{0:T(1024)(128)(4,1)} %bitcast.48), calls=%async_computation | async-start | bytes 4194304
  30.6 4.6 %slice-start.1 = ((s8[6291456]{0:T(1024)(128)(4,1)}), s8[4194304]{0:T(1024)(128)(4,1)S(1)}, s32[]{:S(2)}) async-start(s8[6291456]{0:T(1024)(128)(4,1)} %bitcast.48), calls=%async_computation.1 | async-start | bytes 8388608
  31.7 7.4 %collective-permute-start.6 = (f32[2,2048]{1,0:T(2,128)S(1)}, f32[2,2048]{1,0:T(2,128)S(1)}, u32[]{:S(2)}, u32[]{:S(2)}) collective-permute-start(f32[2,2048]{1,0:T(2,128)S(1)} %fusion.56), channel_id=1, source_target_pairs={{0,1},{1,0},{2,3},{3,2},{4,5},{5,4},{6,7},{7,6},{8,9},{9,8},{10,11... | collective-permute-start | bytes 49160 | tf_op jit(solution)/shard_map/ppermute | solution.py:233
  33.2 11.8 %collective-permute-start.2 = (bf16[256,2048]{1,0:T(8,128)(2,1)}, bf16[256,2048]{1,0:T(8,128)(2,1)}, u32[]{:S(2)}, u32[]{:S(2)}) collective-permute-start(bf16[256,2048]{1,0:T(8,128)(2,1)} %collective-permute-done), channel_id=1, source_target_pairs={{0,1},{1,0},{2,3},{3,2},{4,5},{5,4},{6,7},{7,6},{8,9},{9,8},{10,11... | collective-permute-start | bytes 3145736 | tf_op jit(solution)/shard_map/ppermute | solution.py:254
  35.1 6.5 %copy-start.5 = (bf16[2048]{0:T(1024)(128)(2,1)S(1)}, bf16[2048]{0:T(1024)(128)(2,1)}, u32[]{:S(2)}) copy-start(bf16[2048]{0:T(1024)(128)(2,1)} %param.22) | copy-start | bytes 12292
  39.1 4.0 %collective-permute-start.7 = (f32[4,2048]{1,0:T(4,128)S(1)}, f32[4,2048]{1,0:T(4,128)S(1)}, u32[]{:S(2)}, u32[]{:S(2)}) collective-permute-start(f32[4,2048]{1,0:T(4,128)S(1)} %pad_maximum_fusion.2), channel_id=1, source_target_pairs={{0,2},{1,3},{2,0},{3,1},{4,6},{5,7},{6,4},{7,5},{8,10},{9,11},{10,... | collective-permute-start | bytes 98312 | tf_op jit(solution)/shard_map/ppermute | solution.py:233
  43.2 10.9 %slice-start.2 = ((s8[6291456]{0:T(1024)(128)(4,1)}), s8[4194304]{0:T(1024)(128)(4,1)S(1)}, s32[]{:S(2)}) async-start(s8[6291456]{0:T(1024)(128)(4,1)} %bitcast.50), calls=%async_computation.2 | async-start | bytes 8388608
  43.2 10.8 %slice-start.3 = ((s8[6291456]{0:T(1024)(128)(4,1)}), s8[2097152]{0:T(1024)(128)(4,1)S(1)}, s32[]{:S(2)}) async-start(s8[6291456]{0:T(1024)(128)(4,1)} %bitcast.50), calls=%async_computation.3 | async-start | bytes 4194304
  43.2 47.1 %collective-permute-start.11 = (bf16[512,2048]{1,0:T(8,128)(2,1)S(1)}, bf16[512,2048]{1,0:T(8,128)(2,1)}, u32[]{:S(2)}, u32[]{:S(2)}) collective-permute-start(bf16[512,2048]{1,0:T(8,128)(2,1)S(1)} %copy-done.1), channel_id=1, source_target_pairs={{0,2},{1,3},{2,0},{3,1},{4,6},{5,7},{6,4},{7,5},{8,10},{9,11},{10,... | collective-permute-start | bytes 6291464 | tf_op jit(solution)/shard_map/ppermute | solution.py:256
  45.0 7.3 %collective-permute-start.8 = (bf16[2,2048]{1,0:T(2,128)(2,1)S(1)}, bf16[2,2048]{1,0:T(2,128)(2,1)S(1)}, u32[]{:S(2)}, u32[]{:S(2)}) collective-permute-start(bf16[2,2048]{1,0:T(2,128)(2,1)S(1)} %fusion.41), channel_id=1, source_target_pairs={{0,4},{4,0},{8,12},{12,8},{16,20},{20,16},{24,28},{28,24},{1,5},{5... | collective-permute-start | bytes 24584 | tf_op jit(solution)/shard_map/ppermute | solution.py:270
  52.4 5.6 %collective-permute-start.9 = (bf16[4,2048]{1,0:T(4,128)(2,1)S(1)}, bf16[4,2048]{1,0:T(4,128)(2,1)S(1)}, u32[]{:S(2)}, u32[]{:S(2)}) collective-permute-start(bf16[4,2048]{1,0:T(4,128)(2,1)S(1)} %pad_maximum_fusion.5), channel_id=1, source_target_pairs={{0,8},{4,12},{8,0},{12,4},{16,24},{20,28},{24,16},{28,20},{1,9},{5... | collective-permute-start | bytes 49160 | tf_op jit(solution)/shard_map/ppermute | solution.py:270
  58.0 6.6 %collective-permute-start.10 = (bf16[8,2048]{1,0:T(8,128)(2,1)S(1)}, bf16[8,2048]{1,0:T(8,128)(2,1)S(1)}, u32[]{:S(2)}, u32[]{:S(2)}) collective-permute-start(bf16[8,2048]{1,0:T(8,128)(2,1)S(1)} %pad_maximum_fusion.3), channel_id=1, source_target_pairs={{0,16},{4,20},{8,24},{12,28},{16,0},{20,4},{24,8},{28,12},{1,17},{... | collective-permute-start | bytes 98312 | tf_op jit(solution)/shard_map/ppermute | solution.py:270
  90.3 9.7 %collective-permute-start.16 = (bf16[512,2048]{1,0:T(8,128)(2,1)}, bf16[512,2048]{1,0:T(8,128)(2,1)}, u32[]{:S(2)}, u32[]{:S(2)}) collective-permute-start(bf16[512,2048]{1,0:T(8,128)(2,1)} %collective-permute-done.11), channel_id=1, source_target_pairs={{0,1},{1,0},{2,3},{3,2},{4,5},{5,4},{6,7},{7,6},{8,9},{9,8},{10,11... | collective-permute-start | bytes 6291464 | tf_op jit(solution)/shard_map/ppermute | solution.py:283
  91.4 8.6 %collective-permute-start.15 = (bf16[256,512]{1,0:T(8,128)(2,1)S(1)}, bf16[256,512]{1,0:T(8,128)(2,1)S(1)}, u32[]{:S(2)}, u32[]{:S(2)}) collective-permute-start(bf16[256,512]{1,0:T(8,128)(2,1)S(1)} %get-tuple-element.25), channel_id=1, source_target_pairs={{0,3},{1,2},{2,1},{3,0},{4,7},{5,6},{6,5},{7,4},{8,11},{9,10},{10,... | collective-permute-start | bytes 786440 | tf_op jit(solution)/shard_map/ppermute | solution.py:292
  93.4 2.2 %collective-permute-start.13 = (bf16[256,512]{1,0:T(8,128)(2,1)S(1)}, bf16[256,512]{1,0:T(8,128)(2,1)S(1)}, u32[]{:S(2)}, u32[]{:S(2)}) collective-permute-start(bf16[256,512]{1,0:T(8,128)(2,1)S(1)} %get-tuple-element.26), channel_id=1, source_target_pairs={{0,1},{1,0},{2,3},{3,2},{4,5},{5,4},{6,7},{7,6},{8,9},{9,8},{10,11... | collective-permute-start | bytes 786440 | tf_op jit(solution)/shard_map/ppermute | solution.py:292
  93.4 12.5 %collective-permute-start.12 = (bf16[256,512]{1,0:T(8,128)(2,1)S(1)}, bf16[256,512]{1,0:T(8,128)(2,1)S(1)}, u32[]{:S(2)}, u32[]{:S(2)}) collective-permute-start(bf16[256,512]{1,0:T(8,128)(2,1)S(1)} %get-tuple-element.24), channel_id=1, source_target_pairs={{0,2},{1,3},{2,0},{3,1},{4,6},{5,7},{6,4},{7,5},{8,10},{9,11},{10,... | collective-permute-start | bytes 786440 | tf_op jit(solution)/shard_map/ppermute | solution.py:292

commit v18 on v17

--- a/solution.py
+++ b/solution.py
@@ -74,7 +74,7 @@
     return context.astype(jnp.bfloat16).reshape(group_size, -1)
 
 
-def _prefill_kernel(prefix_ref, slopes_ref, q_ref, kn_ref, vn_ref, kc_ref, vc_ref, o_ref, *, tq):
+def _prefill_kernel(prefix_ref, slopes_ref, place_ref, q_ref, kn_ref, vn_ref, kc_ref, vc_ref, o_ref, *, tq):
     h = pl.program_id(0)
     i = pl.program_id(1)
     prefix = prefix_ref[0]
@@ -109,7 +109,7 @@
         pl.when(i == last)(functools.partial(tile, last, (last + 1) * tq))
 
 
-def prefill_attention_kernel(merged, cache_keys, cache_values, prefix, slopes, head_size, tq=256):
+def prefill_attention_kernel(merged, cache_keys, cache_values, prefix, slopes, place, head_size, tq):
     group = merged.shape[0]
     heads = merged.shape[1] // (3 * head_size)
     cache_size = cache_keys.shape[0]
@@ -118,7 +118,7 @@
         functools.partial(_prefill_kernel, tq=tq),
         out_shape=jax.ShapeDtypeStruct((group, heads * head_size), jnp.bfloat16),
         grid_spec=pltpu.PrefetchScalarGridSpec(
-            num_scalar_prefetch=2,
+            num_scalar_prefetch=3,
             grid=(heads, group // tq),
             in_specs=[
                 pl.BlockSpec((tq, head_size), lambda h, i, *_: (i, h * 3)),
@@ -127,14 +127,14 @@
                 pl.BlockSpec((cache_size, head_size), lambda h, i, *_: (0, h)),
                 pl.BlockSpec((cache_size, head_size), lambda h, i, *_: (0, h)),
             ],
-            out_specs=pl.BlockSpec((tq, head_size), lambda h, i, *_: (i, h)),
+            out_specs=pl.BlockSpec((tq, head_size), lambda h, i, p, s, place: (place[i], h)),
         ),
         cost_estimate=pl.CostEstimate(
             flops=4 * heads * group * (group + cache_size) * head_size,
             transcendentals=heads * group * (group + cache_size),
             bytes_accessed=2 * (group * heads * 3 * head_size + 2 * cache_size * heads * head_size + group * heads * head_size),
         ),
-    )(prefix, slopes, merged, merged, merged, cache_keys, cache_values)
+    )(prefix, slopes, place, merged, merged, merged, cache_keys, cache_values)
 
 
 def decode_attention(query_row, new_key, new_value, cache_keys, cache_values, length, slopes):
@@ -275,8 +275,10 @@
     take = (back[:, None] == jnp.arange(returned.shape[0], dtype=jnp.int32)[None, :]).astype(jnp.bfloat16)
     dec_output = jnp.dot(take, returned, preferred_element_type=jnp.float32).astype(jnp.bfloat16)
     merged_rows, dec_output = lax.optimization_barrier((merged_rows, dec_output))
+    members = jnp.arange(tensor_size, dtype=jnp.int32)
+    place = ((members % 2) ^ core) * chips + (members // 2 - chip) % chips
     context = prefill_attention_kernel(
-        merged_rows, pre_keys[0], pre_values[0], prefix_lengths, slopes, head_size
+        merged_rows, pre_keys[0], pre_values[0], prefix_lengths, slopes, place, head_size, block
     )
     context, across_chips = lax.optimization_barrier((context, across_chips))
     same_core = [out_weight] + list(across_chips)
@@ -284,11 +286,11 @@
     pieces = []
     for flip in (0, 1):
         for k in range(chips):
+            position = flip * chips + k
+            outgoing = context[position * block:(position + 1) * block]
             if k == 0 and flip == 0:
-                pieces.append(lax.dynamic_slice_in_dim(context, member * block, block))
+                pieces.append(outgoing)
                 continue
-            target = ((chip + k) % chips) * 2 + (core ^ flip)
-            outgoing = lax.dynamic_slice_in_dim(context, target * block, block)
             pieces.append(lax.ppermute(outgoing, "tensor", route(k, flip)))
     summed = pre_hidden.astype(jnp.float32) + bias_sum
     for piece, weight in zip(pieces, weight_blocks):

time: 110 us -> 109 us (level)
  starting transfers between devices: 20.8 us -> 18 us
  waiting for transfers between devices: 16 us -> 17.1 us
    dot_general x4, matrix products: 17.6 us -> 19.9 us  [per_device(): jnp.dot(token_block, qkv_weight, preferred_element_type=jnp.float32)]
    ppermute x3, waiting for transfers between devices: 5.68 us -> 7.37 us  [per_device(): pieces.append(lax.ppermute(outgoing, 'tensor', route(k, flip)))]
    dot_general x4, matrix products: 9.77 us -> 8.15 us  [per_device(): summed = summed + jnp.dot(piece, weight, preferred_element_type=jnp.float32)]
    ppermute x1, waiting for transfers between devices: 1.57 us -> 0.01 us  [per_device(): lax.ppermute(normed, 'tensor', route(k, 0))]
    ppermute x3, waiting for transfers between devices: 5.79 us -> 4.36 us  [per_device(): lax.ppermute(shifted_rows, 'dp', [(i, i ^ step) for i in range(dp_size)])]
    ppermute x2, waiting for transfers between devices: 1.38 us -> 2.71 us  [per_device(): lax.ppermute(partials, 'tensor', [(i, i ^ step) for i in range(tensor_siz...]
    ppermute x1, starting transfers between devices: 1.8 us -> 0.6 us  [per_device(): lax.ppermute(held_weight, 'tensor', route(k, 0))]
    ppermute x2, starting transfers between devices: 1.81 us -> 0.6 us  [per_device(): lax.ppermute(partials, 'tensor', [(i, i ^ step) for i in range(tensor_siz...]
  transfers between devices with their start and end apart: 17 -> 17, of which waited for: 8 -> 7; matrix products, arithmetic and copies ran while one was open for 35% -> 36% of each run, Pallas kernels for 21% -> 21%
where the time goes in v18:
time: 109 us
  matrix products  37.7 us (35%)
  Pallas kernels  23.4 us (21%)
  starting transfers between devices  18 us (17%)
  waiting for transfers between devices  17.1 us (16%)
  other arithmetic  7.9 us (7%)
  local copies, waits for them, and re-layouts  3.24 us (3%)
  between operations  1.59 us (1%)
    pallas_call x1, Pallas kernels, prefill_attention_kernel(): pl.pallas_call(functools.partial(_prefill_kernel, tq=tq), out_shape=jax.S...  23.4 us
    dot_general x4, matrix products, per_device(): jnp.dot(token_block, qkv_weight, preferred_element_type=jnp.float32)  19.9 us
    dot_general x4, matrix products, per_device(): summed = summed + jnp.dot(piece, weight, preferred_element_type=jnp.float32)  8.15 us
    ppermute x3, waiting for transfers between devices, per_device(): pieces.append(lax.ppermute(outgoing, 'tensor', route(k, flip)))  7.37 us
    ppermute x3, starting transfers between devices, per_device(): lax.ppermute(shifted_rows, 'dp', [(i, i ^ step) for i in range(dp_size)])  5.82 us
    ppermute x3, starting transfers between devices, per_device(): lax.ppermute(returned, 'dp', [(i, i ^ step) for i in range(dp_size)])  5.07 us
    ppermute x3, waiting for transfers between devices, per_device(): lax.ppermute(shifted_rows, 'dp', [(i, i ^ step) for i in range(dp_size)])  4.36 us
    dot_general x1, matrix products, per_device(): jnp.dot(normed_slots, qkv_weight, preferred_element_type=jnp.float32)  3.75 us
  transfers between devices with their start and end apart: 17, of which 7 were waited for; matrix products, arithmetic and copies ran while one was open for 36% of the time, Pallas kernels for 21%

profile of v18, /device:TPU:0, one launch (start us, length us, event | category | flops | bytes accessed | tf_op | source)
XLA Modules:
  0.0 108.9 jit_solution(5586039581077123543)
XLA Ops:
  0.6 0.0 copy-start
  0.6 0.8 convert_element_type.98
  1.4 0.7 convert_element_type.97
  2.1 1.6 %convert_reduce_fusion = f32[256]{0:T(256)S(1)} fusion(bf16[256,2048]{1,0:T(8,128)(2,1)} %param.15), kind=kLoop, calls=%fused_computation.1 | loop fusion | flops 1048320 | bytes 1049600 | tf_op jit(solution)/shard_map/reduce_sum | solution.py:20
  3.7 1.6 %fusion.17 = f32[256]{0:T(256)S(1)} fusion(bf16[256,2048]{1,0:T(8,128)(2,1)} %param.15, f32[256]{0:T(256)S(1)} %broadcast_multiply_fusion), kind=kLoop, calls=%fused_computation.30 | loop fusion | flops 2096896 | bytes 1050624 | tf_op jit(solution)/shard_map/reduce_sum | solution.py:21
  5.4 1.4 %fusion.20 = bf16[256,2048]{1,0:T(8,128)(2,1)} fusion(bf16[256,2048]{1,0:T(8,128)(2,1)S(1)} %copy-done, f32[2048]{0:T(1024)S(1)} %convert_element_type.98, f32[2048]{0:T(1024)S(1)} %convert_element_type.97, f32[256]{0:T(256)S(1)} %add_rsqrt_fusion, f32[256]{0:T(256)S(1)} %broadcast_multiply_fusion), kind=kLoop, calls=%fused_computation.33 | loop fusion | flops 3145728 | bytes 2115584 | tf_op jit(solution)/shard_map/convert_element_type | solution.py:23
  6.8 2.9 %collective-permute-start = (bf16[256,2048]{1,0:T(8,128)(2,1)}, bf16[256,2048]{1,0:T(8,128)(2,1)}, u32[]{:S(2)}, u32[]{:S(2)}) collective-permute-start(bf16[256,2048]{1,0:T(8,128)(2,1)} %fusion.20), channel_id=1, source_target_pairs={{0,2},{1,3},{2,0},{3,1},{4,6},{5,7},{6,4},{7,5},{8,10},{9,11},{10,... | collective-permute-start | bytes 3145736 | tf_op jit(solution)/shard_map/ppermute | solution.py:251
  9.8 0.0 collective-permute-start.1
  9.8 1.5 %collective-permute-start.3 = (bf16[2,2048]{1,0:T(2,128)(2,1)S(1)}, bf16[2,2048]{1,0:T(2,128)(2,1)S(1)}, u32[]{:S(2)}, u32[]{:S(2)}) collective-permute-start(bf16[2,2048]{1,0:T(2,128)(2,1)S(1)} %copy-done.3), channel_id=1, source_target_pairs={{0,4},{4,0},{8,12},{12,8},{16,20},{20,16},{24,28},{28,24},{1,5},{5... | collective-permute-start | bytes 24584 | tf_op jit(solution)/shard_map/ppermute | solution.py:200
  11.3 0.2 collective-permute-start.14
  11.5 0.1 subtract_convert_fusion
  11.6 0.1 iota_compare_fusion
  11.8 1.9 %broadcast_in_dim.54 = bf16[1024,1536]{1,0:T(8,128)(2,1)} broadcast(bf16[]{:T(256)} %constant.145.clone.1), dimensions={} | broadcast | bytes 3145730 | tf_op jit(solution)/shard_map/broadcast_in_dim | solution.py:258
  13.6 5.8 %fusion.3 = bf16[1024,1536]{1,0:T(8,128)(2,1)} fusion(bf16[1024,1536]{1,0:T(8,128)(2,1)} %broadcast_in_dim.54, s32[]{:T(128)S(6)} %select_n.124, bf16[256,2048]{1,0:T(8,128)(2,1)} %fusion.20, bf16[2048,1536]{1,0:T(8,128)(2,1)} %param.19, f32[1536]{0:T(1024)S(1)} %convert_element_type.100), kind=kOutput, calls=%fused_computation.12 | convolution fusion | flops 1611399168 | bytes 8132612 | tf_op jit(solution)/shard_map/dot_general | solution.py:263
  19.5 0.2 fusion.60
  19.6 0.0 collective-permute-done.3
  19.7 1.6 %collective-permute-start.4 = (bf16[4,2048]{1,0:T(4,128)(2,1)S(1)}, bf16[4,2048]{1,0:T(4,128)(2,1)S(1)}, u32[]{:S(2)}, u32[]{:S(2)}) collective-permute-start(bf16[4,2048]{1,0:T(4,128)(2,1)S(1)} %pad_maximum_fusion.4), channel_id=1, source_target_pairs={{0,8},{4,12},{8,0},{12,4},{16,24},{20,28},{24,16},{28,20},{1,9},{5... | collective-permute-start | bytes 49160 | tf_op jit(solution)/shard_map/ppermute | solution.py:200
  21.3 2.1 %collective-permute-done.4 = bf16[4,2048]{1,0:T(4,128)(2,1)S(1)} collective-permute-done((bf16[4,2048]{1,0:T(4,128)(2,1)S(1)}, bf16[4,2048]{1,0:T(4,128)(2,1)S(1)}, u32[]{:S(2)}, u32[]{:S(2)}) %collective-permute-start.4) | collective-permute-done | bytes 16416 | tf_op jit(solution)/shard_map/ppermute | solution.py:200
  23.5 2.7 %collective-permute-start.5 = (bf16[8,2048]{1,0:T(8,128)(2,1)S(1)}, bf16[8,2048]{1,0:T(8,128)(2,1)S(1)}, u32[]{:S(2)}, u32[]{:S(2)}) collective-permute-start(bf16[8,2048]{1,0:T(8,128)(2,1)S(1)} %pad_maximum_fusion.1), channel_id=1, source_target_pairs={{0,16},{4,20},{8,24},{12,28},{16,0},{20,4},{24,8},{28,12},{1,17},{... | collective-permute-start | bytes 98312 | tf_op jit(solution)/shard_map/ppermute | solution.py:200
  26.2 2.2 %collective-permute-done.5 = bf16[8,2048]{1,0:T(8,128)(2,1)S(1)} collective-permute-done((bf16[8,2048]{1,0:T(8,128)(2,1)S(1)}, bf16[8,2048]{1,0:T(8,128)(2,1)S(1)}, u32[]{:S(2)}, u32[]{:S(2)}) %collective-permute-start.5) | collective-permute-done | bytes 32800 | tf_op jit(solution)/shard_map/ppermute | solution.py:200
  28.4 0.3 fusion.79
  28.7 0.2 multiply_reduce_fusion
  28.9 3.8 %fusion.15 = bf16[2,1536]{1,0:T(2,128)(2,1)S(1)} fusion(bf16[2048,1536]{1,0:T(8,128)(2,1)} %param.19, f32[2,2048]{1,0:T(2,128)S(1)} %get-tuple-element.33, f32[2]{0:T(128)S(1)} %add_rsqrt_fusion.1, f32[2]{0:T(128)S(1)} %broadcast_multiply_fusion.1, f32[2048]{0:T(1024)S(1)} %convert_element_type.98, f32[2048]{0:T(1024)S(1)} %convert_element_type.97, ...), kind=kOutput, calls=%fused_computation.26 | convolution fusion | flops 12609536 | bytes 6336528 | tf_op jit(solution)/shard_map/dot_general | solution.py:214
  32.8 0.1 fusion.50
  32.9 3.6 %fusion.80 = (f32[2,4]{1,0:T(2,128)S(1)}, f32[2,4,2048]{2,1,0:T(4,128)S(1)}) fusion(f32[2,2048]{1,0:T(2,128)S(1)} %subtract_convert_fusion, f32[4]{0:T(128)S(1)} %multiply_exponential_fusion.slopes_ref, bf16[2,2048,512]{2,1,0:T(8,128)(2,1)} %param.25, pred[512,4]{0,1:T(4,128)(4,1)S(1)} %iota_compare_fusion.1, bf16[2,512]{1,0:T(2,128)(2,1)S(1)} %bitcast.51, ...), kind=kOutput, calls=%fused_computation.145 | convolution fusion | flops 16863224 | bytes 4284464 | tf_op jit(solution)/shard_map/vmap()/dot_general | solution.py:148
  36.5 0.2 fusion.37
  36.7 0.1 broadcast_bitcast_fusion
  36.8 0.7 fusion.21
  37.5 0.0 copy-start.5
  37.5 0.4 fusion.55
  37.9 0.0 collective-permute-start.6
  37.9 0.5 collective-permute-start.2
  38.4 0.5 fusion.63.place_ref
  38.9 0.1 collective-permute-done.6
  39.1 0.6 collective-permute-start.7
  39.7 0.1 fusion.65
  40.5 2.6 %collective-permute-done.7 = f32[4,2048]{1,0:T(4,128)S(1)} collective-permute-done((f32[4,2048]{1,0:T(4,128)S(1)}, f32[4,2048]{1,0:T(4,128)S(1)}, u32[]{:S(2)}, u32[]{:S(2)}) %collective-permute-start.7) | collective-permute-done | bytes 32800 | tf_op jit(solution)/shard_map/ppermute | solution.py:233
  43.1 0.0 slice-start
  43.2 0.0 slice-start.1
  43.2 0.6 collective-permute-start.11
  43.8 0.0 collective-permute-done.1
  43.8 0.0 collective-permute-done.2
  43.8 0.4 collective-permute-start.8
  44.3 6.3 %fusion.5 = bf16[1024,1536]{1,0:T(8,128)(2,1)} fusion(bf16[1024,1536]{1,0:T(8,128)(2,1)} %fusion.3, s32[]{:T(128)S(6)} %select_n.126, bf16[256,2048]{1,0:T(8,128)(2,1)} %collective-permute-done, bf16[2048,1536]{1,0:T(8,128)(2,1)} %param.19, f32[1536]{0:T(1024)S(1)} %convert_element_type.100), kind=kOutput, calls=%fused_computation.14 | convolution fusion | flops 1611399168 | bytes 8132612 | tf_op jit(solution)/shard_map/dot_general | solution.py:263
  50.6 1.7 %collective-permute-start.9 = (bf16[4,2048]{1,0:T(4,128)(2,1)S(1)}, bf16[4,2048]{1,0:T(4,128)(2,1)S(1)}, u32[]{:S(2)}, u32[]{:S(2)}) collective-permute-start(bf16[4,2048]{1,0:T(4,128)(2,1)S(1)} %pad_maximum_fusion.5), channel_id=1, source_target_pairs={{0,8},{4,12},{8,0},{12,4},{16,24},{20,28},{24,16},{28,20},{1,9},{5... | collective-permute-start | bytes 49160 | tf_op jit(solution)/shard_map/ppermute | solution.py:270
  52.3 3.9 %fusion.7 = bf16[1024,1536]{1,0:T(8,128)(2,1)} fusion(bf16[1024,1536]{1,0:T(8,128)(2,1)} %fusion.5, s32[]{:T(128)S(6)} %select_n.138, bf16[256,2048]{1,0:T(8,128)(2,1)} %collective-permute-done.1, bf16[2048,1536]{1,0:T(8,128)(2,1)S(1)} %bitcast.49, f32[1536]{0:T(1024)S(1)} %convert_element_type.100), kind=kOutput, calls=%fused_computation.16 | convolution fusion | flops 1611399168 | bytes 8132612 | tf_op jit(solution)/shard_map/dot_general | solution.py:263
  56.3 0.0 collective-permute-done.9
  56.3 2.9 %collective-permute-start.10 = (bf16[8,2048]{1,0:T(8,128)(2,1)S(1)}, bf16[8,2048]{1,0:T(8,128)(2,1)S(1)}, u32[]{:S(2)}, u32[]{:S(2)}) collective-permute-start(bf16[8,2048]{1,0:T(8,128)(2,1)S(1)} %pad_maximum_fusion.3), channel_id=1, source_target_pairs={{0,16},{4,20},{8,24},{12,28},{16,0},{20,4},{24,8},{28,12},{1,17},{... | collective-permute-start | bytes 98312 | tf_op jit(solution)/shard_map/ppermute | solution.py:270
  59.2 3.9 %fusion.9.q_ref.kn_ref.vn_ref = bf16[1024,1536]{1,0:T(8,128)(2,1)} fusion(bf16[1024,1536]{1,0:T(8,128)(2,1)} %fusion.7, s32[]{:T(128)S(6)} %select_n.139, bf16[256,2048]{1,0:T(8,128)(2,1)} %collective-permute-done.2, bf16[2048,1536]{1,0:T(8,128)(2,1)S(1)} %bitcast.49, f32[1536]{0:T(1024)S(1)} %convert_element_type.100), kind=kOutput, calls=%fused_computation.18 | convolution fusion | flops 1611399168 | bytes 8132612 | tf_op jit(solution)/shard_map/dot_general | solution.py:263
  63.1 0.8 convolution_convert_fusion
  63.9 23.4 %shard_map.158 = bf16[1024,512]{1,0:T(8,128)(2,1)} custom-call(s32[1]{0:T(128)S(6)} %copy.39.prefix_ref, f32[4]{0:T(128)} %copy-done.7, s32[4]{0:T(128)} %fusion.63.place_ref, bf16[1024,1536]{1,0:T(8,128)(2,1)} %fusion.9.q_ref.kn_ref.vn_ref, bf16[1024,1536]{1,0:T(8,128)(2,1)} %fusion.9.q_ref.kn_ref.vn_ref, bf16[1024,1536]{1,0:T(8,128)(2,1)} %fusion.9.q_ref.kn_ref.vn_ref, ...), custom_call_target="tpu_custom_call" | custom-call | flops 4294967296 | bytes 6291456 | tf_op jit(solution)/shard_map/pallas_call | solution.py:117
  87.3 2.6 %collective-permute-done.11 = bf16[512,2048]{1,0:T(8,128)(2,1)} collective-permute-done((bf16[512,2048]{1,0:T(8,128)(2,1)S(1)}, bf16[512,2048]{1,0:T(8,128)(2,1)}, u32[]{:S(2)}, u32[]{:S(2)}) %collective-permute-start.11) | collective-permute-done | bytes 2097184 | tf_op jit(solution)/shard_map/ppermute | solution.py:256
  89.9 0.0 collective-permute-start.16
  89.9 1.2 %fusion.77 = (bf16[256,512]{1,0:T(8,128)(2,1)S(1)}, bf16[256,512]{1,0:T(8,128)(2,1)S(1)}, bf16[256,512]{1,0:T(8,128)(2,1)S(1)}) fusion(bf16[1024,512]{1,0:T(8,128)(2,1)} %shard_map.158), kind=kLoop, calls=%fused_computation.142 | loop fusion | bytes 1572864 | tf_op jit(solution)/shard_map/slice | solution.py:290
  91.1 0.7 collective-permute-start.15
  91.8 0.0 collective-permute-start.13
  91.8 1.5 %collective-permute-start.12 = (bf16[256,512]{1,0:T(8,128)(2,1)S(1)}, bf16[256,512]{1,0:T(8,128)(2,1)S(1)}, u32[]{:S(2)}, u32[]{:S(2)}) collective-permute-start(bf16[256,512]{1,0:T(8,128)(2,1)S(1)} %get-tuple-element.24), channel_id=1, source_target_pairs={{0,2},{1,3},{2,0},{3,1},{4,6},{5,7},{6,4},{7,5},{8,10},{9,11},{10,... | collective-permute-start | bytes 786440 | tf_op jit(solution)/shard_map/ppermute | solution.py:294
  93.3 1.7 %convolution_add_fusion.1 = f32[256,2048]{1,0:T(8,128)S(1)} fusion(bf16[512,2048]{1,0:T(8,128)(2,1)S(1)} %copy-done.1, bf16[256,2048]{1,0:T(8,128)(2,1)S(1)} %copy-done, f32[2048]{0:T(1024)S(1)} %convert_element_type.95, bf16[1024,512]{1,0:T(8,128)(2,1)} %shard_map.158), kind=kOutput, calls=%fused_computation.5 | convolution fusion | flops 538443776 | bytes 5513216 | tf_op jit(solution)/shard_map/dot_general | solution.py:297
  95.0 0.0 collective-permute-done.13
  95.0 2.3 %fusion.81 = f32[256,2048]{1,0:T(8,128)S(1)} fusion(bf16[256,512]{1,0:T(8,128)(2,1)S(1)} %collective-permute-done.13, bf16[512,2048]{1,0:T(8,128)(2,1)} %collective-permute-done.14), kind=kOutput, calls=%fused_computation.146 | convolution fusion | flops 536870912 | bytes 4456448 | tf_op jit(solution)/shard_map/dot_general | solution.py:297
  97.3 1.8 %collective-permute-done.15 = bf16[256,512]{1,0:T(8,128)(2,1)S(1)} collective-permute-done((bf16[256,512]{1,0:T(8,128)(2,1)S(1)}, bf16[256,512]{1,0:T(8,128)(2,1)S(1)}, u32[]{:S(2)}, u32[]{:S(2)}) %collective-permute-start.15) | collective-permute-done | bytes 262176 | tf_op jit(solution)/shard_map/ppermute | solution.py:294
  99.1 0.7 fusion.82
  99.8 5.5 %collective-permute-done.12 = bf16[256,512]{1,0:T(8,128)(2,1)S(1)} collective-permute-done((bf16[256,512]{1,0:T(8,128)(2,1)S(1)}, bf16[256,512]{1,0:T(8,128)(2,1)S(1)}, u32[]{:S(2)}, u32[]{:S(2)}) %collective-permute-start.12) | collective-permute-done | bytes 262176 | tf_op jit(solution)/shard_map/ppermute | solution.py:294
  105.4 3.5 %fusion.10 = bf16[256,2048]{1,0:T(8,128)(2,1)} fusion(f32[256,2048]{1,0:T(8,128)S(1)} %fusion.82, f32[256,2048]{1,0:T(8,128)S(1)} %fusion.81, f32[256,2048]{1,0:T(8,128)S(1)} %convolution_add_fusion.1, bf16[256,512]{1,0:T(8,128)(2,1)S(1)} %collective-permute-done.12, bf16[512,2048]{1,0:T(8,128)(2,1)} %collective-permute-done.11), kind=kOutput, calls=%fused_computation.19 | convolution fusion | flops 538968064 | bytes 9699328 | tf_op jit(solution)/shard_map/dot_general | solution.py:297
  (50 shorter events, 0.5 us)
Async XLA Ops:
  0.6 4.8 %copy-start = (bf16[256,2048]{1,0:T(8,128)(2,1)S(1)}, bf16[256,2048]{1,0:T(8,128)(2,1)}, u32[]{:S(2)}) copy-start(bf16[256,2048]{1,0:T(8,128)(2,1)} %param.15) | copy-start | bytes 3145732
  2.1 7.7 %copy-start.3 = (bf16[2,2048]{1,0:T(2,128)(2,1)S(1)}, bf16[2,2048]{1,0:T(2,128)(2,1)}, u32[]{:S(2)}) copy-start(bf16[2,2048]{1,0:T(2,128)(2,1)} %param.16) | copy-start | bytes 24580
  2.1 9.2 %copy-start.1 = (bf16[512,2048]{1,0:T(8,128)(2,1)S(1)}, bf16[512,2048]{1,0:T(8,128)(2,1)}, u32[]{:S(2)}) copy-start(bf16[512,2048]{1,0:T(8,128)(2,1)} %param.21) | copy-start | bytes 6291460
  2.1 9.4 %copy-start.6 = (s32[2]{0:T(128)S(1)}, s32[2]{0:T(128)}, u32[]{:S(2)}) copy-start(s32[2]{0:T(128)} %param.28) | copy-start | bytes 28
  2.1 9.6 %copy-start.4 = (bf16[1536]{0:T(1024)(128)(2,1)S(1)}, bf16[1536]{0:T(1024)(128)(2,1)}, u32[]{:S(2)}) copy-start(bf16[1536]{0:T(1024)(128)(2,1)} %param.20) | copy-start | bytes 9220
  6.8 31.1 %collective-permute-start = (bf16[256,2048]{1,0:T(8,128)(2,1)}, bf16[256,2048]{1,0:T(8,128)(2,1)}, u32[]{:S(2)}, u32[]{:S(2)}) collective-permute-start(bf16[256,2048]{1,0:T(8,128)(2,1)} %fusion.20), channel_id=1, source_target_pairs={{0,2},{1,3},{2,0},{3,1},{4,6},{5,7},{6,4},{7,5},{8,10},{9,11},{10,... | collective-permute-start | bytes 3145736 | tf_op jit(solution)/shard_map/ppermute | solution.py:251
  9.8 34.1 %collective-permute-start.1 = (bf16[256,2048]{1,0:T(8,128)(2,1)}, bf16[256,2048]{1,0:T(8,128)(2,1)}, u32[]{:S(2)}, u32[]{:S(2)}) collective-permute-start(bf16[256,2048]{1,0:T(8,128)(2,1)} %fusion.20), channel_id=1, source_target_pairs={{0,1},{1,0},{2,3},{3,2},{4,5},{5,4},{6,7},{7,6},{8,9},{9,8},{10,11... | collective-permute-start | bytes 3145736 | tf_op jit(solution)/shard_map/ppermute | solution.py:254
  9.8 9.9 %collective-permute-start.3 = (bf16[2,2048]{1,0:T(2,128)(2,1)S(1)}, bf16[2,2048]{1,0:T(2,128)(2,1)S(1)}, u32[]{:S(2)}, u32[]{:S(2)}) collective-permute-start(bf16[2,2048]{1,0:T(2,128)(2,1)S(1)} %copy-done.3), channel_id=1, source_target_pairs={{0,4},{4,0},{8,12},{12,8},{16,20},{20,16},{24,28},{28,24},{1,5},{5... | collective-permute-start | bytes 24584 | tf_op jit(solution)/shard_map/ppermute | solution.py:200
  11.3 83.7 %collective-permute-start.14 = (bf16[512,2048]{1,0:T(8,128)(2,1)S(1)}, bf16[512,2048]{1,0:T(8,128)(2,1)}, u32[]{:S(2)}, u32[]{:S(2)}) collective-permute-start(bf16[512,2048]{1,0:T(8,128)(2,1)S(1)} %copy-done.1), channel_id=1, source_target_pairs={{0,1},{1,0},{2,3},{3,2},{4,5},{5,4},{6,7},{7,6},{8,9},{9,8},{10,11... | collective-permute-start | bytes 6291464 | tf_op jit(solution)/shard_map/ppermute | solution.py:285
  13.6 5.8 %copy-start.8 = (s32[16]{0:T(128)S(1)}, s32[16]{0:T(128)}, u32[]{:S(2)}) copy-start(s32[16]{0:T(128)} %param.29) | copy-start | bytes 196
  19.7 3.8 %collective-permute-start.4 = (bf16[4,2048]{1,0:T(4,128)(2,1)S(1)}, bf16[4,2048]{1,0:T(4,128)(2,1)S(1)}, u32[]{:S(2)}, u32[]{:S(2)}) collective-permute-start(bf16[4,2048]{1,0:T(4,128)(2,1)S(1)} %pad_maximum_fusion.4), channel_id=1, source_target_pairs={{0,8},{4,12},{8,0},{12,4},{16,24},{20,28},{24,16},{28,20},{1,9},{5... | collective-permute-start | bytes 49160 | tf_op jit(solution)/shard_map/ppermute | solution.py:200
  23.5 4.9 %collective-permute-start.5 = (bf16[8,2048]{1,0:T(8,128)(2,1)S(1)}, bf16[8,2048]{1,0:T(8,128)(2,1)S(1)}, u32[]{:S(2)}, u32[]{:S(2)}) collective-permute-start(bf16[8,2048]{1,0:T(8,128)(2,1)S(1)} %pad_maximum_fusion.1), channel_id=1, source_target_pairs={{0,16},{4,20},{8,24},{12,28},{16,0},{20,4},{24,8},{28,12},{1,17},{... | collective-permute-start | bytes 98312 | tf_op jit(solution)/shard_map/ppermute | solution.py:200
  26.2 6.7 %copy-start.7 = (f32[4]{0:T(128)}, f32[4]{0:T(128)S(1)}, u32[]{:S(2)}) copy-start(f32[4]{0:T(128)S(1)} %multiply_exponential_fusion.slopes_ref) | copy-start | bytes 52
  32.8 3.9 %copy-start.2 = (bf16[2,2048,512]{2,1,0:T(8,128)(2,1)S(1)}, bf16[2,2048,512]{2,1,0:T(8,128)(2,1)}, u32[]{:S(2)}) copy-start(bf16[2,2048,512]{2,1,0:T(8,128)(2,1)} %param.26) | copy-start | bytes 12582916
  37.5 3.0 %copy-start.5 = (bf16[2048]{0:T(1024)(128)(2,1)S(1)}, bf16[2048]{0:T(1024)(128)(2,1)}, u32[]{:S(2)}) copy-start(bf16[2048]{0:T(1024)(128)(2,1)} %param.22) | copy-start | bytes 12292
  37.9 1.2 %collective-permute-start.6 = (f32[2,2048]{1,0:T(2,128)S(1)}, f32[2,2048]{1,0:T(2,128)S(1)}, u32[]{:S(2)}, u32[]{:S(2)}) collective-permute-start(f32[2,2048]{1,0:T(2,128)S(1)} %fusion.55), channel_id=1, source_target_pairs={{0,1},{1,0},{2,3},{3,2},{4,5},{5,4},{6,7},{7,6},{8,9},{9,8},{10,11... | collective-permute-start | bytes 49160 | tf_op jit(solution)/shard_map/ppermute | solution.py:233
  37.9 5.9 %collective-permute-start.2 = (bf16[256,2048]{1,0:T(8,128)(2,1)}, bf16[256,2048]{1,0:T(8,128)(2,1)}, u32[]{:S(2)}, u32[]{:S(2)}) collective-permute-start(bf16[256,2048]{1,0:T(8,128)(2,1)} %collective-permute-done), channel_id=1, source_target_pairs={{0,1},{1,0},{2,3},{3,2},{4,5},{5,4},{6,7},{7,6},{8,9},{9,8},{10,11... | collective-permute-start | bytes 3145736 | tf_op jit(solution)/shard_map/ppermute | solution.py:254
  39.1 4.0 %collective-permute-start.7 = (f32[4,2048]{1,0:T(4,128)S(1)}, f32[4,2048]{1,0:T(4,128)S(1)}, u32[]{:S(2)}, u32[]{:S(2)}) collective-permute-start(f32[4,2048]{1,0:T(4,128)S(1)} %pad_maximum_fusion.2), channel_id=1, source_target_pairs={{0,2},{1,3},{2,0},{3,1},{4,6},{5,7},{6,4},{7,5},{8,10},{9,11},{10,... | collective-permute-start | bytes 98312 | tf_op jit(solution)/shard_map/ppermute | solution.py:233
  43.1 9.2 %slice-start = ((s8[6291456]{0:T(1024)(128)(4,1)}), s8[4194304]{0:T(1024)(128)(4,1)S(1)}, s32[]{:S(2)}) async-start(s8[6291456]{0:T(1024)(128)(4,1)} %bitcast.48), calls=%async_computation | async-start | bytes 8388608
  43.2 9.1 %slice-start.1 = ((s8[6291456]{0:T(1024)(128)(4,1)}), s8[2097152]{0:T(1024)(128)(4,1)S(1)}, s32[]{:S(2)}) async-start(s8[6291456]{0:T(1024)(128)(4,1)} %bitcast.48), calls=%async_computation.1 | async-start | bytes 4194304
  43.2 46.7 %collective-permute-start.11 = (bf16[512,2048]{1,0:T(8,128)(2,1)S(1)}, bf16[512,2048]{1,0:T(8,128)(2,1)}, u32[]{:S(2)}, u32[]{:S(2)}) collective-permute-start(bf16[512,2048]{1,0:T(8,128)(2,1)S(1)} %copy-done.1), channel_id=1, source_target_pairs={{0,2},{1,3},{2,0},{3,1},{4,6},{5,7},{6,4},{7,5},{8,10},{9,11},{10,... | collective-permute-start | bytes 6291464 | tf_op jit(solution)/shard_map/ppermute | solution.py:256
  43.8 6.7 %collective-permute-start.8 = (bf16[2,2048]{1,0:T(2,128)(2,1)S(1)}, bf16[2,2048]{1,0:T(2,128)(2,1)S(1)}, u32[]{:S(2)}, u32[]{:S(2)}) collective-permute-start(bf16[2,2048]{1,0:T(2,128)(2,1)S(1)} %fusion.41), channel_id=1, source_target_pairs={{0,4},{4,0},{8,12},{12,8},{16,20},{20,16},{24,28},{28,24},{1,5},{5... | collective-permute-start | bytes 24584 | tf_op jit(solution)/shard_map/ppermute | solution.py:270
  50.6 5.7 %collective-permute-start.9 = (bf16[4,2048]{1,0:T(4,128)(2,1)S(1)}, bf16[4,2048]{1,0:T(4,128)(2,1)S(1)}, u32[]{:S(2)}, u32[]{:S(2)}) collective-permute-start(bf16[4,2048]{1,0:T(4,128)(2,1)S(1)} %pad_maximum_fusion.5), channel_id=1, source_target_pairs={{0,8},{4,12},{8,0},{12,4},{16,24},{20,28},{24,16},{28,20},{1,9},{5... | collective-permute-start | bytes 49160 | tf_op jit(solution)/shard_map/ppermute | solution.py:270
  56.3 6.8 %collective-permute-start.10 = (bf16[8,2048]{1,0:T(8,128)(2,1)S(1)}, bf16[8,2048]{1,0:T(8,128)(2,1)S(1)}, u32[]{:S(2)}, u32[]{:S(2)}) collective-permute-start(bf16[8,2048]{1,0:T(8,128)(2,1)S(1)} %pad_maximum_fusion.3), channel_id=1, source_target_pairs={{0,16},{4,20},{8,24},{12,28},{16,0},{20,4},{24,8},{28,12},{1,17},{... | collective-permute-start | bytes 98312 | tf_op jit(solution)/shard_map/ppermute | solution.py:270
  89.9 9.2 %collective-permute-start.16 = (bf16[512,2048]{1,0:T(8,128)(2,1)}, bf16[512,2048]{1,0:T(8,128)(2,1)S(1)}, u32[]{:S(2)}, u32[]{:S(2)}) collective-permute-start(bf16[512,2048]{1,0:T(8,128)(2,1)} %collective-permute-done.11), channel_id=1, source_target_pairs={{0,1},{1,0},{2,3},{3,2},{4,5},{5,4},{6,7},{7,6},{8,9},{9,8},{10,11... | collective-permute-start | bytes 6291464 | tf_op jit(solution)/shard_map/ppermute | solution.py:285
  91.1 8.0 %collective-permute-start.15 = (bf16[256,512]{1,0:T(8,128)(2,1)S(1)}, bf16[256,512]{1,0:T(8,128)(2,1)S(1)}, u32[]{:S(2)}, u32[]{:S(2)}) collective-permute-start(bf16[256,512]{1,0:T(8,128)(2,1)S(1)} %get-tuple-element.25), channel_id=1, source_target_pairs={{0,3},{1,2},{2,1},{3,0},{4,7},{5,6},{6,5},{7,4},{8,11},{9,10},{10,... | collective-permute-start | bytes 786440 | tf_op jit(solution)/shard_map/ppermute | solution.py:294
  91.8 3.2 %collective-permute-start.13 = (bf16[256,512]{1,0:T(8,128)(2,1)S(1)}, bf16[256,512]{1,0:T(8,128)(2,1)S(1)}, u32[]{:S(2)}, u32[]{:S(2)}) collective-permute-start(bf16[256,512]{1,0:T(8,128)(2,1)S(1)} %get-tuple-element.26), channel_id=1, source_target_pairs={{0,1},{1,0},{2,3},{3,2},{4,5},{5,4},{6,7},{7,6},{8,9},{9,8},{10,11... | collective-permute-start | bytes 786440 | tf_op jit(solution)/shard_map/ppermute | solution.py:294
  91.8 13.6 %collective-permute-start.12 = (bf16[256,512]{1,0:T(8,128)(2,1)S(1)}, bf16[256,512]{1,0:T(8,128)(2,1)S(1)}, u32[]{:S(2)}, u32[]{:S(2)}) collective-permute-start(bf16[256,512]{1,0:T(8,128)(2,1)S(1)} %get-tuple-element.24), channel_id=1, source_target_pairs={{0,2},{1,3},{2,0},{3,1},{4,6},{5,7},{6,4},{7,5},{8,10},{9,11},{10,... | collective-permute-start | bytes 786440 | tf_op jit(solution)/shard_map/ppermute | solution.py:294

commit v19 on v18

--- a/solution.py
+++ b/solution.py
@@ -293,8 +293,9 @@
                 continue
             pieces.append(lax.ppermute(outgoing, "tensor", route(k, flip)))
     summed = pre_hidden.astype(jnp.float32) + bias_sum
-    for piece, weight in zip(pieces, weight_blocks):
-        summed = summed + jnp.dot(piece, weight, preferred_element_type=jnp.float32)
+    by_arrival = sorted(range(len(pieces)), key=lambda n: (n % chips != 0, n))
+    for n in by_arrival:
+        summed = summed + jnp.dot(pieces[n], weight_blocks[n], preferred_element_type=jnp.float32)
     pre_output = summed.astype(jnp.bfloat16)
     return (pre_output, dec_output)
 

time: 109 us -> 112 us (1.028)
  waiting for transfers between devices: 17.1 us -> 20.5 us
  matrix products: 37.7 us -> 35.9 us
    ppermute x3, waiting for transfers between devices: 7.37 us -> 10.7 us  [per_device(): pieces.append(lax.ppermute(outgoing, 'tensor', route(k, flip)))]
    dot_general x4, matrix products: 8.15 us -> 6.43 us  [per_device(): jnp.dot(pieces[n], weight_blocks[n], preferred_element_type=jnp.float32)]
  transfers between devices with their start and end apart: 17 -> 17, of which waited for: 7 -> 6; matrix products, arithmetic and copies ran while one was open for 36% -> 35% of each run, Pallas kernels for 21% -> 21%
where the time goes in v19:
time: 112 us; the launch traced here: 111 us
  matrix products  35.9 us (32%)
  Pallas kernels  23.4 us (21%)
  waiting for transfers between devices  20.5 us (18%)
  starting transfers between devices  18 us (16%)
  other arithmetic  7.73 us (7%)
  local copies, waits for them, and re-layouts  4.1 us (4%)
  between operations  1.61 us (1%)
    pallas_call x1, Pallas kernels, prefill_attention_kernel(): pl.pallas_call(functools.partial(_prefill_kernel, tq=tq), out_shape=jax.S...  23.4 us
    dot_general x4, matrix products, per_device(): jnp.dot(token_block, qkv_weight, preferred_element_type=jnp.float32)  19.9 us
    ppermute x3, waiting for transfers between devices, per_device(): pieces.append(lax.ppermute(outgoing, 'tensor', route(k, flip)))  10.7 us
    dot_general x4, matrix products, per_device(): jnp.dot(pieces[n], weight_blocks[n], preferred_element_type=jnp.float32)  6.43 us
    ppermute x3, starting transfers between devices, per_device(): lax.ppermute(shifted_rows, 'dp', [(i, i ^ step) for i in range(dp_size)])  5.82 us
    ppermute x3, starting transfers between devices, per_device(): lax.ppermute(returned, 'dp', [(i, i ^ step) for i in range(dp_size)])  5.1 us
    ppermute x3, waiting for transfers between devices, per_device(): lax.ppermute(shifted_rows, 'dp', [(i, i ^ step) for i in range(dp_size)])  4.36 us
    dot_general x1, matrix products, per_device(): jnp.dot(normed_slots, qkv_weight, preferred_element_type=jnp.float32)  3.75 us
  transfers between devices with their start and end apart: 17, of which 6 were waited for; matrix products, arithmetic and copies ran while one was open for 35% of the time, Pallas kernels for 21%

profile of v19, /device:TPU:0, one launch (start us, length us, event | category | flops | bytes accessed | tf_op | source)
XLA Modules:
  0.0 111.2 jit_solution(10665976273990132010)
XLA Ops:
  0.6 0.0 copy-start
  0.6 0.8 convert_element_type.98
  1.4 0.7 convert_element_type.97
  2.1 1.5 %convert_reduce_fusion = f32[256]{0:T(256)S(1)} fusion(bf16[256,2048]{1,0:T(8,128)(2,1)} %param.15), kind=kLoop, calls=%fused_computation.1 | loop fusion | flops 1048320 | bytes 1049600 | tf_op jit(solution)/shard_map/reduce_sum | solution.py:20
  3.6 1.6 %fusion.17 = f32[256]{0:T(256)S(1)} fusion(bf16[256,2048]{1,0:T(8,128)(2,1)} %param.15, f32[256]{0:T(256)S(1)} %broadcast_multiply_fusion), kind=kLoop, calls=%fused_computation.30 | loop fusion | flops 2096896 | bytes 1050624 | tf_op jit(solution)/shard_map/reduce_sum | solution.py:21
  5.3 1.4 %fusion.20 = bf16[256,2048]{1,0:T(8,128)(2,1)} fusion(bf16[256,2048]{1,0:T(8,128)(2,1)S(1)} %copy-done, f32[2048]{0:T(1024)S(1)} %convert_element_type.98, f32[2048]{0:T(1024)S(1)} %convert_element_type.97, f32[256]{0:T(256)S(1)} %add_rsqrt_fusion, f32[256]{0:T(256)S(1)} %broadcast_multiply_fusion), kind=kLoop, calls=%fused_computation.33 | loop fusion | flops 3145728 | bytes 2115584 | tf_op jit(solution)/shard_map/convert_element_type | solution.py:23
  6.7 2.9 %collective-permute-start = (bf16[256,2048]{1,0:T(8,128)(2,1)}, bf16[256,2048]{1,0:T(8,128)(2,1)}, u32[]{:S(2)}, u32[]{:S(2)}) collective-permute-start(bf16[256,2048]{1,0:T(8,128)(2,1)} %fusion.20), channel_id=1, source_target_pairs={{0,2},{1,3},{2,0},{3,1},{4,6},{5,7},{6,4},{7,5},{8,10},{9,11},{10,... | collective-permute-start | bytes 3145736 | tf_op jit(solution)/shard_map/ppermute | solution.py:251
  9.6 0.0 collective-permute-start.1
  9.6 1.5 %collective-permute-start.3 = (bf16[2,2048]{1,0:T(2,128)(2,1)S(1)}, bf16[2,2048]{1,0:T(2,128)(2,1)S(1)}, u32[]{:S(2)}, u32[]{:S(2)}) collective-permute-start(bf16[2,2048]{1,0:T(2,128)(2,1)S(1)} %copy-done.3), channel_id=1, source_target_pairs={{0,4},{4,0},{8,12},{12,8},{16,20},{20,16},{24,28},{28,24},{1,5},{5... | collective-permute-start | bytes 24584 | tf_op jit(solution)/shard_map/ppermute | solution.py:200
  11.2 0.1 subtract_convert_fusion
  11.2 0.1 iota_compare_fusion
  11.4 1.9 %broadcast_in_dim.54 = bf16[1024,1536]{1,0:T(8,128)(2,1)} broadcast(bf16[]{:T(256)} %constant.145.clone.1), dimensions={} | broadcast | bytes 3145730 | tf_op jit(solution)/shard_map/broadcast_in_dim | solution.py:258
  13.3 5.8 %fusion.3 = bf16[1024,1536]{1,0:T(8,128)(2,1)} fusion(bf16[1024,1536]{1,0:T(8,128)(2,1)} %broadcast_in_dim.54, s32[]{:T(128)S(6)} %select_n.124, bf16[256,2048]{1,0:T(8,128)(2,1)} %fusion.20, bf16[2048,1536]{1,0:T(8,128)(2,1)} %param.19, f32[1536]{0:T(1024)S(1)} %convert_element_type.100), kind=kOutput, calls=%fused_computation.12 | convolution fusion | flops 1611399168 | bytes 8132612 | tf_op jit(solution)/shard_map/dot_general | solution.py:263
  19.1 0.2 fusion.60
  19.3 0.0 collective-permute-done.3
  19.3 1.6 %collective-permute-start.4 = (bf16[4,2048]{1,0:T(4,128)(2,1)S(1)}, bf16[4,2048]{1,0:T(4,128)(2,1)S(1)}, u32[]{:S(2)}, u32[]{:S(2)}) collective-permute-start(bf16[4,2048]{1,0:T(4,128)(2,1)S(1)} %pad_maximum_fusion.4), channel_id=1, source_target_pairs={{0,8},{4,12},{8,0},{12,4},{16,24},{20,28},{24,16},{28,20},{1,9},{5... | collective-permute-start | bytes 49160 | tf_op jit(solution)/shard_map/ppermute | solution.py:200
  21.0 2.1 %collective-permute-done.4 = bf16[4,2048]{1,0:T(4,128)(2,1)S(1)} collective-permute-done((bf16[4,2048]{1,0:T(4,128)(2,1)S(1)}, bf16[4,2048]{1,0:T(4,128)(2,1)S(1)}, u32[]{:S(2)}, u32[]{:S(2)}) %collective-permute-start.4) | collective-permute-done | bytes 16416 | tf_op jit(solution)/shard_map/ppermute | solution.py:200
  23.2 2.7 %collective-permute-start.5 = (bf16[8,2048]{1,0:T(8,128)(2,1)S(1)}, bf16[8,2048]{1,0:T(8,128)(2,1)S(1)}, u32[]{:S(2)}, u32[]{:S(2)}) collective-permute-start(bf16[8,2048]{1,0:T(8,128)(2,1)S(1)} %pad_maximum_fusion.1), channel_id=1, source_target_pairs={{0,16},{4,20},{8,24},{12,28},{16,0},{20,4},{24,8},{28,12},{1,17},{... | collective-permute-start | bytes 98312 | tf_op jit(solution)/shard_map/ppermute | solution.py:200
  25.8 2.2 %collective-permute-done.5 = bf16[8,2048]{1,0:T(8,128)(2,1)S(1)} collective-permute-done((bf16[8,2048]{1,0:T(8,128)(2,1)S(1)}, bf16[8,2048]{1,0:T(8,128)(2,1)S(1)}, u32[]{:S(2)}, u32[]{:S(2)}) %collective-permute-start.5) | collective-permute-done | bytes 32800 | tf_op jit(solution)/shard_map/ppermute | solution.py:200
  28.0 0.3 fusion.79
  28.4 0.2 multiply_reduce_fusion
  28.6 3.8 %fusion.15 = bf16[2,1536]{1,0:T(2,128)(2,1)S(1)} fusion(bf16[2048,1536]{1,0:T(8,128)(2,1)} %param.19, f32[2,2048]{1,0:T(2,128)S(1)} %get-tuple-element.33, f32[2]{0:T(128)S(1)} %add_rsqrt_fusion.1, f32[2]{0:T(128)S(1)} %broadcast_multiply_fusion.1, f32[2048]{0:T(1024)S(1)} %convert_element_type.98, f32[2048]{0:T(1024)S(1)} %convert_element_type.97, ...), kind=kOutput, calls=%fused_computation.26 | convolution fusion | flops 12609536 | bytes 6336528 | tf_op jit(solution)/shard_map/dot_general | solution.py:214
  32.4 0.1 fusion.50
  32.5 3.6 %fusion.80 = (f32[2,4]{1,0:T(2,128)S(1)}, f32[2,4,2048]{2,1,0:T(4,128)S(1)}) fusion(f32[2,2048]{1,0:T(2,128)S(1)} %subtract_convert_fusion, f32[4]{0:T(128)S(1)} %multiply_exponential_fusion.slopes_ref, bf16[2,2048,512]{2,1,0:T(8,128)(2,1)} %param.25, pred[512,4]{0,1:T(4,128)(4,1)S(1)} %iota_compare_fusion.1, bf16[2,512]{1,0:T(2,128)(2,1)S(1)} %bitcast.51, ...), kind=kOutput, calls=%fused_computation.145 | convolution fusion | flops 16863224 | bytes 4284464 | tf_op jit(solution)/shard_map/vmap()/dot_general | solution.py:148
  36.1 0.2 fusion.37
  36.3 0.1 broadcast_bitcast_fusion
  36.4 0.7 fusion.21
  37.1 0.0 copy-start.5
  37.1 0.9 copy-done.1
  38.0 0.4 fusion.55
  38.4 0.0 collective-permute-start.6
  38.4 0.5 collective-permute-start.2
  38.9 0.5 fusion.63.place_ref
  39.4 0.2 collective-permute-done.6
  39.6 0.6 collective-permute-start.7
  40.2 0.1 fusion.65
  41.0 2.6 %collective-permute-done.7 = f32[4,2048]{1,0:T(4,128)S(1)} collective-permute-done((f32[4,2048]{1,0:T(4,128)S(1)}, f32[4,2048]{1,0:T(4,128)S(1)}, u32[]{:S(2)}, u32[]{:S(2)}) %collective-permute-start.7) | collective-permute-done | bytes 32800 | tf_op jit(solution)/shard_map/ppermute | solution.py:233
  43.7 0.0 slice-start
  43.7 0.0 slice-start.1
  43.7 0.6 collective-permute-start.11
  44.3 0.0 collective-permute-done.1
  44.3 0.4 collective-permute-start.8
  44.7 6.3 %fusion.5 = bf16[1024,1536]{1,0:T(8,128)(2,1)} fusion(bf16[1024,1536]{1,0:T(8,128)(2,1)} %fusion.3, s32[]{:T(128)S(6)} %select_n.126, bf16[256,2048]{1,0:T(8,128)(2,1)} %collective-permute-done, bf16[2048,1536]{1,0:T(8,128)(2,1)} %param.19, f32[1536]{0:T(1024)S(1)} %convert_element_type.100), kind=kOutput, calls=%fused_computation.14 | convolution fusion | flops 1611399168 | bytes 8132612 | tf_op jit(solution)/shard_map/dot_general | solution.py:263
  51.0 1.8 %collective-permute-start.9 = (bf16[4,2048]{1,0:T(4,128)(2,1)S(1)}, bf16[4,2048]{1,0:T(4,128)(2,1)S(1)}, u32[]{:S(2)}, u32[]{:S(2)}) collective-permute-start(bf16[4,2048]{1,0:T(4,128)(2,1)S(1)} %pad_maximum_fusion.5), channel_id=1, source_target_pairs={{0,8},{4,12},{8,0},{12,4},{16,24},{20,28},{24,16},{28,20},{1,9},{5... | collective-permute-start | bytes 49160 | tf_op jit(solution)/shard_map/ppermute | solution.py:270
  52.9 3.9 %fusion.7 = bf16[1024,1536]{1,0:T(8,128)(2,1)} fusion(bf16[1024,1536]{1,0:T(8,128)(2,1)} %fusion.5, s32[]{:T(128)S(6)} %select_n.138, bf16[256,2048]{1,0:T(8,128)(2,1)} %collective-permute-done.1, bf16[2048,1536]{1,0:T(8,128)(2,1)S(1)} %bitcast.49, f32[1536]{0:T(1024)S(1)} %convert_element_type.100), kind=kOutput, calls=%fused_computation.16 | convolution fusion | flops 1611399168 | bytes 8132612 | tf_op jit(solution)/shard_map/dot_general | solution.py:263
  56.8 2.9 %collective-permute-start.10 = (bf16[8,2048]{1,0:T(8,128)(2,1)S(1)}, bf16[8,2048]{1,0:T(8,128)(2,1)S(1)}, u32[]{:S(2)}, u32[]{:S(2)}) collective-permute-start(bf16[8,2048]{1,0:T(8,128)(2,1)S(1)} %pad_maximum_fusion.3), channel_id=1, source_target_pairs={{0,16},{4,20},{8,24},{12,28},{16,0},{20,4},{24,8},{28,12},{1,17},{... | collective-permute-start | bytes 98312 | tf_op jit(solution)/shard_map/ppermute | solution.py:270
  59.7 3.9 %fusion.9.q_ref.kn_ref.vn_ref = bf16[1024,1536]{1,0:T(8,128)(2,1)} fusion(bf16[1024,1536]{1,0:T(8,128)(2,1)} %fusion.7, s32[]{:T(128)S(6)} %select_n.139, bf16[256,2048]{1,0:T(8,128)(2,1)} %collective-permute-done.2, bf16[2048,1536]{1,0:T(8,128)(2,1)S(1)} %bitcast.49, f32[1536]{0:T(1024)S(1)} %convert_element_type.100), kind=kOutput, calls=%fused_computation.18 | convolution fusion | flops 1611399168 | bytes 8132612 | tf_op jit(solution)/shard_map/dot_general | solution.py:263
  63.6 0.0 collective-permute-done.10
  63.6 0.8 convolution_convert_fusion
  64.4 23.4 %shard_map.158 = bf16[1024,512]{1,0:T(8,128)(2,1)} custom-call(s32[1]{0:T(128)S(6)} %copy.39.prefix_ref, f32[4]{0:T(128)} %copy-done.7, s32[4]{0:T(128)} %fusion.63.place_ref, bf16[1024,1536]{1,0:T(8,128)(2,1)} %fusion.9.q_ref.kn_ref.vn_ref, bf16[1024,1536]{1,0:T(8,128)(2,1)} %fusion.9.q_ref.kn_ref.vn_ref, bf16[1024,1536]{1,0:T(8,128)(2,1)} %fusion.9.q_ref.kn_ref.vn_ref, ...), custom_call_target="tpu_custom_call" | custom-call | flops 4294967296 | bytes 6291456 | tf_op jit(solution)/shard_map/pallas_call | solution.py:117
  87.8 2.6 %collective-permute-done.11 = bf16[512,2048]{1,0:T(8,128)(2,1)} collective-permute-done((bf16[512,2048]{1,0:T(8,128)(2,1)S(1)}, bf16[512,2048]{1,0:T(8,128)(2,1)}, u32[]{:S(2)}, u32[]{:S(2)}) %collective-permute-start.11) | collective-permute-done | bytes 2097184 | tf_op jit(solution)/shard_map/ppermute | solution.py:256
  90.5 0.0 collective-permute-start.16
  90.5 0.5 collective-permute-start.13
  91.0 1.2 %fusion.77 = (bf16[256,512]{1,0:T(8,128)(2,1)S(1)}, bf16[256,512]{1,0:T(8,128)(2,1)S(1)}, bf16[256,512]{1,0:T(8,128)(2,1)S(1)}) fusion(bf16[1024,512]{1,0:T(8,128)(2,1)} %shard_map.158), kind=kLoop, calls=%fused_computation.142 | loop fusion | bytes 1572864 | tf_op jit(solution)/shard_map/slice | solution.py:290
  92.1 0.2 collective-permute-start.15
  92.3 1.5 %collective-permute-start.14 = (bf16[256,512]{1,0:T(8,128)(2,1)S(1)}, bf16[256,512]{1,0:T(8,128)(2,1)S(1)}, u32[]{:S(2)}, u32[]{:S(2)}) collective-permute-start(bf16[256,512]{1,0:T(8,128)(2,1)S(1)} %get-tuple-element.26), channel_id=1, source_target_pairs={{0,2},{1,3},{2,0},{3,1},{4,6},{5,7},{6,4},{7,5},{8,10},{9,11},{10,... | collective-permute-start | bytes 786440 | tf_op jit(solution)/shard_map/ppermute | solution.py:294
  93.8 0.2 collective-permute-start.12
  94.1 1.7 %convolution_add_fusion.1 = f32[256,2048]{1,0:T(8,128)S(1)} fusion(bf16[512,2048]{1,0:T(8,128)(2,1)S(1)} %copy-done.1, bf16[256,2048]{1,0:T(8,128)(2,1)S(1)} %copy-done, f32[2048]{0:T(1024)S(1)} %convert_element_type.95, bf16[1024,512]{1,0:T(8,128)(2,1)} %shard_map.158), kind=kOutput, calls=%fused_computation.5 | convolution fusion | flops 538443776 | bytes 5513216 | tf_op jit(solution)/shard_map/dot_general | solution.py:298
  95.7 10.7 %collective-permute-done.14 = bf16[256,512]{1,0:T(8,128)(2,1)S(1)} collective-permute-done((bf16[256,512]{1,0:T(8,128)(2,1)S(1)}, bf16[256,512]{1,0:T(8,128)(2,1)S(1)}, u32[]{:S(2)}, u32[]{:S(2)}) %collective-permute-start.14) | collective-permute-done | bytes 262176 | tf_op jit(solution)/shard_map/ppermute | solution.py:294
  106.4 2.3 %fusion.81 = f32[256,2048]{1,0:T(8,128)S(1)} fusion(bf16[256,512]{1,0:T(8,128)(2,1)S(1)} %collective-permute-done.14, bf16[512,2048]{1,0:T(8,128)(2,1)} %collective-permute-done.11), kind=kOutput, calls=%fused_computation.146 | convolution fusion | flops 536870912 | bytes 4456448 | tf_op jit(solution)/shard_map/dot_general | solution.py:298
  108.7 0.0 collective-permute-done.15
  108.7 0.7 fusion.82
  109.5 0.0 collective-permute-done.12
  109.5 1.8 %fusion.10 = bf16[256,2048]{1,0:T(8,128)(2,1)} fusion(f32[256,2048]{1,0:T(8,128)S(1)} %fusion.82, f32[256,2048]{1,0:T(8,128)S(1)} %fusion.81, f32[256,2048]{1,0:T(8,128)S(1)} %convolution_add_fusion.1, bf16[256,512]{1,0:T(8,128)(2,1)S(1)} %collective-permute-done.12, bf16[512,2048]{1,0:T(8,128)(2,1)S(1)} %collective-permute-done.13), kind=kOutput, calls=%fused_computation.19 | convolution fusion | flops 538968064 | bytes 9699328 | tf_op jit(solution)/shard_map/dot_general | solution.py:298
  (50 shorter events, 0.5 us)
Async XLA Ops:
  0.6 4.6 %copy-start = (bf16[256,2048]{1,0:T(8,128)(2,1)S(1)}, bf16[256,2048]{1,0:T(8,128)(2,1)}, u32[]{:S(2)}) copy-start(bf16[256,2048]{1,0:T(8,128)(2,1)} %param.15) | copy-start | bytes 3145732
  2.1 7.5 %copy-start.3 = (bf16[2,2048]{1,0:T(2,128)(2,1)S(1)}, bf16[2,2048]{1,0:T(2,128)(2,1)}, u32[]{:S(2)}) copy-start(bf16[2,2048]{1,0:T(2,128)(2,1)} %param.16) | copy-start | bytes 24580
  2.1 9.1 %copy-start.6 = (s32[2]{0:T(128)S(1)}, s32[2]{0:T(128)}, u32[]{:S(2)}) copy-start(s32[2]{0:T(128)} %param.28) | copy-start | bytes 28
  2.1 9.3 %copy-start.4 = (bf16[1536]{0:T(1024)(128)(2,1)S(1)}, bf16[1536]{0:T(1024)(128)(2,1)}, u32[]{:S(2)}) copy-start(bf16[1536]{0:T(1024)(128)(2,1)} %param.20) | copy-start | bytes 9220
  6.7 31.7 %collective-permute-start = (bf16[256,2048]{1,0:T(8,128)(2,1)}, bf16[256,2048]{1,0:T(8,128)(2,1)}, u32[]{:S(2)}, u32[]{:S(2)}) collective-permute-start(bf16[256,2048]{1,0:T(8,128)(2,1)} %fusion.20), channel_id=1, source_target_pairs={{0,2},{1,3},{2,0},{3,1},{4,6},{5,7},{6,4},{7,5},{8,10},{9,11},{10,... | collective-permute-start | bytes 3145736 | tf_op jit(solution)/shard_map/ppermute | solution.py:251
  9.6 34.7 %collective-permute-start.1 = (bf16[256,2048]{1,0:T(8,128)(2,1)}, bf16[256,2048]{1,0:T(8,128)(2,1)}, u32[]{:S(2)}, u32[]{:S(2)}) collective-permute-start(bf16[256,2048]{1,0:T(8,128)(2,1)} %fusion.20), channel_id=1, source_target_pairs={{0,1},{1,0},{2,3},{3,2},{4,5},{5,4},{6,7},{7,6},{8,9},{9,8},{10,11... | collective-permute-start | bytes 3145736 | tf_op jit(solution)/shard_map/ppermute | solution.py:254
  9.6 9.6 %collective-permute-start.3 = (bf16[2,2048]{1,0:T(2,128)(2,1)S(1)}, bf16[2,2048]{1,0:T(2,128)(2,1)S(1)}, u32[]{:S(2)}, u32[]{:S(2)}) collective-permute-start(bf16[2,2048]{1,0:T(2,128)(2,1)S(1)} %copy-done.3), channel_id=1, source_target_pairs={{0,4},{4,0},{8,12},{12,8},{16,20},{20,16},{24,28},{28,24},{1,5},{5... | collective-permute-start | bytes 24584 | tf_op jit(solution)/shard_map/ppermute | solution.py:200
  13.3 5.8 %copy-start.8 = (s32[16]{0:T(128)S(1)}, s32[16]{0:T(128)}, u32[]{:S(2)}) copy-start(s32[16]{0:T(128)} %param.29) | copy-start | bytes 196
  19.3 3.8 %collective-permute-start.4 = (bf16[4,2048]{1,0:T(4,128)(2,1)S(1)}, bf16[4,2048]{1,0:T(4,128)(2,1)S(1)}, u32[]{:S(2)}, u32[]{:S(2)}) collective-permute-start(bf16[4,2048]{1,0:T(4,128)(2,1)S(1)} %pad_maximum_fusion.4), channel_id=1, source_target_pairs={{0,8},{4,12},{8,0},{12,4},{16,24},{20,28},{24,16},{28,20},{1,9},{5... | collective-permute-start | bytes 49160 | tf_op jit(solution)/shard_map/ppermute | solution.py:200
  23.2 4.9 %collective-permute-start.5 = (bf16[8,2048]{1,0:T(8,128)(2,1)S(1)}, bf16[8,2048]{1,0:T(8,128)(2,1)S(1)}, u32[]{:S(2)}, u32[]{:S(2)}) collective-permute-start(bf16[8,2048]{1,0:T(8,128)(2,1)S(1)} %pad_maximum_fusion.1), channel_id=1, source_target_pairs={{0,16},{4,20},{8,24},{12,28},{16,0},{20,4},{24,8},{28,12},{1,17},{... | collective-permute-start | bytes 98312 | tf_op jit(solution)/shard_map/ppermute | solution.py:200
  25.8 6.7 %copy-start.7 = (f32[4]{0:T(128)}, f32[4]{0:T(128)S(1)}, u32[]{:S(2)}) copy-start(f32[4]{0:T(128)S(1)} %multiply_exponential_fusion.slopes_ref) | copy-start | bytes 52
  32.5 3.9 %copy-start.2 = (bf16[2,2048,512]{2,1,0:T(8,128)(2,1)S(1)}, bf16[2,2048,512]{2,1,0:T(8,128)(2,1)}, u32[]{:S(2)}) copy-start(bf16[2,2048,512]{2,1,0:T(8,128)(2,1)} %param.26) | copy-start | bytes 12582916
  36.4 1.6 %copy-start.1 = (bf16[512,2048]{1,0:T(8,128)(2,1)S(1)}, bf16[512,2048]{1,0:T(8,128)(2,1)}, u32[]{:S(2)}) copy-start(bf16[512,2048]{1,0:T(8,128)(2,1)} %param.21) | copy-start | bytes 6291460
  37.1 3.8 %copy-start.5 = (bf16[2048]{0:T(1024)(128)(2,1)S(1)}, bf16[2048]{0:T(1024)(128)(2,1)}, u32[]{:S(2)}) copy-start(bf16[2048]{0:T(1024)(128)(2,1)} %param.22) | copy-start | bytes 12292
  38.4 1.2 %collective-permute-start.6 = (f32[2,2048]{1,0:T(2,128)S(1)}, f32[2,2048]{1,0:T(2,128)S(1)}, u32[]{:S(2)}, u32[]{:S(2)}) collective-permute-start(f32[2,2048]{1,0:T(2,128)S(1)} %fusion.55), channel_id=1, source_target_pairs={{0,1},{1,0},{2,3},{3,2},{4,5},{5,4},{6,7},{7,6},{8,9},{9,8},{10,11... | collective-permute-start | bytes 49160 | tf_op jit(solution)/shard_map/ppermute | solution.py:233
  38.4 5.9 %collective-permute-start.2 = (bf16[256,2048]{1,0:T(8,128)(2,1)}, bf16[256,2048]{1,0:T(8,128)(2,1)}, u32[]{:S(2)}, u32[]{:S(2)}) collective-permute-start(bf16[256,2048]{1,0:T(8,128)(2,1)} %collective-permute-done), channel_id=1, source_target_pairs={{0,1},{1,0},{2,3},{3,2},{4,5},{5,4},{6,7},{7,6},{8,9},{9,8},{10,11... | collective-permute-start | bytes 3145736 | tf_op jit(solution)/shard_map/ppermute | solution.py:254
  39.6 4.0 %collective-permute-start.7 = (f32[4,2048]{1,0:T(4,128)S(1)}, f32[4,2048]{1,0:T(4,128)S(1)}, u32[]{:S(2)}, u32[]{:S(2)}) collective-permute-start(f32[4,2048]{1,0:T(4,128)S(1)} %pad_maximum_fusion.2), channel_id=1, source_target_pairs={{0,2},{1,3},{2,0},{3,1},{4,6},{5,7},{6,4},{7,5},{8,10},{9,11},{10,... | collective-permute-start | bytes 98312 | tf_op jit(solution)/shard_map/ppermute | solution.py:233
  43.7 9.2 %slice-start = ((s8[6291456]{0:T(1024)(128)(4,1)}), s8[4194304]{0:T(1024)(128)(4,1)S(1)}, s32[]{:S(2)}) async-start(s8[6291456]{0:T(1024)(128)(4,1)} %bitcast.48), calls=%async_computation | async-start | bytes 8388608
  43.7 9.1 %slice-start.1 = ((s8[6291456]{0:T(1024)(128)(4,1)}), s8[2097152]{0:T(1024)(128)(4,1)S(1)}, s32[]{:S(2)}) async-start(s8[6291456]{0:T(1024)(128)(4,1)} %bitcast.48), calls=%async_computation.1 | async-start | bytes 4194304
  43.7 46.7 %collective-permute-start.11 = (bf16[512,2048]{1,0:T(8,128)(2,1)S(1)}, bf16[512,2048]{1,0:T(8,128)(2,1)}, u32[]{:S(2)}, u32[]{:S(2)}) collective-permute-start(bf16[512,2048]{1,0:T(8,128)(2,1)S(1)} %copy-done.1), channel_id=1, source_target_pairs={{0,2},{1,3},{2,0},{3,1},{4,6},{5,7},{6,4},{7,5},{8,10},{9,11},{10,... | collective-permute-start | bytes 6291464 | tf_op jit(solution)/shard_map/ppermute | solution.py:256
  44.3 6.7 %collective-permute-start.8 = (bf16[2,2048]{1,0:T(2,128)(2,1)S(1)}, bf16[2,2048]{1,0:T(2,128)(2,1)S(1)}, u32[]{:S(2)}, u32[]{:S(2)}) collective-permute-start(bf16[2,2048]{1,0:T(2,128)(2,1)S(1)} %fusion.41), channel_id=1, source_target_pairs={{0,4},{4,0},{8,12},{12,8},{16,20},{20,16},{24,28},{28,24},{1,5},{5... | collective-permute-start | bytes 24584 | tf_op jit(solution)/shard_map/ppermute | solution.py:270
  51.0 5.7 %collective-permute-start.9 = (bf16[4,2048]{1,0:T(4,128)(2,1)S(1)}, bf16[4,2048]{1,0:T(4,128)(2,1)S(1)}, u32[]{:S(2)}, u32[]{:S(2)}) collective-permute-start(bf16[4,2048]{1,0:T(4,128)(2,1)S(1)} %pad_maximum_fusion.5), channel_id=1, source_target_pairs={{0,8},{4,12},{8,0},{12,4},{16,24},{20,28},{24,16},{28,20},{1,9},{5... | collective-permute-start | bytes 49160 | tf_op jit(solution)/shard_map/ppermute | solution.py:270
  56.8 6.8 %collective-permute-start.10 = (bf16[8,2048]{1,0:T(8,128)(2,1)S(1)}, bf16[8,2048]{1,0:T(8,128)(2,1)S(1)}, u32[]{:S(2)}, u32[]{:S(2)}) collective-permute-start(bf16[8,2048]{1,0:T(8,128)(2,1)S(1)} %pad_maximum_fusion.3), channel_id=1, source_target_pairs={{0,16},{4,20},{8,24},{12,28},{16,0},{20,4},{24,8},{28,12},{1,17},{... | collective-permute-start | bytes 98312 | tf_op jit(solution)/shard_map/ppermute | solution.py:270
  90.5 18.3 %collective-permute-start.16 = (bf16[512,2048]{1,0:T(8,128)(2,1)}, bf16[512,2048]{1,0:T(8,128)(2,1)S(1)}, u32[]{:S(2)}, u32[]{:S(2)}) collective-permute-start(bf16[512,2048]{1,0:T(8,128)(2,1)} %collective-permute-done.11), channel_id=1, source_target_pairs={{0,1},{1,0},{2,3},{3,2},{4,5},{5,4},{6,7},{7,6},{8,9},{9,8},{10,11... | collective-permute-start | bytes 6291464 | tf_op jit(solution)/shard_map/ppermute | solution.py:285
  90.5 19.0 %collective-permute-start.13 = (bf16[512,2048]{1,0:T(8,128)(2,1)S(1)}, bf16[512,2048]{1,0:T(8,128)(2,1)S(1)}, u32[]{:S(2)}, u32[]{:S(2)}) collective-permute-start(bf16[512,2048]{1,0:T(8,128)(2,1)S(1)} %copy-done.1), channel_id=1, source_target_pairs={{0,1},{1,0},{2,3},{3,2},{4,5},{5,4},{6,7},{7,6},{8,9},{9,8},{10,11... | collective-permute-start | bytes 6291464 | tf_op jit(solution)/shard_map/ppermute | solution.py:285
  92.1 16.6 %collective-permute-start.15 = (bf16[256,512]{1,0:T(8,128)(2,1)S(1)}, bf16[256,512]{1,0:T(8,128)(2,1)S(1)}, u32[]{:S(2)}, u32[]{:S(2)}) collective-permute-start(bf16[256,512]{1,0:T(8,128)(2,1)S(1)} %get-tuple-element.25), channel_id=1, source_target_pairs={{0,3},{1,2},{2,1},{3,0},{4,7},{5,6},{6,5},{7,4},{8,11},{9,10},{10,... | collective-permute-start | bytes 786440 | tf_op jit(solution)/shard_map/ppermute | solution.py:294
  92.3 14.1 %collective-permute-start.14 = (bf16[256,512]{1,0:T(8,128)(2,1)S(1)}, bf16[256,512]{1,0:T(8,128)(2,1)S(1)}, u32[]{:S(2)}, u32[]{:S(2)}) collective-permute-start(bf16[256,512]{1,0:T(8,128)(2,1)S(1)} %get-tuple-element.26), channel_id=1, source_target_pairs={{0,2},{1,3},{2,0},{3,1},{4,6},{5,7},{6,4},{7,5},{8,10},{9,11},{10,... | collective-permute-start | bytes 786440 | tf_op jit(solution)/shard_map/ppermute | solution.py:294
  93.8 15.6 %collective-permute-start.12 = (bf16[256,512]{1,0:T(8,128)(2,1)S(1)}, bf16[256,512]{1,0:T(8,128)(2,1)S(1)}, u32[]{:S(2)}, u32[]{:S(2)}) collective-permute-start(bf16[256,512]{1,0:T(8,128)(2,1)S(1)} %get-tuple-element.24), channel_id=1, source_target_pairs={{0,1},{1,0},{2,3},{3,2},{4,5},{5,4},{6,7},{7,6},{8,9},{9,8},{10,11... | collective-permute-start | bytes 786440 | tf_op jit(solution)/shard_map/ppermute | solution.py:294

commit v20 on v18

--- a/solution.py
+++ b/solution.py
@@ -130,8 +130,8 @@
             out_specs=pl.BlockSpec((tq, head_size), lambda h, i, p, s, place: (place[i], h)),
         ),
         cost_estimate=pl.CostEstimate(
-            flops=4 * heads * group * (group + cache_size) * head_size,
-            transcendentals=heads * group * (group + cache_size),
+            flops=4 * heads * tq * (group // tq * cache_size + tq * (group // tq) * (group // tq + 1) // 2) * head_size,
+            transcendentals=heads * tq * (group // tq * cache_size + tq * (group // tq) * (group // tq + 1) // 2),
             bytes_accessed=2 * (group * heads * 3 * head_size + 2 * cache_size * heads * head_size + group * heads * head_size),
         ),
     )(prefix, slopes, place, merged, merged, merged, cache_keys, cache_values)

time: 109 us -> 109 us (level)
  no operation moved by 1% of the time
where the time goes in v20:
time: 109 us
  matrix products  37.7 us (35%)
  Pallas kernels  23.4 us (21%)
  starting transfers between devices  18 us (17%)
  waiting for transfers between devices  17.1 us (16%)
  other arithmetic  7.9 us (7%)
  local copies, waits for them, and re-layouts  3.24 us (3%)
  between operations  1.59 us (1%)
    pallas_call x1, Pallas kernels, prefill_attention_kernel(): pl.pallas_call(functools.partial(_prefill_kernel, tq=tq), out_shape=jax.S...  23.4 us
    dot_general x4, matrix products, per_device(): jnp.dot(token_block, qkv_weight, preferred_element_type=jnp.float32)  19.9 us
    dot_general x4, matrix products, per_device(): summed = summed + jnp.dot(piece, weight, preferred_element_type=jnp.float32)  8.15 us
    ppermute x3, waiting for transfers between devices, per_device(): pieces.append(lax.ppermute(outgoing, 'tensor', route(k, flip)))  7.37 us
    ppermute x3, starting transfers between devices, per_device(): lax.ppermute(shifted_rows, 'dp', [(i, i ^ step) for i in range(dp_size)])  5.82 us
    ppermute x3, starting transfers between devices, per_device(): lax.ppermute(returned, 'dp', [(i, i ^ step) for i in range(dp_size)])  5.07 us
    ppermute x3, waiting for transfers between devices, per_device(): lax.ppermute(shifted_rows, 'dp', [(i, i ^ step) for i in range(dp_size)])  4.36 us
    dot_general x1, matrix products, per_device(): jnp.dot(normed_slots, qkv_weight, preferred_element_type=jnp.float32)  3.75 us
  transfers between devices with their start and end apart: 17, of which 7 were waited for; matrix products, arithmetic and copies ran while one was open for 36% of the time, Pallas kernels for 21%

profile of v20, /device:TPU:0, one launch (start us, length us, event | category | flops | bytes accessed | tf_op | source)
XLA Modules:
  0.0 108.9 jit_solution(5586039581077123543)
XLA Ops:
  0.6 0.0 copy-start
  0.6 0.8 convert_element_type.98
  1.4 0.7 convert_element_type.97
  2.1 1.6 %convert_reduce_fusion = f32[256]{0:T(256)S(1)} fusion(bf16[256,2048]{1,0:T(8,128)(2,1)} %param.15), kind=kLoop, calls=%fused_computation.1 | loop fusion | flops 1048320 | bytes 1049600 | tf_op jit(solution)/shard_map/reduce_sum | solution.py:20
  3.7 1.6 %fusion.17 = f32[256]{0:T(256)S(1)} fusion(bf16[256,2048]{1,0:T(8,128)(2,1)} %param.15, f32[256]{0:T(256)S(1)} %broadcast_multiply_fusion), kind=kLoop, calls=%fused_computation.30 | loop fusion | flops 2096896 | bytes 1050624 | tf_op jit(solution)/shard_map/reduce_sum | solution.py:21
  5.4 1.4 %fusion.20 = bf16[256,2048]{1,0:T(8,128)(2,1)} fusion(bf16[256,2048]{1,0:T(8,128)(2,1)S(1)} %copy-done, f32[2048]{0:T(1024)S(1)} %convert_element_type.98, f32[2048]{0:T(1024)S(1)} %convert_element_type.97, f32[256]{0:T(256)S(1)} %add_rsqrt_fusion, f32[256]{0:T(256)S(1)} %broadcast_multiply_fusion), kind=kLoop, calls=%fused_computation.33 | loop fusion | flops 3145728 | bytes 2115584 | tf_op jit(solution)/shard_map/convert_element_type | solution.py:23
  6.8 2.9 %collective-permute-start = (bf16[256,2048]{1,0:T(8,128)(2,1)}, bf16[256,2048]{1,0:T(8,128)(2,1)}, u32[]{:S(2)}, u32[]{:S(2)}) collective-permute-start(bf16[256,2048]{1,0:T(8,128)(2,1)} %fusion.20), channel_id=1, source_target_pairs={{0,2},{1,3},{2,0},{3,1},{4,6},{5,7},{6,4},{7,5},{8,10},{9,11},{10,... | collective-permute-start | bytes 3145736 | tf_op jit(solution)/shard_map/ppermute | solution.py:251
  9.8 0.0 collective-permute-start.1
  9.8 1.5 %collective-permute-start.3 = (bf16[2,2048]{1,0:T(2,128)(2,1)S(1)}, bf16[2,2048]{1,0:T(2,128)(2,1)S(1)}, u32[]{:S(2)}, u32[]{:S(2)}) collective-permute-start(bf16[2,2048]{1,0:T(2,128)(2,1)S(1)} %copy-done.3), channel_id=1, source_target_pairs={{0,4},{4,0},{8,12},{12,8},{16,20},{20,16},{24,28},{28,24},{1,5},{5... | collective-permute-start | bytes 24584 | tf_op jit(solution)/shard_map/ppermute | solution.py:200
  11.3 0.2 collective-permute-start.14
  11.5 0.1 subtract_convert_fusion
  11.6 0.1 iota_compare_fusion
  11.8 1.9 %broadcast_in_dim.54 = bf16[1024,1536]{1,0:T(8,128)(2,1)} broadcast(bf16[]{:T(256)} %constant.145.clone.1), dimensions={} | broadcast | bytes 3145730 | tf_op jit(solution)/shard_map/broadcast_in_dim | solution.py:258
  13.6 5.8 %fusion.3 = bf16[1024,1536]{1,0:T(8,128)(2,1)} fusion(bf16[1024,1536]{1,0:T(8,128)(2,1)} %broadcast_in_dim.54, s32[]{:T(128)S(6)} %select_n.124, bf16[256,2048]{1,0:T(8,128)(2,1)} %fusion.20, bf16[2048,1536]{1,0:T(8,128)(2,1)} %param.19, f32[1536]{0:T(1024)S(1)} %convert_element_type.100), kind=kOutput, calls=%fused_computation.12 | convolution fusion | flops 1611399168 | bytes 8132612 | tf_op jit(solution)/shard_map/dot_general | solution.py:263
  19.5 0.2 fusion.60
  19.6 0.0 collective-permute-done.3
  19.7 1.6 %collective-permute-start.4 = (bf16[4,2048]{1,0:T(4,128)(2,1)S(1)}, bf16[4,2048]{1,0:T(4,128)(2,1)S(1)}, u32[]{:S(2)}, u32[]{:S(2)}) collective-permute-start(bf16[4,2048]{1,0:T(4,128)(2,1)S(1)} %pad_maximum_fusion.4), channel_id=1, source_target_pairs={{0,8},{4,12},{8,0},{12,4},{16,24},{20,28},{24,16},{28,20},{1,9},{5... | collective-permute-start | bytes 49160 | tf_op jit(solution)/shard_map/ppermute | solution.py:200
  21.3 2.1 %collective-permute-done.4 = bf16[4,2048]{1,0:T(4,128)(2,1)S(1)} collective-permute-done((bf16[4,2048]{1,0:T(4,128)(2,1)S(1)}, bf16[4,2048]{1,0:T(4,128)(2,1)S(1)}, u32[]{:S(2)}, u32[]{:S(2)}) %collective-permute-start.4) | collective-permute-done | bytes 16416 | tf_op jit(solution)/shard_map/ppermute | solution.py:200
  23.5 2.7 %collective-permute-start.5 = (bf16[8,2048]{1,0:T(8,128)(2,1)S(1)}, bf16[8,2048]{1,0:T(8,128)(2,1)S(1)}, u32[]{:S(2)}, u32[]{:S(2)}) collective-permute-start(bf16[8,2048]{1,0:T(8,128)(2,1)S(1)} %pad_maximum_fusion.1), channel_id=1, source_target_pairs={{0,16},{4,20},{8,24},{12,28},{16,0},{20,4},{24,8},{28,12},{1,17},{... | collective-permute-start | bytes 98312 | tf_op jit(solution)/shard_map/ppermute | solution.py:200
  26.2 2.2 %collective-permute-done.5 = bf16[8,2048]{1,0:T(8,128)(2,1)S(1)} collective-permute-done((bf16[8,2048]{1,0:T(8,128)(2,1)S(1)}, bf16[8,2048]{1,0:T(8,128)(2,1)S(1)}, u32[]{:S(2)}, u32[]{:S(2)}) %collective-permute-start.5) | collective-permute-done | bytes 32800 | tf_op jit(solution)/shard_map/ppermute | solution.py:200
  28.4 0.3 fusion.79
  28.7 0.2 multiply_reduce_fusion
  28.9 3.8 %fusion.15 = bf16[2,1536]{1,0:T(2,128)(2,1)S(1)} fusion(bf16[2048,1536]{1,0:T(8,128)(2,1)} %param.19, f32[2,2048]{1,0:T(2,128)S(1)} %get-tuple-element.33, f32[2]{0:T(128)S(1)} %add_rsqrt_fusion.1, f32[2]{0:T(128)S(1)} %broadcast_multiply_fusion.1, f32[2048]{0:T(1024)S(1)} %convert_element_type.98, f32[2048]{0:T(1024)S(1)} %convert_element_type.97, ...), kind=kOutput, calls=%fused_computation.26 | convolution fusion | flops 12609536 | bytes 6336528 | tf_op jit(solution)/shard_map/dot_general | solution.py:214
  32.8 0.1 fusion.50
  32.9 3.6 %fusion.80 = (f32[2,4]{1,0:T(2,128)S(1)}, f32[2,4,2048]{2,1,0:T(4,128)S(1)}) fusion(f32[2,2048]{1,0:T(2,128)S(1)} %subtract_convert_fusion, f32[4]{0:T(128)S(1)} %multiply_exponential_fusion.slopes_ref, bf16[2,2048,512]{2,1,0:T(8,128)(2,1)} %param.25, pred[512,4]{0,1:T(4,128)(4,1)S(1)} %iota_compare_fusion.1, bf16[2,512]{1,0:T(2,128)(2,1)S(1)} %bitcast.51, ...), kind=kOutput, calls=%fused_computation.145 | convolution fusion | flops 16863224 | bytes 4284464 | tf_op jit(solution)/shard_map/vmap()/dot_general | solution.py:148
  36.5 0.2 fusion.37
  36.7 0.1 broadcast_bitcast_fusion
  36.8 0.7 fusion.21
  37.5 0.0 copy-start.5
  37.5 0.4 fusion.55
  37.9 0.0 collective-permute-start.6
  37.9 0.5 collective-permute-start.2
  38.4 0.5 fusion.63.place_ref
  38.9 0.1 collective-permute-done.6
  39.1 0.6 collective-permute-start.7
  39.7 0.1 fusion.65
  40.5 2.6 %collective-permute-done.7 = f32[4,2048]{1,0:T(4,128)S(1)} collective-permute-done((f32[4,2048]{1,0:T(4,128)S(1)}, f32[4,2048]{1,0:T(4,128)S(1)}, u32[]{:S(2)}, u32[]{:S(2)}) %collective-permute-start.7) | collective-permute-done | bytes 32800 | tf_op jit(solution)/shard_map/ppermute | solution.py:233
  43.1 0.0 slice-start
  43.2 0.0 slice-start.1
  43.2 0.6 collective-permute-start.11
  43.8 0.0 collective-permute-done.1
  43.8 0.0 collective-permute-done.2
  43.8 0.4 collective-permute-start.8
  44.3 6.3 %fusion.5 = bf16[1024,1536]{1,0:T(8,128)(2,1)} fusion(bf16[1024,1536]{1,0:T(8,128)(2,1)} %fusion.3, s32[]{:T(128)S(6)} %select_n.126, bf16[256,2048]{1,0:T(8,128)(2,1)} %collective-permute-done, bf16[2048,1536]{1,0:T(8,128)(2,1)} %param.19, f32[1536]{0:T(1024)S(1)} %convert_element_type.100), kind=kOutput, calls=%fused_computation.14 | convolution fusion | flops 1611399168 | bytes 8132612 | tf_op jit(solution)/shard_map/dot_general | solution.py:263
  50.6 1.7 %collective-permute-start.9 = (bf16[4,2048]{1,0:T(4,128)(2,1)S(1)}, bf16[4,2048]{1,0:T(4,128)(2,1)S(1)}, u32[]{:S(2)}, u32[]{:S(2)}) collective-permute-start(bf16[4,2048]{1,0:T(4,128)(2,1)S(1)} %pad_maximum_fusion.5), channel_id=1, source_target_pairs={{0,8},{4,12},{8,0},{12,4},{16,24},{20,28},{24,16},{28,20},{1,9},{5... | collective-permute-start | bytes 49160 | tf_op jit(solution)/shard_map/ppermute | solution.py:270
  52.3 3.9 %fusion.7 = bf16[1024,1536]{1,0:T(8,128)(2,1)} fusion(bf16[1024,1536]{1,0:T(8,128)(2,1)} %fusion.5, s32[]{:T(128)S(6)} %select_n.138, bf16[256,2048]{1,0:T(8,128)(2,1)} %collective-permute-done.1, bf16[2048,1536]{1,0:T(8,128)(2,1)S(1)} %bitcast.49, f32[1536]{0:T(1024)S(1)} %convert_element_type.100), kind=kOutput, calls=%fused_computation.16 | convolution fusion | flops 1611399168 | bytes 8132612 | tf_op jit(solution)/shard_map/dot_general | solution.py:263
  56.3 0.0 collective-permute-done.9
  56.3 2.9 %collective-permute-start.10 = (bf16[8,2048]{1,0:T(8,128)(2,1)S(1)}, bf16[8,2048]{1,0:T(8,128)(2,1)S(1)}, u32[]{:S(2)}, u32[]{:S(2)}) collective-permute-start(bf16[8,2048]{1,0:T(8,128)(2,1)S(1)} %pad_maximum_fusion.3), channel_id=1, source_target_pairs={{0,16},{4,20},{8,24},{12,28},{16,0},{20,4},{24,8},{28,12},{1,17},{... | collective-permute-start | bytes 98312 | tf_op jit(solution)/shard_map/ppermute | solution.py:270
  59.2 3.9 %fusion.9.q_ref.kn_ref.vn_ref = bf16[1024,1536]{1,0:T(8,128)(2,1)} fusion(bf16[1024,1536]{1,0:T(8,128)(2,1)} %fusion.7, s32[]{:T(128)S(6)} %select_n.139, bf16[256,2048]{1,0:T(8,128)(2,1)} %collective-permute-done.2, bf16[2048,1536]{1,0:T(8,128)(2,1)S(1)} %bitcast.49, f32[1536]{0:T(1024)S(1)} %convert_element_type.100), kind=kOutput, calls=%fused_computation.18 | convolution fusion | flops 1611399168 | bytes 8132612 | tf_op jit(solution)/shard_map/dot_general | solution.py:263
  63.1 0.8 convolution_convert_fusion
  63.9 23.4 %shard_map.158 = bf16[1024,512]{1,0:T(8,128)(2,1)} custom-call(s32[1]{0:T(128)S(6)} %copy.39.prefix_ref, f32[4]{0:T(128)} %copy-done.7, s32[4]{0:T(128)} %fusion.63.place_ref, bf16[1024,1536]{1,0:T(8,128)(2,1)} %fusion.9.q_ref.kn_ref.vn_ref, bf16[1024,1536]{1,0:T(8,128)(2,1)} %fusion.9.q_ref.kn_ref.vn_ref, bf16[1024,1536]{1,0:T(8,128)(2,1)} %fusion.9.q_ref.kn_ref.vn_ref, ...), custom_call_target="tpu_custom_call" | custom-call | flops 3489660928 | bytes 6291456 | tf_op jit(solution)/shard_map/pallas_call | solution.py:117
  87.3 2.6 %collective-permute-done.11 = bf16[512,2048]{1,0:T(8,128)(2,1)} collective-permute-done((bf16[512,2048]{1,0:T(8,128)(2,1)S(1)}, bf16[512,2048]{1,0:T(8,128)(2,1)}, u32[]{:S(2)}, u32[]{:S(2)}) %collective-permute-start.11) | collective-permute-done | bytes 2097184 | tf_op jit(solution)/shard_map/ppermute | solution.py:256
  89.9 0.0 collective-permute-start.16
  89.9 1.2 %fusion.77 = (bf16[256,512]{1,0:T(8,128)(2,1)S(1)}, bf16[256,512]{1,0:T(8,128)(2,1)S(1)}, bf16[256,512]{1,0:T(8,128)(2,1)S(1)}) fusion(bf16[1024,512]{1,0:T(8,128)(2,1)} %shard_map.158), kind=kLoop, calls=%fused_computation.142 | loop fusion | bytes 1572864 | tf_op jit(solution)/shard_map/slice | solution.py:290
  91.1 0.7 collective-permute-start.15
  91.8 0.0 collective-permute-start.13
  91.8 1.5 %collective-permute-start.12 = (bf16[256,512]{1,0:T(8,128)(2,1)S(1)}, bf16[256,512]{1,0:T(8,128)(2,1)S(1)}, u32[]{:S(2)}, u32[]{:S(2)}) collective-permute-start(bf16[256,512]{1,0:T(8,128)(2,1)S(1)} %get-tuple-element.24), channel_id=1, source_target_pairs={{0,2},{1,3},{2,0},{3,1},{4,6},{5,7},{6,4},{7,5},{8,10},{9,11},{10,... | collective-permute-start | bytes 786440 | tf_op jit(solution)/shard_map/ppermute | solution.py:294
  93.3 1.7 %convolution_add_fusion.1 = f32[256,2048]{1,0:T(8,128)S(1)} fusion(bf16[512,2048]{1,0:T(8,128)(2,1)S(1)} %copy-done.1, bf16[256,2048]{1,0:T(8,128)(2,1)S(1)} %copy-done, f32[2048]{0:T(1024)S(1)} %convert_element_type.95, bf16[1024,512]{1,0:T(8,128)(2,1)} %shard_map.158), kind=kOutput, calls=%fused_computation.5 | convolution fusion | flops 538443776 | bytes 5513216 | tf_op jit(solution)/shard_map/dot_general | solution.py:297
  95.0 0.0 collective-permute-done.13
  95.0 2.3 %fusion.81 = f32[256,2048]{1,0:T(8,128)S(1)} fusion(bf16[256,512]{1,0:T(8,128)(2,1)S(1)} %collective-permute-done.13, bf16[512,2048]{1,0:T(8,128)(2,1)} %collective-permute-done.14), kind=kOutput, calls=%fused_computation.146 | convolution fusion | flops 536870912 | bytes 4456448 | tf_op jit(solution)/shard_map/dot_general | solution.py:297
  97.3 1.8 %collective-permute-done.15 = bf16[256,512]{1,0:T(8,128)(2,1)S(1)} collective-permute-done((bf16[256,512]{1,0:T(8,128)(2,1)S(1)}, bf16[256,512]{1,0:T(8,128)(2,1)S(1)}, u32[]{:S(2)}, u32[]{:S(2)}) %collective-permute-start.15) | collective-permute-done | bytes 262176 | tf_op jit(solution)/shard_map/ppermute | solution.py:294
  99.1 0.7 fusion.82
  99.8 5.5 %collective-permute-done.12 = bf16[256,512]{1,0:T(8,128)(2,1)S(1)} collective-permute-done((bf16[256,512]{1,0:T(8,128)(2,1)S(1)}, bf16[256,512]{1,0:T(8,128)(2,1)S(1)}, u32[]{:S(2)}, u32[]{:S(2)}) %collective-permute-start.12) | collective-permute-done | bytes 262176 | tf_op jit(solution)/shard_map/ppermute | solution.py:294
  105.4 3.5 %fusion.10 = bf16[256,2048]{1,0:T(8,128)(2,1)} fusion(f32[256,2048]{1,0:T(8,128)S(1)} %fusion.82, f32[256,2048]{1,0:T(8,128)S(1)} %fusion.81, f32[256,2048]{1,0:T(8,128)S(1)} %convolution_add_fusion.1, bf16[256,512]{1,0:T(8,128)(2,1)S(1)} %collective-permute-done.12, bf16[512,2048]{1,0:T(8,128)(2,1)} %collective-permute-done.11), kind=kOutput, calls=%fused_computation.19 | convolution fusion | flops 538968064 | bytes 9699328 | tf_op jit(solution)/shard_map/dot_general | solution.py:297
  (50 shorter events, 0.5 us)
Async XLA Ops:
  0.6 4.8 %copy-start = (bf16[256,2048]{1,0:T(8,128)(2,1)S(1)}, bf16[256,2048]{1,0:T(8,128)(2,1)}, u32[]{:S(2)}) copy-start(bf16[256,2048]{1,0:T(8,128)(2,1)} %param.15) | copy-start | bytes 3145732
  2.1 7.7 %copy-start.3 = (bf16[2,2048]{1,0:T(2,128)(2,1)S(1)}, bf16[2,2048]{1,0:T(2,128)(2,1)}, u32[]{:S(2)}) copy-start(bf16[2,2048]{1,0:T(2,128)(2,1)} %param.16) | copy-start | bytes 24580
  2.1 9.2 %copy-start.1 = (bf16[512,2048]{1,0:T(8,128)(2,1)S(1)}, bf16[512,2048]{1,0:T(8,128)(2,1)}, u32[]{:S(2)}) copy-start(bf16[512,2048]{1,0:T(8,128)(2,1)} %param.21) | copy-start | bytes 6291460
  2.1 9.4 %copy-start.6 = (s32[2]{0:T(128)S(1)}, s32[2]{0:T(128)}, u32[]{:S(2)}) copy-start(s32[2]{0:T(128)} %param.28) | copy-start | bytes 28
  2.1 9.6 %copy-start.4 = (bf16[1536]{0:T(1024)(128)(2,1)S(1)}, bf16[1536]{0:T(1024)(128)(2,1)}, u32[]{:S(2)}) copy-start(bf16[1536]{0:T(1024)(128)(2,1)} %param.20) | copy-start | bytes 9220
  6.8 31.1 %collective-permute-start = (bf16[256,2048]{1,0:T(8,128)(2,1)}, bf16[256,2048]{1,0:T(8,128)(2,1)}, u32[]{:S(2)}, u32[]{:S(2)}) collective-permute-start(bf16[256,2048]{1,0:T(8,128)(2,1)} %fusion.20), channel_id=1, source_target_pairs={{0,2},{1,3},{2,0},{3,1},{4,6},{5,7},{6,4},{7,5},{8,10},{9,11},{10,... | collective-permute-start | bytes 3145736 | tf_op jit(solution)/shard_map/ppermute | solution.py:251
  9.8 34.1 %collective-permute-start.1 = (bf16[256,2048]{1,0:T(8,128)(2,1)}, bf16[256,2048]{1,0:T(8,128)(2,1)}, u32[]{:S(2)}, u32[]{:S(2)}) collective-permute-start(bf16[256,2048]{1,0:T(8,128)(2,1)} %fusion.20), channel_id=1, source_target_pairs={{0,1},{1,0},{2,3},{3,2},{4,5},{5,4},{6,7},{7,6},{8,9},{9,8},{10,11... | collective-permute-start | bytes 3145736 | tf_op jit(solution)/shard_map/ppermute | solution.py:254
  9.8 9.9 %collective-permute-start.3 = (bf16[2,2048]{1,0:T(2,128)(2,1)S(1)}, bf16[2,2048]{1,0:T(2,128)(2,1)S(1)}, u32[]{:S(2)}, u32[]{:S(2)}) collective-permute-start(bf16[2,2048]{1,0:T(2,128)(2,1)S(1)} %copy-done.3), channel_id=1, source_target_pairs={{0,4},{4,0},{8,12},{12,8},{16,20},{20,16},{24,28},{28,24},{1,5},{5... | collective-permute-start | bytes 24584 | tf_op jit(solution)/shard_map/ppermute | solution.py:200
  11.3 83.7 %collective-permute-start.14 = (bf16[512,2048]{1,0:T(8,128)(2,1)S(1)}, bf16[512,2048]{1,0:T(8,128)(2,1)}, u32[]{:S(2)}, u32[]{:S(2)}) collective-permute-start(bf16[512,2048]{1,0:T(8,128)(2,1)S(1)} %copy-done.1), channel_id=1, source_target_pairs={{0,1},{1,0},{2,3},{3,2},{4,5},{5,4},{6,7},{7,6},{8,9},{9,8},{10,11... | collective-permute-start | bytes 6291464 | tf_op jit(solution)/shard_map/ppermute | solution.py:285
  13.6 5.8 %copy-start.8 = (s32[16]{0:T(128)S(1)}, s32[16]{0:T(128)}, u32[]{:S(2)}) copy-start(s32[16]{0:T(128)} %param.29) | copy-start | bytes 196
  19.7 3.8 %collective-permute-start.4 = (bf16[4,2048]{1,0:T(4,128)(2,1)S(1)}, bf16[4,2048]{1,0:T(4,128)(2,1)S(1)}, u32[]{:S(2)}, u32[]{:S(2)}) collective-permute-start(bf16[4,2048]{1,0:T(4,128)(2,1)S(1)} %pad_maximum_fusion.4), channel_id=1, source_target_pairs={{0,8},{4,12},{8,0},{12,4},{16,24},{20,28},{24,16},{28,20},{1,9},{5... | collective-permute-start | bytes 49160 | tf_op jit(solution)/shard_map/ppermute | solution.py:200
  23.5 4.9 %collective-permute-start.5 = (bf16[8,2048]{1,0:T(8,128)(2,1)S(1)}, bf16[8,2048]{1,0:T(8,128)(2,1)S(1)}, u32[]{:S(2)}, u32[]{:S(2)}) collective-permute-start(bf16[8,2048]{1,0:T(8,128)(2,1)S(1)} %pad_maximum_fusion.1), channel_id=1, source_target_pairs={{0,16},{4,20},{8,24},{12,28},{16,0},{20,4},{24,8},{28,12},{1,17},{... | collective-permute-start | bytes 98312 | tf_op jit(solution)/shard_map/ppermute | solution.py:200
  26.2 6.7 %copy-start.7 = (f32[4]{0:T(128)}, f32[4]{0:T(128)S(1)}, u32[]{:S(2)}) copy-start(f32[4]{0:T(128)S(1)} %multiply_exponential_fusion.slopes_ref) | copy-start | bytes 52
  32.8 3.9 %copy-start.2 = (bf16[2,2048,512]{2,1,0:T(8,128)(2,1)S(1)}, bf16[2,2048,512]{2,1,0:T(8,128)(2,1)}, u32[]{:S(2)}) copy-start(bf16[2,2048,512]{2,1,0:T(8,128)(2,1)} %param.26) | copy-start | bytes 12582916
  37.5 3.0 %copy-start.5 = (bf16[2048]{0:T(1024)(128)(2,1)S(1)}, bf16[2048]{0:T(1024)(128)(2,1)}, u32[]{:S(2)}) copy-start(bf16[2048]{0:T(1024)(128)(2,1)} %param.22) | copy-start | bytes 12292
  37.9 1.2 %collective-permute-start.6 = (f32[2,2048]{1,0:T(2,128)S(1)}, f32[2,2048]{1,0:T(2,128)S(1)}, u32[]{:S(2)}, u32[]{:S(2)}) collective-permute-start(f32[2,2048]{1,0:T(2,128)S(1)} %fusion.55), channel_id=1, source_target_pairs={{0,1},{1,0},{2,3},{3,2},{4,5},{5,4},{6,7},{7,6},{8,9},{9,8},{10,11... | collective-permute-start | bytes 49160 | tf_op jit(solution)/shard_map/ppermute | solution.py:233
  37.9 5.9 %collective-permute-start.2 = (bf16[256,2048]{1,0:T(8,128)(2,1)}, bf16[256,2048]{1,0:T(8,128)(2,1)}, u32[]{:S(2)}, u32[]{:S(2)}) collective-permute-start(bf16[256,2048]{1,0:T(8,128)(2,1)} %collective-permute-done), channel_id=1, source_target_pairs={{0,1},{1,0},{2,3},{3,2},{4,5},{5,4},{6,7},{7,6},{8,9},{9,8},{10,11... | collective-permute-start | bytes 3145736 | tf_op jit(solution)/shard_map/ppermute | solution.py:254
  39.1 4.0 %collective-permute-start.7 = (f32[4,2048]{1,0:T(4,128)S(1)}, f32[4,2048]{1,0:T(4,128)S(1)}, u32[]{:S(2)}, u32[]{:S(2)}) collective-permute-start(f32[4,2048]{1,0:T(4,128)S(1)} %pad_maximum_fusion.2), channel_id=1, source_target_pairs={{0,2},{1,3},{2,0},{3,1},{4,6},{5,7},{6,4},{7,5},{8,10},{9,11},{10,... | collective-permute-start | bytes 98312 | tf_op jit(solution)/shard_map/ppermute | solution.py:233
  43.1 9.2 %slice-start = ((s8[6291456]{0:T(1024)(128)(4,1)}), s8[4194304]{0:T(1024)(128)(4,1)S(1)}, s32[]{:S(2)}) async-start(s8[6291456]{0:T(1024)(128)(4,1)} %bitcast.48), calls=%async_computation | async-start | bytes 8388608
  43.2 9.1 %slice-start.1 = ((s8[6291456]{0:T(1024)(128)(4,1)}), s8[2097152]{0:T(1024)(128)(4,1)S(1)}, s32[]{:S(2)}) async-start(s8[6291456]{0:T(1024)(128)(4,1)} %bitcast.48), calls=%async_computation.1 | async-start | bytes 4194304
  43.2 46.7 %collective-permute-start.11 = (bf16[512,2048]{1,0:T(8,128)(2,1)S(1)}, bf16[512,2048]{1,0:T(8,128)(2,1)}, u32[]{:S(2)}, u32[]{:S(2)}) collective-permute-start(bf16[512,2048]{1,0:T(8,128)(2,1)S(1)} %copy-done.1), channel_id=1, source_target_pairs={{0,2},{1,3},{2,0},{3,1},{4,6},{5,7},{6,4},{7,5},{8,10},{9,11},{10,... | collective-permute-start | bytes 6291464 | tf_op jit(solution)/shard_map/ppermute | solution.py:256
  43.8 6.7 %collective-permute-start.8 = (bf16[2,2048]{1,0:T(2,128)(2,1)S(1)}, bf16[2,2048]{1,0:T(2,128)(2,1)S(1)}, u32[]{:S(2)}, u32[]{:S(2)}) collective-permute-start(bf16[2,2048]{1,0:T(2,128)(2,1)S(1)} %fusion.41), channel_id=1, source_target_pairs={{0,4},{4,0},{8,12},{12,8},{16,20},{20,16},{24,28},{28,24},{1,5},{5... | collective-permute-start | bytes 24584 | tf_op jit(solution)/shard_map/ppermute | solution.py:270
  50.6 5.7 %collective-permute-start.9 = (bf16[4,2048]{1,0:T(4,128)(2,1)S(1)}, bf16[4,2048]{1,0:T(4,128)(2,1)S(1)}, u32[]{:S(2)}, u32[]{:S(2)}) collective-permute-start(bf16[4,2048]{1,0:T(4,128)(2,1)S(1)} %pad_maximum_fusion.5), channel_id=1, source_target_pairs={{0,8},{4,12},{8,0},{12,4},{16,24},{20,28},{24,16},{28,20},{1,9},{5... | collective-permute-start | bytes 49160 | tf_op jit(solution)/shard_map/ppermute | solution.py:270
  56.3 6.8 %collective-permute-start.10 = (bf16[8,2048]{1,0:T(8,128)(2,1)S(1)}, bf16[8,2048]{1,0:T(8,128)(2,1)S(1)}, u32[]{:S(2)}, u32[]{:S(2)}) collective-permute-start(bf16[8,2048]{1,0:T(8,128)(2,1)S(1)} %pad_maximum_fusion.3), channel_id=1, source_target_pairs={{0,16},{4,20},{8,24},{12,28},{16,0},{20,4},{24,8},{28,12},{1,17},{... | collective-permute-start | bytes 98312 | tf_op jit(solution)/shard_map/ppermute | solution.py:270
  89.9 9.2 %collective-permute-start.16 = (bf16[512,2048]{1,0:T(8,128)(2,1)}, bf16[512,2048]{1,0:T(8,128)(2,1)S(1)}, u32[]{:S(2)}, u32[]{:S(2)}) collective-permute-start(bf16[512,2048]{1,0:T(8,128)(2,1)} %collective-permute-done.11), channel_id=1, source_target_pairs={{0,1},{1,0},{2,3},{3,2},{4,5},{5,4},{6,7},{7,6},{8,9},{9,8},{10,11... | collective-permute-start | bytes 6291464 | tf_op jit(solution)/shard_map/ppermute | solution.py:285
  91.1 8.0 %collective-permute-start.15 = (bf16[256,512]{1,0:T(8,128)(2,1)S(1)}, bf16[256,512]{1,0:T(8,128)(2,1)S(1)}, u32[]{:S(2)}, u32[]{:S(2)}) collective-permute-start(bf16[256,512]{1,0:T(8,128)(2,1)S(1)} %get-tuple-element.25), channel_id=1, source_target_pairs={{0,3},{1,2},{2,1},{3,0},{4,7},{5,6},{6,5},{7,4},{8,11},{9,10},{10,... | collective-permute-start | bytes 786440 | tf_op jit(solution)/shard_map/ppermute | solution.py:294
  91.8 3.2 %collective-permute-start.13 = (bf16[256,512]{1,0:T(8,128)(2,1)S(1)}, bf16[256,512]{1,0:T(8,128)(2,1)S(1)}, u32[]{:S(2)}, u32[]{:S(2)}) collective-permute-start(bf16[256,512]{1,0:T(8,128)(2,1)S(1)} %get-tuple-element.26), channel_id=1, source_target_pairs={{0,1},{1,0},{2,3},{3,2},{4,5},{5,4},{6,7},{7,6},{8,9},{9,8},{10,11... | collective-permute-start | bytes 786440 | tf_op jit(solution)/shard_map/ppermute | solution.py:294
  91.8 13.6 %collective-permute-start.12 = (bf16[256,512]{1,0:T(8,128)(2,1)S(1)}, bf16[256,512]{1,0:T(8,128)(2,1)S(1)}, u32[]{:S(2)}, u32[]{:S(2)}) collective-permute-start(bf16[256,512]{1,0:T(8,128)(2,1)S(1)} %get-tuple-element.24), channel_id=1, source_target_pairs={{0,2},{1,3},{2,0},{3,1},{4,6},{5,7},{6,4},{7,5},{8,10},{9,11},{10,... | collective-permute-start | bytes 786440 | tf_op jit(solution)/shard_map/ppermute | solution.py:294
